TPU v7x, 128 devices: a whole 4x4x4 slice. The times are simulated.
128 devices in a mesh: wide: 32 (over x, y, core), rep: 4 (over z).
Axes of the slice: x: 4, y: 4, z: 4, core: 2. Of those that a mesh axis runs over, the one named last changes fastest.
Arguments:
- passages: bfloat16 [131072, 1024], P(('wide', 'rep')), may hold values from -6 to 6
- cluster_ids: int32 [131072], P(('wide', 'rep')), may hold values from 0 to 524287, as said below
- w_first: bfloat16 [1024, 1024], replicated, may hold values from -0.1875 to 0.1875
- w_second: bfloat16 [1024, 256], replicated, may hold values from -0.1875 to 0.1875
- centroids: bfloat16 [524288, 256], P('wide'), may hold values from -6 to 6
Outputs:
- refreshed: bfloat16 [524288, 256], P(('wide', 'rep'))
- residuals: bfloat16 [131072, 256], P(('wide', 'rep'))
Inputs may be any that keep to these rules, and one draw needn't show every extreme that they name: The owner of a passage is cluster_ids // 16384. Among the 1024 rows of one device (aligned blocks), at most 96 have any one owner; in every draw one owner gets exactly 96 rows from every device's block.
All inputs are finite; a program needn't handle non-finite values.
Results may differ from a plain program's by a relative error of at most 0.015.
Values may be sent and summed in bfloat16 or wider, within the bound.
No kernel may reach another device: no remote copies, remote signals or barrier semaphores. Data moves between devices by JAX's collectives and lax.ppermute only.
A program may use at most 128 MiB of HBM per device.

v0:
```python
import jax
import jax.numpy as jnp
from jax import lax
from jax.sharding import PartitionSpec as P


def normalize(updated):
    return (
        updated * lax.rsqrt(jnp.mean(updated * updated, axis=-1, keepdims=True) + 1e-06)
    ).astype(jnp.bfloat16)


def match_sums(queries, keys, rows, block_rows=1024):
    count = queries.shape[0]
    padded = -(-count // block_rows) * block_rows
    blocks = jnp.pad(queries, (0, padded - count), constant_values=-1).reshape(-1, block_rows)

    def one_block(block_ids):
        selector = (block_ids[:, None] == keys[None, :]).astype(jnp.bfloat16)
        return jnp.dot(selector, rows, preferred_element_type=jnp.float32)

    return lax.map(one_block, blocks).reshape(padded, -1)[:count]


def body(passages, cluster_ids, w_first, w_second, centroids):
    tok_rows = passages.shape[0]
    owners = lax.axis_size("wide")
    replicas = lax.axis_size("rep")
    cent_rows = centroids.shape[0]
    share_rows = cent_rows // replicas
    capacity = 3 * tok_rows // owners
    slots = owners * capacity
    my_rep = lax.axis_index("rep")

    owner_of = cluster_ids // cent_rows
    local_id = cluster_ids - owner_of * cent_rows
    member = owner_of[:, None] == jnp.arange(owners, dtype=jnp.int32)[None, :]
    row = jnp.arange(tok_rows, dtype=jnp.int32)
    earlier = (row[:, None] > row[None, :]).astype(jnp.bfloat16)
    before = jnp.dot(earlier, member.astype(jnp.bfloat16), preferred_element_type=jnp.float32)
    slot_of = jnp.sum(jnp.where(member, before, 0.0), axis=1).astype(jnp.int32)
    target = owner_of * capacity + slot_of
    place = target[None, :] == jnp.arange(slots, dtype=jnp.int32)[:, None]
    place_bf = place.astype(jnp.bfloat16)
    out_ids = jnp.sum(jnp.where(place, local_id[None, :], 0), axis=1)

    hidden = jax.nn.gelu(
        jnp.dot(passages, w_first, preferred_element_type=jnp.float32), approximate=True
    ).astype(jnp.bfloat16)
    projected = jnp.dot(hidden, w_second, preferred_element_type=jnp.float32)
    embedded = (
        projected * lax.rsqrt(jnp.mean(projected * projected, axis=-1, keepdims=True) + 1e-06)
    ).astype(jnp.bfloat16)

    outgoing = jnp.dot(place_bf, embedded, preferred_element_type=jnp.float32).astype(jnp.bfloat16)
    emb_width = outgoing.shape[1]
    incoming = lax.all_to_all(outgoing, "wide", split_axis=0, concat_axis=0, tiled=True)
    in_ids = lax.all_to_all(out_ids, "wide", split_axis=0, concat_axis=0, tiled=True)

    code_rows = -(-2 * slots // emb_width)
    code_rows = -(-code_rows // 16) * 16
    id_code = jnp.concatenate([in_ids // 128, in_ids % 128]).astype(jnp.bfloat16)
    id_code = jnp.pad(id_code, (0, code_rows * emb_width - 2 * slots))
    payload = jnp.concatenate([incoming, id_code.reshape(code_rows, emb_width)])
    rows_all = lax.all_gather(payload, "rep", axis=0)
    code = rows_all[:, slots:].reshape(replicas, -1)[:, : 2 * slots].astype(jnp.int32)
    keys = code[:, :slots] * 128 + code[:, slots:]
    keys = jnp.pad(keys, ((0, 0), (0, code_rows)), constant_values=-1).reshape(-1)
    rows = rows_all.reshape(-1, emb_width)

    first_row = my_rep * share_rows
    share_ids = first_row + jnp.arange(share_rows, dtype=jnp.int32)
    look_cent = centroids[in_ids].astype(jnp.float32)
    own_cent = lax.dynamic_slice_in_dim(centroids, first_row, share_rows, 0).astype(jnp.float32)

    look_sum = match_sums(in_ids, keys, rows)
    picked = normalize(look_cent + look_sum)
    returned = lax.all_to_all(picked, "wide", split_axis=0, concat_axis=0, tiled=True)

    share_sum = match_sums(share_ids, keys, rows)
    own_rows = normalize(own_cent + share_sum)

    gathered_rows = jnp.dot(place_bf.T, returned, preferred_element_type=jnp.float32)
    residuals = (embedded.astype(jnp.float32) - gathered_rows).astype(jnp.bfloat16)
    return (own_rows, residuals)


def solution(mesh):
    return jax.shard_map(
        body,
        mesh=mesh,
        in_specs=(P(("wide", "rep"), None), P(("wide", "rep")), P(), P(), P("wide", None)),
        out_specs=(P(("wide", "rep"), None), P(("wide", "rep"), None)),
        check_vma=False,
    )
```

profile of v0, /device:TPU:1, one launch (start us, length us, event | category | flops | bytes accessed | tf_op | source)
XLA Modules:
  0.0 238.2 jit_solution(11460072286577327346)
XLA Ops:
  7.2 0.8 add_select_fusion.2
  8.6 0.7 convert_add_fusion
  9.3 1.3 select_reduce_fusion
  10.6 0.7 all_to_all.27
  11.3 8.6 %all-to-all-start.1 = ((s32[32,96,1]{1,2,0:T(1,128)}), s32[32,96,1]{1,2,0:T(1,128)S(1)}, u32[]{:S(2)}, u32[]{:S(2)}) async-start(s32[32,96,1]{1,2,0:T(1,128)} %all_to_all.27), calls=%async_computation.1 | async-start | bytes 32768 | tf_op jit(solution)/shard_map/all_to_all | solution.py:58
  19.9 5.0 %multiply_reduce_fusion.2 = (f32[1024]{0:T(1024)S(1)}, f32[1024,256]{0,1:T(8,128)S(1)}) fusion(bf16[1024,256]{1,0:T(8,128)(2,1)} %param.12, bf16[1024,1024]{1,0:T(8,128)(2,1)S(1)} %copy-done, bf16[1024,1024]{1,0:T(8,128)(2,1)} %param.11), kind=kOutput, calls=%fused_computation.45 | convolution fusion | flops 2694315008 | bytes 5771264 | tf_op jit(solution)/shard_map/dot_general | solution.py:50
  24.9 0.6 copy-done.2
  25.6 3.6 %fusion.33 = bf16[3072,256]{1,0:T(8,128)(2,1)} fusion(s32[1024]{0:T(1024)S(1)} %get-tuple-element.86, f32[1024,256]{0,1:T(8,128)S(1)} %get-tuple-element.89, f32[1024]{0:T(1024)S(1)} %add_rsqrt_fusion.2), kind=kOutput, calls=%fused_computation.35 | convolution fusion | flops 1615069184 | bytes 2629632 | tf_op jit(solution)/shard_map/dot_general | solution.py:55
  29.2 7.4 %all-to-all-start = ((bf16[32,96,256]{2,1,0:T(8,128)(2,1)}), bf16[32,96,256]{2,1,0:T(8,128)(2,1)}, u32[]{:S(2)}, u32[]{:S(2)}) async-start(bf16[32,96,256]{2,1,0:T(8,128)(2,1)} %bitcast.50), calls=%async_computation | async-start | bytes 3145728 | tf_op jit(solution)/shard_map/all_to_all | solution.py:57
  37.4 0.6 reduce.8
  38.1 21.3 %all-to-all-done = bf16[32,96,256]{2,1,0:T(8,128)(2,1)} async-done(((bf16[32,96,256]{2,1,0:T(8,128)(2,1)}), bf16[32,96,256]{2,1,0:T(8,128)(2,1)}, u32[]{:S(2)}, u32[]{:S(2)}) %all-to-all-start) | async-done | bytes 1572896 | tf_op jit(solution)/shard_map/all_to_all | solution.py:57
  59.4 2.7 %pad_maximum_fusion = bf16[3104,256]{1,0:T(8,128)(2,1)} fusion(bf16[32,256]{1,0:T(8,128)(2,1)S(1)} %reshape.113, bf16[3072,256]{1,0:T(8,128)(2,1)} %bitcast.5), kind=kLoop, calls=%fused_computation.39 | loop fusion | flops 3178496 | bytes 3178496 | tf_op jit(solution)/shard_map/concatenate | solution.py:64
  62.3 16.6 %gather_fusion = bf16[3072,256]{1,0:T(8,128)(2,1)} fusion(bf16[16384,256]{1,0:T(8,128)(2,1)} %param.13, s32[3072]{0:T(1024)S(1)} %broadcast_clamp_fusion), kind=kCustom, calls=%fused_computation | custom fusion | bytes 3158016 | tf_op jit(solution)/shard_map/gather | solution.py:73
  78.9 3.4 %convert_element_type.66 = f32[3072,256]{1,0:T(8,128)} convert(bf16[3072,256]{1,0:T(8,128)(2,1)} %gather_fusion) | non-fusion elementwise | flops 786432 | bytes 4718592 | tf_op jit(solution)/shard_map/convert_element_type | solution.py:73
  82.3 44.5 %all-gather.3.cloned.1.call-done = bf16[12416,256]{1,0:T(8,128)(2,1)} async-done(((bf16[3104,256]{1,0:T(8,128)(2,1)}), bf16[12416,256]{1,0:T(8,128)(2,1)}) %all-gather.3.cloned.1.call-update) | async-done | bytes 6357008 | tf_op jit(solution)/shard_map/all_gather | solution.py:65
  126.8 0.8 slice_bitcast_fusion
  127.8 32.3 %while.21 = (s32[]{:T(128)}, f32[3,1024,256]{2,1,0:T(8,128)}, s32[3,1024]{1,0:T(4,128)S(1)}, s32[4,3104]{1,0:T(4,128)S(1)}, bf16[12416,256]{1,0:T(8,128)(2,1)}, /*index=5*/s32[]{:T(128)}) while((s32[]{:T(128)}, f32[3,1024,256]{2,1,0:T(8,128)}, s32[3,1024]{1,0:T(4,128)S(1)}, s32[4,3104]{1,0:T(4,128)S(1)}, bf16[12416,256]{1,0:T(8,128)(2,1)}, ...), condition=%wide.region_7.8_spmd, body=%wide.region_6.7_spmd.sunk | while | flops 6522273792 | bytes 7567433 | solution.py:22
  128.0 10.7 %fusion.73 = f32[3,1024,256]{2,1,0:T(8,128)} fusion(f32[3,1024,256]{2,1,0:T(8,128)} %get-tuple-element.177, s32[]{:T(128)} %get-tuple-element.176, bf16[12416,256]{1,0:T(8,128)(2,1)} %get-tuple-element.186, s32[12416]{0:T(1024)S(1)} %eq.178, s32[1024]{0:T(1024)S(1)} %bitcast.54), kind=kOutput, calls=%fused_computation.13.clone.1 | convolution fusion | flops 6522273792 | bytes 7459840 | tf_op jit(solution)/shard_map/while/body/eval_jaxpr/dot_general | solution.py:20
  138.7 10.7 %fusion.73 = f32[3,1024,256]{2,1,0:T(8,128)} fusion(f32[3,1024,256]{2,1,0:T(8,128)} %get-tuple-element.177, s32[]{:T(128)} %get-tuple-element.176, bf16[12416,256]{1,0:T(8,128)(2,1)} %get-tuple-element.186, s32[12416]{0:T(1024)S(1)} %eq.178, s32[1024]{0:T(1024)S(1)} %bitcast.54), kind=kOutput, calls=%fused_computation.13.clone.1 | convolution fusion | flops 6522273792 | bytes 7459840 | tf_op jit(solution)/shard_map/while/body/eval_jaxpr/dot_general | solution.py:20
  149.5 10.6 %fusion.73 = f32[3,1024,256]{2,1,0:T(8,128)} fusion(f32[3,1024,256]{2,1,0:T(8,128)} %get-tuple-element.177, s32[]{:T(128)} %get-tuple-element.176, bf16[12416,256]{1,0:T(8,128)(2,1)} %get-tuple-element.186, s32[12416]{0:T(1024)S(1)} %eq.178, s32[1024]{0:T(1024)S(1)} %bitcast.54), kind=kOutput, calls=%fused_computation.13.clone.1 | convolution fusion | flops 6522273792 | bytes 7459840 | tf_op jit(solution)/shard_map/while/body/eval_jaxpr/dot_general | solution.py:20
  160.1 3.3 %multiply_reduce_fusion.1 = f32[3,1024]{1,0:T(4,128)S(1)} fusion(f32[3,1024,256]{2,1,0:T(8,128)} %bitcast.47, f32[3,1024,256]{2,1,0:T(8,128)} %get-tuple-element.57), kind=kLoop, calls=%fused_computation.37 | loop fusion | flops 2356224 | bytes 6303744 | tf_op jit(solution)/shard_map/reduce_sum | solution.py:9
  163.6 4.5 %multiply_convert_fusion.1 = bf16[32,96,256]{2,1,0:T(8,128)(2,1)} fusion(f32[32,96,256]{2,1,0:T(8,128)} %bitcast.48, f32[32,96,256]{2,1,0:T(8,128)} %bitcast.49, f32[32,96]{1,0:T(8,128)S(1)} %rsqrt.30), kind=kLoop, calls=%fused_computation.36 | loop fusion | flops 2359296 | bytes 7876608 | tf_op jit(solution)/shard_map/convert_element_type | solution.py:10
  168.1 7.8 %all-to-all-start.2 = ((bf16[32,96,256]{2,1,0:T(8,128)(2,1)}), bf16[32,96,256]{2,1,0:T(8,128)(2,1)}, u32[]{:S(2)}, u32[]{:S(2)}) async-start(bf16[32,96,256]{2,1,0:T(8,128)(2,1)} %multiply_convert_fusion.1), calls=%async_computation.2 | async-start | bytes 3145728 | tf_op jit(solution)/shard_map/all_to_all | solution.py:78
  175.9 43.1 %while.20 = (s32[]{:T(128)}, f32[4,1024,256]{2,1,0:T(8,128)}, s32[4,1024]{1,0:T(4,128)S(1)}, s32[4,3104]{1,0:T(4,128)S(1)}, bf16[12416,256]{1,0:T(8,128)(2,1)}, /*index=5*/s32[]{:T(128)}) while((s32[]{:T(128)}, f32[4,1024,256]{2,1,0:T(8,128)}, s32[4,1024]{1,0:T(4,128)S(1)}, s32[4,3104]{1,0:T(4,128)S(1)}, bf16[12416,256]{1,0:T(8,128)(2,1)}, ...), condition=%wide.region_4.5_spmd, body=%wide.region_3.4_spmd.sunk | while | flops 6522273792 | bytes 7567433 | solution.py:22
  176.0 10.7 %fusion.70 = f32[4,1024,256]{2,1,0:T(8,128)} fusion(f32[4,1024,256]{2,1,0:T(8,128)} %get-tuple-element.159, s32[]{:T(128)} %get-tuple-element.158, bf16[12416,256]{1,0:T(8,128)(2,1)} %get-tuple-element.168, s32[12416]{0:T(1024)S(1)} %eq.174, s32[1024]{0:T(1024)S(1)} %bitcast.55), kind=kOutput, calls=%fused_computation.6.clone.1 | convolution fusion | flops 6522273792 | bytes 7459840 | tf_op jit(solution)/shard_map/while/body/eval_jaxpr/dot_general | solution.py:20
  186.8 10.7 %fusion.70 = f32[4,1024,256]{2,1,0:T(8,128)} fusion(f32[4,1024,256]{2,1,0:T(8,128)} %get-tuple-element.159, s32[]{:T(128)} %get-tuple-element.158, bf16[12416,256]{1,0:T(8,128)(2,1)} %get-tuple-element.168, s32[12416]{0:T(1024)S(1)} %eq.174, s32[1024]{0:T(1024)S(1)} %bitcast.55), kind=kOutput, calls=%fused_computation.6.clone.1 | convolution fusion | flops 6522273792 | bytes 7459840 | tf_op jit(solution)/shard_map/while/body/eval_jaxpr/dot_general | solution.py:20
  197.5 10.7 %fusion.70 = f32[4,1024,256]{2,1,0:T(8,128)} fusion(f32[4,1024,256]{2,1,0:T(8,128)} %get-tuple-element.159, s32[]{:T(128)} %get-tuple-element.158, bf16[12416,256]{1,0:T(8,128)(2,1)} %get-tuple-element.168, s32[12416]{0:T(1024)S(1)} %eq.174, s32[1024]{0:T(1024)S(1)} %bitcast.55), kind=kOutput, calls=%fused_computation.6.clone.1 | convolution fusion | flops 6522273792 | bytes 7459840 | tf_op jit(solution)/shard_map/while/body/eval_jaxpr/dot_general | solution.py:20
  208.4 10.6 %fusion.70 = f32[4,1024,256]{2,1,0:T(8,128)} fusion(f32[4,1024,256]{2,1,0:T(8,128)} %get-tuple-element.159, s32[]{:T(128)} %get-tuple-element.158, bf16[12416,256]{1,0:T(8,128)(2,1)} %get-tuple-element.168, s32[12416]{0:T(1024)S(1)} %eq.174, s32[1024]{0:T(1024)S(1)} %bitcast.55), kind=kOutput, calls=%fused_computation.6.clone.1 | convolution fusion | flops 6522273792 | bytes 7459840 | tf_op jit(solution)/shard_map/while/body/eval_jaxpr/dot_general | solution.py:20
  219.0 3.6 %multiply_reduce_fusion = f32[4096]{0:T(1024)S(1)} fusion(f32[4,1024,256]{2,1,0:T(8,128)} %get-tuple-element.56, bf16[16384,256]{1,0:T(8,128)(2,1)} %param.13, s32[]{:T(128)S(6)} %select_n.38), kind=kLoop, calls=%fused_computation.32 | loop fusion | flops 4190208 | bytes 6307844 | tf_op jit(solution)/shard_map/reduce_sum | solution.py:9
  223.0 3.0 %multiply_convert_fusion = bf16[4096,256]{1,0:T(8,128)(2,1)} fusion(f32[4,1024,256]{2,1,0:T(8,128)S(1)} %copy-done.1, f32[4096]{0:T(1024)S(1)} %add_rsqrt_fusion.1, bf16[16384,256]{1,0:T(8,128)(2,1)} %param.13, s32[]{:T(128)S(6)} %select_n.38), kind=kLoop, calls=%fused_computation.31 | loop fusion | flops 4194304 | bytes 8404996 | tf_op jit(solution)/shard_map/convert_element_type | solution.py:10
  226.1 4.3 %fusion.37 = bf16[1024,256]{0,1:T(8,128)(2,1)S(1)} fusion(bf16[3072,256]{1,0:T(8,128)(2,1)} %bitcast.12, s32[1024]{0:T(1024)S(1)} %copy-done.5, f32[1024,256]{0,1:T(8,128)} %copy-done.6, f32[1024]{0:T(1024)S(1)} %copy-done.3), kind=kOutput, calls=%fused_computation.41 | convolution fusion | flops 1615069184 | bytes 3153920 | tf_op jit(solution)/shard_map/dot_general | solution.py:83
  230.4 1.0 copy.12
  (52 shorter events, 2.9 us)
Async XLA Ops:
  7.2 12.7 %copy-start = (bf16[1024,1024]{1,0:T(8,128)(2,1)S(1)}, bf16[1024,1024]{1,0:T(8,128)(2,1)}, u32[]{:S(2)}) copy-start(bf16[1024,1024]{1,0:T(8,128)(2,1)} %param.9) | copy-start | bytes 6291460
  9.3 15.7 %copy-start.4 = (s32[1024]{0:T(1024)}, s32[1024]{0:T(1024)S(1)}, u32[]{:S(2)}) copy-start(s32[1024]{0:T(1024)S(1)} %get-tuple-element.86) | copy-start | bytes 12292
  11.3 17.9 %all-to-all-start.1 = ((s32[32,96,1]{1,2,0:T(1,128)}), s32[32,96,1]{1,2,0:T(1,128)S(1)}, u32[]{:S(2)}, u32[]{:S(2)}) async-start(s32[32,96,1]{1,2,0:T(1,128)} %all_to_all.27), calls=%async_computation.1 | async-start | bytes 32768 | tf_op jit(solution)/shard_map/all_to_all | solution.py:58
  24.9 12.0 %copy-start.6 = (f32[1024,256]{0,1:T(8,128)}, f32[1024,256]{0,1:T(8,128)S(1)}, u32[]{:S(2)}) copy-start(f32[1024,256]{0,1:T(8,128)S(1)} %get-tuple-element.89) | copy-start | bytes 3145732
  24.9 0.6 copy-start.2
  29.2 30.2 %all-to-all-start = ((bf16[32,96,256]{2,1,0:T(8,128)(2,1)}), bf16[32,96,256]{2,1,0:T(8,128)(2,1)}, u32[]{:S(2)}, u32[]{:S(2)}) async-start(bf16[32,96,256]{2,1,0:T(8,128)(2,1)} %bitcast.50), calls=%async_computation | async-start | bytes 3145728 | tf_op jit(solution)/shard_map/all_to_all | solution.py:57
  36.6 90.2 %all-gather.3.cloned.1.call-start = ((), (), s32[]{:S(2)}) async-start(), calls=%async_computation.3 | async-start | bytes 7946240 | tf_op jit(solution)/shard_map/all_gather | solution.py:65
  168.1 58.0 %all-to-all-start.2 = ((bf16[32,96,256]{2,1,0:T(8,128)(2,1)}), bf16[32,96,256]{2,1,0:T(8,128)(2,1)}, u32[]{:S(2)}, u32[]{:S(2)}) async-start(bf16[32,96,256]{2,1,0:T(8,128)(2,1)} %multiply_convert_fusion.1), calls=%async_computation.2 | async-start | bytes 3145728 | tf_op jit(solution)/shard_map/all_to_all | solution.py:78
  219.0 4.1 %copy-start.1 = (f32[4,1024,256]{2,1,0:T(8,128)S(1)}, f32[4,1024,256]{2,1,0:T(8,128)}, u32[]{:S(2)}) copy-start(f32[4,1024,256]{2,1,0:T(8,128)} %get-tuple-element.56) | copy-start | bytes 12582916
  223.0 3.0 %copy-start.3 = (f32[1024]{0:T(1024)S(1)}, f32[1024]{0:T(1024)}, u32[]{:S(2)}) copy-start(f32[1024]{0:T(1024)} %copy-done.2) | copy-start | bytes 12292
  223.0 3.0 %copy-start.5 = (s32[1024]{0:T(1024)S(1)}, s32[1024]{0:T(1024)}, u32[]{:S(2)}) copy-start(s32[1024]{0:T(1024)} %copy-done.4) | copy-start | bytes 12292
Sparse Core Ops, SparseCore 0:
  62.2 64.6 all-gather.2
where the time goes:
time: 239 us; the launch traced here: 238 us
  matrix products  88 us (37%)
  waiting for transfers between devices  65.8 us (28%)
  other arithmetic  24.2 us (10%)
  starting transfers between devices  24 us (10%)
  local copies, waits for them, and re-layouts  21.8 us (9%)
  between operations  14.3 us (6%)
    dot_general x7, matrix products, one_block(): return jnp.dot(selector, rows, preferred_element_type=jnp.float32)  74.6 us
    all_gather x1, waiting for transfers between devices, body(): rows_all = lax.all_gather(payload, 'rep', axis=0)  44.5 us
    all_to_all x1, waiting for transfers between devices, body(): lax.all_to_all(outgoing, 'wide', split_axis=0, concat_axis=0, tiled=True)  21.3 us
    gather x1, local copies, waits for them, and re-layouts, body(): look_cent = centroids[in_ids].astype(jnp.float32)  16.6 us
    all_to_all x1, starting transfers between devices, body(): lax.all_to_all(out_ids, 'wide', split_axis=0, concat_axis=0, tiled=True)  8.58 us
    all_to_all x1, starting transfers between devices, body(): lax.all_to_all(picked, 'wide', split_axis=0, concat_axis=0, tiled=True)  7.75 us
    convert_element_type x2, other arithmetic, normalize(): return (updated * lax.rsqrt(jnp.mean(updated * updated, axis=-1, keepdims...  7.54 us
    all_to_all x1, starting transfers between devices, body(): lax.all_to_all(outgoing, 'wide', split_axis=0, concat_axis=0, tiled=True)  7.43 us
  transfers between devices with their start and end apart: 4, of which 2 were waited for; matrix products, arithmetic and copies ran while one was open for 33% of the time, Pallas kernels for 0%

commit v1 on v0

--- a/solution.py
+++ b/solution.py
@@ -57,27 +57,40 @@
     incoming = lax.all_to_all(outgoing, "wide", split_axis=0, concat_axis=0, tiled=True)
     in_ids = lax.all_to_all(out_ids, "wide", split_axis=0, concat_axis=0, tiled=True)
 
-    code_rows = -(-2 * slots // emb_width)
-    code_rows = -(-code_rows // 16) * 16
-    id_code = jnp.concatenate([in_ids // 128, in_ids % 128]).astype(jnp.bfloat16)
-    id_code = jnp.pad(id_code, (0, code_rows * emb_width - 2 * slots))
-    payload = jnp.concatenate([incoming, id_code.reshape(code_rows, emb_width)])
-    rows_all = lax.all_gather(payload, "rep", axis=0)
-    code = rows_all[:, slots:].reshape(replicas, -1)[:, : 2 * slots].astype(jnp.int32)
-    keys = code[:, :slots] * 128 + code[:, slots:]
-    keys = jnp.pad(keys, ((0, 0), (0, code_rows)), constant_values=-1).reshape(-1)
-    rows = rows_all.reshape(-1, emb_width)
-
     first_row = my_rep * share_rows
     share_ids = first_row + jnp.arange(share_rows, dtype=jnp.int32)
+
+    pieces = 2
+    piece_rows = slots // pieces
+    code_rows = -(-2 * piece_rows // emb_width)
+    code_rows = -(-code_rows // 16) * 16
+    halves = []
+    for part in range(pieces):
+        part_ids = in_ids[part * piece_rows : (part + 1) * piece_rows]
+        id_code = jnp.concatenate([part_ids // 128, part_ids % 128]).astype(jnp.bfloat16)
+        id_code = jnp.pad(id_code, (0, code_rows * emb_width - 2 * piece_rows))
+        payload = jnp.concatenate(
+            [incoming[part * piece_rows : (part + 1) * piece_rows],
+             id_code.reshape(code_rows, emb_width)]
+        )
+        gathered = lax.all_gather(payload, "rep", axis=0)
+        code = gathered[:, piece_rows:].reshape(replicas, -1)[:, : 2 * piece_rows]
+        code = code.astype(jnp.int32)
+        keys = code[:, :piece_rows] * 128 + code[:, piece_rows:]
+        keys = jnp.pad(keys, ((0, 0), (0, code_rows)), constant_values=-1).reshape(-1)
+        halves.append((keys, gathered.reshape(-1, emb_width)))
+
     look_cent = centroids[in_ids].astype(jnp.float32)
     own_cent = lax.dynamic_slice_in_dim(centroids, first_row, share_rows, 0).astype(jnp.float32)
 
-    look_sum = match_sums(in_ids, keys, rows)
+    keys_a, rows_a = halves[0]
+    keys_b, rows_b = halves[1]
+    first_sums = match_sums(jnp.concatenate([in_ids, share_ids]), keys_a, rows_a)
+    look_sum = first_sums[:slots] + match_sums(in_ids, keys_b, rows_b)
     picked = normalize(look_cent + look_sum)
     returned = lax.all_to_all(picked, "wide", split_axis=0, concat_axis=0, tiled=True)
 
-    share_sum = match_sums(share_ids, keys, rows)
+    share_sum = first_sums[slots:] + match_sums(share_ids, keys_b, rows_b)
     own_rows = normalize(own_cent + share_sum)
 
     gathered_rows = jnp.dot(place_bf.T, returned, preferred_element_type=jnp.float32)

time: 239 us -> 238 us (level)
  waiting for transfers between devices: 65.8 us -> 38.1 us
  matrix products: 88 us -> 107 us
  other arithmetic: 24.2 us -> 28.9 us
    all_gather x1 -> x2, waiting for transfers between devices: 44.5 us -> 15.5 us  [body(): gathered = lax.all_gather(payload, 'rep', axis=0)]
    dot_general x7 -> x14, matrix products: 74.6 us -> 91.3 us  [one_block(): return jnp.dot(selector, rows, preferred_element_type=jnp.float32)]
    add x1 -> x3, other arithmetic: 0.02 us -> 4.03 us  [the longest x1 4.01 us: body(): share_sum = first_sums[slots:] + match_sums(share_ids, keys_b, rows_b)]
  transfers between devices with their start and end apart: 4 -> 5, of which waited for: 2 -> 2; matrix products, arithmetic and copies ran while one was open for 33% -> 49% of each run, Pallas kernels for 0% -> 0%
where the time goes in v1:
time: 238 us; the launch traced here: 236 us
  matrix products  107 us (45%)
  waiting for transfers between devices  38.1 us (16%)
  other arithmetic  28.9 us (12%)
  starting transfers between devices  24 us (10%)
  local copies, waits for them, and re-layouts  23.8 us (10%)
  between operations  14.3 us (6%)
    dot_general x14, matrix products, one_block(): return jnp.dot(selector, rows, preferred_element_type=jnp.float32)  91.3 us
    all_to_all x1, waiting for transfers between devices, body(): lax.all_to_all(outgoing, 'wide', split_axis=0, concat_axis=0, tiled=True)  22.5 us
    gather x1, local copies, waits for them, and re-layouts, body(): look_cent = centroids[in_ids].astype(jnp.float32)  16.7 us
    all_gather x2, waiting for transfers between devices, body(): gathered = lax.all_gather(payload, 'rep', axis=0)  15.5 us
    all_to_all x1, starting transfers between devices, body(): lax.all_to_all(out_ids, 'wide', split_axis=0, concat_axis=0, tiled=True)  8.58 us
    reduce_sum x2, other arithmetic, normalize(): jnp.mean(updated * updated, axis=-1, keepdims=True) + 1e-06  8.33 us
    all_to_all x1, starting transfers between devices, body(): lax.all_to_all(picked, 'wide', split_axis=0, concat_axis=0, tiled=True)  7.73 us
    convert_element_type x2, other arithmetic, normalize(): return (updated * lax.rsqrt(jnp.mean(updated * updated, axis=-1, keepdims...  7.61 us
  transfers between devices with their start and end apart: 5, of which 2 were waited for; matrix products, arithmetic and copies ran while one was open for 49% of the time, Pallas kernels for 0%

profile of v1, /device:TPU:1, one launch (start us, length us, event | category | flops | bytes accessed | tf_op | source)
XLA Modules:
  0.0 236.2 jit_solution(834482701555045196)
XLA Ops:
  11.3 8.6 %all-to-all-start = ((s32[32,96,1]{1,2,0:T(1,128)}), s32[32,96,1]{1,2,0:T(1,128)S(1)}, u32[]{:S(2)}, u32[]{:S(2)}) async-start(s32[32,96,1]{1,2,0:T(1,128)} %all_to_all.22), calls=%async_computation | async-start | bytes 32768 | tf_op jit(solution)/shard_map/all_to_all | solution.py:58
  19.9 6.0 %multiply_reduce_fusion.2 = (f32[1024]{0:T(1024)S(1)}, f32[1024,256]{0,1:T(8,128)}) fusion(bf16[1024,256]{1,0:T(8,128)(2,1)} %param.14, bf16[1024,1024]{1,0:T(8,128)(2,1)S(1)} %copy-done, bf16[1024,1024]{1,0:T(8,128)(2,1)} %param.13), kind=kOutput, calls=%fused_computation.53 | convolution fusion | flops 2694315008 | bytes 5771264 | tf_op jit(solution)/shard_map/dot_general | solution.py:50
  25.9 4.8 %fusion.43 = bf16[3072,256]{1,0:T(8,128)(2,1)} fusion(s32[1024]{0:T(1024)S(1)} %get-tuple-element.132, f32[1024,256]{0,1:T(8,128)} %get-tuple-element.135, f32[1024]{0:T(1024)S(1)} %add_rsqrt_fusion.2), kind=kOutput, calls=%fused_computation.43 | convolution fusion | flops 1615069184 | bytes 2629632 | tf_op jit(solution)/shard_map/dot_general | solution.py:55
  30.7 7.4 %all-to-all-start.1 = ((bf16[32,96,256]{2,1,0:T(8,128)(2,1)}), bf16[32,96,256]{2,1,0:T(8,128)(2,1)}, u32[]{:S(2)}, u32[]{:S(2)}) async-start(bf16[32,96,256]{2,1,0:T(8,128)(2,1)} %bitcast.69), calls=%async_computation.1 | async-start | bytes 3145728 | tf_op jit(solution)/shard_map/all_to_all | solution.py:57
  38.4 22.5 %all-to-all-done.1 = bf16[32,96,256]{2,1,0:T(8,128)(2,1)} async-done(((bf16[32,96,256]{2,1,0:T(8,128)(2,1)}), bf16[32,96,256]{2,1,0:T(8,128)(2,1)}, u32[]{:S(2)}, u32[]{:S(2)}) %all-to-all-start.1) | async-done | bytes 1572896 | tf_op jit(solution)/shard_map/all_to_all | solution.py:57
  65.3 16.7 %gather_fusion = bf16[3072,256]{1,0:T(8,128)(2,1)} fusion(bf16[16384,256]{1,0:T(8,128)(2,1)} %param.15, s32[3072]{0:T(1024)S(1)} %broadcast_clamp_fusion), kind=kCustom, calls=%fused_computation | custom fusion | bytes 3158016 | tf_op jit(solution)/shard_map/gather | solution.py:83
  82.0 3.3 %convert_element_type.73 = f32[3072,256]{1,0:T(8,128)} convert(bf16[3072,256]{1,0:T(8,128)(2,1)} %gather_fusion) | non-fusion elementwise | flops 786432 | bytes 4718592 | tf_op jit(solution)/shard_map/convert_element_type | solution.py:83
  86.3 15.5 %all-gather.5.cloned.1.call-done = bf16[6208,256]{1,0:T(8,128)(2,1)} async-done(((bf16[1552,256]{1,0:T(8,128)(2,1)}), bf16[6208,256]{1,0:T(8,128)(2,1)}) %all-gather.5.cloned.1.call-update) | async-done | bytes 3178512 | tf_op jit(solution)/shard_map/all_gather | solution.py:76
  102.6 46.5 %while.30 = (s32[]{:T(128)}, f32[7,1024,256]{2,1,0:T(8,128)}, s32[7,1024]{1,0:T(8,128)S(1)}, s32[4,1552]{1,0:T(4,128)S(1)}, bf16[6208,256]{1,0:T(8,128)(2,1)}, /*index=5*/s32[]{:T(128)}) while((s32[]{:T(128)}, f32[7,1024,256]{2,1,0:T(8,128)}, s32[7,1024]{1,0:T(8,128)S(1)}, s32[4,1552]{1,0:T(4,128)S(1)}, bf16[6208,256]{1,0:T(8,128)(2,1)}, ...), condition=%wide.region_4.5_spmd, body=%wide.region_3.4_spmd.sunk | while | flops 3261136896 | bytes 4314441 | solution.py:22
  102.7 6.5 %fusion.92 = f32[7,1024,256]{2,1,0:T(8,128)} fusion(f32[7,1024,256]{2,1,0:T(8,128)} %get-tuple-element.254, s32[]{:T(128)} %get-tuple-element.253, bf16[6208,256]{1,0:T(8,128)(2,1)} %get-tuple-element.263, s32[6208]{0:T(1024)S(1)} %eq.218, s32[1024]{0:T(1024)S(1)} %bitcast.72), kind=kOutput, calls=%fused_computation.6.clone.1 | convolution fusion | flops 3261136896 | bytes 4256512 | tf_op jit(solution)/shard_map/while/body/eval_jaxpr/dot_general | solution.py:20
  109.4 6.5 %fusion.92 = f32[7,1024,256]{2,1,0:T(8,128)} fusion(f32[7,1024,256]{2,1,0:T(8,128)} %get-tuple-element.254, s32[]{:T(128)} %get-tuple-element.253, bf16[6208,256]{1,0:T(8,128)(2,1)} %get-tuple-element.263, s32[6208]{0:T(1024)S(1)} %eq.218, s32[1024]{0:T(1024)S(1)} %bitcast.72), kind=kOutput, calls=%fused_computation.6.clone.1 | convolution fusion | flops 3261136896 | bytes 4256512 | tf_op jit(solution)/shard_map/while/body/eval_jaxpr/dot_general | solution.py:20
  116.0 6.5 %fusion.92 = f32[7,1024,256]{2,1,0:T(8,128)} fusion(f32[7,1024,256]{2,1,0:T(8,128)} %get-tuple-element.254, s32[]{:T(128)} %get-tuple-element.253, bf16[6208,256]{1,0:T(8,128)(2,1)} %get-tuple-element.263, s32[6208]{0:T(1024)S(1)} %eq.218, s32[1024]{0:T(1024)S(1)} %bitcast.72), kind=kOutput, calls=%fused_computation.6.clone.1 | convolution fusion | flops 3261136896 | bytes 4256512 | tf_op jit(solution)/shard_map/while/body/eval_jaxpr/dot_general | solution.py:20
  122.6 6.5 %fusion.92 = f32[7,1024,256]{2,1,0:T(8,128)} fusion(f32[7,1024,256]{2,1,0:T(8,128)} %get-tuple-element.254, s32[]{:T(128)} %get-tuple-element.253, bf16[6208,256]{1,0:T(8,128)(2,1)} %get-tuple-element.263, s32[6208]{0:T(1024)S(1)} %eq.218, s32[1024]{0:T(1024)S(1)} %bitcast.72), kind=kOutput, calls=%fused_computation.6.clone.1 | convolution fusion | flops 3261136896 | bytes 4256512 | tf_op jit(solution)/shard_map/while/body/eval_jaxpr/dot_general | solution.py:20
  129.3 6.5 %fusion.92 = f32[7,1024,256]{2,1,0:T(8,128)} fusion(f32[7,1024,256]{2,1,0:T(8,128)} %get-tuple-element.254, s32[]{:T(128)} %get-tuple-element.253, bf16[6208,256]{1,0:T(8,128)(2,1)} %get-tuple-element.263, s32[6208]{0:T(1024)S(1)} %eq.218, s32[1024]{0:T(1024)S(1)} %bitcast.72), kind=kOutput, calls=%fused_computation.6.clone.1 | convolution fusion | flops 3261136896 | bytes 4256512 | tf_op jit(solution)/shard_map/while/body/eval_jaxpr/dot_general | solution.py:20
  135.9 6.6 %fusion.92 = f32[7,1024,256]{2,1,0:T(8,128)} fusion(f32[7,1024,256]{2,1,0:T(8,128)} %get-tuple-element.254, s32[]{:T(128)} %get-tuple-element.253, bf16[6208,256]{1,0:T(8,128)(2,1)} %get-tuple-element.263, s32[6208]{0:T(1024)S(1)} %eq.218, s32[1024]{0:T(1024)S(1)} %bitcast.72), kind=kOutput, calls=%fused_computation.6.clone.1 | convolution fusion | flops 3261136896 | bytes 4256512 | tf_op jit(solution)/shard_map/while/body/eval_jaxpr/dot_general | solution.py:20
  142.6 6.5 %fusion.92 = f32[7,1024,256]{2,1,0:T(8,128)} fusion(f32[7,1024,256]{2,1,0:T(8,128)} %get-tuple-element.254, s32[]{:T(128)} %get-tuple-element.253, bf16[6208,256]{1,0:T(8,128)(2,1)} %get-tuple-element.263, s32[6208]{0:T(1024)S(1)} %eq.218, s32[1024]{0:T(1024)S(1)} %bitcast.72), kind=kOutput, calls=%fused_computation.6.clone.1 | convolution fusion | flops 3261136896 | bytes 4256512 | tf_op jit(solution)/shard_map/while/body/eval_jaxpr/dot_general | solution.py:20
  150.0 19.8 %while.32 = (s32[]{:T(128)}, f32[3,1024,256]{2,1,0:T(8,128)}, s32[3,1024]{1,0:T(4,128)S(1)}, s32[4,1552]{1,0:T(4,128)S(1)}, bf16[6208,256]{1,0:T(8,128)(2,1)}, /*index=5*/s32[]{:T(128)}) while((s32[]{:T(128)}, f32[3,1024,256]{2,1,0:T(8,128)}, s32[3,1024]{1,0:T(4,128)S(1)}, s32[4,1552]{1,0:T(4,128)S(1)}, bf16[6208,256]{1,0:T(8,128)(2,1)}, ...), condition=%wide.region_9.10_spmd, body=%wide.region_8.9_spmd.sunk | while | flops 3261136896 | bytes 4314441 | solution.py:22
  150.1 6.5 %fusion.98 = f32[3,1024,256]{2,1,0:T(8,128)} fusion(f32[3,1024,256]{2,1,0:T(8,128)} %get-tuple-element.272, s32[]{:T(128)} %get-tuple-element.271, bf16[6208,256]{1,0:T(8,128)(2,1)} %get-tuple-element.281, s32[6208]{0:T(1024)S(1)} %eq.226, s32[1024]{0:T(1024)S(1)} %bitcast.73), kind=kOutput, calls=%fused_computation.20.clone.1 | convolution fusion | flops 3261136896 | bytes 4256512 | tf_op jit(solution)/shard_map/while/body/eval_jaxpr/dot_general | solution.py:20
  156.7 6.5 %fusion.98 = f32[3,1024,256]{2,1,0:T(8,128)} fusion(f32[3,1024,256]{2,1,0:T(8,128)} %get-tuple-element.272, s32[]{:T(128)} %get-tuple-element.271, bf16[6208,256]{1,0:T(8,128)(2,1)} %get-tuple-element.281, s32[6208]{0:T(1024)S(1)} %eq.226, s32[1024]{0:T(1024)S(1)} %bitcast.73), kind=kOutput, calls=%fused_computation.20.clone.1 | convolution fusion | flops 3261136896 | bytes 4256512 | tf_op jit(solution)/shard_map/while/body/eval_jaxpr/dot_general | solution.py:20
  163.3 6.5 %fusion.98 = f32[3,1024,256]{2,1,0:T(8,128)} fusion(f32[3,1024,256]{2,1,0:T(8,128)} %get-tuple-element.272, s32[]{:T(128)} %get-tuple-element.271, bf16[6208,256]{1,0:T(8,128)(2,1)} %get-tuple-element.281, s32[6208]{0:T(1024)S(1)} %eq.226, s32[1024]{0:T(1024)S(1)} %bitcast.73), kind=kOutput, calls=%fused_computation.20.clone.1 | convolution fusion | flops 3261136896 | bytes 4256512 | tf_op jit(solution)/shard_map/while/body/eval_jaxpr/dot_general | solution.py:20
  169.8 5.8 %multiply_reduce_fusion.1 = (f32[3,1024]{1,0:T(4,128)S(1)}, f32[3,1024,256]{2,1,0:T(8,128)}) fusion(f32[3,1024,256]{2,1,0:T(8,128)} %bitcast.64, f32[3,1024,256]{2,1,0:T(8,128)} %get-tuple-element.85, f32[7,1024,256]{2,1,0:T(8,128)} %get-tuple-element.83), kind=kLoop, calls=%fused_computation.45 | loop fusion | flops 3142656 | bytes 12595200 | tf_op jit(solution)/shard_map/reduce_sum | solution.py:9
  175.7 4.6 %multiply_convert_fusion.1 = bf16[32,96,256]{2,1,0:T(8,128)(2,1)} fusion(f32[32,96,256]{2,1,0:T(8,128)} %bitcast.65, f32[32,96,256]{2,1,0:T(8,128)} %bitcast.66, f32[32,96]{1,0:T(8,128)S(1)} %rsqrt.30), kind=kLoop, calls=%fused_computation.44 | loop fusion | flops 2359296 | bytes 7876608 | tf_op jit(solution)/shard_map/convert_element_type | solution.py:10
  180.3 7.7 %all-to-all-start.2 = ((bf16[32,96,256]{2,1,0:T(8,128)(2,1)}), bf16[32,96,256]{2,1,0:T(8,128)(2,1)}, u32[]{:S(2)}, u32[]{:S(2)}) async-start(bf16[32,96,256]{2,1,0:T(8,128)(2,1)} %multiply_convert_fusion.1), calls=%async_computation.2 | async-start | bytes 3145728 | tf_op jit(solution)/shard_map/all_to_all | solution.py:91
  188.0 26.5 %while.31 = (s32[]{:T(128)}, f32[4,1024,256]{2,1,0:T(8,128)}, s32[4,1024]{1,0:T(4,128)S(1)}, s32[4,1552]{1,0:T(4,128)S(1)}, bf16[6208,256]{1,0:T(8,128)(2,1)}, /*index=5*/s32[]{:T(128)}) while((s32[]{:T(128)}, f32[4,1024,256]{2,1,0:T(8,128)}, s32[4,1024]{1,0:T(4,128)S(1)}, s32[4,1552]{1,0:T(4,128)S(1)}, bf16[6208,256]{1,0:T(8,128)(2,1)}, ...), condition=%wide.region_6.7_spmd, body=%wide.region_5.6_spmd.sunk | while | flops 3261136896 | bytes 4314441 | solution.py:22
  188.2 6.5 %fusion.95 = f32[4,1024,256]{2,1,0:T(8,128)} fusion(f32[4,1024,256]{2,1,0:T(8,128)} %get-tuple-element.236, s32[]{:T(128)} %get-tuple-element.235, bf16[6208,256]{1,0:T(8,128)(2,1)} %get-tuple-element.245, s32[6208]{0:T(1024)S(1)} %eq.222, s32[1024]{0:T(1024)S(1)} %bitcast.74), kind=kOutput, calls=%fused_computation.13.clone.1 | convolution fusion | flops 3261136896 | bytes 4256512 | tf_op jit(solution)/shard_map/while/body/eval_jaxpr/dot_general | solution.py:20
  194.8 6.6 %fusion.95 = f32[4,1024,256]{2,1,0:T(8,128)} fusion(f32[4,1024,256]{2,1,0:T(8,128)} %get-tuple-element.236, s32[]{:T(128)} %get-tuple-element.235, bf16[6208,256]{1,0:T(8,128)(2,1)} %get-tuple-element.245, s32[6208]{0:T(1024)S(1)} %eq.222, s32[1024]{0:T(1024)S(1)} %bitcast.74), kind=kOutput, calls=%fused_computation.13.clone.1 | convolution fusion | flops 3261136896 | bytes 4256512 | tf_op jit(solution)/shard_map/while/body/eval_jaxpr/dot_general | solution.py:20
  201.4 6.5 %fusion.95 = f32[4,1024,256]{2,1,0:T(8,128)} fusion(f32[4,1024,256]{2,1,0:T(8,128)} %get-tuple-element.236, s32[]{:T(128)} %get-tuple-element.235, bf16[6208,256]{1,0:T(8,128)(2,1)} %get-tuple-element.245, s32[6208]{0:T(1024)S(1)} %eq.222, s32[1024]{0:T(1024)S(1)} %bitcast.74), kind=kOutput, calls=%fused_computation.13.clone.1 | convolution fusion | flops 3261136896 | bytes 4256512 | tf_op jit(solution)/shard_map/while/body/eval_jaxpr/dot_general | solution.py:20
  208.0 6.5 %fusion.95 = f32[4,1024,256]{2,1,0:T(8,128)} fusion(f32[4,1024,256]{2,1,0:T(8,128)} %get-tuple-element.236, s32[]{:T(128)} %get-tuple-element.235, bf16[6208,256]{1,0:T(8,128)(2,1)} %get-tuple-element.245, s32[6208]{0:T(1024)S(1)} %eq.222, s32[1024]{0:T(1024)S(1)} %bitcast.74), kind=kOutput, calls=%fused_computation.13.clone.1 | convolution fusion | flops 3261136896 | bytes 4256512 | tf_op jit(solution)/shard_map/while/body/eval_jaxpr/dot_general | solution.py:20
  214.5 4.0 %slice_add_fusion = f32[4,1024,256]{2,1,0:T(8,128)S(1)} fusion(f32[4,1024,256]{2,1,0:T(8,128)} %get-tuple-element.84, f32[7,1024,256]{2,1,0:T(8,128)} %get-tuple-element.83), kind=kLoop, calls=%fused_computation.40 | loop fusion | flops 1048576 | bytes 12582912 | tf_op jit(solution)/shard_map/add | solution.py:93
  218.5 2.5 %multiply_reduce_fusion = f32[4096]{0:T(1024)S(1)} fusion(f32[4,1024,256]{2,1,0:T(8,128)S(1)} %slice_add_fusion, bf16[16384,256]{1,0:T(8,128)(2,1)} %param.15, s32[]{:T(128)S(6)} %select_n.45), kind=kLoop, calls=%fused_computation.39 | loop fusion | flops 4190208 | bytes 6307844 | tf_op jit(solution)/shard_map/reduce_sum | solution.py:9
  221.0 3.0 %multiply_convert_fusion = bf16[4096,256]{1,0:T(8,128)(2,1)} fusion(f32[4,1024,256]{2,1,0:T(8,128)S(1)} %slice_add_fusion, f32[4096]{0:T(1024)S(1)} %add_rsqrt_fusion.1, bf16[16384,256]{1,0:T(8,128)(2,1)} %param.15, s32[]{:T(128)S(6)} %select_n.45), kind=kLoop, calls=%fused_computation.38 | loop fusion | flops 4194304 | bytes 8404996 | tf_op jit(solution)/shard_map/convert_element_type | solution.py:10
  224.1 4.3 %fusion.47 = bf16[1024,256]{0,1:T(8,128)(2,1)S(1)} fusion(bf16[3072,256]{1,0:T(8,128)(2,1)} %bitcast.16, s32[1024]{0:T(1024)S(1)} %get-tuple-element.132, f32[1024,256]{0,1:T(8,128)} %get-tuple-element.135, f32[1024]{0:T(1024)S(1)} %add_rsqrt_fusion.2), kind=kOutput, calls=%fused_computation.49 | convolution fusion | flops 1615069184 | bytes 3153920 | tf_op jit(solution)/shard_map/dot_general | solution.py:96
  (83 shorter events, 13.7 us)
Async XLA Ops:
  7.2 12.7 %copy-start = (bf16[1024,1024]{1,0:T(8,128)(2,1)S(1)}, bf16[1024,1024]{1,0:T(8,128)(2,1)}, u32[]{:S(2)}) copy-start(bf16[1024,1024]{1,0:T(8,128)(2,1)} %param.11) | copy-start | bytes 6291460
  11.3 19.4 %all-to-all-start = ((s32[32,96,1]{1,2,0:T(1,128)}), s32[32,96,1]{1,2,0:T(1,128)S(1)}, u32[]{:S(2)}, u32[]{:S(2)}) async-start(s32[32,96,1]{1,2,0:T(1,128)} %all_to_all.22), calls=%async_computation | async-start | bytes 32768 | tf_op jit(solution)/shard_map/all_to_all | solution.py:58
  30.7 30.2 %all-to-all-start.1 = ((bf16[32,96,256]{2,1,0:T(8,128)(2,1)}), bf16[32,96,256]{2,1,0:T(8,128)(2,1)}, u32[]{:S(2)}, u32[]{:S(2)}) async-start(bf16[32,96,256]{2,1,0:T(8,128)(2,1)} %bitcast.69), calls=%async_computation.1 | async-start | bytes 3145728 | tf_op jit(solution)/shard_map/all_to_all | solution.py:57
  38.2 63.6 %all-gather.5.cloned.1.call-start = ((), (), s32[]{:S(2)}) async-start(), calls=%async_computation.3 | async-start | bytes 3973120 | tf_op jit(solution)/shard_map/all_gather | solution.py:76
  63.4 85.7 %all-gather.7.cloned.1.call-start = ((), (), s32[]{:S(2)}) async-start(), calls=%async_computation.4 | async-start | bytes 3973120 | tf_op jit(solution)/shard_map/all_gather | solution.py:76
  180.3 43.8 %all-to-all-start.2 = ((bf16[32,96,256]{2,1,0:T(8,128)(2,1)}), bf16[32,96,256]{2,1,0:T(8,128)(2,1)}, u32[]{:S(2)}, u32[]{:S(2)}) async-start(bf16[32,96,256]{2,1,0:T(8,128)(2,1)} %multiply_convert_fusion.1), calls=%async_computation.2 | async-start | bytes 3145728 | tf_op jit(solution)/shard_map/all_to_all | solution.py:91
Sparse Core Ops, SparseCore 0:
  63.5 38.2 all-gather.4
  104.0 40.0 all-gather.6

commit v2 on v1

--- a/solution.py
+++ b/solution.py
@@ -10,16 +10,25 @@
     ).astype(jnp.bfloat16)
 
 
-def match_sums(queries, keys, rows, block_rows=1024):
-    count = queries.shape[0]
-    padded = -(-count // block_rows) * block_rows
-    blocks = jnp.pad(queries, (0, padded - count), constant_values=-1).reshape(-1, block_rows)
+def match_sums(queries, keys, rows, base=None, cent=None, block_rows=1024):
+    block_count = queries.shape[0] // block_rows
+    xs = {"ids": queries.reshape(block_count, block_rows)}
+    if base is not None:
+        xs["base"] = base.reshape(block_count, block_rows, -1)
+    if cent is not None:
+        xs["cent"] = cent.reshape(block_count, block_rows, -1)
 
-    def one_block(block_ids):
-        selector = (block_ids[:, None] == keys[None, :]).astype(jnp.bfloat16)
-        return jnp.dot(selector, rows, preferred_element_type=jnp.float32)
+    def one_block(x):
+        selector = (x["ids"][:, None] == keys[None, :]).astype(jnp.bfloat16)
+        sums = jnp.dot(selector, rows, preferred_element_type=jnp.float32)
+        if "base" in x:
+            sums = sums + x["base"]
+        if "cent" in x:
+            return normalize(x["cent"].astype(jnp.float32) + sums)
+        return sums
 
-    return lax.map(one_block, blocks).reshape(padded, -1)[:count]
+    out = lax.map(one_block, xs)
+    return out.reshape(block_count * block_rows, -1)
 
 
 def body(passages, cluster_ids, w_first, w_second, centroids):
@@ -80,18 +89,15 @@
         keys = jnp.pad(keys, ((0, 0), (0, code_rows)), constant_values=-1).reshape(-1)
         halves.append((keys, gathered.reshape(-1, emb_width)))
 
-    look_cent = centroids[in_ids].astype(jnp.float32)
-    own_cent = lax.dynamic_slice_in_dim(centroids, first_row, share_rows, 0).astype(jnp.float32)
+    look_cent = centroids[in_ids]
+    own_cent = lax.dynamic_slice_in_dim(centroids, first_row, share_rows, 0)
 
     keys_a, rows_a = halves[0]
     keys_b, rows_b = halves[1]
     first_sums = match_sums(jnp.concatenate([in_ids, share_ids]), keys_a, rows_a)
-    look_sum = first_sums[:slots] + match_sums(in_ids, keys_b, rows_b)
-    picked = normalize(look_cent + look_sum)
+    picked = match_sums(in_ids, keys_b, rows_b, base=first_sums[:slots], cent=look_cent)
     returned = lax.all_to_all(picked, "wide", split_axis=0, concat_axis=0, tiled=True)
-
-    share_sum = first_sums[slots:] + match_sums(share_ids, keys_b, rows_b)
-    own_rows = normalize(own_cent + share_sum)
+    own_rows = match_sums(share_ids, keys_b, rows_b, base=first_sums[slots:], cent=own_cent)
 
     gathered_rows = jnp.dot(place_bf.T, returned, preferred_element_type=jnp.float32)
     residuals = (embedded.astype(jnp.float32) - gathered_rows).astype(jnp.bfloat16)

time: 238 us -> 256 us (1.076)
  local copies, waits for them, and re-layouts: 23.8 us -> 52.4 us
  other arithmetic: 28.9 us -> 6.35 us
  matrix products: 107 us -> 119 us
    dot_general x14, matrix products: 91.3 us -> 104 us  [one_block(): sums = jnp.dot(selector, rows, preferred_element_type=jnp.float32)]
    dynamic_slice x14 -> x29, local copies, waits for them, and re-layouts: 0.11 us -> 12.2 us  [the longest x28 9.11 us: match_sums(): out = lax.map(one_block, xs)]
    convert_element_type x3 -> x0, other arithmetic: 10.9 us -> none  [the longest x2 7.61 us: normalize(): return (updated * lax.rsqrt(jnp.mean(updated * updated, axis=-1, keepdims...]
    slice x0 -> x2, local copies, waits for them, and re-layouts: none -> 8.81 us  [the longest x1 4.87 us: body(): first_sums[slots:]]
    reduce_sum x2 -> x0, other arithmetic: 8.33 us -> none  [normalize(): jnp.mean(updated * updated, axis=-1, keepdims=True) + 1e-06]
    dynamic_update_slice x0 -> x14, local copies, waits for them, and re-layouts: none -> 7.33 us  [match_sums(): out = lax.map(one_block, xs)]
    add x1 -> x0, other arithmetic: 4.01 us -> none  [body(): share_sum = first_sums[slots:] + match_sums(share_ids, keys_b, rows_b)]
  transfers between devices with their start and end apart: 5 -> 5, of which waited for: 2 -> 2; matrix products, arithmetic and copies ran while one was open for 49% -> 54% of each run, Pallas kernels for 0% -> 0%
where the time goes in v2:
time: 256 us; the launch traced here: 255 us
  matrix products  119 us (46%)
  local copies, waits for them, and re-layouts  52.4 us (20%)
  waiting for transfers between devices  38 us (15%)
  starting transfers between devices  23.9 us (9%)
  between operations  14.3 us (6%)
  other arithmetic  6.35 us (2%)
    dot_general x14, matrix products, one_block(): sums = jnp.dot(selector, rows, preferred_element_type=jnp.float32)  104 us
    all_to_all x1, waiting for transfers between devices, body(): lax.all_to_all(outgoing, 'wide', split_axis=0, concat_axis=0, tiled=True)  22.5 us
    gather x1, local copies, waits for them, and re-layouts, body(): look_cent = centroids[in_ids]  17.1 us
    all_gather x2, waiting for transfers between devices, body(): gathered = lax.all_gather(payload, 'rep', axis=0)  15.5 us
    dynamic_slice x28, local copies, waits for them, and re-layouts, match_sums(): out = lax.map(one_block, xs)  9.11 us
    all_to_all x1, starting transfers between devices, body(): lax.all_to_all(out_ids, 'wide', split_axis=0, concat_axis=0, tiled=True)  8.58 us
    all_to_all x1, starting transfers between devices, body(): lax.all_to_all(picked, 'wide', split_axis=0, concat_axis=0, tiled=True)  7.81 us
    all_to_all x1, starting transfers between devices, body(): lax.all_to_all(outgoing, 'wide', split_axis=0, concat_axis=0, tiled=True)  7.44 us
  transfers between devices with their start and end apart: 5, of which 2 were waited for; matrix products, arithmetic and copies ran while one was open for 54% of the time, Pallas kernels for 0%

profile of v2, /device:TPU:1, one launch (start us, length us, event | category | flops | bytes accessed | tf_op | source)
XLA Modules:
  0.0 254.6 jit_solution(14256733875889791658)
XLA Ops:
  9.3 1.4 select_reduce_fusion
  11.3 8.6 %all-to-all-start.1 = ((s32[32,96,1]{1,2,0:T(1,128)}), s32[32,96,1]{1,2,0:T(1,128)S(1)}, u32[]{:S(2)}, u32[]{:S(2)}) async-start(s32[32,96,1]{1,2,0:T(1,128)} %all_to_all.26), calls=%async_computation.1 | async-start | bytes 32768 | tf_op jit(solution)/shard_map/all_to_all | solution.py:67
  19.9 6.0 %multiply_reduce_fusion.2 = (f32[1024]{0:T(1024)S(1)}, f32[1024,256]{0,1:T(8,128)}) fusion(bf16[1024,256]{1,0:T(8,128)(2,1)} %param.14, bf16[1024,1024]{1,0:T(8,128)(2,1)S(1)} %copy-done, bf16[1024,1024]{1,0:T(8,128)(2,1)} %param.13), kind=kOutput, calls=%fused_computation.58 | convolution fusion | flops 2694315008 | bytes 5771264 | tf_op jit(solution)/shard_map/dot_general | solution.py:59
  25.9 4.8 %fusion.45 = bf16[3072,256]{1,0:T(8,128)(2,1)} fusion(s32[1024]{0:T(1024)S(1)} %get-tuple-element.213, f32[1024,256]{0,1:T(8,128)} %get-tuple-element.216, f32[1024]{0:T(1024)S(1)} %add_rsqrt_fusion.2), kind=kOutput, calls=%fused_computation.51 | convolution fusion | flops 1615069184 | bytes 2629632 | tf_op jit(solution)/shard_map/dot_general | solution.py:64
  30.7 7.4 %all-to-all-start = ((bf16[32,96,256]{2,1,0:T(8,128)(2,1)}), bf16[32,96,256]{2,1,0:T(8,128)(2,1)}, u32[]{:S(2)}, u32[]{:S(2)}) async-start(bf16[32,96,256]{2,1,0:T(8,128)(2,1)} %bitcast.71), calls=%async_computation | async-start | bytes 3145728 | tf_op jit(solution)/shard_map/all_to_all | solution.py:66
  38.4 22.5 %all-to-all-done = bf16[32,96,256]{2,1,0:T(8,128)(2,1)} async-done(((bf16[32,96,256]{2,1,0:T(8,128)(2,1)}), bf16[32,96,256]{2,1,0:T(8,128)(2,1)}, u32[]{:S(2)}, u32[]{:S(2)}) %all-to-all-start) | async-done | bytes 1572896 | tf_op jit(solution)/shard_map/all_to_all | solution.py:66
  60.9 1.5 fusion.73
  63.5 3.1 %constant_dynamic-slice_fusion.5 = bf16[4096,256]{1,0:T(8,128)(2,1)} fusion(bf16[16384,256]{1,0:T(8,128)(2,1)} %param.15, s32[]{:T(128)S(6)} %select_n.45), kind=kLoop, calls=%fused_computation.115 | loop fusion | bytes 4194308 | tf_op jit(solution)/shard_map/dynamic_slice | solution.py:93
  68.2 17.1 %gather_fusion = bf16[3072,256]{1,0:T(8,128)(2,1)} fusion(bf16[16384,256]{1,0:T(8,128)(2,1)} %param.15, s32[3072]{0:T(1024)S(1)} %broadcast_clamp_fusion), kind=kCustom, calls=%fused_computation | custom fusion | bytes 3158016 | tf_op jit(solution)/shard_map/gather | solution.py:92
  86.2 15.5 %all-gather.7.cloned.1.call-done = bf16[6208,256]{1,0:T(8,128)(2,1)} async-done(((bf16[1552,256]{1,0:T(8,128)(2,1)}), bf16[6208,256]{1,0:T(8,128)(2,1)}) %all-gather.7.cloned.1.call-update) | async-done | bytes 3178512 | tf_op jit(solution)/shard_map/all_gather | solution.py:85
  102.6 55.0 %while.30 = (s32[]{:T(128)}, f32[7,1024,256]{1,2,0:T(8,128)}, s32[7,1024]{1,0:T(8,128)S(1)}, s32[4,1552]{1,0:T(4,128)S(1)}, bf16[6208,256]{1,0:T(8,128)(2,1)}, /*index=5*/s32[]{:T(128)}) while((s32[]{:T(128)}, f32[7,1024,256]{1,2,0:T(8,128)}, s32[7,1024]{1,0:T(8,128)S(1)}, s32[4,1552]{1,0:T(4,128)S(1)}, bf16[6208,256]{1,0:T(8,128)(2,1)}, ...), condition=%wide.region_4.5_spmd, body=%wide.region_3.4_spmd.sunk | while | flops 3261136896 | bytes 4314441 | solution.py:30
  102.7 7.7 %fusion.92 = f32[7,1024,256]{1,2,0:T(8,128)} fusion(f32[7,1024,256]{1,2,0:T(8,128)} %get-tuple-element.349, s32[]{:T(128)} %get-tuple-element.348, bf16[6208,256]{1,0:T(8,128)(2,1)} %get-tuple-element.358, s32[6208]{0:T(1024)S(1)} %eq.230, s32[1024]{0:T(1024)S(1)} %bitcast.76), kind=kOutput, calls=%fused_computation.6.clone.1 | convolution fusion | flops 3261136896 | bytes 4256512 | tf_op jit(solution)/shard_map/while/body/eval_jaxpr/dot_general | solution.py:23
  110.5 7.8 %fusion.92 = f32[7,1024,256]{1,2,0:T(8,128)} fusion(f32[7,1024,256]{1,2,0:T(8,128)} %get-tuple-element.349, s32[]{:T(128)} %get-tuple-element.348, bf16[6208,256]{1,0:T(8,128)(2,1)} %get-tuple-element.358, s32[6208]{0:T(1024)S(1)} %eq.230, s32[1024]{0:T(1024)S(1)} %bitcast.76), kind=kOutput, calls=%fused_computation.6.clone.1 | convolution fusion | flops 3261136896 | bytes 4256512 | tf_op jit(solution)/shard_map/while/body/eval_jaxpr/dot_general | solution.py:23
  118.4 7.7 %fusion.92 = f32[7,1024,256]{1,2,0:T(8,128)} fusion(f32[7,1024,256]{1,2,0:T(8,128)} %get-tuple-element.349, s32[]{:T(128)} %get-tuple-element.348, bf16[6208,256]{1,0:T(8,128)(2,1)} %get-tuple-element.358, s32[6208]{0:T(1024)S(1)} %eq.230, s32[1024]{0:T(1024)S(1)} %bitcast.76), kind=kOutput, calls=%fused_computation.6.clone.1 | convolution fusion | flops 3261136896 | bytes 4256512 | tf_op jit(solution)/shard_map/while/body/eval_jaxpr/dot_general | solution.py:23
  126.2 7.8 %fusion.92 = f32[7,1024,256]{1,2,0:T(8,128)} fusion(f32[7,1024,256]{1,2,0:T(8,128)} %get-tuple-element.349, s32[]{:T(128)} %get-tuple-element.348, bf16[6208,256]{1,0:T(8,128)(2,1)} %get-tuple-element.358, s32[6208]{0:T(1024)S(1)} %eq.230, s32[1024]{0:T(1024)S(1)} %bitcast.76), kind=kOutput, calls=%fused_computation.6.clone.1 | convolution fusion | flops 3261136896 | bytes 4256512 | tf_op jit(solution)/shard_map/while/body/eval_jaxpr/dot_general | solution.py:23
  134.1 7.7 %fusion.92 = f32[7,1024,256]{1,2,0:T(8,128)} fusion(f32[7,1024,256]{1,2,0:T(8,128)} %get-tuple-element.349, s32[]{:T(128)} %get-tuple-element.348, bf16[6208,256]{1,0:T(8,128)(2,1)} %get-tuple-element.358, s32[6208]{0:T(1024)S(1)} %eq.230, s32[1024]{0:T(1024)S(1)} %bitcast.76), kind=kOutput, calls=%fused_computation.6.clone.1 | convolution fusion | flops 3261136896 | bytes 4256512 | tf_op jit(solution)/shard_map/while/body/eval_jaxpr/dot_general | solution.py:23
  141.9 7.7 %fusion.92 = f32[7,1024,256]{1,2,0:T(8,128)} fusion(f32[7,1024,256]{1,2,0:T(8,128)} %get-tuple-element.349, s32[]{:T(128)} %get-tuple-element.348, bf16[6208,256]{1,0:T(8,128)(2,1)} %get-tuple-element.358, s32[6208]{0:T(1024)S(1)} %eq.230, s32[1024]{0:T(1024)S(1)} %bitcast.76), kind=kOutput, calls=%fused_computation.6.clone.1 | convolution fusion | flops 3261136896 | bytes 4256512 | tf_op jit(solution)/shard_map/while/body/eval_jaxpr/dot_general | solution.py:23
  149.8 7.7 %fusion.92 = f32[7,1024,256]{1,2,0:T(8,128)} fusion(f32[7,1024,256]{1,2,0:T(8,128)} %get-tuple-element.349, s32[]{:T(128)} %get-tuple-element.348, bf16[6208,256]{1,0:T(8,128)(2,1)} %get-tuple-element.358, s32[6208]{0:T(1024)S(1)} %eq.230, s32[1024]{0:T(1024)S(1)} %bitcast.76), kind=kOutput, calls=%fused_computation.6.clone.1 | convolution fusion | flops 3261136896 | bytes 4256512 | tf_op jit(solution)/shard_map/while/body/eval_jaxpr/dot_general | solution.py:23
  157.5 3.9 %slice.73 = f32[3,1024,256]{1,2,0:T(8,128)} slice(f32[7,1024,256]{1,2,0:T(8,128)} %get-tuple-element.103), slice={[0:3], [0:1024], [0:256]} | slice | bytes 6291456 | tf_op jit(solution)/shard_map/slice | solution.py:98
  161.5 4.9 %slice.72 = f32[4,1024,256]{1,2,0:T(8,128)} slice(f32[7,1024,256]{1,2,0:T(8,128)} %get-tuple-element.103), slice={[3:7], [0:1024], [0:256]} | slice | bytes 8388608 | tf_op jit(solution)/shard_map/slice | solution.py:100
  167.2 29.0 %while.32 = (s32[]{:T(128)}, bf16[3,1024,256]{2,1,0:T(8,128)(2,1)}, bf16[3,1024,256]{2,1,0:T(8,128)(2,1)}, s32[3,1024]{1,0:T(4,128)S(1)}, s32[4,1552]{1,0:T(4,12...) while((s32[]{:T(128)}, bf16[3,1024,256]{2,1,0:T(8,128)(2,1)}, ...), condition=%wide.region_10.11_spmd, body=%wide.region_8.10_spmd.sunk | while | flops 3262972928 | bytes 11670881 | solution.py:30
  167.2 1.1 constant_dynamic-slice_fusion.15
  168.6 7.1 %multiply_reduce_fusion.6 = (f32[1024]{0:T(1024)S(1)}, f32[1024,256]{0,1:T(8,128)S(1)}) fusion(f32[3,1024,256]{1,2,0:T(8,128)} %get-tuple-element.406, s32[]{:T(128)} %get-tuple-element.392, bf16[6208,256]{1,0:T(8,128)(2,1)} %get-tuple-element.405, s32[6208]{0:T(1024)S(1)} %eq.238, s32[1024]{0:T(1024)S(1)} %bitcast.74, ...), kind=kOutput, calls=%fused_computation.28.clone.1 | convolution fusion | flops 3262446592 | bytes 5832964 | tf_op jit(solution)/shard_map/while/body/eval_jaxpr/dot_general | solution.py:23
  178.3 7.0 %multiply_reduce_fusion.6 = (f32[1024]{0:T(1024)S(1)}, f32[1024,256]{0,1:T(8,128)S(1)}) fusion(f32[3,1024,256]{1,2,0:T(8,128)} %get-tuple-element.406, s32[]{:T(128)} %get-tuple-element.392, bf16[6208,256]{1,0:T(8,128)(2,1)} %get-tuple-element.405, s32[6208]{0:T(1024)S(1)} %eq.238, s32[1024]{0:T(1024)S(1)} %bitcast.74, ...), kind=kOutput, calls=%fused_computation.28.clone.1 | convolution fusion | flops 3262446592 | bytes 5832964 | tf_op jit(solution)/shard_map/while/body/eval_jaxpr/dot_general | solution.py:23
  187.9 7.1 %multiply_reduce_fusion.6 = (f32[1024]{0:T(1024)S(1)}, f32[1024,256]{0,1:T(8,128)S(1)}) fusion(f32[3,1024,256]{1,2,0:T(8,128)} %get-tuple-element.406, s32[]{:T(128)} %get-tuple-element.392, bf16[6208,256]{1,0:T(8,128)(2,1)} %get-tuple-element.405, s32[6208]{0:T(1024)S(1)} %eq.238, s32[1024]{0:T(1024)S(1)} %bitcast.74, ...), kind=kOutput, calls=%fused_computation.28.clone.1 | convolution fusion | flops 3262446592 | bytes 5832964 | tf_op jit(solution)/shard_map/while/body/eval_jaxpr/dot_general | solution.py:23
  196.2 7.8 %all-to-all-start.2 = ((bf16[32,96,256]{2,1,0:T(8,128)(2,1)}), bf16[32,96,256]{2,1,0:T(8,128)(2,1)}, u32[]{:S(2)}, u32[]{:S(2)}) async-start(bf16[32,96,256]{2,1,0:T(8,128)(2,1)} %bitcast.70), calls=%async_computation.2 | async-start | bytes 3145728 | tf_op jit(solution)/shard_map/all_to_all | solution.py:99
  204.0 38.5 %while.31 = (s32[]{:T(128)}, bf16[4,1024,256]{2,1,0:T(8,128)(2,1)}, bf16[4,1024,256]{2,1,0:T(8,128)(2,1)}, s32[4,1024]{1,0:T(4,128)S(1)}, s32[4,1552]{1,0:T(4,12...) while((s32[]{:T(128)}, bf16[4,1024,256]{2,1,0:T(8,128)(2,1)}, ...), condition=%wide.region_7.8_spmd, body=%wide.region_5.7_spmd.sunk | while | flops 3262972928 | bytes 11670881 | solution.py:30
  205.4 7.1 %multiply_reduce_fusion.5 = (f32[1024]{0:T(1024)S(1)}, f32[1024,256]{0,1:T(8,128)S(1)}) fusion(f32[4,1024,256]{1,2,0:T(8,128)} %get-tuple-element.382, s32[]{:T(128)} %get-tuple-element.368, bf16[6208,256]{1,0:T(8,128)(2,1)} %get-tuple-element.381, s32[6208]{0:T(1024)S(1)} %eq.234, s32[1024]{0:T(1024)S(1)} %bitcast.75, ...), kind=kOutput, calls=%fused_computation.15.clone.1 | convolution fusion | flops 3262446592 | bytes 5832964 | tf_op jit(solution)/shard_map/while/body/eval_jaxpr/dot_general | solution.py:23
  215.0 7.1 %multiply_reduce_fusion.5 = (f32[1024]{0:T(1024)S(1)}, f32[1024,256]{0,1:T(8,128)S(1)}) fusion(f32[4,1024,256]{1,2,0:T(8,128)} %get-tuple-element.382, s32[]{:T(128)} %get-tuple-element.368, bf16[6208,256]{1,0:T(8,128)(2,1)} %get-tuple-element.381, s32[6208]{0:T(1024)S(1)} %eq.234, s32[1024]{0:T(1024)S(1)} %bitcast.75, ...), kind=kOutput, calls=%fused_computation.15.clone.1 | convolution fusion | flops 3262446592 | bytes 5832964 | tf_op jit(solution)/shard_map/while/body/eval_jaxpr/dot_general | solution.py:23
  224.7 7.0 %multiply_reduce_fusion.5 = (f32[1024]{0:T(1024)S(1)}, f32[1024,256]{0,1:T(8,128)S(1)}) fusion(f32[4,1024,256]{1,2,0:T(8,128)} %get-tuple-element.382, s32[]{:T(128)} %get-tuple-element.368, bf16[6208,256]{1,0:T(8,128)(2,1)} %get-tuple-element.381, s32[6208]{0:T(1024)S(1)} %eq.234, s32[1024]{0:T(1024)S(1)} %bitcast.75, ...), kind=kOutput, calls=%fused_computation.15.clone.1 | convolution fusion | flops 3262446592 | bytes 5832964 | tf_op jit(solution)/shard_map/while/body/eval_jaxpr/dot_general | solution.py:23
  234.3 7.0 %multiply_reduce_fusion.5 = (f32[1024]{0:T(1024)S(1)}, f32[1024,256]{0,1:T(8,128)S(1)}) fusion(f32[4,1024,256]{1,2,0:T(8,128)} %get-tuple-element.382, s32[]{:T(128)} %get-tuple-element.368, bf16[6208,256]{1,0:T(8,128)(2,1)} %get-tuple-element.381, s32[6208]{0:T(1024)S(1)} %eq.234, s32[1024]{0:T(1024)S(1)} %bitcast.75, ...), kind=kOutput, calls=%fused_computation.15.clone.1 | convolution fusion | flops 3262446592 | bytes 5832964 | tf_op jit(solution)/shard_map/while/body/eval_jaxpr/dot_general | solution.py:23
  242.5 4.3 %fusion.49 = bf16[1024,256]{0,1:T(8,128)(2,1)S(1)} fusion(bf16[3072,256]{1,0:T(8,128)(2,1)} %bitcast.20, s32[1024]{0:T(1024)S(1)} %get-tuple-element.213, f32[1024,256]{0,1:T(8,128)} %get-tuple-element.216, f32[1024]{0:T(1024)S(1)} %add_rsqrt_fusion.2), kind=kOutput, calls=%fused_computation.54 | convolution fusion | flops 1615069184 | bytes 3153920 | tf_op jit(solution)/shard_map/dot_general | solution.py:102
  (119 shorter events, 26.5 us)
Async XLA Ops:
  7.2 12.7 %copy-start = (bf16[1024,1024]{1,0:T(8,128)(2,1)S(1)}, bf16[1024,1024]{1,0:T(8,128)(2,1)}, u32[]{:S(2)}) copy-start(bf16[1024,1024]{1,0:T(8,128)(2,1)} %param.11) | copy-start | bytes 6291460
  11.3 19.4 %all-to-all-start.1 = ((s32[32,96,1]{1,2,0:T(1,128)}), s32[32,96,1]{1,2,0:T(1,128)S(1)}, u32[]{:S(2)}, u32[]{:S(2)}) async-start(s32[32,96,1]{1,2,0:T(1,128)} %all_to_all.26), calls=%async_computation.1 | async-start | bytes 32768 | tf_op jit(solution)/shard_map/all_to_all | solution.py:67
  30.7 30.2 %all-to-all-start = ((bf16[32,96,256]{2,1,0:T(8,128)(2,1)}), bf16[32,96,256]{2,1,0:T(8,128)(2,1)}, u32[]{:S(2)}, u32[]{:S(2)}) async-start(bf16[32,96,256]{2,1,0:T(8,128)(2,1)} %bitcast.71), calls=%async_computation | async-start | bytes 3145728 | tf_op jit(solution)/shard_map/all_to_all | solution.py:66
  38.2 63.5 %all-gather.7.cloned.1.call-start = ((), (), s32[]{:S(2)}) async-start(), calls=%async_computation.4 | async-start | bytes 3973120 | tf_op jit(solution)/shard_map/all_gather | solution.py:85
  63.4 103.0 %all-gather.5.cloned.1.call-start = ((), (), s32[]{:S(2)}) async-start(), calls=%async_computation.3 | async-start | bytes 3973120 | tf_op jit(solution)/shard_map/all_gather | solution.py:85
  196.2 46.3 %all-to-all-start.2 = ((bf16[32,96,256]{2,1,0:T(8,128)(2,1)}), bf16[32,96,256]{2,1,0:T(8,128)(2,1)}, u32[]{:S(2)}, u32[]{:S(2)}) async-start(bf16[32,96,256]{2,1,0:T(8,128)(2,1)} %bitcast.70), calls=%async_computation.2 | async-start | bytes 3145728 | tf_op jit(solution)/shard_map/all_to_all | solution.py:99
Sparse Core Ops, SparseCore 0:
  63.5 38.2 all-gather.6
  103.4 39.9 all-gather.4

commit v3 on v0

--- a/solution.py
+++ b/solution.py
@@ -62,22 +62,27 @@
     id_code = jnp.concatenate([in_ids // 128, in_ids % 128]).astype(jnp.bfloat16)
     id_code = jnp.pad(id_code, (0, code_rows * emb_width - 2 * slots))
     payload = jnp.concatenate([incoming, id_code.reshape(code_rows, emb_width)])
-    rows_all = lax.all_gather(payload, "rep", axis=0)
-    code = rows_all[:, slots:].reshape(replicas, -1)[:, : 2 * slots].astype(jnp.int32)
-    keys = code[:, :slots] * 128 + code[:, slots:]
-    keys = jnp.pad(keys, ((0, 0), (0, code_rows)), constant_values=-1).reshape(-1)
-    rows = rows_all.reshape(-1, emb_width)
+    shifted = [
+        lax.ppermute(payload, "rep", [(i, (i + step) % replicas) for i in range(replicas)])
+        for step in range(1, replicas)
+    ]
+    rows_oth = jnp.concatenate(shifted)
+    code = rows_oth.reshape(replicas - 1, -1, emb_width)[:, slots:]
+    code = code.reshape(replicas - 1, -1)[:, : 2 * slots].astype(jnp.int32)
+    keys_oth = code[:, :slots] * 128 + code[:, slots:]
+    keys_oth = jnp.pad(keys_oth, ((0, 0), (0, code_rows)), constant_values=-1).reshape(-1)
 
     first_row = my_rep * share_rows
     share_ids = first_row + jnp.arange(share_rows, dtype=jnp.int32)
     look_cent = centroids[in_ids].astype(jnp.float32)
     own_cent = lax.dynamic_slice_in_dim(centroids, first_row, share_rows, 0).astype(jnp.float32)
 
-    look_sum = match_sums(in_ids, keys, rows)
+    own_sums = match_sums(jnp.concatenate([in_ids, share_ids]), in_ids, incoming)
+    look_sum = own_sums[:slots] + match_sums(in_ids, keys_oth, rows_oth)
     picked = normalize(look_cent + look_sum)
     returned = lax.all_to_all(picked, "wide", split_axis=0, concat_axis=0, tiled=True)
 
-    share_sum = match_sums(share_ids, keys, rows)
+    share_sum = own_sums[slots:] + match_sums(share_ids, keys_oth, rows_oth)
     own_rows = normalize(own_cent + share_sum)
 
     gathered_rows = jnp.dot(place_bf.T, returned, preferred_element_type=jnp.float32)

time: 239 us -> 231 us (0.967)
  waiting for transfers between devices: 65.8 us -> 37.7 us
  matrix products: 88 us -> 106 us
  between operations: 14.3 us -> 0.86 us
  other arithmetic: 24.2 us -> 29.6 us
  local copies, waits for them, and re-layouts: 21.8 us -> 26.7 us
  starting transfers between devices: 24 us -> 28.9 us
    all_gather x1 -> x0, waiting for transfers between devices: 44.5 us -> none  [body(): rows_all = lax.all_gather(payload, 'rep', axis=0)]
    ppermute x0 -> x3, waiting for transfers between devices: none -> 36.5 us  [body(): lax.ppermute(payload, 'rep', [(i, (i + step) % replicas) for i in range(r...]
    all_to_all x1, waiting for transfers between devices: 21.3 us -> 1.2 us  [body(): lax.all_to_all(outgoing, 'wide', split_axis=0, concat_axis=0, tiled=True)]
    dot_general x7 -> x14, matrix products: 74.6 us -> 89.9 us  [one_block(): return jnp.dot(selector, rows, preferred_element_type=jnp.float32)]
    ppermute x0 -> x3, starting transfers between devices: none -> 5.67 us  [body(): lax.ppermute(payload, 'rep', [(i, (i + step) % replicas) for i in range(r...]
    add x1 -> x2, other arithmetic: 0.02 us -> 4.02 us  [the longest x1 4.01 us: body(): share_sum = own_sums[slots:] + match_sums(share_ids, keys_oth, rows_oth)]
    unnamed x17 -> x11, local copies, waits for them, and re-layouts: 2.95 us -> 6.7 us
  transfers between devices with their start and end apart: 4 -> 6, of which waited for: 2 -> 3; matrix products, arithmetic and copies ran while one was open for 33% -> 48% of each run, Pallas kernels for 0% -> 0%
where the time goes in v3:
time: 231 us; the launch traced here: 229 us
  matrix products  106 us (46%)
  waiting for transfers between devices  37.7 us (16%)
  other arithmetic  29.6 us (13%)
  starting transfers between devices  28.9 us (13%)
  local copies, waits for them, and re-layouts  26.7 us (12%)
    dot_general x14, matrix products, one_block(): return jnp.dot(selector, rows, preferred_element_type=jnp.float32)  89.9 us
    ppermute x3, waiting for transfers between devices, body(): lax.ppermute(payload, 'rep', [(i, (i + step) % replicas) for i in range(r...  36.5 us
    gather x1, local copies, waits for them, and re-layouts, body(): look_cent = centroids[in_ids].astype(jnp.float32)  16.6 us
    all_to_all x1, starting transfers between devices, body(): lax.all_to_all(out_ids, 'wide', split_axis=0, concat_axis=0, tiled=True)  8.58 us
    reduce_sum x2, other arithmetic, normalize(): jnp.mean(updated * updated, axis=-1, keepdims=True) + 1e-06  8.42 us
    convert_element_type x2, other arithmetic, normalize(): return (updated * lax.rsqrt(jnp.mean(updated * updated, axis=-1, keepdims...  7.53 us
    all_to_all x1, starting transfers between devices, body(): lax.all_to_all(outgoing, 'wide', split_axis=0, concat_axis=0, tiled=True)  7.43 us
    all_to_all x1, starting transfers between devices, body(): lax.all_to_all(picked, 'wide', split_axis=0, concat_axis=0, tiled=True)  7.25 us
  transfers between devices with their start and end apart: 6, of which 3 were waited for; matrix products, arithmetic and copies ran while one was open for 48% of the time, Pallas kernels for 0%

profile of v3, /device:TPU:1, one launch (start us, length us, event | category | flops | bytes accessed | tf_op | source)
XLA Modules:
  0.0 229.4 jit_solution(11129604945873946995)
XLA Ops:
  4.8 8.6 %all-to-all-start = ((s32[32,96,1]{1,2,0:T(1,128)}), s32[32,96,1]{1,2,0:T(1,128)S(1)}, u32[]{:S(2)}, u32[]{:S(2)}) async-start(s32[32,96,1]{1,2,0:T(1,128)} %all_to_all.24), calls=%async_computation | async-start | bytes 32768 | tf_op jit(solution)/shard_map/all_to_all | solution.py:58
  13.4 6.0 %multiply_reduce_fusion.2 = (f32[1024]{0:T(1024)S(1)}, f32[1024,256]{0,1:T(8,128)}) fusion(bf16[1024,256]{1,0:T(8,128)(2,1)} %param.14, bf16[1024,1024]{1,0:T(8,128)(2,1)S(1)} %copy-done, bf16[1024,1024]{1,0:T(8,128)(2,1)} %param.13), kind=kOutput, calls=%fused_computation.54 | convolution fusion | flops 2694315008 | bytes 5771264 | tf_op jit(solution)/shard_map/dot_general | solution.py:50
  19.4 4.8 %fusion.43 = bf16[3072,256]{1,0:T(8,128)(2,1)} fusion(s32[1024]{0:T(1024)S(1)} %get-tuple-element.126, f32[1024,256]{0,1:T(8,128)} %get-tuple-element.129, f32[1024]{0:T(1024)S(1)} %add_rsqrt_fusion.2), kind=kOutput, calls=%fused_computation.43 | convolution fusion | flops 1615069184 | bytes 2629632 | tf_op jit(solution)/shard_map/dot_general | solution.py:55
  24.2 7.4 %all-to-all-start.1 = ((bf16[32,96,256]{2,1,0:T(8,128)(2,1)}), bf16[32,96,256]{2,1,0:T(8,128)(2,1)}, u32[]{:S(2)}, u32[]{:S(2)}) async-start(bf16[32,96,256]{2,1,0:T(8,128)(2,1)} %bitcast.68), calls=%async_computation.1 | async-start | bytes 3145728 | tf_op jit(solution)/shard_map/all_to_all | solution.py:57
  33.3 16.6 %gather_fusion = bf16[3072,256]{1,0:T(8,128)(2,1)} fusion(bf16[16384,256]{1,0:T(8,128)(2,1)} %param.15, s32[3072]{0:T(1024)S(1)} %broadcast_clamp_fusion), kind=kCustom, calls=%fused_computation | custom fusion | bytes 3158016 | tf_op jit(solution)/shard_map/gather | solution.py:77
  49.9 3.3 %convert_element_type.67 = f32[3072,256]{1,0:T(8,128)} convert(bf16[3072,256]{1,0:T(8,128)(2,1)} %gather_fusion) | non-fusion elementwise | flops 786432 | bytes 4718592 | tf_op jit(solution)/shard_map/convert_element_type | solution.py:77
  58.7 3.3 %collective-permute-start.1 = (bf16[3104,256]{1,0:T(8,128)(2,1)}, bf16[3104,256]{1,0:T(8,128)(2,1)}, u32[]{:S(2)}, u32[]{:S(2)}) collective-permute-start(bf16[3104,256]{1,0:T(8,128)(2,1)} %pad_maximum_fusion), channel_id=1, source_target_pairs={{0,2},{1,3},{2,0},{3,1},{4,6},{5,7},{6,4},{7,5},{8,10},{9,11},{10,... | collective-permute-start | bytes 4767752 | tf_op jit(solution)/shard_map/ppermute | solution.py:66
  62.7 29.9 %while.32 = (s32[]{:T(128)}, f32[7,1024,256]{2,1,0:T(8,128)}, s32[7,1024]{1,0:T(8,128)S(1)}, s32[3072]{0:T(1024)S(1)}, bf16[3072,256]{1,0:T(8,128)(2,1)}, /*index=5*/s32[]{:T(128)}) while((s32[]{:T(128)}, f32[7,1024,256]{2,1,0:T(8,128)}, s32[7,1024]{1,0:T(8,128)S(1)}, s32[3072]{0:T(1024)S(1)}, bf16[3072,256]{1,0:T(8,128)(2,1)}, ...), condition=%wide.region_4.5_spmd, body=%wide.region_3.4_spmd.sunk | while | flops 1613758464 | bytes 2646601 | solution.py:22
  62.7 4.3 %fusion.90 = f32[7,1024,256]{2,1,0:T(8,128)} fusion(f32[7,1024,256]{2,1,0:T(8,128)} %get-tuple-element.303, s32[]{:T(128)} %get-tuple-element.302, bf16[3072,256]{1,0:T(8,128)(2,1)} %get-tuple-element.312, s32[3072]{0:T(1024)S(1)} %get-tuple-element.311, s32[1024]{0:T(1024)S(1)} %bitcast.73), kind=kOutput, calls=%fused_computation.6.clone.1 | convolution fusion | flops 1613758464 | bytes 2638336 | tf_op jit(solution)/shard_map/while/body/eval_jaxpr/dot_general | solution.py:20
  67.0 4.3 %fusion.90 = f32[7,1024,256]{2,1,0:T(8,128)} fusion(f32[7,1024,256]{2,1,0:T(8,128)} %get-tuple-element.303, s32[]{:T(128)} %get-tuple-element.302, bf16[3072,256]{1,0:T(8,128)(2,1)} %get-tuple-element.312, s32[3072]{0:T(1024)S(1)} %get-tuple-element.311, s32[1024]{0:T(1024)S(1)} %bitcast.73), kind=kOutput, calls=%fused_computation.6.clone.1 | convolution fusion | flops 1613758464 | bytes 2638336 | tf_op jit(solution)/shard_map/while/body/eval_jaxpr/dot_general | solution.py:20
  71.3 4.3 %fusion.90 = f32[7,1024,256]{2,1,0:T(8,128)} fusion(f32[7,1024,256]{2,1,0:T(8,128)} %get-tuple-element.303, s32[]{:T(128)} %get-tuple-element.302, bf16[3072,256]{1,0:T(8,128)(2,1)} %get-tuple-element.312, s32[3072]{0:T(1024)S(1)} %get-tuple-element.311, s32[1024]{0:T(1024)S(1)} %bitcast.73), kind=kOutput, calls=%fused_computation.6.clone.1 | convolution fusion | flops 1613758464 | bytes 2638336 | tf_op jit(solution)/shard_map/while/body/eval_jaxpr/dot_general | solution.py:20
  75.6 4.3 %fusion.90 = f32[7,1024,256]{2,1,0:T(8,128)} fusion(f32[7,1024,256]{2,1,0:T(8,128)} %get-tuple-element.303, s32[]{:T(128)} %get-tuple-element.302, bf16[3072,256]{1,0:T(8,128)(2,1)} %get-tuple-element.312, s32[3072]{0:T(1024)S(1)} %get-tuple-element.311, s32[1024]{0:T(1024)S(1)} %bitcast.73), kind=kOutput, calls=%fused_computation.6.clone.1 | convolution fusion | flops 1613758464 | bytes 2638336 | tf_op jit(solution)/shard_map/while/body/eval_jaxpr/dot_general | solution.py:20
  79.8 4.2 %fusion.90 = f32[7,1024,256]{2,1,0:T(8,128)} fusion(f32[7,1024,256]{2,1,0:T(8,128)} %get-tuple-element.303, s32[]{:T(128)} %get-tuple-element.302, bf16[3072,256]{1,0:T(8,128)(2,1)} %get-tuple-element.312, s32[3072]{0:T(1024)S(1)} %get-tuple-element.311, s32[1024]{0:T(1024)S(1)} %bitcast.73), kind=kOutput, calls=%fused_computation.6.clone.1 | convolution fusion | flops 1613758464 | bytes 2638336 | tf_op jit(solution)/shard_map/while/body/eval_jaxpr/dot_general | solution.py:20
  84.1 4.3 %fusion.90 = f32[7,1024,256]{2,1,0:T(8,128)} fusion(f32[7,1024,256]{2,1,0:T(8,128)} %get-tuple-element.303, s32[]{:T(128)} %get-tuple-element.302, bf16[3072,256]{1,0:T(8,128)(2,1)} %get-tuple-element.312, s32[3072]{0:T(1024)S(1)} %get-tuple-element.311, s32[1024]{0:T(1024)S(1)} %bitcast.73), kind=kOutput, calls=%fused_computation.6.clone.1 | convolution fusion | flops 1613758464 | bytes 2638336 | tf_op jit(solution)/shard_map/while/body/eval_jaxpr/dot_general | solution.py:20
  88.4 4.3 %fusion.90 = f32[7,1024,256]{2,1,0:T(8,128)} fusion(f32[7,1024,256]{2,1,0:T(8,128)} %get-tuple-element.303, s32[]{:T(128)} %get-tuple-element.302, bf16[3072,256]{1,0:T(8,128)(2,1)} %get-tuple-element.312, s32[3072]{0:T(1024)S(1)} %get-tuple-element.311, s32[1024]{0:T(1024)S(1)} %bitcast.73), kind=kOutput, calls=%fused_computation.6.clone.1 | convolution fusion | flops 1613758464 | bytes 2638336 | tf_op jit(solution)/shard_map/while/body/eval_jaxpr/dot_general | solution.py:20
  92.7 3.0 %collective-permute-done = bf16[3104,256]{1,0:T(8,128)(2,1)} collective-permute-done((bf16[3104,256]{1,0:T(8,128)(2,1)}, bf16[3104,256]{1,0:T(8,128)(2,1)}, u32[]{:S(2)}, u32[]{:S(2)}) %collective-permute-start) | collective-permute-done | bytes 1589280 | tf_op jit(solution)/shard_map/ppermute | solution.py:66
  97.2 33.4 %collective-permute-done.1 = bf16[3104,256]{1,0:T(8,128)(2,1)} collective-permute-done((bf16[3104,256]{1,0:T(8,128)(2,1)}, bf16[3104,256]{1,0:T(8,128)(2,1)}, u32[]{:S(2)}, u32[]{:S(2)}) %collective-permute-start.1) | collective-permute-done | bytes 1589280 | tf_op jit(solution)/shard_map/ppermute | solution.py:66
  136.7 25.7 %while.34 = (s32[]{:T(128)}, f32[3,1024,256]{2,1,0:T(8,128)}, s32[3,1024]{1,0:T(4,128)S(1)}, s32[3,3104]{1,0:T(4,128)}, bf16[9312,256]{1,0:T(8,128)(2,1)}, /*index=5*/s32[9312]{0:T(1024)S(1)}, s32[]{:T(128)}) while((s32[]{:T(128)}, f32[3,1024,256]{2,1,0:T(8,128)}, s32[3,1024]{1,0:T(4,128)S(1)}, s32[3,3104]{1,0:T(4,128)}, ...), condition=%wide.wide.region_9.10_spmd, body=%wide.wide.region_8.9_spmd.sunk | while | flops 4891705344 | bytes 5866449 | solution.py:22
  136.7 8.6 %fusion.96 = f32[3,1024,256]{2,1,0:T(8,128)} fusion(f32[3,1024,256]{2,1,0:T(8,128)} %get-tuple-element.322, s32[]{:T(128)} %get-tuple-element.321, bf16[9312,256]{1,0:T(8,128)(2,1)} %get-tuple-element.332, s32[9312]{0:T(1024)S(1)} %get-tuple-element.333, s32[1024]{0:T(1024)S(1)} %bitcast.74), kind=kOutput, calls=%fused_computation.20.clone.clone.1 | convolution fusion | flops 4891705344 | bytes 5858176 | tf_op jit(solution)/shard_map/while/body/eval_jaxpr/dot_general | solution.py:20
  145.2 8.5 %fusion.96 = f32[3,1024,256]{2,1,0:T(8,128)} fusion(f32[3,1024,256]{2,1,0:T(8,128)} %get-tuple-element.322, s32[]{:T(128)} %get-tuple-element.321, bf16[9312,256]{1,0:T(8,128)(2,1)} %get-tuple-element.332, s32[9312]{0:T(1024)S(1)} %get-tuple-element.333, s32[1024]{0:T(1024)S(1)} %bitcast.74), kind=kOutput, calls=%fused_computation.20.clone.clone.1 | convolution fusion | flops 4891705344 | bytes 5858176 | tf_op jit(solution)/shard_map/while/body/eval_jaxpr/dot_general | solution.py:20
  153.8 8.6 %fusion.96 = f32[3,1024,256]{2,1,0:T(8,128)} fusion(f32[3,1024,256]{2,1,0:T(8,128)} %get-tuple-element.322, s32[]{:T(128)} %get-tuple-element.321, bf16[9312,256]{1,0:T(8,128)(2,1)} %get-tuple-element.332, s32[9312]{0:T(1024)S(1)} %get-tuple-element.333, s32[1024]{0:T(1024)S(1)} %bitcast.74), kind=kOutput, calls=%fused_computation.20.clone.clone.1 | convolution fusion | flops 4891705344 | bytes 5858176 | tf_op jit(solution)/shard_map/while/body/eval_jaxpr/dot_general | solution.py:20
  162.4 5.9 %multiply_reduce_fusion.1 = (f32[3,1024]{1,0:T(4,128)S(1)}, f32[3,1024,256]{2,1,0:T(8,128)}) fusion(f32[3,1024,256]{2,1,0:T(8,128)} %bitcast.65, f32[3,1024,256]{2,1,0:T(8,128)} %get-tuple-element.85, f32[7,1024,256]{2,1,0:T(8,128)} %get-tuple-element.83), kind=kLoop, calls=%fused_computation.45 | loop fusion | flops 3142656 | bytes 12595200 | tf_op jit(solution)/shard_map/reduce_sum | solution.py:9
  168.4 4.5 %multiply_convert_fusion.1 = bf16[32,96,256]{2,1,0:T(8,128)(2,1)} fusion(f32[32,96,256]{2,1,0:T(8,128)} %bitcast.66, f32[32,96,256]{2,1,0:T(8,128)} %bitcast.67, f32[32,96]{1,0:T(8,128)S(1)} %rsqrt.30), kind=kLoop, calls=%fused_computation.44 | loop fusion | flops 2359296 | bytes 7876608 | tf_op jit(solution)/shard_map/convert_element_type | solution.py:10
  172.9 7.2 %all-to-all-start.2 = ((bf16[32,96,256]{2,1,0:T(8,128)(2,1)}), bf16[32,96,256]{2,1,0:T(8,128)(2,1)}, u32[]{:S(2)}, u32[]{:S(2)}) async-start(bf16[32,96,256]{2,1,0:T(8,128)(2,1)} %multiply_convert_fusion.1), calls=%async_computation.2 | async-start | bytes 3145728 | tf_op jit(solution)/shard_map/all_to_all | solution.py:83
  180.2 34.4 %while.33 = (s32[]{:T(128)}, f32[4,1024,256]{2,1,0:T(8,128)}, s32[4,1024]{1,0:T(4,128)S(1)}, s32[3,3104]{1,0:T(4,128)}, bf16[9312,256]{1,0:T(8,128)(2,1)}, /*index=5*/s32[9312]{0:T(1024)S(1)}, s32[]{:T(128)}) while((s32[]{:T(128)}, f32[4,1024,256]{2,1,0:T(8,128)}, s32[4,1024]{1,0:T(4,128)S(1)}, s32[3,3104]{1,0:T(4,128)}, ...), condition=%wide.wide.region_6.7_spmd, body=%wide.wide.region_5.6_spmd.sunk | while | flops 4891705344 | bytes 5866449 | solution.py:22
  180.2 8.6 %fusion.93 = f32[4,1024,256]{2,1,0:T(8,128)} fusion(f32[4,1024,256]{2,1,0:T(8,128)} %get-tuple-element.283, s32[]{:T(128)} %get-tuple-element.282, bf16[9312,256]{1,0:T(8,128)(2,1)} %get-tuple-element.293, s32[9312]{0:T(1024)S(1)} %get-tuple-element.294, s32[1024]{0:T(1024)S(1)} %bitcast.75), kind=kOutput, calls=%fused_computation.13.clone.clone.1 | convolution fusion | flops 4891705344 | bytes 5858176 | tf_op jit(solution)/shard_map/while/body/eval_jaxpr/dot_general | solution.py:20
  188.8 8.6 %fusion.93 = f32[4,1024,256]{2,1,0:T(8,128)} fusion(f32[4,1024,256]{2,1,0:T(8,128)} %get-tuple-element.283, s32[]{:T(128)} %get-tuple-element.282, bf16[9312,256]{1,0:T(8,128)(2,1)} %get-tuple-element.293, s32[9312]{0:T(1024)S(1)} %get-tuple-element.294, s32[1024]{0:T(1024)S(1)} %bitcast.75), kind=kOutput, calls=%fused_computation.13.clone.clone.1 | convolution fusion | flops 4891705344 | bytes 5858176 | tf_op jit(solution)/shard_map/while/body/eval_jaxpr/dot_general | solution.py:20
  197.4 8.6 %fusion.93 = f32[4,1024,256]{2,1,0:T(8,128)} fusion(f32[4,1024,256]{2,1,0:T(8,128)} %get-tuple-element.283, s32[]{:T(128)} %get-tuple-element.282, bf16[9312,256]{1,0:T(8,128)(2,1)} %get-tuple-element.293, s32[9312]{0:T(1024)S(1)} %get-tuple-element.294, s32[1024]{0:T(1024)S(1)} %bitcast.75), kind=kOutput, calls=%fused_computation.13.clone.clone.1 | convolution fusion | flops 4891705344 | bytes 5858176 | tf_op jit(solution)/shard_map/while/body/eval_jaxpr/dot_general | solution.py:20
  206.0 8.6 %fusion.93 = f32[4,1024,256]{2,1,0:T(8,128)} fusion(f32[4,1024,256]{2,1,0:T(8,128)} %get-tuple-element.283, s32[]{:T(128)} %get-tuple-element.282, bf16[9312,256]{1,0:T(8,128)(2,1)} %get-tuple-element.293, s32[9312]{0:T(1024)S(1)} %get-tuple-element.294, s32[1024]{0:T(1024)S(1)} %bitcast.75), kind=kOutput, calls=%fused_computation.13.clone.clone.1 | convolution fusion | flops 4891705344 | bytes 5858176 | tf_op jit(solution)/shard_map/while/body/eval_jaxpr/dot_general | solution.py:20
  214.5 4.0 %slice_add_fusion = f32[4,1024,256]{2,1,0:T(8,128)S(1)} fusion(f32[4,1024,256]{2,1,0:T(8,128)} %get-tuple-element.84, f32[7,1024,256]{2,1,0:T(8,128)} %get-tuple-element.83), kind=kLoop, calls=%fused_computation.40 | loop fusion | flops 1048576 | bytes 12582912 | tf_op jit(solution)/shard_map/add | solution.py:85
  221.1 3.0 %multiply_convert_fusion = bf16[4096,256]{1,0:T(8,128)(2,1)} fusion(f32[4,1024,256]{2,1,0:T(8,128)S(1)} %slice_add_fusion, f32[4096]{0:T(1024)S(1)} %add_rsqrt_fusion.1, bf16[16384,256]{1,0:T(8,128)(2,1)} %param.15, s32[]{:T(128)S(6)} %select_n.38), kind=kLoop, calls=%fused_computation.38 | loop fusion | flops 4194304 | bytes 8404996 | tf_op jit(solution)/shard_map/convert_element_type | solution.py:10
  224.1 4.3 %fusion.47 = bf16[1024,256]{0,1:T(8,128)(2,1)S(1)} fusion(bf16[3072,256]{1,0:T(8,128)(2,1)} %bitcast.14, s32[1024]{0:T(1024)S(1)} %get-tuple-element.126, f32[1024,256]{0,1:T(8,128)} %get-tuple-element.129, f32[1024]{0:T(1024)S(1)} %add_rsqrt_fusion.2), kind=kOutput, calls=%fused_computation.50 | convolution fusion | flops 1615069184 | bytes 3153920 | tf_op jit(solution)/shard_map/dot_general | solution.py:88
  (65 shorter events, 23.1 us)
Async XLA Ops:
  0.6 12.7 %copy-start = (bf16[1024,1024]{1,0:T(8,128)(2,1)S(1)}, bf16[1024,1024]{1,0:T(8,128)(2,1)}, u32[]{:S(2)}) copy-start(bf16[1024,1024]{1,0:T(8,128)(2,1)} %param.11) | copy-start | bytes 6291460
  4.8 19.4 %all-to-all-start = ((s32[32,96,1]{1,2,0:T(1,128)}), s32[32,96,1]{1,2,0:T(1,128)S(1)}, u32[]{:S(2)}, u32[]{:S(2)}) async-start(s32[32,96,1]{1,2,0:T(1,128)} %all_to_all.24), calls=%async_computation | async-start | bytes 32768 | tf_op jit(solution)/shard_map/all_to_all | solution.py:58
  24.2 30.2 %all-to-all-start.1 = ((bf16[32,96,256]{2,1,0:T(8,128)(2,1)}), bf16[32,96,256]{2,1,0:T(8,128)(2,1)}, u32[]{:S(2)}, u32[]{:S(2)}) async-start(bf16[32,96,256]{2,1,0:T(8,128)(2,1)} %bitcast.68), calls=%async_computation.1 | async-start | bytes 3145728 | tf_op jit(solution)/shard_map/all_to_all | solution.py:57
  57.0 38.7 %collective-permute-start = (bf16[3104,256]{1,0:T(8,128)(2,1)}, bf16[3104,256]{1,0:T(8,128)(2,1)}, u32[]{:S(2)}, u32[]{:S(2)}) collective-permute-start(bf16[3104,256]{1,0:T(8,128)(2,1)} %pad_maximum_fusion), channel_id=1, source_target_pairs={{0,1},{1,2},{2,3},{3,0},{4,5},{5,6},{6,7},{7,4},{8,9},{9,10},{10,1... | collective-permute-start | bytes 4767752 | tf_op jit(solution)/shard_map/ppermute | solution.py:66
  58.7 72.0 %collective-permute-start.1 = (bf16[3104,256]{1,0:T(8,128)(2,1)}, bf16[3104,256]{1,0:T(8,128)(2,1)}, u32[]{:S(2)}, u32[]{:S(2)}) collective-permute-start(bf16[3104,256]{1,0:T(8,128)(2,1)} %pad_maximum_fusion), channel_id=1, source_target_pairs={{0,2},{1,3},{2,0},{3,1},{4,6},{5,7},{6,4},{7,5},{8,10},{9,11},{10,... | collective-permute-start | bytes 4767752 | tf_op jit(solution)/shard_map/ppermute | solution.py:66
  62.0 70.2 %collective-permute-start.2 = (bf16[3104,256]{1,0:T(8,128)(2,1)}, bf16[3104,256]{1,0:T(8,128)(2,1)}, u32[]{:S(2)}, u32[]{:S(2)}) collective-permute-start(bf16[3104,256]{1,0:T(8,128)(2,1)} %pad_maximum_fusion), channel_id=1, source_target_pairs={{0,3},{1,0},{2,1},{3,2},{4,7},{5,4},{6,5},{7,6},{8,11},{9,8},{10,9... | collective-permute-start | bytes 4767752 | tf_op jit(solution)/shard_map/ppermute | solution.py:66
  133.7 2.2 copy-start.1
  136.0 0.6 copy-start.2
  172.9 51.2 %all-to-all-start.2 = ((bf16[32,96,256]{2,1,0:T(8,128)(2,1)}), bf16[32,96,256]{2,1,0:T(8,128)(2,1)}, u32[]{:S(2)}, u32[]{:S(2)}) async-start(bf16[32,96,256]{2,1,0:T(8,128)(2,1)} %multiply_convert_fusion.1), calls=%async_computation.2 | async-start | bytes 3145728 | tf_op jit(solution)/shard_map/all_to_all | solution.py:83

commit v4 on v0

--- a/solution.py
+++ b/solution.py
@@ -62,22 +62,38 @@
     id_code = jnp.concatenate([in_ids // 128, in_ids % 128]).astype(jnp.bfloat16)
     id_code = jnp.pad(id_code, (0, code_rows * emb_width - 2 * slots))
     payload = jnp.concatenate([incoming, id_code.reshape(code_rows, emb_width)])
-    rows_all = lax.all_gather(payload, "rep", axis=0)
-    code = rows_all[:, slots:].reshape(replicas, -1)[:, : 2 * slots].astype(jnp.int32)
-    keys = code[:, :slots] * 128 + code[:, slots:]
-    keys = jnp.pad(keys, ((0, 0), (0, code_rows)), constant_values=-1).reshape(-1)
-    rows = rows_all.reshape(-1, emb_width)
+    def shift(x, step):
+        return lax.ppermute(x, "rep", [(i, (i + step) % replicas) for i in range(replicas)])
+
+    from_prev = shift(payload, 1)
+    from_next = shift(payload, -1)
+    half = payload.shape[0] // 2
+    from_far = jnp.concatenate([shift(from_prev[:half], 1), shift(from_next[half:], -1)])
+
+    def keys_of(pieces):
+        count = pieces.shape[0] // payload.shape[0]
+        code = pieces.reshape(count, -1, emb_width)[:, slots:]
+        code = code.reshape(count, -1)[:, : 2 * slots].astype(jnp.int32)
+        ids = code[:, :slots] * 128 + code[:, slots:]
+        return jnp.pad(ids, ((0, 0), (0, code_rows)), constant_values=-1).reshape(-1)
+
+    rows_near = jnp.concatenate([from_prev, from_next])
+    keys_near = keys_of(rows_near)
+    keys_far = keys_of(from_far)
 
     first_row = my_rep * share_rows
     share_ids = first_row + jnp.arange(share_rows, dtype=jnp.int32)
     look_cent = centroids[in_ids].astype(jnp.float32)
     own_cent = lax.dynamic_slice_in_dim(centroids, first_row, share_rows, 0).astype(jnp.float32)
 
-    look_sum = match_sums(in_ids, keys, rows)
+    queries = jnp.concatenate([in_ids, share_ids])
+    own_sums = match_sums(queries, in_ids, incoming)
+    near_sums = match_sums(queries, keys_near, rows_near)
+    look_sum = own_sums[:slots] + near_sums[:slots] + match_sums(in_ids, keys_far, from_far)
     picked = normalize(look_cent + look_sum)
     returned = lax.all_to_all(picked, "wide", split_axis=0, concat_axis=0, tiled=True)
 
-    share_sum = match_sums(share_ids, keys, rows)
+    share_sum = own_sums[slots:] + near_sums[slots:] + match_sums(share_ids, keys_far, from_far)
     own_rows = normalize(own_cent + share_sum)
 
     gathered_rows = jnp.dot(place_bf.T, returned, preferred_element_type=jnp.float32)

time: 239 us -> 218 us (0.912)
  waiting for transfers between devices: 65.8 us -> 12.3 us
  matrix products: 88 us -> 106 us
  local copies, waits for them, and re-layouts: 21.8 us -> 35.6 us
  between operations: 14.3 us -> 0.95 us
  other arithmetic: 24.2 us -> 31.2 us
  starting transfers between devices: 24 us -> 30.1 us
    all_gather x1 -> x0, waiting for transfers between devices: 44.5 us -> none  [body(): rows_all = lax.all_gather(payload, 'rep', axis=0)]
    all_to_all x1, waiting for transfers between devices: 21.3 us -> 1.17 us  [body(): lax.all_to_all(outgoing, 'wide', split_axis=0, concat_axis=0, tiled=True)]
    dot_general x7 -> x21, matrix products: 74.6 us -> 90.7 us  [one_block(): return jnp.dot(selector, rows, preferred_element_type=jnp.float32)]
    ppermute x0 -> x4, waiting for transfers between devices: none -> 11.1 us  [shift(): lax.ppermute(x, 'rep', [(i, (i + step) % replicas) for i in range(replica...]
    another operation x0 -> x2, local copies, waits for them, and re-layouts: none -> 7.25 us
    ppermute x0 -> x4, starting transfers between devices: none -> 6.57 us  [shift(): lax.ppermute(x, 'rep', [(i, (i + step) % replicas) for i in range(replica...]
    add x1 -> x3, other arithmetic: 0.02 us -> 5.51 us  [the longest x1 5.47 us: body(): own_sums[slots:] + near_sums[slots:]]
    slice x0 -> x2, local copies, waits for them, and re-layouts: none -> 2.97 us  [the longest x1 1.78 us: body(): from_prev[:half]]
  transfers between devices with their start and end apart: 4 -> 7, of which waited for: 2 -> 2; matrix products, arithmetic and copies ran while one was open for 33% -> 61% of each run, Pallas kernels for 0% -> 0%
where the time goes in v4:
time: 218 us; the launch traced here: 217 us
  matrix products  106 us (49%)
  local copies, waits for them, and re-layouts  35.6 us (16%)
  other arithmetic  31.2 us (14%)
  starting transfers between devices  30.1 us (14%)
  waiting for transfers between devices  12.3 us (6%)
    dot_general x21, matrix products, one_block(): return jnp.dot(selector, rows, preferred_element_type=jnp.float32)  90.7 us
    gather x1, local copies, waits for them, and re-layouts, body(): look_cent = centroids[in_ids].astype(jnp.float32)  16.6 us
    ppermute x4, waiting for transfers between devices, shift(): lax.ppermute(x, 'rep', [(i, (i + step) % replicas) for i in range(replica...  11.1 us
    reduce_sum x2, other arithmetic, normalize(): jnp.mean(updated * updated, axis=-1, keepdims=True) + 1e-06  9.4 us
    all_to_all x1, starting transfers between devices, body(): lax.all_to_all(out_ids, 'wide', split_axis=0, concat_axis=0, tiled=True)  8.57 us
    convert_element_type x2, other arithmetic, normalize(): return (updated * lax.rsqrt(jnp.mean(updated * updated, axis=-1, keepdims...  7.73 us
    all_to_all x1, starting transfers between devices, body(): lax.all_to_all(picked, 'wide', split_axis=0, concat_axis=0, tiled=True)  7.56 us
    all_to_all x1, starting transfers between devices, body(): lax.all_to_all(outgoing, 'wide', split_axis=0, concat_axis=0, tiled=True)  7.38 us
  transfers between devices with their start and end apart: 7, of which 2 were waited for; matrix products, arithmetic and copies ran while one was open for 61% of the time, Pallas kernels for 0%

profile of v4, /device:TPU:1, one launch (start us, length us, event | category | flops | bytes accessed | tf_op | source)
XLA Modules:
  0.0 216.6 jit_solution(4078984503665288550)
XLA Ops:
  4.8 8.6 %all-to-all-start = ((s32[32,96,1]{1,2,0:T(1,128)}), s32[32,96,1]{1,2,0:T(1,128)S(1)}, u32[]{:S(2)}, u32[]{:S(2)}) async-start(s32[32,96,1]{1,2,0:T(1,128)} %all_to_all.24), calls=%async_computation | async-start | bytes 32768 | tf_op jit(solution)/shard_map/all_to_all | solution.py:58
  13.4 6.0 %multiply_reduce_fusion.2 = (f32[1024]{0:T(1024)S(1)}, f32[1024,256]{0,1:T(8,128)}) fusion(bf16[1024,256]{1,0:T(8,128)(2,1)} %param.16, bf16[1024,1024]{1,0:T(8,128)(2,1)S(1)} %copy-done, bf16[1024,1024]{1,0:T(8,128)(2,1)} %param.15), kind=kOutput, calls=%fused_computation.61 | convolution fusion | flops 2694315008 | bytes 5771264 | tf_op jit(solution)/shard_map/dot_general | solution.py:50
  19.3 4.9 %fusion.53 = bf16[3072,256]{1,0:T(8,128)(2,1)} fusion(s32[1024]{0:T(1024)S(1)} %get-tuple-element.164, f32[1024,256]{0,1:T(8,128)} %get-tuple-element.167, f32[1024]{0:T(1024)S(1)} %add_rsqrt_fusion.2), kind=kOutput, calls=%fused_computation.50 | convolution fusion | flops 1615069184 | bytes 2629632 | tf_op jit(solution)/shard_map/dot_general | solution.py:55
  24.2 7.4 %all-to-all-start.1 = ((bf16[32,96,256]{2,1,0:T(8,128)(2,1)}), bf16[32,96,256]{2,1,0:T(8,128)(2,1)S(1)}, u32[]{:S(2)}, u32[]{:S(2)}) async-start(bf16[32,96,256]{2,1,0:T(8,128)(2,1)} %bitcast.80), calls=%async_computation.1 | async-start | bytes 3145728 | tf_op jit(solution)/shard_map/all_to_all | solution.py:57
  33.2 16.6 %gather_fusion = bf16[3072,256]{1,0:T(8,128)(2,1)} fusion(bf16[16384,256]{1,0:T(8,128)(2,1)} %param.17, s32[3072]{0:T(1024)S(1)} %broadcast_clamp_fusion), kind=kCustom, calls=%fused_computation | custom fusion | bytes 3158016 | tf_op jit(solution)/shard_map/gather | solution.py:86
  49.8 3.3 %convert_element_type.72 = f32[3072,256]{1,0:T(8,128)} convert(bf16[3072,256]{1,0:T(8,128)(2,1)} %gather_fusion) | non-fusion elementwise | flops 786432 | bytes 4718592 | tf_op jit(solution)/shard_map/convert_element_type | solution.py:86
  59.3 3.7 %broadcast.87.clone.1 = f32[7,1024,256]{2,1,0:T(8,128)} broadcast(f32[]{:T(128)} %constant.102.clone.1), dimensions={} | broadcast | bytes 7340036 | tf_op jit(solution)/shard_map/broadcast.3
  62.9 20.2 %while.40 = (s32[]{:T(128)}, f32[7,1024,256]{2,1,0:T(8,128)}, s32[7,1024]{1,0:T(8,128)S(1)}, s32[3072]{0:T(1024)S(1)}, bf16[3072,256]{1,0:T(8,128)(2,1)S(1)}, /*index=5*/s32[]{:T(128)}) while((s32[]{:T(128)}, f32[7,1024,256]{2,1,0:T(8,128)}, s32[7,1024]{1,0:T(8,128)S(1)}, s32[3072]{0:T(1024)S(1)}, bf16[3072,256]{1,0:T(8,128)(2,1)S(1)}, ...), condition=%wide.region_4.5_spmd, body=%wide.region_3.4_spmd.sunk | while | flops 1613758464 | bytes 2646601 | solution.py:22
  83.1 11.1 %collective-permute-done = bf16[3104,256]{1,0:T(8,128)(2,1)} collective-permute-done((bf16[3104,256]{1,0:T(8,128)(2,1)}, bf16[3104,256]{1,0:T(8,128)(2,1)}, u32[]{:S(2)}, u32[]{:S(2)}) %collective-permute-start) | collective-permute-done | bytes 1589280 | tf_op jit(solution)/shard_map/ppermute | solution.py:66
  103.2 3.6 %broadcast.87.clone = f32[7,1024,256]{2,1,0:T(8,128)} broadcast(f32[]{:T(128)} %constant.102.clone.1), dimensions={} | broadcast | bytes 7340036 | tf_op jit(solution)/shard_map/broadcast.3
  106.8 46.2 %while.41 = (s32[]{:T(128)}, f32[7,1024,256]{2,1,0:T(8,128)}, s32[7,1024]{1,0:T(8,128)S(1)}, s32[2,3104]{1,0:T(2,128)S(1)}, bf16[6208,256]{1,0:T(8,128)(2,1)}, /*index=5*/s32[]{:T(128)}) while((s32[]{:T(128)}, f32[7,1024,256]{2,1,0:T(8,128)}, s32[7,1024]{1,0:T(8,128)S(1)}, s32[2,3104]{1,0:T(2,128)S(1)}, bf16[6208,256]{1,0:T(8,128)(2,1)}, ...), condition=%wide.region_6.7_spmd, body=%wide.region_5.6_spmd.sunk | while | flops 3261136896 | bytes 4314441 | solution.py:22
  106.9 6.5 %fusion.101 = f32[7,1024,256]{2,1,0:T(8,128)} fusion(f32[7,1024,256]{2,1,0:T(8,128)} %get-tuple-element.320, s32[]{:T(128)} %get-tuple-element.319, bf16[6208,256]{1,0:T(8,128)(2,1)} %get-tuple-element.329, s32[6208]{0:T(1024)S(1)} %eq.258, s32[1024]{0:T(1024)S(1)} %bitcast.87), kind=kOutput, calls=%fused_computation.13.clone.1 | convolution fusion | flops 3261136896 | bytes 4256512 | tf_op jit(solution)/shard_map/while/body/eval_jaxpr/dot_general | solution.py:20
  113.5 6.5 %fusion.101 = f32[7,1024,256]{2,1,0:T(8,128)} fusion(f32[7,1024,256]{2,1,0:T(8,128)} %get-tuple-element.320, s32[]{:T(128)} %get-tuple-element.319, bf16[6208,256]{1,0:T(8,128)(2,1)} %get-tuple-element.329, s32[6208]{0:T(1024)S(1)} %eq.258, s32[1024]{0:T(1024)S(1)} %bitcast.87), kind=kOutput, calls=%fused_computation.13.clone.1 | convolution fusion | flops 3261136896 | bytes 4256512 | tf_op jit(solution)/shard_map/while/body/eval_jaxpr/dot_general | solution.py:20
  120.1 6.5 %fusion.101 = f32[7,1024,256]{2,1,0:T(8,128)} fusion(f32[7,1024,256]{2,1,0:T(8,128)} %get-tuple-element.320, s32[]{:T(128)} %get-tuple-element.319, bf16[6208,256]{1,0:T(8,128)(2,1)} %get-tuple-element.329, s32[6208]{0:T(1024)S(1)} %eq.258, s32[1024]{0:T(1024)S(1)} %bitcast.87), kind=kOutput, calls=%fused_computation.13.clone.1 | convolution fusion | flops 3261136896 | bytes 4256512 | tf_op jit(solution)/shard_map/while/body/eval_jaxpr/dot_general | solution.py:20
  126.7 6.5 %fusion.101 = f32[7,1024,256]{2,1,0:T(8,128)} fusion(f32[7,1024,256]{2,1,0:T(8,128)} %get-tuple-element.320, s32[]{:T(128)} %get-tuple-element.319, bf16[6208,256]{1,0:T(8,128)(2,1)} %get-tuple-element.329, s32[6208]{0:T(1024)S(1)} %eq.258, s32[1024]{0:T(1024)S(1)} %bitcast.87), kind=kOutput, calls=%fused_computation.13.clone.1 | convolution fusion | flops 3261136896 | bytes 4256512 | tf_op jit(solution)/shard_map/while/body/eval_jaxpr/dot_general | solution.py:20
  133.3 6.5 %fusion.101 = f32[7,1024,256]{2,1,0:T(8,128)} fusion(f32[7,1024,256]{2,1,0:T(8,128)} %get-tuple-element.320, s32[]{:T(128)} %get-tuple-element.319, bf16[6208,256]{1,0:T(8,128)(2,1)} %get-tuple-element.329, s32[6208]{0:T(1024)S(1)} %eq.258, s32[1024]{0:T(1024)S(1)} %bitcast.87), kind=kOutput, calls=%fused_computation.13.clone.1 | convolution fusion | flops 3261136896 | bytes 4256512 | tf_op jit(solution)/shard_map/while/body/eval_jaxpr/dot_general | solution.py:20
  139.9 6.5 %fusion.101 = f32[7,1024,256]{2,1,0:T(8,128)} fusion(f32[7,1024,256]{2,1,0:T(8,128)} %get-tuple-element.320, s32[]{:T(128)} %get-tuple-element.319, bf16[6208,256]{1,0:T(8,128)(2,1)} %get-tuple-element.329, s32[6208]{0:T(1024)S(1)} %eq.258, s32[1024]{0:T(1024)S(1)} %bitcast.87), kind=kOutput, calls=%fused_computation.13.clone.1 | convolution fusion | flops 3261136896 | bytes 4256512 | tf_op jit(solution)/shard_map/while/body/eval_jaxpr/dot_general | solution.py:20
  146.5 6.5 %fusion.101 = f32[7,1024,256]{2,1,0:T(8,128)} fusion(f32[7,1024,256]{2,1,0:T(8,128)} %get-tuple-element.320, s32[]{:T(128)} %get-tuple-element.319, bf16[6208,256]{1,0:T(8,128)(2,1)} %get-tuple-element.329, s32[6208]{0:T(1024)S(1)} %eq.258, s32[1024]{0:T(1024)S(1)} %bitcast.87), kind=kOutput, calls=%fused_computation.13.clone.1 | convolution fusion | flops 3261136896 | bytes 4256512 | tf_op jit(solution)/shard_map/while/body/eval_jaxpr/dot_general | solution.py:20
  155.4 13.3 %while.43 = (s32[]{:T(128)}, f32[3,1024,256]{2,1,0:T(8,128)}, s32[3,1024]{1,0:T(4,128)S(1)}, s32[1,3104]{1,0:T(1,128)S(1)}, bf16[3104,256]{1,0:T(8,128)(2,1)}, /*index=5*/s32[]{:T(128)}, s32[]{:T(128)}) while((s32[]{:T(128)}, f32[3,1024,256]{2,1,0:T(8,128)}, s32[3,1024]{1,0:T(4,128)S(1)}, s32[1,3104]{1,0:T(1,128)S(1)}, ...), condition=%wide.region_11.12_spmd, body=%wide.region_10.11_spmd.sunk | while | flops 1630568448 | bytes 2687957 | solution.py:22
  155.5 4.4 %fusion.107 = f32[3,1024,256]{2,1,0:T(8,128)} fusion(f32[3,1024,256]{2,1,0:T(8,128)} %get-tuple-element.357, s32[]{:T(128)} %get-tuple-element.356, bf16[3104,256]{1,0:T(8,128)(2,1)} %get-tuple-element.367, s32[3104]{0:T(1024)S(1)} %reduce.14, s32[1024]{0:T(1024)S(1)} %bitcast.85), kind=kOutput, calls=%fused_computation.27.clone.1 | convolution fusion | flops 1630568448 | bytes 2654848 | tf_op jit(solution)/shard_map/while/body/eval_jaxpr/dot_general | solution.py:20
  160.0 4.4 %fusion.107 = f32[3,1024,256]{2,1,0:T(8,128)} fusion(f32[3,1024,256]{2,1,0:T(8,128)} %get-tuple-element.357, s32[]{:T(128)} %get-tuple-element.356, bf16[3104,256]{1,0:T(8,128)(2,1)} %get-tuple-element.367, s32[3104]{0:T(1024)S(1)} %reduce.14, s32[1024]{0:T(1024)S(1)} %bitcast.85), kind=kOutput, calls=%fused_computation.27.clone.1 | convolution fusion | flops 1630568448 | bytes 2654848 | tf_op jit(solution)/shard_map/while/body/eval_jaxpr/dot_general | solution.py:20
  164.4 4.4 %fusion.107 = f32[3,1024,256]{2,1,0:T(8,128)} fusion(f32[3,1024,256]{2,1,0:T(8,128)} %get-tuple-element.357, s32[]{:T(128)} %get-tuple-element.356, bf16[3104,256]{1,0:T(8,128)(2,1)} %get-tuple-element.367, s32[3104]{0:T(1024)S(1)} %reduce.14, s32[1024]{0:T(1024)S(1)} %bitcast.85), kind=kOutput, calls=%fused_computation.27.clone.1 | convolution fusion | flops 1630568448 | bytes 2654848 | tf_op jit(solution)/shard_map/while/body/eval_jaxpr/dot_general | solution.py:20
  168.7 6.9 %multiply_reduce_fusion.1 = (f32[3,1024]{1,0:T(4,128)S(1)}, f32[3,1024,256]{2,1,0:T(8,128)}) fusion(f32[3,1024,256]{2,1,0:T(8,128)} %bitcast.75, f32[3,1024,256]{2,1,0:T(8,128)} %get-tuple-element.113, f32[7,1024,256]{2,1,0:T(8,128)} %get-tuple-element.111, f32[7,1024,256]{2,1,0:T(8,128)} %get-tuple-element.110), kind=kLoop, calls=%fused_computation.52 | loop fusion | flops 3929088 | bytes 15740928 | tf_op jit(solution)/shard_map/reduce_sum | solution.py:9
  175.7 4.7 %multiply_convert_fusion.1 = bf16[32,96,256]{2,1,0:T(8,128)(2,1)} fusion(f32[32,96,256]{2,1,0:T(8,128)} %bitcast.76, f32[32,96,256]{2,1,0:T(8,128)} %bitcast.77, f32[32,96]{1,0:T(8,128)S(1)} %rsqrt.30), kind=kLoop, calls=%fused_computation.51 | loop fusion | flops 2359296 | bytes 7876608 | tf_op jit(solution)/shard_map/convert_element_type | solution.py:10
  180.4 7.6 %all-to-all-start.2 = ((bf16[32,96,256]{2,1,0:T(8,128)(2,1)}), bf16[32,96,256]{2,1,0:T(8,128)(2,1)}, u32[]{:S(2)}, u32[]{:S(2)}) async-start(bf16[32,96,256]{2,1,0:T(8,128)(2,1)} %multiply_convert_fusion.1), calls=%async_computation.2 | async-start | bytes 3145728 | tf_op jit(solution)/shard_map/all_to_all | solution.py:94
  188.0 12.2 %while.42 = (s32[]{:T(128)}, f32[4,1024,256]{2,1,0:T(8,128)}, s32[4,1024]{1,0:T(4,128)S(1)}, s32[1,3104]{1,0:T(1,128)S(1)}, bf16[3104,256]{1,0:T(8,128)(2,1)S(1)}, /*index=5*/s32[]{:T(128)}, s32[]{:T(128)}) while((s32[]{:T(128)}, f32[4,1024,256]{2,1,0:T(8,128)}, s32[4,1024]{1,0:T(4,128)S(1)}, s32[1,3104]{1,0:T(1,128)S(1)}, ...), condition=%wide.region_8.9_spmd, body=%wide.region_7.8_spmd.sunk | while | flops 1630568448 | bytes 2687957 | solution.py:22
  191.1 3.0 %fusion.104 = f32[4,1024,256]{2,1,0:T(8,128)} fusion(f32[4,1024,256]{2,1,0:T(8,128)} %get-tuple-element.300, s32[]{:T(128)} %get-tuple-element.299, bf16[3104,256]{1,0:T(8,128)(2,1)S(1)} %get-tuple-element.310, s32[3104]{0:T(1024)S(1)} %reduce.13, s32[1024]{0:T(1024)S(1)} %bitcast.86), kind=kOutput, calls=%fused_computation.20.clone.1 | convolution fusion | flops 1630568448 | bytes 2654848 | tf_op jit(solution)/shard_map/while/body/eval_jaxpr/dot_general | solution.py:20
  194.1 3.0 %fusion.104 = f32[4,1024,256]{2,1,0:T(8,128)} fusion(f32[4,1024,256]{2,1,0:T(8,128)} %get-tuple-element.300, s32[]{:T(128)} %get-tuple-element.299, bf16[3104,256]{1,0:T(8,128)(2,1)S(1)} %get-tuple-element.310, s32[3104]{0:T(1024)S(1)} %reduce.13, s32[1024]{0:T(1024)S(1)} %bitcast.86), kind=kOutput, calls=%fused_computation.20.clone.1 | convolution fusion | flops 1630568448 | bytes 2654848 | tf_op jit(solution)/shard_map/while/body/eval_jaxpr/dot_general | solution.py:20
  197.2 3.0 %fusion.104 = f32[4,1024,256]{2,1,0:T(8,128)} fusion(f32[4,1024,256]{2,1,0:T(8,128)} %get-tuple-element.300, s32[]{:T(128)} %get-tuple-element.299, bf16[3104,256]{1,0:T(8,128)(2,1)S(1)} %get-tuple-element.310, s32[3104]{0:T(1024)S(1)} %reduce.13, s32[1024]{0:T(1024)S(1)} %bitcast.86), kind=kOutput, calls=%fused_computation.20.clone.1 | convolution fusion | flops 1630568448 | bytes 2654848 | tf_op jit(solution)/shard_map/while/body/eval_jaxpr/dot_general | solution.py:20
  200.2 5.5 %add_add_fusion = f32[4,1024,256]{2,1,0:T(8,128)S(1)} fusion(f32[4,1024,256]{2,1,0:T(8,128)} %get-tuple-element.112, f32[7,1024,256]{2,1,0:T(8,128)} %get-tuple-element.111, f32[7,1024,256]{2,1,0:T(8,128)} %get-tuple-element.110), kind=kLoop, calls=%fused_computation.47 | loop fusion | flops 2097152 | bytes 16777216 | tf_op jit(solution)/shard_map/add | solution.py:96
  208.2 3.0 %multiply_convert_fusion = bf16[4096,256]{1,0:T(8,128)(2,1)} fusion(f32[4,1024,256]{2,1,0:T(8,128)S(1)} %add_add_fusion, f32[4096]{0:T(1024)S(1)} %add_rsqrt_fusion.1, bf16[16384,256]{1,0:T(8,128)(2,1)} %param.17, s32[]{:T(128)S(6)} %select_n.38), kind=kLoop, calls=%fused_computation.45 | loop fusion | flops 4194304 | bytes 8404996 | tf_op jit(solution)/shard_map/convert_element_type | solution.py:10
  211.2 4.4 %fusion.57 = bf16[1024,256]{0,1:T(8,128)(2,1)S(1)} fusion(bf16[3072,256]{1,0:T(8,128)(2,1)} %bitcast.17, s32[1024]{0:T(1024)S(1)} %get-tuple-element.164, f32[1024,256]{0,1:T(8,128)} %get-tuple-element.167, f32[1024]{0:T(1024)S(1)} %add_rsqrt_fusion.2), kind=kOutput, calls=%fused_computation.57 | convolution fusion | flops 1615069184 | bytes 3153920 | tf_op jit(solution)/shard_map/dot_general | solution.py:99
  (107 shorter events, 50.8 us)
Async XLA Ops:
  0.6 12.7 %copy-start = (bf16[1024,1024]{1,0:T(8,128)(2,1)S(1)}, bf16[1024,1024]{1,0:T(8,128)(2,1)}, u32[]{:S(2)}) copy-start(bf16[1024,1024]{1,0:T(8,128)(2,1)} %param.13) | copy-start | bytes 6291460
  4.8 19.4 %all-to-all-start = ((s32[32,96,1]{1,2,0:T(1,128)}), s32[32,96,1]{1,2,0:T(1,128)S(1)}, u32[]{:S(2)}, u32[]{:S(2)}) async-start(s32[32,96,1]{1,2,0:T(1,128)} %all_to_all.24), calls=%async_computation | async-start | bytes 32768 | tf_op jit(solution)/shard_map/all_to_all | solution.py:58
  24.2 30.1 %all-to-all-start.1 = ((bf16[32,96,256]{2,1,0:T(8,128)(2,1)}), bf16[32,96,256]{2,1,0:T(8,128)(2,1)S(1)}, u32[]{:S(2)}, u32[]{:S(2)}) async-start(bf16[32,96,256]{2,1,0:T(8,128)(2,1)} %bitcast.80), calls=%async_computation.1 | async-start | bytes 3145728 | tf_op jit(solution)/shard_map/all_to_all | solution.py:57
  55.5 38.7 %collective-permute-start = (bf16[3104,256]{1,0:T(8,128)(2,1)}, bf16[3104,256]{1,0:T(8,128)(2,1)}, u32[]{:S(2)}, u32[]{:S(2)}) collective-permute-start(bf16[3104,256]{1,0:T(8,128)(2,1)} %pad_maximum_fusion), channel_id=1, source_target_pairs={{0,1},{1,2},{2,3},{3,0},{4,5},{5,6},{6,7},{7,4},{8,9},{9,10},{10,1... | collective-permute-start | bytes 4767752 | tf_op jit(solution)/shard_map/ppermute | solution.py:66
  57.2 38.5 %collective-permute-start.1 = (bf16[3104,256]{1,0:T(8,128)(2,1)}, bf16[3104,256]{1,0:T(8,128)(2,1)}, u32[]{:S(2)}, u32[]{:S(2)}) collective-permute-start(bf16[3104,256]{1,0:T(8,128)(2,1)} %pad_maximum_fusion), channel_id=1, source_target_pairs={{0,3},{1,0},{2,1},{3,2},{4,7},{5,4},{6,5},{7,6},{8,11},{9,8},{10,9... | collective-permute-start | bytes 4767752 | tf_op jit(solution)/shard_map/ppermute | solution.py:66
  97.2 3.2 %copy-start.2 = (bf16[6208,256]{1,0:T(8,128)(2,1)}, bf16[6208,256]{1,0:T(8,128)(2,1)S(1)}, u32[]{:S(2)}) copy-start(bf16[6208,256]{1,0:T(8,128)(2,1)S(1)} %constant_dynamic-update-slice_fusion) | copy-start | bytes 9535492
  99.1 53.9 %collective-permute-start.2 = (bf16[1552,256]{1,0:T(8,128)(2,1)S(1)}, bf16[1552,256]{1,0:T(8,128)(2,1)S(1)}, u32[]{:S(2)}, u32[]{:S(2)}) collective-permute-start(bf16[1552,256]{1,0:T(8,128)(2,1)S(1)} %slice.66), channel_id=1, source_target_pairs={{0,1},{1,2},{2,3},{3,0},{4,5},{5,6},{6,7},{7,4},{8,9},{9,10},{10,1... | collective-permute-start | bytes 2383880 | tf_op jit(solution)/shard_map/ppermute | solution.py:66
  100.4 52.6 %collective-permute-start.3 = (bf16[1552,256]{1,0:T(8,128)(2,1)S(1)}, bf16[1552,256]{1,0:T(8,128)(2,1)}, u32[]{:S(2)}, u32[]{:S(2)}) collective-permute-start(bf16[1552,256]{1,0:T(8,128)(2,1)S(1)} %slice.67), channel_id=1, source_target_pairs={{0,3},{1,0},{2,1},{3,2},{4,7},{5,4},{6,5},{7,6},{8,11},{9,8},{10,9... | collective-permute-start | bytes 2383880 | tf_op jit(solution)/shard_map/ppermute | solution.py:66
  154.3 1.2 copy-start.3
  175.7 12.3 %copy-start.4 = (bf16[3104,256]{1,0:T(8,128)(2,1)S(1)}, bf16[3104,256]{1,0:T(8,128)(2,1)}, u32[]{:S(2)}) copy-start(bf16[3104,256]{1,0:T(8,128)(2,1)} %get-tuple-element.377) | copy-start | bytes 4767748
  180.4 30.8 %all-to-all-start.2 = ((bf16[32,96,256]{2,1,0:T(8,128)(2,1)}), bf16[32,96,256]{2,1,0:T(8,128)(2,1)}, u32[]{:S(2)}, u32[]{:S(2)}) async-start(bf16[32,96,256]{2,1,0:T(8,128)(2,1)} %multiply_convert_fusion.1), calls=%async_computation.2 | async-start | bytes 3145728 | tf_op jit(solution)/shard_map/all_to_all | solution.py:94
  211.2 5.4 %copy-start.1 = (bf16[1024,1024]{1,0:T(8,128)(2,1)S(1)}, bf16[1024,1024]{1,0:T(8,128)(2,1)}, u32[]{:S(2)}) copy-start(bf16[1024,1024]{1,0:T(8,128)(2,1)} %param.13) | copy-start | bytes 6291460

commit v5 on v0

--- a/solution.py
+++ b/solution.py
@@ -57,28 +57,60 @@
     incoming = lax.all_to_all(outgoing, "wide", split_axis=0, concat_axis=0, tiled=True)
     in_ids = lax.all_to_all(out_ids, "wide", split_axis=0, concat_axis=0, tiled=True)
 
-    code_rows = -(-2 * slots // emb_width)
+    half_rows = slots // 2
+    code_rows = -(-2 * half_rows // emb_width)
     code_rows = -(-code_rows // 16) * 16
-    id_code = jnp.concatenate([in_ids // 128, in_ids % 128]).astype(jnp.bfloat16)
-    id_code = jnp.pad(id_code, (0, code_rows * emb_width - 2 * slots))
-    payload = jnp.concatenate([incoming, id_code.reshape(code_rows, emb_width)])
-    rows_all = lax.all_gather(payload, "rep", axis=0)
-    code = rows_all[:, slots:].reshape(replicas, -1)[:, : 2 * slots].astype(jnp.int32)
-    keys = code[:, :slots] * 128 + code[:, slots:]
-    keys = jnp.pad(keys, ((0, 0), (0, code_rows)), constant_values=-1).reshape(-1)
-    rows = rows_all.reshape(-1, emb_width)
+
+    def with_code(part):
+        part_ids = in_ids[part * half_rows : (part + 1) * half_rows]
+        id_code = jnp.concatenate([part_ids // 128, part_ids % 128]).astype(jnp.bfloat16)
+        id_code = jnp.pad(id_code, (0, code_rows * emb_width - 2 * half_rows))
+        return jnp.concatenate(
+            [incoming[part * half_rows : (part + 1) * half_rows],
+             id_code.reshape(code_rows, emb_width)]
+        )
+
+    def keys_of(pieces):
+        count = pieces.shape[0] // (half_rows + code_rows)
+        code = pieces.reshape(count, -1, emb_width)[:, half_rows:]
+        code = code.reshape(count, -1)[:, : 2 * half_rows].astype(jnp.int32)
+        ids = code[:, :half_rows] * 128 + code[:, half_rows:]
+        return jnp.pad(ids, ((0, 0), (0, code_rows)), constant_values=-1).reshape(-1)
+
+    def shift(x, step):
+        return lax.ppermute(x, "rep", [(i, (i + step) % replicas) for i in range(replicas)])
+
+    payload_a = with_code(0)
+    prev_a = shift(payload_a, 1)
+    next_a = shift(payload_a, -1)
+    payload_b, _, _ = lax.optimization_barrier((with_code(1), prev_a, next_a))
+    prev_b = shift(payload_b, 1)
+    next_b = shift(payload_b, -1)
+    far_a = shift(prev_a, 1)
+    far_b = shift(next_b, -1)
+
+    near_a = jnp.concatenate([prev_a, next_a])
+    near_b = jnp.concatenate([prev_b, next_b])
+    far = jnp.concatenate([far_a, far_b])
 
     first_row = my_rep * share_rows
     share_ids = first_row + jnp.arange(share_rows, dtype=jnp.int32)
-    look_cent = centroids[in_ids].astype(jnp.float32)
-    own_cent = lax.dynamic_slice_in_dim(centroids, first_row, share_rows, 0).astype(jnp.float32)
+    look_cent = centroids[in_ids]
+    own_cent = lax.dynamic_slice_in_dim(centroids, first_row, share_rows, 0)
 
-    look_sum = match_sums(in_ids, keys, rows)
-    picked = normalize(look_cent + look_sum)
+    queries = jnp.concatenate([in_ids, share_ids])
+    own_sums = match_sums(queries, in_ids, incoming)
+    sums_a = match_sums(queries, keys_of(near_a), near_a)
+    sums_b = match_sums(queries, keys_of(near_b), near_b)
+    keys_far = keys_of(far)
+    look_sum = (own_sums[:slots] + sums_a[:slots] + sums_b[:slots]
+                + match_sums(in_ids, keys_far, far))
+    picked = normalize(look_cent.astype(jnp.float32) + look_sum)
     returned = lax.all_to_all(picked, "wide", split_axis=0, concat_axis=0, tiled=True)
 
-    share_sum = match_sums(share_ids, keys, rows)
-    own_rows = normalize(own_cent + share_sum)
+    share_sum = (own_sums[slots:] + sums_a[slots:] + sums_b[slots:]
+                 + match_sums(share_ids, keys_far, far))
+    own_rows = normalize(own_cent.astype(jnp.float32) + share_sum)
 
     gathered_rows = jnp.dot(place_bf.T, returned, preferred_element_type=jnp.float32)
     residuals = (embedded.astype(jnp.float32) - gathered_rows).astype(jnp.bfloat16)

time: 239 us -> 230 us (0.962)
  waiting for transfers between devices: 65.8 us -> 0.89 us
  matrix products: 88 us -> 122 us
  local copies, waits for them, and re-layouts: 21.8 us -> 39.3 us
  between operations: 14.3 us -> 1.04 us
  other arithmetic: 24.2 us -> 33 us
  starting transfers between devices: 24 us -> 32 us
    all_gather x1 -> x0, waiting for transfers between devices: 44.5 us -> none  [body(): rows_all = lax.all_gather(payload, 'rep', axis=0)]
    dot_general x7 -> x28, matrix products: 74.6 us -> 107 us  [one_block(): return jnp.dot(selector, rows, preferred_element_type=jnp.float32)]
    all_to_all x1, waiting for transfers between devices: 21.3 us -> 0.87 us  [body(): lax.all_to_all(outgoing, 'wide', split_axis=0, concat_axis=0, tiled=True)]
    another operation x0 -> x3, local copies, waits for them, and re-layouts: none -> 10.8 us
    ppermute x0 -> x6, starting transfers between devices: none -> 7.98 us  [shift(): lax.ppermute(x, 'rep', [(i, (i + step) % replicas) for i in range(replica...]
    add x1 -> x4, other arithmetic: 0.02 us -> 6.96 us  [the longest x1 6.93 us: body(): own_sums[slots:] + sums_a[slots:] + sums_b[slots:]]
    unnamed x17 -> x22, local copies, waits for them, and re-layouts: 2.95 us -> 6.7 us
    reduce_sum x2, other arithmetic: 6.97 us -> 10.4 us  [normalize(): jnp.mean(updated * updated, axis=-1, keepdims=True) + 1e-06]
  transfers between devices with their start and end apart: 4 -> 9, of which waited for: 2 -> 1; matrix products, arithmetic and copies ran while one was open for 33% -> 68% of each run, Pallas kernels for 0% -> 0%
where the time goes in v5:
time: 230 us; the launch traced here: 229 us
  matrix products  122 us (53%)
  local copies, waits for them, and re-layouts  39.3 us (17%)
  other arithmetic  33 us (14%)
  starting transfers between devices  32 us (14%)
    dot_general x28, matrix products, one_block(): return jnp.dot(selector, rows, preferred_element_type=jnp.float32)  107 us
    gather x1, local copies, waits for them, and re-layouts, body(): look_cent = centroids[in_ids]  16.7 us
    another operation x3, local copies, waits for them, and re-layouts  10.8 us
    reduce_sum x2, other arithmetic, normalize(): jnp.mean(updated * updated, axis=-1, keepdims=True) + 1e-06  10.4 us
    all_to_all x1, starting transfers between devices, body(): lax.all_to_all(out_ids, 'wide', split_axis=0, concat_axis=0, tiled=True)  8.57 us
    all_to_all x1, starting transfers between devices, body(): lax.all_to_all(picked, 'wide', split_axis=0, concat_axis=0, tiled=True)  8.11 us
    ppermute x6, starting transfers between devices, shift(): lax.ppermute(x, 'rep', [(i, (i + step) % replicas) for i in range(replica...  7.98 us
    convert_element_type x2, other arithmetic, normalize(): return (updated * lax.rsqrt(jnp.mean(updated * updated, axis=-1, keepdims...  7.61 us
  transfers between devices with their start and end apart: 9, of which 1 were waited for; matrix products, arithmetic and copies ran while one was open for 68% of the time, Pallas kernels for 0%

profile of v5, /device:TPU:1, one launch (start us, length us, event | category | flops | bytes accessed | tf_op | source)
XLA Modules:
  0.0 228.8 jit_solution(2348517252849022634)
XLA Ops:
  4.8 8.6 %all-to-all-start = ((s32[32,96,1]{1,2,0:T(1,128)}), s32[32,96,1]{1,2,0:T(1,128)S(1)}, u32[]{:S(2)}, u32[]{:S(2)}) async-start(s32[32,96,1]{1,2,0:T(1,128)} %all_to_all.24), calls=%async_computation | async-start | bytes 32768 | tf_op jit(solution)/shard_map/all_to_all | solution.py:58
  13.4 6.0 %multiply_reduce_fusion.2 = (f32[1024]{0:T(1024)S(1)}, f32[1024,256]{0,1:T(8,128)}) fusion(bf16[1024,256]{1,0:T(8,128)(2,1)} %param.18, bf16[1024,1024]{1,0:T(8,128)(2,1)S(1)} %copy-done, bf16[1024,1024]{1,0:T(8,128)(2,1)} %param.17), kind=kOutput, calls=%fused_computation.67 | convolution fusion | flops 2694315008 | bytes 5771264 | tf_op jit(solution)/shard_map/dot_general | solution.py:50
  19.4 4.9 %fusion.63 = bf16[3072,256]{1,0:T(8,128)(2,1)} fusion(s32[1024]{0:T(1024)S(1)} %get-tuple-element.210, f32[1024,256]{0,1:T(8,128)} %get-tuple-element.213, f32[1024]{0:T(1024)S(1)} %add_rsqrt_fusion.2), kind=kOutput, calls=%fused_computation.57 | convolution fusion | flops 1615069184 | bytes 2629632 | tf_op jit(solution)/shard_map/dot_general | solution.py:55
  24.3 7.4 %all-to-all-start.1 = ((bf16[32,96,256]{2,1,0:T(8,128)(2,1)}), bf16[32,96,256]{2,1,0:T(8,128)(2,1)S(1)}, u32[]{:S(2)}, u32[]{:S(2)}) async-start(bf16[32,96,256]{2,1,0:T(8,128)(2,1)} %bitcast.99), calls=%async_computation.1 | async-start | bytes 3145728 | tf_op jit(solution)/shard_map/all_to_all | solution.py:57
  33.5 16.7 %gather_fusion = bf16[3072,256]{1,0:T(8,128)(2,1)} fusion(bf16[16384,256]{1,0:T(8,128)(2,1)} %param.19, s32[3072]{0:T(1024)S(1)} %broadcast_clamp_fusion), kind=kCustom, calls=%fused_computation | custom fusion | bytes 3158016 | tf_op jit(solution)/shard_map/gather | solution.py:98
  62.7 20.1 %while.50 = (s32[]{:T(128)}, f32[7,1024,256]{2,1,0:T(8,128)}, s32[7,1024]{1,0:T(8,128)S(1)}, s32[3072]{0:T(1024)S(1)}, bf16[3072,256]{1,0:T(8,128)(2,1)S(1)}, /*index=5*/s32[]{:T(128)}) while((s32[]{:T(128)}, f32[7,1024,256]{2,1,0:T(8,128)}, s32[7,1024]{1,0:T(8,128)S(1)}, s32[3072]{0:T(1024)S(1)}, bf16[3072,256]{1,0:T(8,128)(2,1)S(1)}, ...), condition=%wide.region_4.5_spmd, body=%wide.region_3.4_spmd.sunk | while | flops 1613758464 | bytes 2646601 | solution.py:22
  91.6 31.4 %while.51 = (s32[]{:T(128)}, f32[7,1024,256]{2,1,0:T(8,128)}, s32[7,1024]{1,0:T(8,128)S(1)}, s32[2,1552]{1,0:T(2,128)S(1)}, bf16[3104,256]{1,0:T(8,128)(2,1)}, /*index=5*/s32[]{:T(128)}) while((s32[]{:T(128)}, f32[7,1024,256]{2,1,0:T(8,128)}, s32[7,1024]{1,0:T(8,128)S(1)}, s32[2,1552]{1,0:T(2,128)S(1)}, bf16[3104,256]{1,0:T(8,128)(2,1)}, ...), condition=%wide.region_6.7_spmd, body=%wide.region_5.6_spmd.sunk | while | flops 1630568448 | bytes 2687945 | solution.py:22
  91.7 4.4 %fusion.123 = f32[7,1024,256]{2,1,0:T(8,128)} fusion(f32[7,1024,256]{2,1,0:T(8,128)} %get-tuple-element.412, s32[]{:T(128)} %get-tuple-element.411, bf16[3104,256]{1,0:T(8,128)(2,1)} %get-tuple-element.421, s32[3104]{0:T(1024)S(1)} %eq.304, s32[1024]{0:T(1024)S(1)} %bitcast.105), kind=kOutput, calls=%fused_computation.13.clone.1 | convolution fusion | flops 1630568448 | bytes 2654848 | tf_op jit(solution)/shard_map/while/body/eval_jaxpr/dot_general | solution.py:20
  96.2 4.4 %fusion.123 = f32[7,1024,256]{2,1,0:T(8,128)} fusion(f32[7,1024,256]{2,1,0:T(8,128)} %get-tuple-element.412, s32[]{:T(128)} %get-tuple-element.411, bf16[3104,256]{1,0:T(8,128)(2,1)} %get-tuple-element.421, s32[3104]{0:T(1024)S(1)} %eq.304, s32[1024]{0:T(1024)S(1)} %bitcast.105), kind=kOutput, calls=%fused_computation.13.clone.1 | convolution fusion | flops 1630568448 | bytes 2654848 | tf_op jit(solution)/shard_map/while/body/eval_jaxpr/dot_general | solution.py:20
  100.8 4.4 %fusion.123 = f32[7,1024,256]{2,1,0:T(8,128)} fusion(f32[7,1024,256]{2,1,0:T(8,128)} %get-tuple-element.412, s32[]{:T(128)} %get-tuple-element.411, bf16[3104,256]{1,0:T(8,128)(2,1)} %get-tuple-element.421, s32[3104]{0:T(1024)S(1)} %eq.304, s32[1024]{0:T(1024)S(1)} %bitcast.105), kind=kOutput, calls=%fused_computation.13.clone.1 | convolution fusion | flops 1630568448 | bytes 2654848 | tf_op jit(solution)/shard_map/while/body/eval_jaxpr/dot_general | solution.py:20
  105.2 4.4 %fusion.123 = f32[7,1024,256]{2,1,0:T(8,128)} fusion(f32[7,1024,256]{2,1,0:T(8,128)} %get-tuple-element.412, s32[]{:T(128)} %get-tuple-element.411, bf16[3104,256]{1,0:T(8,128)(2,1)} %get-tuple-element.421, s32[3104]{0:T(1024)S(1)} %eq.304, s32[1024]{0:T(1024)S(1)} %bitcast.105), kind=kOutput, calls=%fused_computation.13.clone.1 | convolution fusion | flops 1630568448 | bytes 2654848 | tf_op jit(solution)/shard_map/while/body/eval_jaxpr/dot_general | solution.py:20
  109.7 4.4 %fusion.123 = f32[7,1024,256]{2,1,0:T(8,128)} fusion(f32[7,1024,256]{2,1,0:T(8,128)} %get-tuple-element.412, s32[]{:T(128)} %get-tuple-element.411, bf16[3104,256]{1,0:T(8,128)(2,1)} %get-tuple-element.421, s32[3104]{0:T(1024)S(1)} %eq.304, s32[1024]{0:T(1024)S(1)} %bitcast.105), kind=kOutput, calls=%fused_computation.13.clone.1 | convolution fusion | flops 1630568448 | bytes 2654848 | tf_op jit(solution)/shard_map/while/body/eval_jaxpr/dot_general | solution.py:20
  114.2 4.4 %fusion.123 = f32[7,1024,256]{2,1,0:T(8,128)} fusion(f32[7,1024,256]{2,1,0:T(8,128)} %get-tuple-element.412, s32[]{:T(128)} %get-tuple-element.411, bf16[3104,256]{1,0:T(8,128)(2,1)} %get-tuple-element.421, s32[3104]{0:T(1024)S(1)} %eq.304, s32[1024]{0:T(1024)S(1)} %bitcast.105), kind=kOutput, calls=%fused_computation.13.clone.1 | convolution fusion | flops 1630568448 | bytes 2654848 | tf_op jit(solution)/shard_map/while/body/eval_jaxpr/dot_general | solution.py:20
  118.7 4.4 %fusion.123 = f32[7,1024,256]{2,1,0:T(8,128)} fusion(f32[7,1024,256]{2,1,0:T(8,128)} %get-tuple-element.412, s32[]{:T(128)} %get-tuple-element.411, bf16[3104,256]{1,0:T(8,128)(2,1)} %get-tuple-element.421, s32[3104]{0:T(1024)S(1)} %eq.304, s32[1024]{0:T(1024)S(1)} %bitcast.105), kind=kOutput, calls=%fused_computation.13.clone.1 | convolution fusion | flops 1630568448 | bytes 2654848 | tf_op jit(solution)/shard_map/while/body/eval_jaxpr/dot_general | solution.py:20
  131.7 31.3 %while.52 = (s32[]{:T(128)}, f32[7,1024,256]{2,1,0:T(8,128)}, s32[7,1024]{1,0:T(8,128)S(1)}, s32[2,1552]{1,0:T(2,128)S(1)}, bf16[3104,256]{1,0:T(8,128)(2,1)}, /*index=5*/s32[]{:T(128)}) while((s32[]{:T(128)}, f32[7,1024,256]{2,1,0:T(8,128)}, s32[7,1024]{1,0:T(8,128)S(1)}, s32[2,1552]{1,0:T(2,128)S(1)}, bf16[3104,256]{1,0:T(8,128)(2,1)}, ...), condition=%wide.region_8.9_spmd, body=%wide.region_7.8_spmd.sunk | while | flops 1630568448 | bytes 2687945 | solution.py:22
  131.8 4.4 %fusion.126 = f32[7,1024,256]{2,1,0:T(8,128)} fusion(f32[7,1024,256]{2,1,0:T(8,128)} %get-tuple-element.394, s32[]{:T(128)} %get-tuple-element.393, bf16[3104,256]{1,0:T(8,128)(2,1)} %get-tuple-element.403, s32[3104]{0:T(1024)S(1)} %eq.308, s32[1024]{0:T(1024)S(1)} %bitcast.106), kind=kOutput, calls=%fused_computation.20.clone.1 | convolution fusion | flops 1630568448 | bytes 2654848 | tf_op jit(solution)/shard_map/while/body/eval_jaxpr/dot_general | solution.py:20
  136.3 4.4 %fusion.126 = f32[7,1024,256]{2,1,0:T(8,128)} fusion(f32[7,1024,256]{2,1,0:T(8,128)} %get-tuple-element.394, s32[]{:T(128)} %get-tuple-element.393, bf16[3104,256]{1,0:T(8,128)(2,1)} %get-tuple-element.403, s32[3104]{0:T(1024)S(1)} %eq.308, s32[1024]{0:T(1024)S(1)} %bitcast.106), kind=kOutput, calls=%fused_computation.20.clone.1 | convolution fusion | flops 1630568448 | bytes 2654848 | tf_op jit(solution)/shard_map/while/body/eval_jaxpr/dot_general | solution.py:20
  140.8 4.4 %fusion.126 = f32[7,1024,256]{2,1,0:T(8,128)} fusion(f32[7,1024,256]{2,1,0:T(8,128)} %get-tuple-element.394, s32[]{:T(128)} %get-tuple-element.393, bf16[3104,256]{1,0:T(8,128)(2,1)} %get-tuple-element.403, s32[3104]{0:T(1024)S(1)} %eq.308, s32[1024]{0:T(1024)S(1)} %bitcast.106), kind=kOutput, calls=%fused_computation.20.clone.1 | convolution fusion | flops 1630568448 | bytes 2654848 | tf_op jit(solution)/shard_map/while/body/eval_jaxpr/dot_general | solution.py:20
  145.3 4.4 %fusion.126 = f32[7,1024,256]{2,1,0:T(8,128)} fusion(f32[7,1024,256]{2,1,0:T(8,128)} %get-tuple-element.394, s32[]{:T(128)} %get-tuple-element.393, bf16[3104,256]{1,0:T(8,128)(2,1)} %get-tuple-element.403, s32[3104]{0:T(1024)S(1)} %eq.308, s32[1024]{0:T(1024)S(1)} %bitcast.106), kind=kOutput, calls=%fused_computation.20.clone.1 | convolution fusion | flops 1630568448 | bytes 2654848 | tf_op jit(solution)/shard_map/while/body/eval_jaxpr/dot_general | solution.py:20
  149.8 4.4 %fusion.126 = f32[7,1024,256]{2,1,0:T(8,128)} fusion(f32[7,1024,256]{2,1,0:T(8,128)} %get-tuple-element.394, s32[]{:T(128)} %get-tuple-element.393, bf16[3104,256]{1,0:T(8,128)(2,1)} %get-tuple-element.403, s32[3104]{0:T(1024)S(1)} %eq.308, s32[1024]{0:T(1024)S(1)} %bitcast.106), kind=kOutput, calls=%fused_computation.20.clone.1 | convolution fusion | flops 1630568448 | bytes 2654848 | tf_op jit(solution)/shard_map/while/body/eval_jaxpr/dot_general | solution.py:20
  154.2 4.4 %fusion.126 = f32[7,1024,256]{2,1,0:T(8,128)} fusion(f32[7,1024,256]{2,1,0:T(8,128)} %get-tuple-element.394, s32[]{:T(128)} %get-tuple-element.393, bf16[3104,256]{1,0:T(8,128)(2,1)} %get-tuple-element.403, s32[3104]{0:T(1024)S(1)} %eq.308, s32[1024]{0:T(1024)S(1)} %bitcast.106), kind=kOutput, calls=%fused_computation.20.clone.1 | convolution fusion | flops 1630568448 | bytes 2654848 | tf_op jit(solution)/shard_map/while/body/eval_jaxpr/dot_general | solution.py:20
  158.7 4.4 %fusion.126 = f32[7,1024,256]{2,1,0:T(8,128)} fusion(f32[7,1024,256]{2,1,0:T(8,128)} %get-tuple-element.394, s32[]{:T(128)} %get-tuple-element.393, bf16[3104,256]{1,0:T(8,128)(2,1)} %get-tuple-element.403, s32[3104]{0:T(1024)S(1)} %eq.308, s32[1024]{0:T(1024)S(1)} %bitcast.106), kind=kOutput, calls=%fused_computation.20.clone.1 | convolution fusion | flops 1630568448 | bytes 2654848 | tf_op jit(solution)/shard_map/while/body/eval_jaxpr/dot_general | solution.py:20
  164.4 13.5 %while.54 = (s32[]{:T(128)}, f32[3,1024,256]{2,1,0:T(8,128)}, s32[3,1024]{1,0:T(4,128)S(1)}, s32[2,1552]{1,0:T(2,128)S(1)}, bf16[3104,256]{1,0:T(8,128)(2,1)}, /*index=5*/s32[]{:T(128)}) while((s32[]{:T(128)}, f32[3,1024,256]{2,1,0:T(8,128)}, s32[3,1024]{1,0:T(4,128)S(1)}, s32[2,1552]{1,0:T(2,128)S(1)}, bf16[3104,256]{1,0:T(8,128)(2,1)}, ...), condition=%wide.region_13.14_spmd, body=%wide.region_12.13_spmd.sunk | while | flops 1630568448 | bytes 2687945 | solution.py:22
  164.5 4.4 %fusion.132 = f32[3,1024,256]{2,1,0:T(8,128)} fusion(f32[3,1024,256]{2,1,0:T(8,128)} %get-tuple-element.448, s32[]{:T(128)} %get-tuple-element.447, bf16[3104,256]{1,0:T(8,128)(2,1)} %get-tuple-element.457, s32[3104]{0:T(1024)S(1)} %eq.316, s32[1024]{0:T(1024)S(1)} %bitcast.107), kind=kOutput, calls=%fused_computation.34.clone.1 | convolution fusion | flops 1630568448 | bytes 2654848 | tf_op jit(solution)/shard_map/while/body/eval_jaxpr/dot_general | solution.py:20
  169.0 4.4 %fusion.132 = f32[3,1024,256]{2,1,0:T(8,128)} fusion(f32[3,1024,256]{2,1,0:T(8,128)} %get-tuple-element.448, s32[]{:T(128)} %get-tuple-element.447, bf16[3104,256]{1,0:T(8,128)(2,1)} %get-tuple-element.457, s32[3104]{0:T(1024)S(1)} %eq.316, s32[1024]{0:T(1024)S(1)} %bitcast.107), kind=kOutput, calls=%fused_computation.34.clone.1 | convolution fusion | flops 1630568448 | bytes 2654848 | tf_op jit(solution)/shard_map/while/body/eval_jaxpr/dot_general | solution.py:20
  173.4 4.4 %fusion.132 = f32[3,1024,256]{2,1,0:T(8,128)} fusion(f32[3,1024,256]{2,1,0:T(8,128)} %get-tuple-element.448, s32[]{:T(128)} %get-tuple-element.447, bf16[3104,256]{1,0:T(8,128)(2,1)} %get-tuple-element.457, s32[3104]{0:T(1024)S(1)} %eq.316, s32[1024]{0:T(1024)S(1)} %bitcast.107), kind=kOutput, calls=%fused_computation.34.clone.1 | convolution fusion | flops 1630568448 | bytes 2654848 | tf_op jit(solution)/shard_map/while/body/eval_jaxpr/dot_general | solution.py:20
  177.8 7.9 %multiply_reduce_fusion.1 = (f32[3,1024]{1,0:T(4,128)S(1)}, f32[3,1024,256]{2,1,0:T(8,128)}) fusion(f32[3,1024,256]{2,1,0:T(8,128)} %bitcast.93, f32[3,1024,256]{2,1,0:T(8,128)} %get-tuple-element.143, f32[7,1024,256]{2,1,0:T(8,128)} %get-tuple-element.141, f32[7,1024,256]{2,1,0:T(8,128)} %get-tuple-element.139, f32[7,1024,256]{2,1,0:T(8,128)} %get-tuple-element.138), kind=kLoop, calls=%fused_computation.59 | loop fusion | flops 4715520 | bytes 18886656 | tf_op jit(solution)/shard_map/reduce_sum | solution.py:9
  185.8 4.6 %multiply_convert_fusion.1 = bf16[32,96,256]{2,1,0:T(8,128)(2,1)} fusion(f32[32,96,256]{2,1,0:T(8,128)} %bitcast.94, f32[32,96,256]{2,1,0:T(8,128)} %bitcast.95, f32[32,96]{1,0:T(8,128)S(1)} %rsqrt.30), kind=kLoop, calls=%fused_computation.58 | loop fusion | flops 2359296 | bytes 7876608 | tf_op jit(solution)/shard_map/convert_element_type | solution.py:10
  190.4 8.1 %all-to-all-start.2 = ((bf16[32,96,256]{2,1,0:T(8,128)(2,1)}), bf16[32,96,256]{2,1,0:T(8,128)(2,1)}, u32[]{:S(2)}, u32[]{:S(2)}) async-start(bf16[32,96,256]{2,1,0:T(8,128)(2,1)} %multiply_convert_fusion.1), calls=%async_computation.2 | async-start | bytes 3145728 | tf_op jit(solution)/shard_map/all_to_all | solution.py:109
  198.5 12.3 %while.53 = (s32[]{:T(128)}, f32[4,1024,256]{2,1,0:T(8,128)}, s32[4,1024]{1,0:T(4,128)S(1)}, s32[2,1552]{1,0:T(2,128)S(1)}, bf16[3104,256]{1,0:T(8,128)(2,1)S(1)}, /*index=5*/s32[]{:T(128)}) while((s32[]{:T(128)}, f32[4,1024,256]{2,1,0:T(8,128)}, s32[4,1024]{1,0:T(4,128)S(1)}, s32[2,1552]{1,0:T(2,128)S(1)}, ...), condition=%wide.region_10.11_spmd, body=%wide.region_9.10_spmd.sunk | while | flops 1630568448 | bytes 2687945 | solution.py:22
  210.9 6.9 %add_add_fusion = f32[4,1024,256]{2,1,0:T(8,128)S(1)} fusion(f32[4,1024,256]{2,1,0:T(8,128)} %get-tuple-element.142, f32[7,1024,256]{2,1,0:T(8,128)} %get-tuple-element.141, f32[7,1024,256]{2,1,0:T(8,128)} %get-tuple-element.139, f32[7,1024,256]{2,1,0:T(8,128)} %get-tuple-element.138), kind=kLoop, calls=%fused_computation.54 | loop fusion | flops 3145728 | bytes 20971520 | tf_op jit(solution)/shard_map/add | solution.py:111
  223.4 4.4 %fusion.67 = bf16[1024,256]{0,1:T(8,128)(2,1)S(1)} fusion(bf16[3072,256]{1,0:T(8,128)(2,1)} %bitcast.22, s32[1024]{0:T(1024)S(1)} %get-tuple-element.210, f32[1024,256]{0,1:T(8,128)} %get-tuple-element.213, f32[1024]{0:T(1024)S(1)} %add_rsqrt_fusion.2), kind=kOutput, calls=%fused_computation.63 | convolution fusion | flops 1615069184 | bytes 3153920 | tf_op jit(solution)/shard_map/dot_general | solution.py:115
  (149 shorter events, 77.6 us)
Async XLA Ops:
  0.6 12.7 %copy-start = (bf16[1024,1024]{1,0:T(8,128)(2,1)S(1)}, bf16[1024,1024]{1,0:T(8,128)(2,1)}, u32[]{:S(2)}) copy-start(bf16[1024,1024]{1,0:T(8,128)(2,1)} %param.15) | copy-start | bytes 6291460
  4.8 19.5 %all-to-all-start = ((s32[32,96,1]{1,2,0:T(1,128)}), s32[32,96,1]{1,2,0:T(1,128)S(1)}, u32[]{:S(2)}, u32[]{:S(2)}) async-start(s32[32,96,1]{1,2,0:T(1,128)} %all_to_all.24), calls=%async_computation | async-start | bytes 32768 | tf_op jit(solution)/shard_map/all_to_all | solution.py:58
  24.3 30.1 %all-to-all-start.1 = ((bf16[32,96,256]{2,1,0:T(8,128)(2,1)}), bf16[32,96,256]{2,1,0:T(8,128)(2,1)S(1)}, u32[]{:S(2)}, u32[]{:S(2)}) async-start(bf16[32,96,256]{2,1,0:T(8,128)(2,1)} %bitcast.99), calls=%async_computation.1 | async-start | bytes 3145728 | tf_op jit(solution)/shard_map/all_to_all | solution.py:57
  55.4 27.5 %collective-permute-start = (bf16[1552,256]{1,0:T(8,128)(2,1)}, bf16[1552,256]{1,0:T(8,128)(2,1)}, u32[]{:S(2)}, u32[]{:S(2)}) collective-permute-start(bf16[1552,256]{1,0:T(8,128)(2,1)} %pad_maximum_fusion), channel_id=1, source_target_pairs={{0,1},{1,2},{2,3},{3,0},{4,5},{5,6},{6,7},{7,4},{8,9},{9,10},{10,1... | collective-permute-start | bytes 2383880 | tf_op jit(solution)/shard_map/ppermute | solution.py:81
  57.0 25.9 %collective-permute-start.1 = (bf16[1552,256]{1,0:T(8,128)(2,1)}, bf16[1552,256]{1,0:T(8,128)(2,1)}, u32[]{:S(2)}, u32[]{:S(2)}) collective-permute-start(bf16[1552,256]{1,0:T(8,128)(2,1)} %pad_maximum_fusion), channel_id=1, source_target_pairs={{0,3},{1,0},{2,1},{3,2},{4,7},{5,4},{6,5},{7,6},{8,11},{9,8},{10,9... | collective-permute-start | bytes 2383880 | tf_op jit(solution)/shard_map/ppermute | solution.py:81
  82.9 41.3 %collective-permute-start.3 = (bf16[1552,256]{1,0:T(8,128)(2,1)S(1)}, bf16[1552,256]{1,0:T(8,128)(2,1)S(1)}, u32[]{:S(2)}, u32[]{:S(2)}) collective-permute-start(bf16[1552,256]{1,0:T(8,128)(2,1)S(1)} %pad_maximum_fusion.1), channel_id=1, source_target_pairs={{0,3},{1,0},{2,1},{3,2},{4,7},{5,4},{6,5},{7,6},{8,11},{9,8},{10,9... | collective-permute-start | bytes 2383880 | tf_op jit(solution)/shard_map/ppermute | solution.py:81
  84.4 38.6 %collective-permute-start.2 = (bf16[1552,256]{1,0:T(8,128)(2,1)S(1)}, bf16[1552,256]{1,0:T(8,128)(2,1)}, u32[]{:S(2)}, u32[]{:S(2)}) collective-permute-start(bf16[1552,256]{1,0:T(8,128)(2,1)S(1)} %pad_maximum_fusion.1), channel_id=1, source_target_pairs={{0,1},{1,2},{2,3},{3,0},{4,5},{5,6},{6,7},{7,4},{8,9},{9,10},{10,1... | collective-permute-start | bytes 2383880 | tf_op jit(solution)/shard_map/ppermute | solution.py:81
  86.8 1.2 copy-start.5
  123.0 40.0 %collective-permute-start.4 = (bf16[1552,256]{1,0:T(8,128)(2,1)}, bf16[1552,256]{1,0:T(8,128)(2,1)S(1)}, u32[]{:S(2)}, u32[]{:S(2)}) collective-permute-start(bf16[1552,256]{1,0:T(8,128)(2,1)} %collective-permute-done), channel_id=1, source_target_pairs={{0,1},{1,2},{2,3},{3,0},{4,5},{5,6},{6,7},{7,4},{8,9},{9,10},{10,1... | collective-permute-start | bytes 2383880 | tf_op jit(solution)/shard_map/ppermute | solution.py:81
  124.3 1.2 copy-start.4
  125.5 37.7 %collective-permute-start.5 = (bf16[1552,256]{1,0:T(8,128)(2,1)S(1)}, bf16[1552,256]{1,0:T(8,128)(2,1)S(1)}, u32[]{:S(2)}, u32[]{:S(2)}) collective-permute-start(bf16[1552,256]{1,0:T(8,128)(2,1)S(1)} %collective-permute-done.3), channel_id=1, source_target_pairs={{0,3},{1,0},{2,1},{3,2},{4,7},{5,4},{6,5},{7,6},{8,11},{9,8},{10,9... | collective-permute-start | bytes 2383880 | tf_op jit(solution)/shard_map/ppermute | solution.py:81
  163.2 1.2 copy-start.2
  190.4 8.1 %copy-start.3 = (bf16[3104,256]{1,0:T(8,128)(2,1)S(1)}, bf16[3104,256]{1,0:T(8,128)(2,1)}, u32[]{:S(2)}) copy-start(bf16[3104,256]{1,0:T(8,128)(2,1)} %get-tuple-element.469) | copy-start | bytes 4767748
  190.4 33.0 %all-to-all-start.2 = ((bf16[32,96,256]{2,1,0:T(8,128)(2,1)}), bf16[32,96,256]{2,1,0:T(8,128)(2,1)}, u32[]{:S(2)}, u32[]{:S(2)}) async-start(bf16[32,96,256]{2,1,0:T(8,128)(2,1)} %multiply_convert_fusion.1), calls=%async_computation.2 | async-start | bytes 3145728 | tf_op jit(solution)/shard_map/all_to_all | solution.py:109
  223.4 5.4 %copy-start.1 = (bf16[1024,1024]{1,0:T(8,128)(2,1)S(1)}, bf16[1024,1024]{1,0:T(8,128)(2,1)}, u32[]{:S(2)}) copy-start(bf16[1024,1024]{1,0:T(8,128)(2,1)} %param.15) | copy-start | bytes 6291460

commit v6 on v5

--- a/solution.py
+++ b/solution.py
@@ -70,12 +70,13 @@
              id_code.reshape(code_rows, emb_width)]
         )
 
-    def keys_of(pieces):
-        count = pieces.shape[0] // (half_rows + code_rows)
-        code = pieces.reshape(count, -1, emb_width)[:, half_rows:]
-        code = code.reshape(count, -1)[:, : 2 * half_rows].astype(jnp.int32)
-        ids = code[:, :half_rows] * 128 + code[:, half_rows:]
-        return jnp.pad(ids, ((0, 0), (0, code_rows)), constant_values=-1).reshape(-1)
+    def split(pieces):
+        blocks = [piece[:half_rows] for piece in pieces]
+        ids = []
+        for piece in pieces:
+            code = piece[half_rows:].reshape(-1)[: 2 * half_rows].astype(jnp.int32)
+            ids.append(code[:half_rows] * 128 + code[half_rows:])
+        return jnp.concatenate(ids), jnp.concatenate(blocks)
 
     def shift(x, step):
         return lax.ppermute(x, "rep", [(i, (i + step) % replicas) for i in range(replicas)])
@@ -89,9 +90,9 @@
     far_a = shift(prev_a, 1)
     far_b = shift(next_b, -1)
 
-    near_a = jnp.concatenate([prev_a, next_a])
-    near_b = jnp.concatenate([prev_b, next_b])
-    far = jnp.concatenate([far_a, far_b])
+    keys_a, near_a = split([prev_a, next_a])
+    keys_b, near_b = split([prev_b, next_b])
+    keys_far, far = split([far_a, far_b])
 
     first_row = my_rep * share_rows
     share_ids = first_row + jnp.arange(share_rows, dtype=jnp.int32)
@@ -100,9 +101,8 @@
 
     queries = jnp.concatenate([in_ids, share_ids])
     own_sums = match_sums(queries, in_ids, incoming)
-    sums_a = match_sums(queries, keys_of(near_a), near_a)
-    sums_b = match_sums(queries, keys_of(near_b), near_b)
-    keys_far = keys_of(far)
+    sums_a = match_sums(queries, keys_a, near_a)
+    sums_b = match_sums(queries, keys_b, near_b)
     look_sum = (own_sums[:slots] + sums_a[:slots] + sums_b[:slots]
                 + match_sums(in_ids, keys_far, far))
     picked = normalize(look_cent.astype(jnp.float32) + look_sum)

time: 230 us -> 213 us (0.926)
  matrix products: 122 us -> 100 us
  other arithmetic: 33 us -> 41.1 us
  local copies, waits for them, and re-layouts: 39.3 us -> 36.5 us
    dot_general x28, matrix products: 107 us -> 84.5 us  [one_block(): return jnp.dot(selector, rows, preferred_element_type=jnp.float32)]
    slice x0 -> x6, local copies, waits for them, and re-layouts: none -> 5.98 us  [split(): blocks = [piece[:half_rows] for piece in pieces]]
    unnamed x22 -> x12, local copies, waits for them, and re-layouts: 6.7 us -> 1.03 us
    concatenate x0 -> x5, other arithmetic: none -> 3.75 us  [split(): return (jnp.concatenate(ids), jnp.concatenate(blocks))]
    convert_element_type x3 -> x6, other arithmetic: 0.05 us -> 3.52 us  [split(): code = piece[half_rows:].reshape(-1)[:2 * half_rows].astype(jnp.int32)]
  transfers between devices with their start and end apart: 9 -> 9, of which waited for: 1 -> 1; matrix products, arithmetic and copies ran while one was open for 68% -> 65% of each run, Pallas kernels for 0% -> 0%
where the time goes in v6:
time: 213 us; the launch traced here: 212 us
  matrix products  100 us (47%)
  other arithmetic  41.1 us (19%)
  local copies, waits for them, and re-layouts  36.5 us (17%)
  starting transfers between devices  32.2 us (15%)
    dot_general x28, matrix products, one_block(): return jnp.dot(selector, rows, preferred_element_type=jnp.float32)  84.5 us
    gather x1, local copies, waits for them, and re-layouts, body(): look_cent = centroids[in_ids]  16.6 us
    another operation x3, local copies, waits for them, and re-layouts  10.8 us
    reduce_sum x2, other arithmetic, normalize(): jnp.mean(updated * updated, axis=-1, keepdims=True) + 1e-06  10.4 us
    all_to_all x1, starting transfers between devices, body(): lax.all_to_all(out_ids, 'wide', split_axis=0, concat_axis=0, tiled=True)  8.57 us
    ppermute x6, starting transfers between devices, shift(): lax.ppermute(x, 'rep', [(i, (i + step) % replicas) for i in range(replica...  8.2 us
    all_to_all x1, starting transfers between devices, body(): lax.all_to_all(picked, 'wide', split_axis=0, concat_axis=0, tiled=True)  8.03 us
    convert_element_type x2, other arithmetic, normalize(): return (updated * lax.rsqrt(jnp.mean(updated * updated, axis=-1, keepdims...  7.6 us
  transfers between devices with their start and end apart: 9, of which 1 were waited for; matrix products, arithmetic and copies ran while one was open for 65% of the time, Pallas kernels for 0%

profile of v6, /device:TPU:1, one launch (start us, length us, event | category | flops | bytes accessed | tf_op | source)
XLA Modules:
  0.0 212.1 jit_solution(178625265696958245)
XLA Ops:
  4.8 8.6 %all-to-all-start = ((s32[32,96,1]{1,2,0:T(1,128)}), s32[32,96,1]{1,2,0:T(1,128)S(1)}, u32[]{:S(2)}, u32[]{:S(2)}) async-start(s32[32,96,1]{1,2,0:T(1,128)} %all_to_all.24), calls=%async_computation | async-start | bytes 32768 | tf_op jit(solution)/shard_map/all_to_all | solution.py:58
  13.4 5.9 %multiply_reduce_fusion.2 = (f32[1024]{0:T(1024)S(1)}, f32[1024,256]{0,1:T(8,128)}) fusion(bf16[1024,256]{1,0:T(8,128)(2,1)} %param.18, bf16[1024,1024]{1,0:T(8,128)(2,1)S(1)} %copy-done, bf16[1024,1024]{1,0:T(8,128)(2,1)} %param.17), kind=kOutput, calls=%fused_computation.70 | convolution fusion | flops 2694315008 | bytes 5771264 | tf_op jit(solution)/shard_map/dot_general | solution.py:50
  19.3 4.9 %fusion.63 = bf16[3072,256]{1,0:T(8,128)(2,1)} fusion(s32[1024]{0:T(1024)S(1)} %get-tuple-element.210, f32[1024,256]{0,1:T(8,128)} %get-tuple-element.213, f32[1024]{0:T(1024)S(1)} %add_rsqrt_fusion.2), kind=kOutput, calls=%fused_computation.57 | convolution fusion | flops 1615069184 | bytes 2629632 | tf_op jit(solution)/shard_map/dot_general | solution.py:55
  24.2 7.4 %all-to-all-start.1 = ((bf16[32,96,256]{2,1,0:T(8,128)(2,1)}), bf16[32,96,256]{2,1,0:T(8,128)(2,1)S(1)}, u32[]{:S(2)}, u32[]{:S(2)}) async-start(bf16[32,96,256]{2,1,0:T(8,128)(2,1)} %bitcast.87), calls=%async_computation.1 | async-start | bytes 3145728 | tf_op jit(solution)/shard_map/all_to_all | solution.py:57
  33.5 16.6 %gather_fusion = bf16[3072,256]{1,0:T(8,128)(2,1)} fusion(bf16[16384,256]{1,0:T(8,128)(2,1)} %param.19, s32[3072]{0:T(1024)S(1)} %broadcast_clamp_fusion), kind=kCustom, calls=%fused_computation | custom fusion | bytes 3158016 | tf_op jit(solution)/shard_map/gather | solution.py:99
  50.1 3.3 %convert_element_type.97 = f32[3072,256]{1,0:T(8,128)} convert(bf16[3072,256]{1,0:T(8,128)(2,1)} %gather_fusion) | non-fusion elementwise | flops 786432 | bytes 4718592 | tf_op jit(solution)/shard_map/convert_element_type | solution.py:108
  59.1 3.6 %broadcast.105.clone.2 = f32[7,1024,256]{2,1,0:T(8,128)} broadcast(f32[]{:T(128)} %constant.120.clone.1), dimensions={} | broadcast | bytes 7340036 | tf_op jit(solution)/shard_map/broadcast.4
  62.7 20.1 %while.50 = (s32[]{:T(128)}, f32[7,1024,256]{2,1,0:T(8,128)}, s32[7,1024]{1,0:T(8,128)S(1)}, s32[3072]{0:T(1024)S(1)}, bf16[3072,256]{1,0:T(8,128)(2,1)S(1)}, /*index=5*/s32[]{:T(128)}) while((s32[]{:T(128)}, f32[7,1024,256]{2,1,0:T(8,128)}, s32[7,1024]{1,0:T(8,128)S(1)}, s32[3072]{0:T(1024)S(1)}, bf16[3072,256]{1,0:T(8,128)(2,1)S(1)}, ...), condition=%wide.region_4.5_spmd, body=%wide.region_3.4_spmd.sunk | while | flops 1613758464 | bytes 2646601 | solution.py:22
  62.7 2.9 %fusion.120 = f32[7,1024,256]{2,1,0:T(8,128)} fusion(f32[7,1024,256]{2,1,0:T(8,128)} %get-tuple-element.430, s32[]{:T(128)} %get-tuple-element.429, bf16[3072,256]{1,0:T(8,128)(2,1)S(1)} %get-tuple-element.439, s32[3072]{0:T(1024)S(1)} %get-tuple-element.438, s32[1024]{0:T(1024)S(1)} %bitcast.90), kind=kOutput, calls=%fused_computation.6.clone.1 | convolution fusion | flops 1613758464 | bytes 2638336 | tf_op jit(solution)/shard_map/while/body/eval_jaxpr/dot_general | solution.py:20
  71.3 2.9 %fusion.120 = f32[7,1024,256]{2,1,0:T(8,128)} fusion(f32[7,1024,256]{2,1,0:T(8,128)} %get-tuple-element.430, s32[]{:T(128)} %get-tuple-element.429, bf16[3072,256]{1,0:T(8,128)(2,1)S(1)} %get-tuple-element.439, s32[3072]{0:T(1024)S(1)} %get-tuple-element.438, s32[1024]{0:T(1024)S(1)} %bitcast.90), kind=kOutput, calls=%fused_computation.6.clone.1 | convolution fusion | flops 1613758464 | bytes 2638336 | tf_op jit(solution)/shard_map/while/body/eval_jaxpr/dot_general | solution.py:20
  90.3 3.6 %broadcast.105.clone.1 = f32[7,1024,256]{2,1,0:T(8,128)} broadcast(f32[]{:T(128)} %constant.120.clone.1), dimensions={} | broadcast | bytes 7340036 | tf_op jit(solution)/shard_map/broadcast.4
  94.0 20.2 %while.51 = (s32[]{:T(128)}, f32[7,1024,256]{2,1,0:T(8,128)}, s32[7,1024]{1,0:T(8,128)S(1)}, s32[3072]{0:T(1024)S(1)}, bf16[3072,256]{1,0:T(8,128)(2,1)S(1)}, /*index=5*/s32[]{:T(128)}) while((s32[]{:T(128)}, f32[7,1024,256]{2,1,0:T(8,128)}, s32[7,1024]{1,0:T(8,128)S(1)}, s32[3072]{0:T(1024)S(1)}, bf16[3072,256]{1,0:T(8,128)(2,1)S(1)}, ...), condition=%wide.region_6.7_spmd, body=%wide.region_5.6_spmd.sunk | while | flops 1613758464 | bytes 2646601 | solution.py:22
  94.0 2.9 %fusion.123 = f32[7,1024,256]{2,1,0:T(8,128)} fusion(f32[7,1024,256]{2,1,0:T(8,128)} %get-tuple-element.412, s32[]{:T(128)} %get-tuple-element.411, bf16[3072,256]{1,0:T(8,128)(2,1)S(1)} %get-tuple-element.421, s32[3072]{0:T(1024)S(1)} %get-tuple-element.420, s32[1024]{0:T(1024)S(1)} %bitcast.91), kind=kOutput, calls=%fused_computation.13.clone.1 | convolution fusion | flops 1613758464 | bytes 2638336 | tf_op jit(solution)/shard_map/while/body/eval_jaxpr/dot_general | solution.py:20
  96.9 2.9 %fusion.123 = f32[7,1024,256]{2,1,0:T(8,128)} fusion(f32[7,1024,256]{2,1,0:T(8,128)} %get-tuple-element.412, s32[]{:T(128)} %get-tuple-element.411, bf16[3072,256]{1,0:T(8,128)(2,1)S(1)} %get-tuple-element.421, s32[3072]{0:T(1024)S(1)} %get-tuple-element.420, s32[1024]{0:T(1024)S(1)} %bitcast.91), kind=kOutput, calls=%fused_computation.13.clone.1 | convolution fusion | flops 1613758464 | bytes 2638336 | tf_op jit(solution)/shard_map/while/body/eval_jaxpr/dot_general | solution.py:20
  108.4 2.9 %fusion.123 = f32[7,1024,256]{2,1,0:T(8,128)} fusion(f32[7,1024,256]{2,1,0:T(8,128)} %get-tuple-element.412, s32[]{:T(128)} %get-tuple-element.411, bf16[3072,256]{1,0:T(8,128)(2,1)S(1)} %get-tuple-element.421, s32[3072]{0:T(1024)S(1)} %get-tuple-element.420, s32[1024]{0:T(1024)S(1)} %bitcast.91), kind=kOutput, calls=%fused_computation.13.clone.1 | convolution fusion | flops 1613758464 | bytes 2638336 | tf_op jit(solution)/shard_map/while/body/eval_jaxpr/dot_general | solution.py:20
  117.4 3.0 %collective-permute-start.5 = (bf16[1552,256]{1,0:T(8,128)(2,1)S(1)}, bf16[1552,256]{1,0:T(8,128)(2,1)}, u32[]{:S(2)}, u32[]{:S(2)}) collective-permute-start(bf16[1552,256]{1,0:T(8,128)(2,1)S(1)} %collective-permute-done.3), channel_id=1, source_target_pairs={{0,3},{1,0},{2,1},{3,2},{4,7},{5,4},{6,5},{7,6},{8,11},{9,8},{10,9... | collective-permute-start | bytes 2383880 | tf_op jit(solution)/shard_map/ppermute | solution.py:82
  120.4 3.6 %broadcast.105.clone = f32[7,1024,256]{2,1,0:T(8,128)} broadcast(f32[]{:T(128)} %constant.120.clone.1), dimensions={} | broadcast | bytes 7340036 | tf_op jit(solution)/shard_map/broadcast.4
  123.9 20.1 %while.52 = (s32[]{:T(128)}, f32[7,1024,256]{2,1,0:T(8,128)}, s32[7,1024]{1,0:T(8,128)S(1)}, s32[3072]{0:T(1024)S(1)}, bf16[3072,256]{1,0:T(8,128)(2,1)S(1)}, /*index=5*/s32[]{:T(128)}) while((s32[]{:T(128)}, f32[7,1024,256]{2,1,0:T(8,128)}, s32[7,1024]{1,0:T(8,128)S(1)}, s32[3072]{0:T(1024)S(1)}, bf16[3072,256]{1,0:T(8,128)(2,1)S(1)}, ...), condition=%wide.region_8.9_spmd, body=%wide.region_7.8_spmd.sunk | while | flops 1613758464 | bytes 2646601 | solution.py:22
  126.8 2.9 %fusion.126 = f32[7,1024,256]{2,1,0:T(8,128)} fusion(f32[7,1024,256]{2,1,0:T(8,128)} %get-tuple-element.394, s32[]{:T(128)} %get-tuple-element.393, bf16[3072,256]{1,0:T(8,128)(2,1)S(1)} %get-tuple-element.403, s32[3072]{0:T(1024)S(1)} %get-tuple-element.402, s32[1024]{0:T(1024)S(1)} %bitcast.92), kind=kOutput, calls=%fused_computation.20.clone.1 | convolution fusion | flops 1613758464 | bytes 2638336 | tf_op jit(solution)/shard_map/while/body/eval_jaxpr/dot_general | solution.py:20
  138.3 2.9 %fusion.126 = f32[7,1024,256]{2,1,0:T(8,128)} fusion(f32[7,1024,256]{2,1,0:T(8,128)} %get-tuple-element.394, s32[]{:T(128)} %get-tuple-element.393, bf16[3072,256]{1,0:T(8,128)(2,1)S(1)} %get-tuple-element.403, s32[3072]{0:T(1024)S(1)} %get-tuple-element.402, s32[1024]{0:T(1024)S(1)} %bitcast.92), kind=kOutput, calls=%fused_computation.20.clone.1 | convolution fusion | flops 1613758464 | bytes 2638336 | tf_op jit(solution)/shard_map/while/body/eval_jaxpr/dot_general | solution.py:20
  149.1 12.9 %while.54 = (s32[]{:T(128)}, f32[3,1024,256]{2,1,0:T(8,128)}, s32[3,1024]{1,0:T(4,128)S(1)}, s32[3072]{0:T(1024)S(1)}, bf16[3072,256]{1,0:T(8,128)(2,1)}, /*index=5*/s32[]{:T(128)}) while((s32[]{:T(128)}, f32[3,1024,256]{2,1,0:T(8,128)}, s32[3,1024]{1,0:T(4,128)S(1)}, s32[3072]{0:T(1024)S(1)}, bf16[3072,256]{1,0:T(8,128)(2,1)}, ...), condition=%wide.region_13.14_spmd, body=%wide.region_12.13_spmd.sunk | while | flops 1613758464 | bytes 2646601 | solution.py:22
  149.1 4.3 %fusion.132 = f32[3,1024,256]{2,1,0:T(8,128)} fusion(f32[3,1024,256]{2,1,0:T(8,128)} %get-tuple-element.448, s32[]{:T(128)} %get-tuple-element.447, bf16[3072,256]{1,0:T(8,128)(2,1)} %get-tuple-element.457, s32[3072]{0:T(1024)S(1)} %get-tuple-element.456, s32[1024]{0:T(1024)S(1)} %bitcast.93), kind=kOutput, calls=%fused_computation.34.clone.1 | convolution fusion | flops 1613758464 | bytes 2638336 | tf_op jit(solution)/shard_map/while/body/eval_jaxpr/dot_general | solution.py:20
  153.5 4.3 %fusion.132 = f32[3,1024,256]{2,1,0:T(8,128)} fusion(f32[3,1024,256]{2,1,0:T(8,128)} %get-tuple-element.448, s32[]{:T(128)} %get-tuple-element.447, bf16[3072,256]{1,0:T(8,128)(2,1)} %get-tuple-element.457, s32[3072]{0:T(1024)S(1)} %get-tuple-element.456, s32[1024]{0:T(1024)S(1)} %bitcast.93), kind=kOutput, calls=%fused_computation.34.clone.1 | convolution fusion | flops 1613758464 | bytes 2638336 | tf_op jit(solution)/shard_map/while/body/eval_jaxpr/dot_general | solution.py:20
  157.7 4.3 %fusion.132 = f32[3,1024,256]{2,1,0:T(8,128)} fusion(f32[3,1024,256]{2,1,0:T(8,128)} %get-tuple-element.448, s32[]{:T(128)} %get-tuple-element.447, bf16[3072,256]{1,0:T(8,128)(2,1)} %get-tuple-element.457, s32[3072]{0:T(1024)S(1)} %get-tuple-element.456, s32[1024]{0:T(1024)S(1)} %bitcast.93), kind=kOutput, calls=%fused_computation.34.clone.1 | convolution fusion | flops 1613758464 | bytes 2638336 | tf_op jit(solution)/shard_map/while/body/eval_jaxpr/dot_general | solution.py:20
  162.0 7.9 %multiply_reduce_fusion.1 = (f32[3,1024]{1,0:T(4,128)S(1)}, f32[3,1024,256]{2,1,0:T(8,128)}) fusion(f32[3,1024,256]{2,1,0:T(8,128)} %bitcast.81, f32[3,1024,256]{2,1,0:T(8,128)} %get-tuple-element.143, f32[7,1024,256]{2,1,0:T(8,128)} %get-tuple-element.141, f32[7,1024,256]{2,1,0:T(8,128)} %get-tuple-element.139, f32[7,1024,256]{2,1,0:T(8,128)} %get-tuple-element.138), kind=kLoop, calls=%fused_computation.59 | loop fusion | flops 4715520 | bytes 18886656 | tf_op jit(solution)/shard_map/reduce_sum | solution.py:9
  170.0 4.6 %multiply_convert_fusion.1 = bf16[32,96,256]{2,1,0:T(8,128)(2,1)} fusion(f32[32,96,256]{2,1,0:T(8,128)} %bitcast.82, f32[32,96,256]{2,1,0:T(8,128)} %bitcast.83, f32[32,96]{1,0:T(8,128)S(1)} %rsqrt.30), kind=kLoop, calls=%fused_computation.58 | loop fusion | flops 2359296 | bytes 7876608 | tf_op jit(solution)/shard_map/convert_element_type | solution.py:10
  174.5 8.0 %all-to-all-start.2 = ((bf16[32,96,256]{2,1,0:T(8,128)(2,1)}), bf16[32,96,256]{2,1,0:T(8,128)(2,1)}, u32[]{:S(2)}, u32[]{:S(2)}) async-start(bf16[32,96,256]{2,1,0:T(8,128)(2,1)} %multiply_convert_fusion.1), calls=%async_computation.2 | async-start | bytes 3145728 | tf_op jit(solution)/shard_map/all_to_all | solution.py:109
  182.6 11.6 %while.53 = (s32[]{:T(128)}, f32[4,1024,256]{2,1,0:T(8,128)}, s32[4,1024]{1,0:T(4,128)S(1)}, s32[3072]{0:T(1024)S(1)}, bf16[3072,256]{1,0:T(8,128)(2,1)S(1)}, /*index=5*/s32[]{:T(128)}) while((s32[]{:T(128)}, f32[4,1024,256]{2,1,0:T(8,128)}, s32[4,1024]{1,0:T(4,128)S(1)}, s32[3072]{0:T(1024)S(1)}, bf16[3072,256]{1,0:T(8,128)(2,1)S(1)}, ...), condition=%wide.region_10.11_spmd, body=%wide.region_9.10_spmd.sunk | while | flops 1613758464 | bytes 2646601 | solution.py:22
  191.3 2.9 %fusion.129 = f32[4,1024,256]{2,1,0:T(8,128)} fusion(f32[4,1024,256]{2,1,0:T(8,128)} %get-tuple-element.376, s32[]{:T(128)} %get-tuple-element.375, bf16[3072,256]{1,0:T(8,128)(2,1)S(1)} %get-tuple-element.385, s32[3072]{0:T(1024)S(1)} %get-tuple-element.384, s32[1024]{0:T(1024)S(1)} %bitcast.94), kind=kOutput, calls=%fused_computation.27.clone.1 | convolution fusion | flops 1613758464 | bytes 2638336 | tf_op jit(solution)/shard_map/while/body/eval_jaxpr/dot_general | solution.py:20
  194.2 6.9 %add_add_fusion = f32[4,1024,256]{2,1,0:T(8,128)S(1)} fusion(f32[4,1024,256]{2,1,0:T(8,128)} %get-tuple-element.142, f32[7,1024,256]{2,1,0:T(8,128)} %get-tuple-element.141, f32[7,1024,256]{2,1,0:T(8,128)} %get-tuple-element.139, f32[7,1024,256]{2,1,0:T(8,128)} %get-tuple-element.138), kind=kLoop, calls=%fused_computation.54 | loop fusion | flops 3145728 | bytes 20971520 | tf_op jit(solution)/shard_map/add | solution.py:111
  203.6 3.0 %multiply_convert_fusion = bf16[4096,256]{1,0:T(8,128)(2,1)} fusion(f32[4,1024,256]{2,1,0:T(8,128)S(1)} %add_add_fusion, f32[4096]{0:T(1024)S(1)} %add_rsqrt_fusion.1, bf16[16384,256]{1,0:T(8,128)(2,1)} %param.19, s32[]{:T(128)S(6)} %select_n.45), kind=kLoop, calls=%fused_computation.52 | loop fusion | flops 4194304 | bytes 8404996 | tf_op jit(solution)/shard_map/convert_element_type | solution.py:10
  206.7 4.4 %fusion.67 = bf16[1024,256]{0,1:T(8,128)(2,1)S(1)} fusion(bf16[3072,256]{1,0:T(8,128)(2,1)} %bitcast.19, s32[1024]{0:T(1024)S(1)} %get-tuple-element.210, f32[1024,256]{0,1:T(8,128)} %get-tuple-element.213, f32[1024]{0:T(1024)S(1)} %add_rsqrt_fusion.2), kind=kOutput, calls=%fused_computation.66 | convolution fusion | flops 1615069184 | bytes 3153920 | tf_op jit(solution)/shard_map/dot_general | solution.py:115
  (137 shorter events, 79.8 us)
Async XLA Ops:
  0.6 12.7 %copy-start = (bf16[1024,1024]{1,0:T(8,128)(2,1)S(1)}, bf16[1024,1024]{1,0:T(8,128)(2,1)}, u32[]{:S(2)}) copy-start(bf16[1024,1024]{1,0:T(8,128)(2,1)} %param.15) | copy-start | bytes 6291460
  4.8 19.5 %all-to-all-start = ((s32[32,96,1]{1,2,0:T(1,128)}), s32[32,96,1]{1,2,0:T(1,128)S(1)}, u32[]{:S(2)}, u32[]{:S(2)}) async-start(s32[32,96,1]{1,2,0:T(1,128)} %all_to_all.24), calls=%async_computation | async-start | bytes 32768 | tf_op jit(solution)/shard_map/all_to_all | solution.py:58
  24.2 30.1 %all-to-all-start.1 = ((bf16[32,96,256]{2,1,0:T(8,128)(2,1)}), bf16[32,96,256]{2,1,0:T(8,128)(2,1)S(1)}, u32[]{:S(2)}, u32[]{:S(2)}) async-start(bf16[32,96,256]{2,1,0:T(8,128)(2,1)} %bitcast.87), calls=%async_computation.1 | async-start | bytes 3145728 | tf_op jit(solution)/shard_map/all_to_all | solution.py:57
  55.4 28.4 %collective-permute-start = (bf16[1552,256]{1,0:T(8,128)(2,1)}, bf16[1552,256]{1,0:T(8,128)(2,1)}, u32[]{:S(2)}, u32[]{:S(2)}) collective-permute-start(bf16[1552,256]{1,0:T(8,128)(2,1)} %pad_maximum_fusion.3), channel_id=1, source_target_pairs={{0,1},{1,2},{2,3},{3,0},{4,5},{5,6},{6,7},{7,4},{8,9},{9,10},{10,1... | collective-permute-start | bytes 2383880 | tf_op jit(solution)/shard_map/ppermute | solution.py:82
  57.0 26.8 %collective-permute-start.1 = (bf16[1552,256]{1,0:T(8,128)(2,1)}, bf16[1552,256]{1,0:T(8,128)(2,1)}, u32[]{:S(2)}, u32[]{:S(2)}) collective-permute-start(bf16[1552,256]{1,0:T(8,128)(2,1)} %pad_maximum_fusion.3), channel_id=1, source_target_pairs={{0,3},{1,0},{2,1},{3,2},{4,7},{5,4},{6,5},{7,6},{8,11},{9,8},{10,9... | collective-permute-start | bytes 2383880 | tf_op jit(solution)/shard_map/ppermute | solution.py:82
  83.8 30.3 %collective-permute-start.3 = (bf16[1552,256]{1,0:T(8,128)(2,1)}, bf16[1552,256]{1,0:T(8,128)(2,1)S(1)}, u32[]{:S(2)}, u32[]{:S(2)}) collective-permute-start(bf16[1552,256]{1,0:T(8,128)(2,1)} %pad_maximum_fusion.4), channel_id=1, source_target_pairs={{0,3},{1,0},{2,1},{3,2},{4,7},{5,4},{6,5},{7,6},{8,11},{9,8},{10,9... | collective-permute-start | bytes 2383880 | tf_op jit(solution)/shard_map/ppermute | solution.py:82
  85.2 28.9 %collective-permute-start.2 = (bf16[1552,256]{1,0:T(8,128)(2,1)}, bf16[1552,256]{1,0:T(8,128)(2,1)}, u32[]{:S(2)}, u32[]{:S(2)}) collective-permute-start(bf16[1552,256]{1,0:T(8,128)(2,1)} %pad_maximum_fusion.4), channel_id=1, source_target_pairs={{0,1},{1,2},{2,3},{3,0},{4,5},{5,6},{6,7},{7,4},{8,9},{9,10},{10,1... | collective-permute-start | bytes 2383880 | tf_op jit(solution)/shard_map/ppermute | solution.py:82
  90.3 3.7 %copy-start.4 = (bf16[3072,256]{1,0:T(8,128)(2,1)S(1)}, bf16[3072,256]{1,0:T(8,128)(2,1)}, u32[]{:S(2)}) copy-start(bf16[3072,256]{1,0:T(8,128)(2,1)} %pad_maximum_fusion) | copy-start | bytes 4718596
  114.1 29.9 %collective-permute-start.4 = (bf16[1552,256]{1,0:T(8,128)(2,1)}, bf16[1552,256]{1,0:T(8,128)(2,1)}, u32[]{:S(2)}, u32[]{:S(2)}) collective-permute-start(bf16[1552,256]{1,0:T(8,128)(2,1)} %collective-permute-done), channel_id=1, source_target_pairs={{0,1},{1,2},{2,3},{3,0},{4,5},{5,6},{6,7},{7,4},{8,9},{9,10},{10,1... | collective-permute-start | bytes 2383880 | tf_op jit(solution)/shard_map/ppermute | solution.py:82
  117.4 6.5 %copy-start.3 = (bf16[3072,256]{1,0:T(8,128)(2,1)S(1)}, bf16[3072,256]{1,0:T(8,128)(2,1)}, u32[]{:S(2)}) copy-start(bf16[3072,256]{1,0:T(8,128)(2,1)} %pad_maximum_fusion.1) | copy-start | bytes 4718596
  117.4 28.6 %collective-permute-start.5 = (bf16[1552,256]{1,0:T(8,128)(2,1)S(1)}, bf16[1552,256]{1,0:T(8,128)(2,1)}, u32[]{:S(2)}, u32[]{:S(2)}) collective-permute-start(bf16[1552,256]{1,0:T(8,128)(2,1)S(1)} %collective-permute-done.3), channel_id=1, source_target_pairs={{0,3},{1,0},{2,1},{3,2},{4,7},{5,4},{6,5},{7,6},{8,11},{9,8},{10,9... | collective-permute-start | bytes 2383880 | tf_op jit(solution)/shard_map/ppermute | solution.py:82
  174.5 8.0 %copy-start.2 = (bf16[3072,256]{1,0:T(8,128)(2,1)S(1)}, bf16[3072,256]{1,0:T(8,128)(2,1)}, u32[]{:S(2)}) copy-start(bf16[3072,256]{1,0:T(8,128)(2,1)} %get-tuple-element.460) | copy-start | bytes 4718596
  174.5 32.1 %all-to-all-start.2 = ((bf16[32,96,256]{2,1,0:T(8,128)(2,1)}), bf16[32,96,256]{2,1,0:T(8,128)(2,1)}, u32[]{:S(2)}, u32[]{:S(2)}) async-start(bf16[32,96,256]{2,1,0:T(8,128)(2,1)} %multiply_convert_fusion.1), calls=%async_computation.2 | async-start | bytes 3145728 | tf_op jit(solution)/shard_map/all_to_all | solution.py:109
  206.7 5.4 %copy-start.1 = (bf16[1024,1024]{1,0:T(8,128)(2,1)S(1)}, bf16[1024,1024]{1,0:T(8,128)(2,1)}, u32[]{:S(2)}) copy-start(bf16[1024,1024]{1,0:T(8,128)(2,1)} %param.15) | copy-start | bytes 6291460

commit v7 on v6

--- a/solution.py
+++ b/solution.py
@@ -58,41 +58,29 @@
     in_ids = lax.all_to_all(out_ids, "wide", split_axis=0, concat_axis=0, tiled=True)
 
     half_rows = slots // 2
-    code_rows = -(-2 * half_rows // emb_width)
-    code_rows = -(-code_rows // 16) * 16
-
-    def with_code(part):
-        part_ids = in_ids[part * half_rows : (part + 1) * half_rows]
-        id_code = jnp.concatenate([part_ids // 128, part_ids % 128]).astype(jnp.bfloat16)
-        id_code = jnp.pad(id_code, (0, code_rows * emb_width - 2 * half_rows))
-        return jnp.concatenate(
-            [incoming[part * half_rows : (part + 1) * half_rows],
-             id_code.reshape(code_rows, emb_width)]
-        )
-
-    def split(pieces):
-        blocks = [piece[:half_rows] for piece in pieces]
-        ids = []
-        for piece in pieces:
-            code = piece[half_rows:].reshape(-1)[: 2 * half_rows].astype(jnp.int32)
-            ids.append(code[:half_rows] * 128 + code[half_rows:])
-        return jnp.concatenate(ids), jnp.concatenate(blocks)
 
     def shift(x, step):
         return lax.ppermute(x, "rep", [(i, (i + step) % replicas) for i in range(replicas)])
 
-    payload_a = with_code(0)
+    def half(part):
+        return (incoming[part * half_rows : (part + 1) * half_rows],
+                in_ids[part * half_rows : (part + 1) * half_rows])
+
+    payload_a = half(0)
     prev_a = shift(payload_a, 1)
     next_a = shift(payload_a, -1)
-    payload_b, _, _ = lax.optimization_barrier((with_code(1), prev_a, next_a))
+    payload_b, _, _ = lax.optimization_barrier((half(1), prev_a, next_a))
     prev_b = shift(payload_b, 1)
     next_b = shift(payload_b, -1)
     far_a = shift(prev_a, 1)
     far_b = shift(next_b, -1)
 
-    keys_a, near_a = split([prev_a, next_a])
-    keys_b, near_b = split([prev_b, next_b])
-    keys_far, far = split([far_a, far_b])
+    def join(first, second):
+        return jnp.concatenate([first[1], second[1]]), jnp.concatenate([first[0], second[0]])
+
+    keys_a, near_a = join(prev_a, next_a)
+    keys_b, near_b = join(prev_b, next_b)
+    keys_far, far = join(far_a, far_b)
 
     first_row = my_rep * share_rows
     share_ids = first_row + jnp.arange(share_rows, dtype=jnp.int32)

time: 213 us -> 213 us (level)
  starting transfers between devices: 32.2 us -> 43.7 us
  other arithmetic: 41.1 us -> 34.6 us
  matrix products: 100 us -> 96 us
  local copies, waits for them, and re-layouts: 36.5 us -> 32.8 us
  waiting for transfers between devices: 0.97 us -> 4.5 us
    ppermute x6 -> x12, starting transfers between devices: 8.2 us -> 15.4 us  [shift(): lax.ppermute(x, 'rep', [(i, (i + step) % replicas) for i in range(replica...]
    slice x10 -> x4, local copies, waits for them, and re-layouts: 6.27 us -> 1.45 us  [the longest x1 1.27 us: half(): incoming[part * half_rows:(part + 1) * half_rows]]
    ppermute x6 -> x12, waiting for transfers between devices: 0.02 us -> 4.5 us  [shift(): lax.ppermute(x, 'rep', [(i, (i + step) % replicas) for i in range(replica...]
    all_to_all x1, starting transfers between devices: 8.03 us -> 12.3 us  [body(): lax.all_to_all(picked, 'wide', split_axis=0, concat_axis=0, tiled=True)]
    dot_general x28, matrix products: 84.5 us -> 80.2 us  [one_block(): return jnp.dot(selector, rows, preferred_element_type=jnp.float32)]
    convert_element_type x6 -> x0, other arithmetic: 3.52 us -> none  [split(): code = piece[half_rows:].reshape(-1)[:2 * half_rows].astype(jnp.int32)]
    concatenate x9 -> x4, other arithmetic: 5.68 us -> 2.72 us  [the longest x2 2.71 us: join(): jnp.concatenate([first[0], second[0]])]
  transfers between devices with their start and end apart: 9 -> 15, of which waited for: 1 -> 2; matrix products, arithmetic and copies ran while one was open for 65% -> 61% of each run, Pallas kernels for 0% -> 0%
where the time goes in v7:
time: 213 us
  matrix products  96 us (45%)
  starting transfers between devices  43.7 us (21%)
  other arithmetic  34.6 us (16%)
  local copies, waits for them, and re-layouts  32.8 us (15%)
  waiting for transfers between devices  4.5 us (2%)
    dot_general x28, matrix products, one_block(): return jnp.dot(selector, rows, preferred_element_type=jnp.float32)  80.2 us
    gather x1, local copies, waits for them, and re-layouts, body(): look_cent = centroids[in_ids]  16.6 us
    ppermute x12, starting transfers between devices, shift(): lax.ppermute(x, 'rep', [(i, (i + step) % replicas) for i in range(replica...  15.4 us
    all_to_all x1, starting transfers between devices, body(): lax.all_to_all(picked, 'wide', split_axis=0, concat_axis=0, tiled=True)  12.3 us
    another operation x3, local copies, waits for them, and re-layouts  10.8 us
    reduce_sum x2, other arithmetic, normalize(): jnp.mean(updated * updated, axis=-1, keepdims=True) + 1e-06  10.4 us
    all_to_all x1, starting transfers between devices, body(): lax.all_to_all(out_ids, 'wide', split_axis=0, concat_axis=0, tiled=True)  8.57 us
    convert_element_type x2, other arithmetic, normalize(): return (updated * lax.rsqrt(jnp.mean(updated * updated, axis=-1, keepdims...  7.57 us
  transfers between devices with their start and end apart: 15, of which 2 were waited for; matrix products, arithmetic and copies ran while one was open for 61% of the time, Pallas kernels for 0%

profile of v7, /device:TPU:1, one launch (start us, length us, event | category | flops | bytes accessed | tf_op | source)
XLA Modules:
  0.0 212.6 jit_solution(11409720431320696628)
XLA Ops:
  4.8 8.6 %all-to-all-start = ((s32[32,96,1]{1,2,0:T(1,128)}), s32[32,96,1]{1,2,0:T(1,128)S(1)}, u32[]{:S(2)}, u32[]{:S(2)}) async-start(s32[32,96,1]{1,2,0:T(1,128)} %all_to_all.24), calls=%async_computation | async-start | bytes 32768 | tf_op jit(solution)/shard_map/all_to_all | solution.py:58
  13.4 5.9 %multiply_reduce_fusion.2 = (f32[1024]{0:T(1024)S(1)}, f32[1024,256]{0,1:T(8,128)}) fusion(bf16[1024,256]{1,0:T(8,128)(2,1)} %param.18, bf16[1024,1024]{1,0:T(8,128)(2,1)S(1)} %copy-done, bf16[1024,1024]{1,0:T(8,128)(2,1)} %param.17), kind=kOutput, calls=%fused_computation.69 | convolution fusion | flops 2694315008 | bytes 5771264 | tf_op jit(solution)/shard_map/dot_general | solution.py:50
  19.3 4.8 %fusion.63 = bf16[3072,256]{1,0:T(8,128)(2,1)} fusion(s32[1024]{0:T(1024)S(1)} %get-tuple-element.208, f32[1024,256]{0,1:T(8,128)} %get-tuple-element.211, f32[1024]{0:T(1024)S(1)} %add_rsqrt_fusion.2), kind=kOutput, calls=%fused_computation.57 | convolution fusion | flops 1615069184 | bytes 2629632 | tf_op jit(solution)/shard_map/dot_general | solution.py:55
  24.2 7.4 %all-to-all-start.1 = ((bf16[32,96,256]{2,1,0:T(8,128)(2,1)}), bf16[32,96,256]{2,1,0:T(8,128)(2,1)S(1)}, u32[]{:S(2)}, u32[]{:S(2)}) async-start(bf16[32,96,256]{2,1,0:T(8,128)(2,1)} %bitcast.85), calls=%async_computation.1 | async-start | bytes 3145728 | tf_op jit(solution)/shard_map/all_to_all | solution.py:57
  37.2 16.6 %gather_fusion = bf16[3072,256]{1,0:T(8,128)(2,1)} fusion(bf16[16384,256]{1,0:T(8,128)(2,1)} %param.19, s32[3072]{0:T(1024)S(1)} %broadcast_clamp_fusion), kind=kCustom, calls=%fused_computation | custom fusion | bytes 3158016 | tf_op jit(solution)/shard_map/gather | solution.py:87
  53.8 3.3 %convert_element_type.62 = f32[3072,256]{1,0:T(8,128)} convert(bf16[3072,256]{1,0:T(8,128)(2,1)} %gather_fusion) | non-fusion elementwise | flops 786432 | bytes 4718592 | tf_op jit(solution)/shard_map/convert_element_type | solution.py:96
  57.1 3.7 %collective-permute-done.8 = s32[1536]{0:T(1024)S(1)} collective-permute-done((s32[1536]{0:T(1024)S(1)}, s32[1536]{0:T(1024)S(1)}, u32[]{:S(2)}, u32[]{:S(2)}) %collective-permute-start.8) | collective-permute-done | bytes 6176 | tf_op jit(solution)/shard_map/ppermute | solution.py:63
  64.7 3.6 %broadcast.74.clone.2 = f32[7,1024,256]{2,1,0:T(8,128)} broadcast(f32[]{:T(128)} %constant.84.clone.1), dimensions={} | broadcast | bytes 7340036 | tf_op jit(solution)/shard_map/broadcast.1
  68.3 20.1 %while.50 = (s32[]{:T(128)}, f32[7,1024,256]{2,1,0:T(8,128)}, s32[7,1024]{1,0:T(8,128)S(1)}, s32[3072]{0:T(1024)S(1)}, bf16[3072,256]{1,0:T(8,128)(2,1)S(1)}, /*index=5*/s32[]{:T(128)}) while((s32[]{:T(128)}, f32[7,1024,256]{2,1,0:T(8,128)}, s32[7,1024]{1,0:T(8,128)S(1)}, s32[3072]{0:T(1024)S(1)}, bf16[3072,256]{1,0:T(8,128)(2,1)S(1)}, ...), condition=%wide.region_4.5_spmd, body=%wide.region_3.4_spmd.sunk | while | flops 1613758464 | bytes 2646601 | solution.py:22
  76.9 2.9 %fusion.106 = f32[7,1024,256]{2,1,0:T(8,128)} fusion(f32[7,1024,256]{2,1,0:T(8,128)} %get-tuple-element.428, s32[]{:T(128)} %get-tuple-element.427, bf16[3072,256]{1,0:T(8,128)(2,1)S(1)} %get-tuple-element.437, s32[3072]{0:T(1024)S(1)} %get-tuple-element.436, s32[1024]{0:T(1024)S(1)} %bitcast.90), kind=kOutput, calls=%fused_computation.6.clone.1 | convolution fusion | flops 1613758464 | bytes 2638336 | tf_op jit(solution)/shard_map/while/body/eval_jaxpr/dot_general | solution.py:20
  92.6 3.6 %broadcast.74.clone.1 = f32[7,1024,256]{2,1,0:T(8,128)} broadcast(f32[]{:T(128)} %constant.84.clone.1), dimensions={} | broadcast | bytes 7340036 | tf_op jit(solution)/shard_map/broadcast.1
  96.2 20.2 %while.51 = (s32[]{:T(128)}, f32[7,1024,256]{2,1,0:T(8,128)}, s32[7,1024]{1,0:T(8,128)S(1)}, s32[3072]{0:T(1024)S(1)}, bf16[3072,256]{1,0:T(8,128)(2,1)S(1)}, /*index=5*/s32[]{:T(128)}) while((s32[]{:T(128)}, f32[7,1024,256]{2,1,0:T(8,128)}, s32[7,1024]{1,0:T(8,128)S(1)}, s32[3072]{0:T(1024)S(1)}, bf16[3072,256]{1,0:T(8,128)(2,1)S(1)}, ...), condition=%wide.region_6.7_spmd, body=%wide.region_5.6_spmd.sunk | while | flops 1613758464 | bytes 2646601 | solution.py:22
  96.3 2.9 %fusion.109 = f32[7,1024,256]{2,1,0:T(8,128)} fusion(f32[7,1024,256]{2,1,0:T(8,128)} %get-tuple-element.410, s32[]{:T(128)} %get-tuple-element.409, bf16[3072,256]{1,0:T(8,128)(2,1)S(1)} %get-tuple-element.419, s32[3072]{0:T(1024)S(1)} %get-tuple-element.418, s32[1024]{0:T(1024)S(1)} %bitcast.91), kind=kOutput, calls=%fused_computation.13.clone.1 | convolution fusion | flops 1613758464 | bytes 2638336 | tf_op jit(solution)/shard_map/while/body/eval_jaxpr/dot_general | solution.py:20
  99.1 2.9 %fusion.109 = f32[7,1024,256]{2,1,0:T(8,128)} fusion(f32[7,1024,256]{2,1,0:T(8,128)} %get-tuple-element.410, s32[]{:T(128)} %get-tuple-element.409, bf16[3072,256]{1,0:T(8,128)(2,1)S(1)} %get-tuple-element.419, s32[3072]{0:T(1024)S(1)} %get-tuple-element.418, s32[1024]{0:T(1024)S(1)} %bitcast.91), kind=kOutput, calls=%fused_computation.13.clone.1 | convolution fusion | flops 1613758464 | bytes 2638336 | tf_op jit(solution)/shard_map/while/body/eval_jaxpr/dot_general | solution.py:20
  107.8 2.9 %fusion.109 = f32[7,1024,256]{2,1,0:T(8,128)} fusion(f32[7,1024,256]{2,1,0:T(8,128)} %get-tuple-element.410, s32[]{:T(128)} %get-tuple-element.409, bf16[3072,256]{1,0:T(8,128)(2,1)S(1)} %get-tuple-element.419, s32[3072]{0:T(1024)S(1)} %get-tuple-element.418, s32[1024]{0:T(1024)S(1)} %bitcast.91), kind=kOutput, calls=%fused_computation.13.clone.1 | convolution fusion | flops 1613758464 | bytes 2638336 | tf_op jit(solution)/shard_map/while/body/eval_jaxpr/dot_general | solution.py:20
  110.7 2.9 %fusion.109 = f32[7,1024,256]{2,1,0:T(8,128)} fusion(f32[7,1024,256]{2,1,0:T(8,128)} %get-tuple-element.410, s32[]{:T(128)} %get-tuple-element.409, bf16[3072,256]{1,0:T(8,128)(2,1)S(1)} %get-tuple-element.419, s32[3072]{0:T(1024)S(1)} %get-tuple-element.418, s32[1024]{0:T(1024)S(1)} %bitcast.91), kind=kOutput, calls=%fused_computation.13.clone.1 | convolution fusion | flops 1613758464 | bytes 2638336 | tf_op jit(solution)/shard_map/while/body/eval_jaxpr/dot_general | solution.py:20
  119.9 3.2 %collective-permute-start.11 = (bf16[1536,256]{1,0:T(8,128)(2,1)}, bf16[1536,256]{1,0:T(8,128)(2,1)}, u32[]{:S(2)}, u32[]{:S(2)}) collective-permute-start(bf16[1536,256]{1,0:T(8,128)(2,1)} %collective-permute-done.7), channel_id=1, source_target_pairs={{0,3},{1,0},{2,1},{3,2},{4,7},{5,4},{6,5},{7,6},{8,11},{9,8},{10,9... | collective-permute-start | bytes 2359304 | tf_op jit(solution)/shard_map/ppermute | solution.py:63
  124.6 3.6 %broadcast.74.clone = f32[7,1024,256]{2,1,0:T(8,128)} broadcast(f32[]{:T(128)} %constant.84.clone.1), dimensions={} | broadcast | bytes 7340036 | tf_op jit(solution)/shard_map/broadcast.1
  128.2 20.1 %while.52 = (s32[]{:T(128)}, f32[7,1024,256]{2,1,0:T(8,128)}, s32[7,1024]{1,0:T(8,128)S(1)}, s32[3072]{0:T(1024)S(1)}, bf16[3072,256]{1,0:T(8,128)(2,1)S(1)}, /*index=5*/s32[]{:T(128)}) while((s32[]{:T(128)}, f32[7,1024,256]{2,1,0:T(8,128)}, s32[7,1024]{1,0:T(8,128)S(1)}, s32[3072]{0:T(1024)S(1)}, bf16[3072,256]{1,0:T(8,128)(2,1)S(1)}, ...), condition=%wide.region_8.9_spmd, body=%wide.region_7.8_spmd.sunk | while | flops 1613758464 | bytes 2646601 | solution.py:22
  131.0 2.9 %fusion.112 = f32[7,1024,256]{2,1,0:T(8,128)} fusion(f32[7,1024,256]{2,1,0:T(8,128)} %get-tuple-element.392, s32[]{:T(128)} %get-tuple-element.391, bf16[3072,256]{1,0:T(8,128)(2,1)S(1)} %get-tuple-element.401, s32[3072]{0:T(1024)S(1)} %get-tuple-element.400, s32[1024]{0:T(1024)S(1)} %bitcast.92), kind=kOutput, calls=%fused_computation.20.clone.1 | convolution fusion | flops 1613758464 | bytes 2638336 | tf_op jit(solution)/shard_map/while/body/eval_jaxpr/dot_general | solution.py:20
  142.5 2.9 %fusion.112 = f32[7,1024,256]{2,1,0:T(8,128)} fusion(f32[7,1024,256]{2,1,0:T(8,128)} %get-tuple-element.392, s32[]{:T(128)} %get-tuple-element.391, bf16[3072,256]{1,0:T(8,128)(2,1)S(1)} %get-tuple-element.401, s32[3072]{0:T(1024)S(1)} %get-tuple-element.400, s32[1024]{0:T(1024)S(1)} %bitcast.92), kind=kOutput, calls=%fused_computation.20.clone.1 | convolution fusion | flops 1613758464 | bytes 2638336 | tf_op jit(solution)/shard_map/while/body/eval_jaxpr/dot_general | solution.py:20
  149.5 8.7 %while.54 = (s32[]{:T(128)}, f32[3,1024,256]{2,1,0:T(8,128)}, s32[3,1024]{1,0:T(4,128)S(1)}, s32[3072]{0:T(1024)S(1)}, bf16[3072,256]{1,0:T(8,128)(2,1)S(1)}, /*index=5*/s32[]{:T(128)}) while((s32[]{:T(128)}, f32[3,1024,256]{2,1,0:T(8,128)}, s32[3,1024]{1,0:T(4,128)S(1)}, s32[3072]{0:T(1024)S(1)}, bf16[3072,256]{1,0:T(8,128)(2,1)S(1)}, ...), condition=%wide.region_13.14_spmd, body=%wide.region_12.13_spmd.sunk | while | flops 1613758464 | bytes 2646601 | solution.py:22
  149.6 2.9 %fusion.118 = f32[3,1024,256]{2,1,0:T(8,128)} fusion(f32[3,1024,256]{2,1,0:T(8,128)} %get-tuple-element.446, s32[]{:T(128)} %get-tuple-element.445, bf16[3072,256]{1,0:T(8,128)(2,1)S(1)} %get-tuple-element.455, s32[3072]{0:T(1024)S(1)} %get-tuple-element.454, s32[1024]{0:T(1024)S(1)} %bitcast.93), kind=kOutput, calls=%fused_computation.34.clone.1 | convolution fusion | flops 1613758464 | bytes 2638336 | tf_op jit(solution)/shard_map/while/body/eval_jaxpr/dot_general | solution.py:20
  158.2 7.9 %multiply_reduce_fusion.1 = (f32[3,1024]{1,0:T(4,128)S(1)}, f32[3,1024,256]{2,1,0:T(8,128)}) fusion(f32[3,1024,256]{2,1,0:T(8,128)} %bitcast.81, f32[3,1024,256]{2,1,0:T(8,128)} %get-tuple-element.145, f32[7,1024,256]{2,1,0:T(8,128)} %get-tuple-element.143, f32[7,1024,256]{2,1,0:T(8,128)} %get-tuple-element.140, f32[7,1024,256]{2,1,0:T(8,128)} %get-tuple-element.139), kind=kLoop, calls=%fused_computation.59 | loop fusion | flops 4715520 | bytes 18886656 | tf_op jit(solution)/shard_map/reduce_sum | solution.py:9
  166.2 4.5 %multiply_convert_fusion.1 = bf16[32,96,256]{2,1,0:T(8,128)(2,1)} fusion(f32[32,96,256]{2,1,0:T(8,128)} %bitcast.82, f32[32,96,256]{2,1,0:T(8,128)} %bitcast.83, f32[32,96]{1,0:T(8,128)S(1)} %rsqrt.30), kind=kLoop, calls=%fused_computation.58 | loop fusion | flops 2359296 | bytes 7876608 | tf_op jit(solution)/shard_map/convert_element_type | solution.py:10
  170.7 12.3 %all-to-all-start.2 = ((bf16[32,96,256]{2,1,0:T(8,128)(2,1)}), bf16[32,96,256]{2,1,0:T(8,128)(2,1)}, u32[]{:S(2)}, u32[]{:S(2)}) async-start(bf16[32,96,256]{2,1,0:T(8,128)(2,1)} %multiply_convert_fusion.1), calls=%async_computation.2 | async-start | bytes 3145728 | tf_op jit(solution)/shard_map/all_to_all | solution.py:97
  183.1 11.6 %while.53 = (s32[]{:T(128)}, f32[4,1024,256]{2,1,0:T(8,128)}, s32[4,1024]{1,0:T(4,128)S(1)}, s32[3072]{0:T(1024)S(1)}, bf16[3072,256]{1,0:T(8,128)(2,1)S(1)}, /*index=5*/s32[]{:T(128)}) while((s32[]{:T(128)}, f32[4,1024,256]{2,1,0:T(8,128)}, s32[4,1024]{1,0:T(4,128)S(1)}, s32[3072]{0:T(1024)S(1)}, bf16[3072,256]{1,0:T(8,128)(2,1)S(1)}, ...), condition=%wide.region_10.11_spmd, body=%wide.region_9.10_spmd.sunk | while | flops 1613758464 | bytes 2646601 | solution.py:22
  183.1 2.9 %fusion.115 = f32[4,1024,256]{2,1,0:T(8,128)} fusion(f32[4,1024,256]{2,1,0:T(8,128)} %get-tuple-element.374, s32[]{:T(128)} %get-tuple-element.373, bf16[3072,256]{1,0:T(8,128)(2,1)S(1)} %get-tuple-element.383, s32[3072]{0:T(1024)S(1)} %get-tuple-element.382, s32[1024]{0:T(1024)S(1)} %bitcast.94), kind=kOutput, calls=%fused_computation.27.clone.1 | convolution fusion | flops 1613758464 | bytes 2638336 | tf_op jit(solution)/shard_map/while/body/eval_jaxpr/dot_general | solution.py:20
  191.7 2.9 %fusion.115 = f32[4,1024,256]{2,1,0:T(8,128)} fusion(f32[4,1024,256]{2,1,0:T(8,128)} %get-tuple-element.374, s32[]{:T(128)} %get-tuple-element.373, bf16[3072,256]{1,0:T(8,128)(2,1)S(1)} %get-tuple-element.383, s32[3072]{0:T(1024)S(1)} %get-tuple-element.382, s32[1024]{0:T(1024)S(1)} %bitcast.94), kind=kOutput, calls=%fused_computation.27.clone.1 | convolution fusion | flops 1613758464 | bytes 2638336 | tf_op jit(solution)/shard_map/while/body/eval_jaxpr/dot_general | solution.py:20
  194.7 6.9 %add_add_fusion = f32[4,1024,256]{2,1,0:T(8,128)S(1)} fusion(f32[4,1024,256]{2,1,0:T(8,128)} %get-tuple-element.144, f32[7,1024,256]{2,1,0:T(8,128)} %get-tuple-element.143, f32[7,1024,256]{2,1,0:T(8,128)} %get-tuple-element.140, f32[7,1024,256]{2,1,0:T(8,128)} %get-tuple-element.139), kind=kLoop, calls=%fused_computation.54 | loop fusion | flops 3145728 | bytes 20971520 | tf_op jit(solution)/shard_map/add | solution.py:99
  204.1 3.0 %multiply_convert_fusion = bf16[4096,256]{1,0:T(8,128)(2,1)} fusion(f32[4,1024,256]{2,1,0:T(8,128)S(1)} %add_add_fusion, f32[4096]{0:T(1024)S(1)} %add_rsqrt_fusion.1, bf16[16384,256]{1,0:T(8,128)(2,1)} %param.19, s32[]{:T(128)S(6)} %select_n.26), kind=kLoop, calls=%fused_computation.52 | loop fusion | flops 4194304 | bytes 8404996 | tf_op jit(solution)/shard_map/convert_element_type | solution.py:10
  207.2 4.4 %fusion.67 = bf16[1024,256]{0,1:T(8,128)(2,1)S(1)} fusion(bf16[3072,256]{1,0:T(8,128)(2,1)} %bitcast.19, s32[1024]{0:T(1024)S(1)} %get-tuple-element.208, f32[1024,256]{0,1:T(8,128)} %get-tuple-element.211, f32[1024]{0:T(1024)S(1)} %add_rsqrt_fusion.2), kind=kOutput, calls=%fused_computation.65 | convolution fusion | flops 1615069184 | bytes 3153920 | tf_op jit(solution)/shard_map/dot_general | solution.py:103
  (114 shorter events, 79.2 us)
Async XLA Ops:
  0.6 12.7 %copy-start = (bf16[1024,1024]{1,0:T(8,128)(2,1)S(1)}, bf16[1024,1024]{1,0:T(8,128)(2,1)}, u32[]{:S(2)}) copy-start(bf16[1024,1024]{1,0:T(8,128)(2,1)} %param.15) | copy-start | bytes 6291460
  4.8 19.4 %all-to-all-start = ((s32[32,96,1]{1,2,0:T(1,128)}), s32[32,96,1]{1,2,0:T(1,128)S(1)}, u32[]{:S(2)}, u32[]{:S(2)}) async-start(s32[32,96,1]{1,2,0:T(1,128)} %all_to_all.24), calls=%async_computation | async-start | bytes 32768 | tf_op jit(solution)/shard_map/all_to_all | solution.py:58
  24.2 36.6 %all-to-all-start.1 = ((bf16[32,96,256]{2,1,0:T(8,128)(2,1)}), bf16[32,96,256]{2,1,0:T(8,128)(2,1)S(1)}, u32[]{:S(2)}, u32[]{:S(2)}) async-start(bf16[32,96,256]{2,1,0:T(8,128)(2,1)} %bitcast.85), calls=%async_computation.1 | async-start | bytes 3145728 | tf_op jit(solution)/shard_map/all_to_all | solution.py:57
  31.7 25.3 %collective-permute-start = (s32[1536]{0:T(1024)S(1)}, s32[1536]{0:T(1024)S(1)}, u32[]{:S(2)}, u32[]{:S(2)}) collective-permute-start(s32[1536]{0:T(1024)S(1)} %slice.50), channel_id=1, source_target_pairs={{0,1},{1,2},{2,3},{3,0},{4,5},{5,6},{6,7},{7,4},{8,9},{9,10},{10,1... | collective-permute-start | bytes 18440 | tf_op jit(solution)/shard_map/ppermute | solution.py:63
  33.4 23.7 %collective-permute-start.1 = (s32[1536]{0:T(1024)S(1)}, s32[1536]{0:T(1024)S(1)}, u32[]{:S(2)}, u32[]{:S(2)}) collective-permute-start(s32[1536]{0:T(1024)S(1)} %slice.50), channel_id=1, source_target_pairs={{0,3},{1,0},{2,1},{3,2},{4,7},{5,4},{6,5},{7,6},{8,11},{9,8},{10,9... | collective-permute-start | bytes 18440 | tf_op jit(solution)/shard_map/ppermute | solution.py:63
  57.1 3.7 %collective-permute-start.8 = (s32[1536]{0:T(1024)S(1)}, s32[1536]{0:T(1024)S(1)}, u32[]{:S(2)}, u32[]{:S(2)}) collective-permute-start(s32[1536]{0:T(1024)S(1)} %collective-permute-done), channel_id=1, source_target_pairs={{0,1},{1,2},{2,3},{3,0},{4,5},{5,6},{6,7},{7,4},{8,9},{9,10},{10,1... | collective-permute-start | bytes 18440 | tf_op jit(solution)/shard_map/ppermute | solution.py:63
  62.0 26.3 %collective-permute-start.2 = (bf16[1536,256]{1,0:T(8,128)(2,1)}, bf16[1536,256]{1,0:T(8,128)(2,1)S(1)}, u32[]{:S(2)}, u32[]{:S(2)}) collective-permute-start(bf16[1536,256]{1,0:T(8,128)(2,1)} %bitcast.12), channel_id=1, source_target_pairs={{0,1},{1,2},{2,3},{3,0},{4,5},{5,6},{6,7},{7,4},{8,9},{9,10},{10,1... | collective-permute-start | bytes 2359304 | tf_op jit(solution)/shard_map/ppermute | solution.py:63
  62.1 26.3 %collective-permute-start.3 = (bf16[1536,256]{1,0:T(8,128)(2,1)}, bf16[1536,256]{1,0:T(8,128)(2,1)}, u32[]{:S(2)}, u32[]{:S(2)}) collective-permute-start(bf16[1536,256]{1,0:T(8,128)(2,1)} %bitcast.12), channel_id=1, source_target_pairs={{0,3},{1,0},{2,1},{3,2},{4,7},{5,4},{6,5},{7,6},{8,11},{9,8},{10,9... | collective-permute-start | bytes 2359304 | tf_op jit(solution)/shard_map/ppermute | solution.py:63
  88.4 7.9 %copy-start.2 = (bf16[1536,256]{1,0:T(8,128)(2,1)}, bf16[1536,256]{1,0:T(8,128)(2,1)S(1)}, u32[]{:S(2)}) copy-start(bf16[1536,256]{1,0:T(8,128)(2,1)S(1)} %collective-permute-done.2) | copy-start | bytes 2359300
  88.4 31.6 %collective-permute-start.7 = (bf16[1536,256]{1,0:T(8,128)(2,1)}, bf16[1536,256]{1,0:T(8,128)(2,1)}, u32[]{:S(2)}, u32[]{:S(2)}) collective-permute-start(bf16[1536,256]{1,0:T(8,128)(2,1)} %bitcast.86), channel_id=1, source_target_pairs={{0,3},{1,0},{2,1},{3,2},{4,7},{5,4},{6,5},{7,6},{8,11},{9,8},{10,9... | collective-permute-start | bytes 2359304 | tf_op jit(solution)/shard_map/ppermute | solution.py:63
  88.4 34.7 %collective-permute-start.6 = (bf16[1536,256]{1,0:T(8,128)(2,1)}, bf16[1536,256]{1,0:T(8,128)(2,1)}, u32[]{:S(2)}, u32[]{:S(2)}) collective-permute-start(bf16[1536,256]{1,0:T(8,128)(2,1)} %bitcast.87), channel_id=1, source_target_pairs={{0,1},{1,2},{2,3},{3,0},{4,5},{5,6},{6,7},{7,4},{8,9},{9,10},{10,1... | collective-permute-start | bytes 2359304 | tf_op jit(solution)/shard_map/ppermute | solution.py:63
  89.9 26.5 %collective-permute-start.5 = (s32[1536]{0:T(1024)S(1)}, s32[1536]{0:T(1024)S(1)}, u32[]{:S(2)}, u32[]{:S(2)}) collective-permute-start(s32[1536]{0:T(1024)S(1)} %slice.57), channel_id=1, source_target_pairs={{0,3},{1,0},{2,1},{3,2},{4,7},{5,4},{6,5},{7,6},{8,11},{9,8},{10,9... | collective-permute-start | bytes 18440 | tf_op jit(solution)/shard_map/ppermute | solution.py:63
  91.2 27.9 %collective-permute-start.4 = (s32[1536]{0:T(1024)S(1)}, s32[1536]{0:T(1024)S(1)}, u32[]{:S(2)}, u32[]{:S(2)}) collective-permute-start(s32[1536]{0:T(1024)S(1)} %slice.57), channel_id=1, source_target_pairs={{0,1},{1,2},{2,3},{3,0},{4,5},{5,6},{6,7},{7,4},{8,9},{9,10},{10,1... | collective-permute-start | bytes 18440 | tf_op jit(solution)/shard_map/ppermute | solution.py:63
  116.4 31.8 %collective-permute-start.10 = (bf16[1536,256]{1,0:T(8,128)(2,1)}, bf16[1536,256]{1,0:T(8,128)(2,1)S(1)}, u32[]{:S(2)}, u32[]{:S(2)}) collective-permute-start(bf16[1536,256]{1,0:T(8,128)(2,1)} %copy-done.2), channel_id=1, source_target_pairs={{0,1},{1,2},{2,3},{3,0},{4,5},{5,6},{6,7},{7,4},{8,9},{9,10},{10,1... | collective-permute-start | bytes 2359304 | tf_op jit(solution)/shard_map/ppermute | solution.py:63
  116.4 3.5 %collective-permute-start.9 = (s32[1536]{0:T(1024)S(1)}, s32[1536]{0:T(1024)S(1)}, u32[]{:S(2)}, u32[]{:S(2)}) collective-permute-start(s32[1536]{0:T(1024)S(1)} %collective-permute-done.5), channel_id=1, source_target_pairs={{0,3},{1,0},{2,1},{3,2},{4,7},{5,4},{6,5},{7,6},{8,11},{9,8},{10,9... | collective-permute-start | bytes 18440 | tf_op jit(solution)/shard_map/ppermute | solution.py:63
  119.9 28.4 %collective-permute-start.11 = (bf16[1536,256]{1,0:T(8,128)(2,1)}, bf16[1536,256]{1,0:T(8,128)(2,1)}, u32[]{:S(2)}, u32[]{:S(2)}) collective-permute-start(bf16[1536,256]{1,0:T(8,128)(2,1)} %collective-permute-done.7), channel_id=1, source_target_pairs={{0,3},{1,0},{2,1},{3,2},{4,7},{5,4},{6,5},{7,6},{8,11},{9,8},{10,9... | collective-permute-start | bytes 2359304 | tf_op jit(solution)/shard_map/ppermute | solution.py:63
  170.7 36.4 %all-to-all-start.2 = ((bf16[32,96,256]{2,1,0:T(8,128)(2,1)}), bf16[32,96,256]{2,1,0:T(8,128)(2,1)}, u32[]{:S(2)}, u32[]{:S(2)}) async-start(bf16[32,96,256]{2,1,0:T(8,128)(2,1)} %multiply_convert_fusion.1), calls=%async_computation.2 | async-start | bytes 3145728 | tf_op jit(solution)/shard_map/all_to_all | solution.py:97
  207.2 5.4 %copy-start.1 = (bf16[1024,1024]{1,0:T(8,128)(2,1)S(1)}, bf16[1024,1024]{1,0:T(8,128)(2,1)}, u32[]{:S(2)}) copy-start(bf16[1024,1024]{1,0:T(8,128)(2,1)} %param.15) | copy-start | bytes 6291460

commit v8 on v7

--- a/solution.py
+++ b/solution.py
@@ -10,14 +10,14 @@
     ).astype(jnp.bfloat16)
 
 
-def match_sums(queries, keys, rows, block_rows=1024):
+def match_sums(queries, keys, rows, held=jnp.float32, block_rows=1024):
     count = queries.shape[0]
     padded = -(-count // block_rows) * block_rows
     blocks = jnp.pad(queries, (0, padded - count), constant_values=-1).reshape(-1, block_rows)
 
     def one_block(block_ids):
         selector = (block_ids[:, None] == keys[None, :]).astype(jnp.bfloat16)
-        return jnp.dot(selector, rows, preferred_element_type=jnp.float32)
+        return jnp.dot(selector, rows, preferred_element_type=jnp.float32).astype(held)
 
     return lax.map(one_block, blocks).reshape(padded, -1)[:count]
 
@@ -88,9 +88,9 @@
     own_cent = lax.dynamic_slice_in_dim(centroids, first_row, share_rows, 0)
 
     queries = jnp.concatenate([in_ids, share_ids])
-    own_sums = match_sums(queries, in_ids, incoming)
-    sums_a = match_sums(queries, keys_a, near_a)
-    sums_b = match_sums(queries, keys_b, near_b)
+    own_sums = match_sums(queries, in_ids, incoming, jnp.bfloat16).astype(jnp.float32)
+    sums_a = match_sums(queries, keys_a, near_a, jnp.bfloat16).astype(jnp.float32)
+    sums_b = match_sums(queries, keys_b, near_b, jnp.bfloat16).astype(jnp.float32)
     look_sum = (own_sums[:slots] + sums_a[:slots] + sums_b[:slots]
                 + match_sums(in_ids, keys_far, far))
     picked = normalize(look_cent.astype(jnp.float32) + look_sum)

time: 213 us -> 251 us (1.18)
  matrix products: 96 us -> 126 us
  other arithmetic: 34.6 us -> 45.8 us
  local copies, waits for them, and re-layouts: 32.8 us -> 28.4 us
    dot_general x28, matrix products: 80.2 us -> 110 us  [one_block(): jnp.dot(selector, rows, preferred_element_type=jnp.float32).astype(held)]
    convert_element_type x1 -> x3, other arithmetic: 3.3 us -> 17.1 us  [the longest x1 5.73 us: body(): match_sums(queries, keys_a, near_a, jnp.bfloat16).astype(jnp.float32)]
    reduce_sum x2, other arithmetic: 10.4 us -> 2.98 us  [normalize(): jnp.mean(updated * updated, axis=-1, keepdims=True) + 1e-06]
    add x0 -> x1, other arithmetic: none -> 5.46 us  [body(): own_sums[:slots] + sums_a[:slots] + sums_b[:slots]]
    another operation x3, local copies, waits for them, and re-layouts: 10.8 us -> 6.28 us
    convert_element_type x2, other arithmetic: 7.57 us -> 4.68 us  [normalize(): return (updated * lax.rsqrt(jnp.mean(updated * updated, axis=-1, keepdims...]
  transfers between devices with their start and end apart: 15 -> 15, of which waited for: 2 -> 2; matrix products, arithmetic and copies ran while one was open for 61% -> 66% of each run, Pallas kernels for 0% -> 0%
where the time goes in v8:
time: 251 us; the launch traced here: 250 us
  matrix products  126 us (50%)
  other arithmetic  45.8 us (18%)
  starting transfers between devices  43.9 us (17%)
  local copies, waits for them, and re-layouts  28.4 us (11%)
  waiting for transfers between devices  4.49 us (2%)
    dot_general x28, matrix products, one_block(): jnp.dot(selector, rows, preferred_element_type=jnp.float32).astype(held)  110 us
    ppermute x12, starting transfers between devices, shift(): lax.ppermute(x, 'rep', [(i, (i + step) % replicas) for i in range(replica...  16.8 us
    gather x1, local copies, waits for them, and re-layouts, body(): look_cent = centroids[in_ids]  14.3 us
    all_to_all x1, starting transfers between devices, body(): lax.all_to_all(picked, 'wide', split_axis=0, concat_axis=0, tiled=True)  11.1 us
    all_to_all x1, starting transfers between devices, body(): lax.all_to_all(out_ids, 'wide', split_axis=0, concat_axis=0, tiled=True)  8.57 us
    all_to_all x1, starting transfers between devices, body(): lax.all_to_all(outgoing, 'wide', split_axis=0, concat_axis=0, tiled=True)  7.43 us
    add x1, other arithmetic, body(): own_sums[slots:] + sums_a[slots:] + sums_b[slots:]  6.93 us
    another operation x3, local copies, waits for them, and re-layouts  6.28 us
  transfers between devices with their start and end apart: 15, of which 2 were waited for; matrix products, arithmetic and copies ran while one was open for 66% of the time, Pallas kernels for 0%

profile of v8, /device:TPU:1, one launch (start us, length us, event | category | flops | bytes accessed | tf_op | source)
XLA Modules:
  0.0 249.6 jit_solution(16778313664344212406)
XLA Ops:
  4.8 8.6 %all-to-all-start = ((s32[32,96,1]{1,2,0:T(1,128)}), s32[32,96,1]{1,2,0:T(1,128)S(1)}, u32[]{:S(2)}, u32[]{:S(2)}) async-start(s32[32,96,1]{1,2,0:T(1,128)} %all_to_all.26), calls=%async_computation | async-start | bytes 32768 | tf_op jit(solution)/shard_map/all_to_all | solution.py:58
  13.4 6.0 %multiply_reduce_fusion.2 = (f32[1024]{0:T(1024)S(1)}, f32[1024,256]{0,1:T(8,128)}) fusion(bf16[1024,256]{1,0:T(8,128)(2,1)} %param.18, bf16[1024,1024]{1,0:T(8,128)(2,1)S(1)} %copy-done, bf16[1024,1024]{1,0:T(8,128)(2,1)} %param.17), kind=kOutput, calls=%fused_computation.77 | convolution fusion | flops 2694315008 | bytes 5771264 | tf_op jit(solution)/shard_map/dot_general | solution.py:50
  19.4 4.8 %fusion.73 = bf16[3072,256]{1,0:T(8,128)(2,1)} fusion(s32[1024]{0:T(1024)S(1)} %get-tuple-element.206, f32[1024,256]{0,1:T(8,128)} %get-tuple-element.209, f32[1024]{0:T(1024)S(1)} %add_rsqrt_fusion.2), kind=kOutput, calls=%fused_computation.62 | convolution fusion | flops 1615069184 | bytes 2629632 | tf_op jit(solution)/shard_map/dot_general | solution.py:55
  24.2 7.4 %all-to-all-start.1 = ((bf16[32,96,256]{2,1,0:T(8,128)(2,1)}), bf16[32,96,256]{2,1,0:T(8,128)(2,1)}, u32[]{:S(2)}, u32[]{:S(2)}) async-start(bf16[32,96,256]{2,1,0:T(8,128)(2,1)} %bitcast.10), calls=%async_computation.1 | async-start | bytes 3145728 | tf_op jit(solution)/shard_map/all_to_all | solution.py:57
  37.2 14.3 %gather_fusion = bf16[3072,256]{1,0:T(8,128)(2,1)S(1)} fusion(bf16[16384,256]{1,0:T(8,128)(2,1)} %param.19, s32[3072]{0:T(1024)S(1)} %broadcast_clamp_fusion), kind=kCustom, calls=%fused_computation | custom fusion | bytes 3158016 | tf_op jit(solution)/shard_map/gather | solution.py:87
  62.9 28.8 %while.50 = (s32[]{:T(128)}, bf16[7,1024,256]{2,1,0:T(8,128)(2,1)}, s32[7,1024]{1,0:T(8,128)S(1)}, s32[3072]{0:T(1024)S(1)}, bf16[3072,256]{1,0:T(8,128)(2,1)}, /*index=5*/s32[]{:T(128)}) while((s32[]{:T(128)}, bf16[7,1024,256]{2,1,0:T(8,128)(2,1)}, s32[7,1024]{1,0:T(8,128)S(1)}, s32[3072]{0:T(1024)S(1)}, bf16[3072,256]{1,0:T(8,128)(2,1)}, ...), condition=%wide.region_4.5_spmd, body=%wide.region_3.4_spmd.sunk | while | flops 1614020608 | bytes 2122313 | solution.py:22
  67.0 4.1 %fusion.117 = bf16[7,1024,256]{2,1,0:T(8,128)(2,1)} fusion(bf16[7,1024,256]{2,1,0:T(8,128)(2,1)} %get-tuple-element.426, s32[]{:T(128)} %get-tuple-element.425, bf16[3072,256]{1,0:T(8,128)(2,1)} %get-tuple-element.435, s32[3072]{0:T(1024)S(1)} %get-tuple-element.434, s32[1024]{0:T(1024)S(1)} %bitcast.88), kind=kOutput, calls=%fused_computation.7.clone.1 | convolution fusion | flops 1614020608 | bytes 2114048 | tf_op jit(solution)/shard_map/while/body/eval_jaxpr/dot_general | solution.py:20
  71.2 4.1 %fusion.117 = bf16[7,1024,256]{2,1,0:T(8,128)(2,1)} fusion(bf16[7,1024,256]{2,1,0:T(8,128)(2,1)} %get-tuple-element.426, s32[]{:T(128)} %get-tuple-element.425, bf16[3072,256]{1,0:T(8,128)(2,1)} %get-tuple-element.435, s32[3072]{0:T(1024)S(1)} %get-tuple-element.434, s32[1024]{0:T(1024)S(1)} %bitcast.88), kind=kOutput, calls=%fused_computation.7.clone.1 | convolution fusion | flops 1614020608 | bytes 2114048 | tf_op jit(solution)/shard_map/while/body/eval_jaxpr/dot_general | solution.py:20
  75.3 4.1 %fusion.117 = bf16[7,1024,256]{2,1,0:T(8,128)(2,1)} fusion(bf16[7,1024,256]{2,1,0:T(8,128)(2,1)} %get-tuple-element.426, s32[]{:T(128)} %get-tuple-element.425, bf16[3072,256]{1,0:T(8,128)(2,1)} %get-tuple-element.435, s32[3072]{0:T(1024)S(1)} %get-tuple-element.434, s32[1024]{0:T(1024)S(1)} %bitcast.88), kind=kOutput, calls=%fused_computation.7.clone.1 | convolution fusion | flops 1614020608 | bytes 2114048 | tf_op jit(solution)/shard_map/while/body/eval_jaxpr/dot_general | solution.py:20
  87.6 4.1 %fusion.117 = bf16[7,1024,256]{2,1,0:T(8,128)(2,1)} fusion(bf16[7,1024,256]{2,1,0:T(8,128)(2,1)} %get-tuple-element.426, s32[]{:T(128)} %get-tuple-element.425, bf16[3072,256]{1,0:T(8,128)(2,1)} %get-tuple-element.435, s32[3072]{0:T(1024)S(1)} %get-tuple-element.434, s32[1024]{0:T(1024)S(1)} %bitcast.88), kind=kOutput, calls=%fused_computation.7.clone.1 | convolution fusion | flops 1614020608 | bytes 2114048 | tf_op jit(solution)/shard_map/while/body/eval_jaxpr/dot_general | solution.py:20
  91.7 5.7 %convert_element_type.64 = f32[7,1024,256]{2,1,0:T(8,128)} convert(bf16[7,1024,256]{2,1,0:T(8,128)(2,1)} %get-tuple-element.139) | non-fusion elementwise | flops 1835008 | bytes 11010048 | tf_op jit(solution)/shard_map/convert_element_type | solution.py:91
  105.9 28.7 %while.51 = (s32[]{:T(128)}, bf16[7,1024,256]{2,1,0:T(8,128)(2,1)}, s32[7,1024]{1,0:T(8,128)S(1)}, s32[3072]{0:T(1024)S(1)}, bf16[3072,256]{1,0:T(8,128)(2,1)}, /*index=5*/s32[]{:T(128)}) while((s32[]{:T(128)}, bf16[7,1024,256]{2,1,0:T(8,128)(2,1)}, s32[7,1024]{1,0:T(8,128)S(1)}, s32[3072]{0:T(1024)S(1)}, bf16[3072,256]{1,0:T(8,128)(2,1)}, ...), condition=%wide.region_6.7_spmd, body=%wide.region_5.6_spmd.sunk | while | flops 1614020608 | bytes 2122313 | solution.py:22
  105.9 4.1 %fusion.120 = bf16[7,1024,256]{2,1,0:T(8,128)(2,1)} fusion(bf16[7,1024,256]{2,1,0:T(8,128)(2,1)} %get-tuple-element.408, s32[]{:T(128)} %get-tuple-element.407, bf16[3072,256]{1,0:T(8,128)(2,1)} %get-tuple-element.417, s32[3072]{0:T(1024)S(1)} %get-tuple-element.416, s32[1024]{0:T(1024)S(1)} %bitcast.89), kind=kOutput, calls=%fused_computation.15.clone.1 | convolution fusion | flops 1614020608 | bytes 2114048 | tf_op jit(solution)/shard_map/while/body/eval_jaxpr/dot_general | solution.py:20
  110.1 4.1 %fusion.120 = bf16[7,1024,256]{2,1,0:T(8,128)(2,1)} fusion(bf16[7,1024,256]{2,1,0:T(8,128)(2,1)} %get-tuple-element.408, s32[]{:T(128)} %get-tuple-element.407, bf16[3072,256]{1,0:T(8,128)(2,1)} %get-tuple-element.417, s32[3072]{0:T(1024)S(1)} %get-tuple-element.416, s32[1024]{0:T(1024)S(1)} %bitcast.89), kind=kOutput, calls=%fused_computation.15.clone.1 | convolution fusion | flops 1614020608 | bytes 2114048 | tf_op jit(solution)/shard_map/while/body/eval_jaxpr/dot_general | solution.py:20
  118.2 4.1 %fusion.120 = bf16[7,1024,256]{2,1,0:T(8,128)(2,1)} fusion(bf16[7,1024,256]{2,1,0:T(8,128)(2,1)} %get-tuple-element.408, s32[]{:T(128)} %get-tuple-element.407, bf16[3072,256]{1,0:T(8,128)(2,1)} %get-tuple-element.417, s32[3072]{0:T(1024)S(1)} %get-tuple-element.416, s32[1024]{0:T(1024)S(1)} %bitcast.89), kind=kOutput, calls=%fused_computation.15.clone.1 | convolution fusion | flops 1614020608 | bytes 2114048 | tf_op jit(solution)/shard_map/while/body/eval_jaxpr/dot_general | solution.py:20
  122.4 4.1 %fusion.120 = bf16[7,1024,256]{2,1,0:T(8,128)(2,1)} fusion(bf16[7,1024,256]{2,1,0:T(8,128)(2,1)} %get-tuple-element.408, s32[]{:T(128)} %get-tuple-element.407, bf16[3072,256]{1,0:T(8,128)(2,1)} %get-tuple-element.417, s32[3072]{0:T(1024)S(1)} %get-tuple-element.416, s32[1024]{0:T(1024)S(1)} %bitcast.89), kind=kOutput, calls=%fused_computation.15.clone.1 | convolution fusion | flops 1614020608 | bytes 2114048 | tf_op jit(solution)/shard_map/while/body/eval_jaxpr/dot_general | solution.py:20
  130.5 4.1 %fusion.120 = bf16[7,1024,256]{2,1,0:T(8,128)(2,1)} fusion(bf16[7,1024,256]{2,1,0:T(8,128)(2,1)} %get-tuple-element.408, s32[]{:T(128)} %get-tuple-element.407, bf16[3072,256]{1,0:T(8,128)(2,1)} %get-tuple-element.417, s32[3072]{0:T(1024)S(1)} %get-tuple-element.416, s32[1024]{0:T(1024)S(1)} %bitcast.89), kind=kOutput, calls=%fused_computation.15.clone.1 | convolution fusion | flops 1614020608 | bytes 2114048 | tf_op jit(solution)/shard_map/while/body/eval_jaxpr/dot_general | solution.py:20
  134.6 5.7 %convert_element_type.65 = f32[7,1024,256]{2,1,0:T(8,128)} convert(bf16[7,1024,256]{2,1,0:T(8,128)(2,1)} %get-tuple-element.140) | non-fusion elementwise | flops 1835008 | bytes 11010048 | tf_op jit(solution)/shard_map/convert_element_type | solution.py:92
  151.8 28.7 %while.52 = (s32[]{:T(128)}, bf16[7,1024,256]{2,1,0:T(8,128)(2,1)}, s32[7,1024]{1,0:T(8,128)S(1)}, s32[3072]{0:T(1024)S(1)}, bf16[3072,256]{1,0:T(8,128)(2,1)}, /*index=5*/s32[]{:T(128)}) while((s32[]{:T(128)}, bf16[7,1024,256]{2,1,0:T(8,128)(2,1)}, s32[7,1024]{1,0:T(8,128)S(1)}, s32[3072]{0:T(1024)S(1)}, bf16[3072,256]{1,0:T(8,128)(2,1)}, ...), condition=%wide.region_8.9_spmd, body=%wide.region_7.8_spmd.sunk | while | flops 1614020608 | bytes 2122313 | solution.py:22
  159.9 4.1 %fusion.123 = bf16[7,1024,256]{2,1,0:T(8,128)(2,1)} fusion(bf16[7,1024,256]{2,1,0:T(8,128)(2,1)} %get-tuple-element.390, s32[]{:T(128)} %get-tuple-element.389, bf16[3072,256]{1,0:T(8,128)(2,1)} %get-tuple-element.399, s32[3072]{0:T(1024)S(1)} %get-tuple-element.398, s32[1024]{0:T(1024)S(1)} %bitcast.90), kind=kOutput, calls=%fused_computation.23.clone.1 | convolution fusion | flops 1614020608 | bytes 2114048 | tf_op jit(solution)/shard_map/while/body/eval_jaxpr/dot_general | solution.py:20
  172.3 4.1 %fusion.123 = bf16[7,1024,256]{2,1,0:T(8,128)(2,1)} fusion(bf16[7,1024,256]{2,1,0:T(8,128)(2,1)} %get-tuple-element.390, s32[]{:T(128)} %get-tuple-element.389, bf16[3072,256]{1,0:T(8,128)(2,1)} %get-tuple-element.399, s32[3072]{0:T(1024)S(1)} %get-tuple-element.398, s32[1024]{0:T(1024)S(1)} %bitcast.90), kind=kOutput, calls=%fused_computation.23.clone.1 | convolution fusion | flops 1614020608 | bytes 2114048 | tf_op jit(solution)/shard_map/while/body/eval_jaxpr/dot_general | solution.py:20
  176.4 4.1 %fusion.123 = bf16[7,1024,256]{2,1,0:T(8,128)(2,1)} fusion(bf16[7,1024,256]{2,1,0:T(8,128)(2,1)} %get-tuple-element.390, s32[]{:T(128)} %get-tuple-element.389, bf16[3072,256]{1,0:T(8,128)(2,1)} %get-tuple-element.399, s32[3072]{0:T(1024)S(1)} %get-tuple-element.398, s32[1024]{0:T(1024)S(1)} %bitcast.90), kind=kOutput, calls=%fused_computation.23.clone.1 | convolution fusion | flops 1614020608 | bytes 2114048 | tf_op jit(solution)/shard_map/while/body/eval_jaxpr/dot_general | solution.py:20
  180.5 5.7 %convert_element_type.66 = f32[7,1024,256]{2,1,0:T(8,128)} convert(bf16[7,1024,256]{2,1,0:T(8,128)(2,1)} %get-tuple-element.143) | non-fusion elementwise | flops 1835008 | bytes 11010048 | tf_op jit(solution)/shard_map/convert_element_type | solution.py:93
  188.5 12.8 %while.54 = (s32[]{:T(128)}, f32[3,1024,256]{2,1,0:T(8,128)}, s32[3,1024]{1,0:T(4,128)S(1)}, s32[3072]{0:T(1024)S(1)}, bf16[3072,256]{1,0:T(8,128)(2,1)}, /*index=5*/s32[]{:T(128)}) while((s32[]{:T(128)}, f32[3,1024,256]{2,1,0:T(8,128)}, s32[3,1024]{1,0:T(4,128)S(1)}, s32[3072]{0:T(1024)S(1)}, bf16[3072,256]{1,0:T(8,128)(2,1)}, ...), condition=%wide.region_13.14_spmd, body=%wide.region_12.13_spmd.sunk | while | flops 1613758464 | bytes 2646601 | solution.py:22
  188.6 4.2 %fusion.129 = f32[3,1024,256]{2,1,0:T(8,128)} fusion(f32[3,1024,256]{2,1,0:T(8,128)} %get-tuple-element.444, s32[]{:T(128)} %get-tuple-element.443, bf16[3072,256]{1,0:T(8,128)(2,1)} %get-tuple-element.453, s32[3072]{0:T(1024)S(1)} %get-tuple-element.452, s32[1024]{0:T(1024)S(1)} %bitcast.91), kind=kOutput, calls=%fused_computation.37.clone.1 | convolution fusion | flops 1613758464 | bytes 2638336 | tf_op jit(solution)/shard_map/while/body/eval_jaxpr/dot_general | solution.py:20
  192.8 4.3 %fusion.129 = f32[3,1024,256]{2,1,0:T(8,128)} fusion(f32[3,1024,256]{2,1,0:T(8,128)} %get-tuple-element.444, s32[]{:T(128)} %get-tuple-element.443, bf16[3072,256]{1,0:T(8,128)(2,1)} %get-tuple-element.453, s32[3072]{0:T(1024)S(1)} %get-tuple-element.452, s32[1024]{0:T(1024)S(1)} %bitcast.91), kind=kOutput, calls=%fused_computation.37.clone.1 | convolution fusion | flops 1613758464 | bytes 2638336 | tf_op jit(solution)/shard_map/while/body/eval_jaxpr/dot_general | solution.py:20
  197.1 4.2 %fusion.129 = f32[3,1024,256]{2,1,0:T(8,128)} fusion(f32[3,1024,256]{2,1,0:T(8,128)} %get-tuple-element.444, s32[]{:T(128)} %get-tuple-element.443, bf16[3072,256]{1,0:T(8,128)(2,1)} %get-tuple-element.453, s32[3072]{0:T(1024)S(1)} %get-tuple-element.452, s32[1024]{0:T(1024)S(1)} %bitcast.91), kind=kOutput, calls=%fused_computation.37.clone.1 | convolution fusion | flops 1613758464 | bytes 2638336 | tf_op jit(solution)/shard_map/while/body/eval_jaxpr/dot_general | solution.py:20
  201.3 5.5 %fusion.74 = f32[3,1024,256]{2,1,0:T(8,128)S(1)} fusion(f32[3,1024,256]{2,1,0:T(8,128)} %get-tuple-element.145, f32[7,1024,256]{2,1,0:T(8,128)} %convert_element_type.66, f32[7,1024,256]{2,1,0:T(8,128)} %convert_element_type.65, f32[7,1024,256]{2,1,0:T(8,128)} %convert_element_type.64), kind=kLoop, calls=%fused_computation.64 | loop fusion | flops 2359296 | bytes 15728640 | tf_op jit(solution)/shard_map/add | solution.py:94
  208.9 11.1 %all-to-all-start.2 = ((bf16[32,96,256]{2,1,0:T(8,128)(2,1)}), bf16[32,96,256]{2,1,0:T(8,128)(2,1)}, u32[]{:S(2)}, u32[]{:S(2)}) async-start(bf16[32,96,256]{2,1,0:T(8,128)(2,1)} %bitcast.85), calls=%async_computation.2 | async-start | bytes 3145728 | tf_op jit(solution)/shard_map/all_to_all | solution.py:97
  220.1 11.6 %while.53 = (s32[]{:T(128)}, f32[4,1024,256]{2,1,0:T(8,128)}, s32[4,1024]{1,0:T(4,128)S(1)}, s32[3072]{0:T(1024)S(1)}, bf16[3072,256]{1,0:T(8,128)(2,1)S(1)}, /*index=5*/s32[]{:T(128)}) while((s32[]{:T(128)}, f32[4,1024,256]{2,1,0:T(8,128)}, s32[4,1024]{1,0:T(4,128)S(1)}, s32[3072]{0:T(1024)S(1)}, bf16[3072,256]{1,0:T(8,128)(2,1)S(1)}, ...), condition=%wide.region_10.11_spmd, body=%wide.region_9.10_spmd.sunk | while | flops 1613758464 | bytes 2646601 | solution.py:22
  231.6 6.9 %fusion.71 = f32[4,1024,256]{2,1,0:T(8,128)S(1)} fusion(f32[4,1024,256]{2,1,0:T(8,128)} %get-tuple-element.144, f32[7,1024,256]{2,1,0:T(8,128)} %convert_element_type.66, f32[7,1024,256]{2,1,0:T(8,128)} %convert_element_type.65, f32[7,1024,256]{2,1,0:T(8,128)} %convert_element_type.64), kind=kLoop, calls=%fused_computation.55 | loop fusion | flops 3145728 | bytes 20971520 | tf_op jit(solution)/shard_map/add | solution.py:99
  244.1 4.4 %fusion.78 = bf16[1024,256]{0,1:T(8,128)(2,1)S(1)} fusion(bf16[3072,256]{1,0:T(8,128)(2,1)} %bitcast.18, s32[1024]{0:T(1024)S(1)} %get-tuple-element.206, f32[1024,256]{0,1:T(8,128)} %get-tuple-element.209, f32[1024]{0:T(1024)S(1)} %add_rsqrt_fusion.2), kind=kOutput, calls=%fused_computation.73 | convolution fusion | flops 1615069184 | bytes 3153920 | tf_op jit(solution)/shard_map/dot_general | solution.py:103
  (118 shorter events, 100.5 us)
Async XLA Ops:
  0.6 12.7 %copy-start = (bf16[1024,1024]{1,0:T(8,128)(2,1)S(1)}, bf16[1024,1024]{1,0:T(8,128)(2,1)}, u32[]{:S(2)}) copy-start(bf16[1024,1024]{1,0:T(8,128)(2,1)} %param.15) | copy-start | bytes 6291460
  4.8 19.4 %all-to-all-start = ((s32[32,96,1]{1,2,0:T(1,128)}), s32[32,96,1]{1,2,0:T(1,128)S(1)}, u32[]{:S(2)}, u32[]{:S(2)}) async-start(s32[32,96,1]{1,2,0:T(1,128)} %all_to_all.26), calls=%async_computation | async-start | bytes 32768 | tf_op jit(solution)/shard_map/all_to_all | solution.py:58
  24.2 31.1 %all-to-all-start.1 = ((bf16[32,96,256]{2,1,0:T(8,128)(2,1)}), bf16[32,96,256]{2,1,0:T(8,128)(2,1)}, u32[]{:S(2)}, u32[]{:S(2)}) async-start(bf16[32,96,256]{2,1,0:T(8,128)(2,1)} %bitcast.10), calls=%async_computation.1 | async-start | bytes 3145728 | tf_op jit(solution)/shard_map/all_to_all | solution.py:57
  31.8 19.7 %collective-permute-start = (s32[1536]{0:T(1024)S(1)}, s32[1536]{0:T(1024)S(1)}, u32[]{:S(2)}, u32[]{:S(2)}) collective-permute-start(s32[1536]{0:T(1024)S(1)} %slice.50), channel_id=1, source_target_pairs={{0,1},{1,2},{2,3},{3,0},{4,5},{5,6},{6,7},{7,4},{8,9},{9,10},{10,1... | collective-permute-start | bytes 18440 | tf_op jit(solution)/shard_map/ppermute | solution.py:63
  33.5 18.2 %collective-permute-start.1 = (s32[1536]{0:T(1024)S(1)}, s32[1536]{0:T(1024)S(1)}, u32[]{:S(2)}, u32[]{:S(2)}) collective-permute-start(s32[1536]{0:T(1024)S(1)} %slice.50), channel_id=1, source_target_pairs={{0,3},{1,0},{2,1},{3,2},{4,7},{5,4},{6,5},{7,6},{8,11},{9,8},{10,9... | collective-permute-start | bytes 18440 | tf_op jit(solution)/shard_map/ppermute | solution.py:63
  51.5 3.8 %collective-permute-start.8 = (s32[1536]{0:T(1024)S(1)}, s32[1536]{0:T(1024)S(1)}, u32[]{:S(2)}, u32[]{:S(2)}) collective-permute-start(s32[1536]{0:T(1024)S(1)} %collective-permute-done), channel_id=1, source_target_pairs={{0,1},{1,2},{2,3},{3,0},{4,5},{5,6},{6,7},{7,4},{8,9},{9,10},{10,1... | collective-permute-start | bytes 18440 | tf_op jit(solution)/shard_map/ppermute | solution.py:63
  58.0 39.4 %collective-permute-start.2 = (bf16[1536,256]{1,0:T(8,128)(2,1)}, bf16[1536,256]{1,0:T(8,128)(2,1)}, u32[]{:S(2)}, u32[]{:S(2)}) collective-permute-start(bf16[1536,256]{1,0:T(8,128)(2,1)} %bitcast.12), channel_id=1, source_target_pairs={{0,1},{1,2},{2,3},{3,0},{4,5},{5,6},{6,7},{7,4},{8,9},{9,10},{10,1... | collective-permute-start | bytes 2359304 | tf_op jit(solution)/shard_map/ppermute | solution.py:63
  58.6 38.7 %collective-permute-start.3 = (bf16[1536,256]{1,0:T(8,128)(2,1)}, bf16[1536,256]{1,0:T(8,128)(2,1)S(1)}, u32[]{:S(2)}, u32[]{:S(2)}) collective-permute-start(bf16[1536,256]{1,0:T(8,128)(2,1)} %bitcast.12), channel_id=1, source_target_pairs={{0,3},{1,0},{2,1},{3,2},{4,7},{5,4},{6,5},{7,6},{8,11},{9,8},{10,9... | collective-permute-start | bytes 2359304 | tf_op jit(solution)/shard_map/ppermute | solution.py:63
  97.4 46.5 %collective-permute-start.7 = (bf16[1536,256]{1,0:T(8,128)(2,1)}, bf16[1536,256]{1,0:T(8,128)(2,1)}, u32[]{:S(2)}, u32[]{:S(2)}) collective-permute-start(bf16[1536,256]{1,0:T(8,128)(2,1)} %bitcast.13), channel_id=1, source_target_pairs={{0,3},{1,0},{2,1},{3,2},{4,7},{5,4},{6,5},{7,6},{8,11},{9,8},{10,9... | collective-permute-start | bytes 2359304 | tf_op jit(solution)/shard_map/ppermute | solution.py:63
  98.8 48.2 %collective-permute-start.6 = (bf16[1536,256]{1,0:T(8,128)(2,1)}, bf16[1536,256]{1,0:T(8,128)(2,1)}, u32[]{:S(2)}, u32[]{:S(2)}) collective-permute-start(bf16[1536,256]{1,0:T(8,128)(2,1)} %bitcast.13), channel_id=1, source_target_pairs={{0,1},{1,2},{2,3},{3,0},{4,5},{5,6},{6,7},{7,4},{8,9},{9,10},{10,1... | collective-permute-start | bytes 2359304 | tf_op jit(solution)/shard_map/ppermute | solution.py:63
  98.9 41.5 %collective-permute-start.5 = (s32[1536]{0:T(1024)S(1)}, s32[1536]{0:T(1024)S(1)}, u32[]{:S(2)}, u32[]{:S(2)}) collective-permute-start(s32[1536]{0:T(1024)S(1)} %slice.57), channel_id=1, source_target_pairs={{0,3},{1,0},{2,1},{3,2},{4,7},{5,4},{6,5},{7,6},{8,11},{9,8},{10,9... | collective-permute-start | bytes 18440 | tf_op jit(solution)/shard_map/ppermute | solution.py:63
  101.5 41.5 %collective-permute-start.4 = (s32[1536]{0:T(1024)S(1)}, s32[1536]{0:T(1024)S(1)}, u32[]{:S(2)}, u32[]{:S(2)}) collective-permute-start(s32[1536]{0:T(1024)S(1)} %slice.57), channel_id=1, source_target_pairs={{0,1},{1,2},{2,3},{3,0},{4,5},{5,6},{6,7},{7,4},{8,9},{9,10},{10,1... | collective-permute-start | bytes 18440 | tf_op jit(solution)/shard_map/ppermute | solution.py:63
  140.4 45.8 %collective-permute-start.10 = (bf16[1536,256]{1,0:T(8,128)(2,1)}, bf16[1536,256]{1,0:T(8,128)(2,1)S(1)}, u32[]{:S(2)}, u32[]{:S(2)}) collective-permute-start(bf16[1536,256]{1,0:T(8,128)(2,1)} %collective-permute-done.2), channel_id=1, source_target_pairs={{0,1},{1,2},{2,3},{3,0},{4,5},{5,6},{6,7},{7,4},{8,9},{9,10},{10,1... | collective-permute-start | bytes 2359304 | tf_op jit(solution)/shard_map/ppermute | solution.py:63
  140.4 3.5 %collective-permute-start.9 = (s32[1536]{0:T(1024)S(1)}, s32[1536]{0:T(1024)S(1)}, u32[]{:S(2)}, u32[]{:S(2)}) collective-permute-start(s32[1536]{0:T(1024)S(1)} %collective-permute-done.5), channel_id=1, source_target_pairs={{0,3},{1,0},{2,1},{3,2},{4,7},{5,4},{6,5},{7,6},{8,11},{9,8},{10,9... | collective-permute-start | bytes 18440 | tf_op jit(solution)/shard_map/ppermute | solution.py:63
  143.9 42.3 %collective-permute-start.11 = (bf16[1536,256]{1,0:T(8,128)(2,1)}, bf16[1536,256]{1,0:T(8,128)(2,1)}, u32[]{:S(2)}, u32[]{:S(2)}) collective-permute-start(bf16[1536,256]{1,0:T(8,128)(2,1)} %collective-permute-done.7), channel_id=1, source_target_pairs={{0,3},{1,0},{2,1},{3,2},{4,7},{5,4},{6,5},{7,6},{8,11},{9,8},{10,9... | collective-permute-start | bytes 2359304 | tf_op jit(solution)/shard_map/ppermute | solution.py:63
  187.4 1.1 copy-start.2
  208.9 11.1 %copy-start.3 = (bf16[3072,256]{1,0:T(8,128)(2,1)S(1)}, bf16[3072,256]{1,0:T(8,128)(2,1)}, u32[]{:S(2)}) copy-start(bf16[3072,256]{1,0:T(8,128)(2,1)} %get-tuple-element.460) | copy-start | bytes 4718596
  208.9 35.2 %all-to-all-start.2 = ((bf16[32,96,256]{2,1,0:T(8,128)(2,1)}), bf16[32,96,256]{2,1,0:T(8,128)(2,1)}, u32[]{:S(2)}, u32[]{:S(2)}) async-start(bf16[32,96,256]{2,1,0:T(8,128)(2,1)} %bitcast.85), calls=%async_computation.2 | async-start | bytes 3145728 | tf_op jit(solution)/shard_map/all_to_all | solution.py:97
  244.1 5.4 %copy-start.1 = (bf16[1024,1024]{1,0:T(8,128)(2,1)S(1)}, bf16[1024,1024]{1,0:T(8,128)(2,1)}, u32[]{:S(2)}) copy-start(bf16[1024,1024]{1,0:T(8,128)(2,1)} %param.15) | copy-start | bytes 6291460

commit v9 on v4

--- a/solution.py
+++ b/solution.py
@@ -68,18 +68,18 @@
     from_prev = shift(payload, 1)
     from_next = shift(payload, -1)
     half = payload.shape[0] // 2
-    from_far = jnp.concatenate([shift(from_prev[:half], 1), shift(from_next[half:], -1)])
+    far_a = shift(from_prev[:half], 1)
+    far_b = shift(from_next[half:], -1)
 
-    def keys_of(pieces):
-        count = pieces.shape[0] // payload.shape[0]
-        code = pieces.reshape(count, -1, emb_width)[:, slots:]
-        code = code.reshape(count, -1)[:, : 2 * slots].astype(jnp.int32)
-        ids = code[:, :slots] * 128 + code[:, slots:]
-        return jnp.pad(ids, ((0, 0), (0, code_rows)), constant_values=-1).reshape(-1)
+    def decode(code):
+        code = code.reshape(-1)[: 2 * slots].astype(jnp.int32)
+        return code[:slots] * 128 + code[slots:]
 
-    rows_near = jnp.concatenate([from_prev, from_next])
-    keys_near = keys_of(rows_near)
-    keys_far = keys_of(from_far)
+    rows_near = jnp.concatenate([from_prev[:slots], from_next[:slots]])
+    keys_near = jnp.concatenate([decode(from_prev[slots:]), decode(from_next[slots:])])
+    far_tail = slots - half
+    rows_far = jnp.concatenate([far_a, far_b[:far_tail]])
+    keys_far = decode(far_b[far_tail:])
 
     first_row = my_rep * share_rows
     share_ids = first_row + jnp.arange(share_rows, dtype=jnp.int32)
@@ -89,11 +89,11 @@
     queries = jnp.concatenate([in_ids, share_ids])
     own_sums = match_sums(queries, in_ids, incoming)
     near_sums = match_sums(queries, keys_near, rows_near)
-    look_sum = own_sums[:slots] + near_sums[:slots] + match_sums(in_ids, keys_far, from_far)
+    look_sum = own_sums[:slots] + near_sums[:slots] + match_sums(in_ids, keys_far, rows_far)
     picked = normalize(look_cent + look_sum)
     returned = lax.all_to_all(picked, "wide", split_axis=0, concat_axis=0, tiled=True)
 
-    share_sum = own_sums[slots:] + near_sums[slots:] + match_sums(share_ids, keys_far, from_far)
+    share_sum = own_sums[slots:] + near_sums[slots:] + match_sums(share_ids, keys_far, rows_far)
     own_rows = normalize(own_cent + share_sum)
 
     gathered_rows = jnp.dot(place_bf.T, returned, preferred_element_type=jnp.float32)

time: 218 us -> 222 us (1.018)
  other arithmetic: 31.2 us -> 36.1 us
  waiting for transfers between devices: 12.3 us -> 14.6 us
    slice x2 -> x5, local copies, waits for them, and re-layouts: 2.97 us -> 8.33 us  [the longest x2 3.02 us: body(): rows_near = jnp.concatenate([from_prev[:slots], from_next[:slots]])]
    concatenate x0 -> x3, other arithmetic: none -> 3.19 us  [the longest x1 1.94 us: body(): rows_near = jnp.concatenate([from_prev[:slots], from_next[:slots]])]
    concatenate x2 -> x0, local copies, waits for them, and re-layouts: 2.71 us -> none  [the longest x1 1.52 us: body(): rows_near = jnp.concatenate([from_prev, from_next])]
    unnamed x17 -> x7, local copies, waits for them, and re-layouts: 3.67 us -> 1.02 us
  transfers between devices with their start and end apart: 7 -> 7, of which waited for: 2 -> 3; matrix products, arithmetic and copies ran while one was open for 61% -> 62% of each run, Pallas kernels for 0% -> 0%
where the time goes in v9:
time: 222 us; the launch traced here: 221 us
  matrix products  105 us (47%)
  other arithmetic  36.1 us (16%)
  local copies, waits for them, and re-layouts  34.9 us (16%)
  starting transfers between devices  29.5 us (13%)
  waiting for transfers between devices  14.6 us (7%)
    dot_general x21, matrix products, one_block(): return jnp.dot(selector, rows, preferred_element_type=jnp.float32)  88.9 us
    gather x1, local copies, waits for them, and re-layouts, body(): look_cent = centroids[in_ids].astype(jnp.float32)  16.6 us
    ppermute x4, waiting for transfers between devices, shift(): lax.ppermute(x, 'rep', [(i, (i + step) % replicas) for i in range(replica...  13.2 us
    reduce_sum x2, other arithmetic, normalize(): jnp.mean(updated * updated, axis=-1, keepdims=True) + 1e-06  9.45 us
    all_to_all x1, starting transfers between devices, body(): lax.all_to_all(out_ids, 'wide', split_axis=0, concat_axis=0, tiled=True)  8.57 us
    all_to_all x1, starting transfers between devices, body(): lax.all_to_all(picked, 'wide', split_axis=0, concat_axis=0, tiled=True)  8.28 us
    convert_element_type x2, other arithmetic, normalize(): return (updated * lax.rsqrt(jnp.mean(updated * updated, axis=-1, keepdims...  7.62 us
    all_to_all x1, starting transfers between devices, body(): lax.all_to_all(outgoing, 'wide', split_axis=0, concat_axis=0, tiled=True)  7.38 us
  transfers between devices with their start and end apart: 7, of which 3 were waited for; matrix products, arithmetic and copies ran while one was open for 62% of the time, Pallas kernels for 0%

profile of v9, /device:TPU:1, one launch (start us, length us, event | category | flops | bytes accessed | tf_op | source)
XLA Modules:
  0.0 220.7 jit_solution(15967094367021160039)
XLA Ops:
  4.8 8.6 %all-to-all-start = ((s32[32,96,1]{1,2,0:T(1,128)}), s32[32,96,1]{1,2,0:T(1,128)S(1)}, u32[]{:S(2)}, u32[]{:S(2)}) async-start(s32[32,96,1]{1,2,0:T(1,128)} %all_to_all.24), calls=%async_computation | async-start | bytes 32768 | tf_op jit(solution)/shard_map/all_to_all | solution.py:58
  13.4 6.0 %multiply_reduce_fusion.2 = (f32[1024]{0:T(1024)S(1)}, f32[1024,256]{0,1:T(8,128)}) fusion(bf16[1024,256]{1,0:T(8,128)(2,1)} %param.16, bf16[1024,1024]{1,0:T(8,128)(2,1)S(1)} %copy-done, bf16[1024,1024]{1,0:T(8,128)(2,1)} %param.15), kind=kOutput, calls=%fused_computation.63 | convolution fusion | flops 2694315008 | bytes 5771264 | tf_op jit(solution)/shard_map/dot_general | solution.py:50
  19.3 4.9 %fusion.53 = bf16[3072,256]{1,0:T(8,128)(2,1)} fusion(s32[1024]{0:T(1024)S(1)} %get-tuple-element.164, f32[1024,256]{0,1:T(8,128)} %get-tuple-element.167, f32[1024]{0:T(1024)S(1)} %add_rsqrt_fusion.2), kind=kOutput, calls=%fused_computation.50 | convolution fusion | flops 1615069184 | bytes 2629632 | tf_op jit(solution)/shard_map/dot_general | solution.py:55
  24.2 7.4 %all-to-all-start.1 = ((bf16[32,96,256]{2,1,0:T(8,128)(2,1)}), bf16[32,96,256]{2,1,0:T(8,128)(2,1)S(1)}, u32[]{:S(2)}, u32[]{:S(2)}) async-start(bf16[32,96,256]{2,1,0:T(8,128)(2,1)} %bitcast.72), calls=%async_computation.1 | async-start | bytes 3145728 | tf_op jit(solution)/shard_map/all_to_all | solution.py:57
  33.2 16.6 %gather_fusion = bf16[3072,256]{1,0:T(8,128)(2,1)} fusion(bf16[16384,256]{1,0:T(8,128)(2,1)} %param.17, s32[3072]{0:T(1024)S(1)} %broadcast_clamp_fusion), kind=kCustom, calls=%fused_computation | custom fusion | bytes 3158016 | tf_op jit(solution)/shard_map/gather | solution.py:86
  49.8 3.3 %convert_element_type.79 = f32[3072,256]{1,0:T(8,128)} convert(bf16[3072,256]{1,0:T(8,128)(2,1)} %gather_fusion) | non-fusion elementwise | flops 786432 | bytes 4718592 | tf_op jit(solution)/shard_map/convert_element_type | solution.py:86
  55.5 3.8 %collective-permute-start.1 = (bf16[3104,256]{1,0:T(8,128)(2,1)}, bf16[3104,256]{1,0:T(8,128)(2,1)}, u32[]{:S(2)}, u32[]{:S(2)}) collective-permute-start(bf16[3104,256]{1,0:T(8,128)(2,1)} %pad_maximum_fusion.1), channel_id=1, source_target_pairs={{0,3},{1,0},{2,1},{3,2},{4,7},{5,4},{6,5},{7,6},{8,11},{9,8},{10,9... | collective-permute-start | bytes 4767752 | tf_op jit(solution)/shard_map/ppermute | solution.py:66
  59.3 3.6 %broadcast.91.clone.1 = f32[7,1024,256]{2,1,0:T(8,128)} broadcast(f32[]{:T(128)} %constant.101.clone.1), dimensions={} | broadcast | bytes 7340036 | tf_op jit(solution)/shard_map/broadcast.4
  62.9 20.1 %while.40 = (s32[]{:T(128)}, f32[7,1024,256]{2,1,0:T(8,128)}, s32[7,1024]{1,0:T(8,128)S(1)}, s32[3072]{0:T(1024)S(1)}, bf16[3072,256]{1,0:T(8,128)(2,1)S(1)}, /*index=5*/s32[]{:T(128)}) while((s32[]{:T(128)}, f32[7,1024,256]{2,1,0:T(8,128)}, s32[7,1024]{1,0:T(8,128)S(1)}, s32[3072]{0:T(1024)S(1)}, bf16[3072,256]{1,0:T(8,128)(2,1)S(1)}, ...), condition=%wide.region_4.5_spmd, body=%wide.region_3.4_spmd.sunk | while | flops 1613758464 | bytes 2646601 | solution.py:22
  65.8 2.9 %fusion.98 = f32[7,1024,256]{2,1,0:T(8,128)} fusion(f32[7,1024,256]{2,1,0:T(8,128)} %get-tuple-element.335, s32[]{:T(128)} %get-tuple-element.334, bf16[3072,256]{1,0:T(8,128)(2,1)S(1)} %get-tuple-element.344, s32[3072]{0:T(1024)S(1)} %get-tuple-element.343, s32[1024]{0:T(1024)S(1)} %bitcast.75), kind=kOutput, calls=%fused_computation.6.clone.1 | convolution fusion | flops 1613758464 | bytes 2638336 | tf_op jit(solution)/shard_map/while/body/eval_jaxpr/dot_general | solution.py:20
  77.3 2.9 %fusion.98 = f32[7,1024,256]{2,1,0:T(8,128)} fusion(f32[7,1024,256]{2,1,0:T(8,128)} %get-tuple-element.335, s32[]{:T(128)} %get-tuple-element.334, bf16[3072,256]{1,0:T(8,128)(2,1)S(1)} %get-tuple-element.344, s32[3072]{0:T(1024)S(1)} %get-tuple-element.343, s32[1024]{0:T(1024)S(1)} %bitcast.75), kind=kOutput, calls=%fused_computation.6.clone.1 | convolution fusion | flops 1613758464 | bytes 2638336 | tf_op jit(solution)/shard_map/while/body/eval_jaxpr/dot_general | solution.py:20
  83.1 13.2 %collective-permute-done = bf16[3104,256]{1,0:T(8,128)(2,1)} collective-permute-done((bf16[3104,256]{1,0:T(8,128)(2,1)}, bf16[3104,256]{1,0:T(8,128)(2,1)}, u32[]{:S(2)}, u32[]{:S(2)}) %collective-permute-start) | collective-permute-done | bytes 1589280 | tf_op jit(solution)/shard_map/ppermute | solution.py:66
  108.3 3.6 %broadcast.91.clone = f32[7,1024,256]{2,1,0:T(8,128)} broadcast(f32[]{:T(128)} %constant.101.clone.1), dimensions={} | broadcast | bytes 7340036 | tf_op jit(solution)/shard_map/broadcast.4
  111.9 44.6 %while.41 = (s32[]{:T(128)}, f32[7,1024,256]{2,1,0:T(8,128)}, s32[7,1024]{1,0:T(8,128)S(1)}, s32[6144]{0:T(1024)S(1)}, bf16[6144,256]{1,0:T(8,128)(2,1)}, /*index=5*/s32[]{:T(128)}) while((s32[]{:T(128)}, f32[7,1024,256]{2,1,0:T(8,128)}, s32[7,1024]{1,0:T(8,128)S(1)}, s32[6144]{0:T(1024)S(1)}, bf16[6144,256]{1,0:T(8,128)(2,1)}, ...), condition=%wide.region_6.7_spmd, body=%wide.region_5.6_spmd.sunk | while | flops 3227516928 | bytes 4231753 | solution.py:22
  111.9 6.3 %fusion.101 = f32[7,1024,256]{2,1,0:T(8,128)} fusion(f32[7,1024,256]{2,1,0:T(8,128)} %get-tuple-element.317, s32[]{:T(128)} %get-tuple-element.316, bf16[6144,256]{1,0:T(8,128)(2,1)} %get-tuple-element.326, s32[6144]{0:T(1024)S(1)} %get-tuple-element.325, s32[1024]{0:T(1024)S(1)} %bitcast.76), kind=kOutput, calls=%fused_computation.13.clone.1 | convolution fusion | flops 3227516928 | bytes 4223488 | tf_op jit(solution)/shard_map/while/body/eval_jaxpr/dot_general | solution.py:20
  118.3 6.4 %fusion.101 = f32[7,1024,256]{2,1,0:T(8,128)} fusion(f32[7,1024,256]{2,1,0:T(8,128)} %get-tuple-element.317, s32[]{:T(128)} %get-tuple-element.316, bf16[6144,256]{1,0:T(8,128)(2,1)} %get-tuple-element.326, s32[6144]{0:T(1024)S(1)} %get-tuple-element.325, s32[1024]{0:T(1024)S(1)} %bitcast.76), kind=kOutput, calls=%fused_computation.13.clone.1 | convolution fusion | flops 3227516928 | bytes 4223488 | tf_op jit(solution)/shard_map/while/body/eval_jaxpr/dot_general | solution.py:20
  124.7 6.4 %fusion.101 = f32[7,1024,256]{2,1,0:T(8,128)} fusion(f32[7,1024,256]{2,1,0:T(8,128)} %get-tuple-element.317, s32[]{:T(128)} %get-tuple-element.316, bf16[6144,256]{1,0:T(8,128)(2,1)} %get-tuple-element.326, s32[6144]{0:T(1024)S(1)} %get-tuple-element.325, s32[1024]{0:T(1024)S(1)} %bitcast.76), kind=kOutput, calls=%fused_computation.13.clone.1 | convolution fusion | flops 3227516928 | bytes 4223488 | tf_op jit(solution)/shard_map/while/body/eval_jaxpr/dot_general | solution.py:20
  131.1 6.4 %fusion.101 = f32[7,1024,256]{2,1,0:T(8,128)} fusion(f32[7,1024,256]{2,1,0:T(8,128)} %get-tuple-element.317, s32[]{:T(128)} %get-tuple-element.316, bf16[6144,256]{1,0:T(8,128)(2,1)} %get-tuple-element.326, s32[6144]{0:T(1024)S(1)} %get-tuple-element.325, s32[1024]{0:T(1024)S(1)} %bitcast.76), kind=kOutput, calls=%fused_computation.13.clone.1 | convolution fusion | flops 3227516928 | bytes 4223488 | tf_op jit(solution)/shard_map/while/body/eval_jaxpr/dot_general | solution.py:20
  137.4 6.3 %fusion.101 = f32[7,1024,256]{2,1,0:T(8,128)} fusion(f32[7,1024,256]{2,1,0:T(8,128)} %get-tuple-element.317, s32[]{:T(128)} %get-tuple-element.316, bf16[6144,256]{1,0:T(8,128)(2,1)} %get-tuple-element.326, s32[6144]{0:T(1024)S(1)} %get-tuple-element.325, s32[1024]{0:T(1024)S(1)} %bitcast.76), kind=kOutput, calls=%fused_computation.13.clone.1 | convolution fusion | flops 3227516928 | bytes 4223488 | tf_op jit(solution)/shard_map/while/body/eval_jaxpr/dot_general | solution.py:20
  143.8 6.4 %fusion.101 = f32[7,1024,256]{2,1,0:T(8,128)} fusion(f32[7,1024,256]{2,1,0:T(8,128)} %get-tuple-element.317, s32[]{:T(128)} %get-tuple-element.316, bf16[6144,256]{1,0:T(8,128)(2,1)} %get-tuple-element.326, s32[6144]{0:T(1024)S(1)} %get-tuple-element.325, s32[1024]{0:T(1024)S(1)} %bitcast.76), kind=kOutput, calls=%fused_computation.13.clone.1 | convolution fusion | flops 3227516928 | bytes 4223488 | tf_op jit(solution)/shard_map/while/body/eval_jaxpr/dot_general | solution.py:20
  150.2 6.4 %fusion.101 = f32[7,1024,256]{2,1,0:T(8,128)} fusion(f32[7,1024,256]{2,1,0:T(8,128)} %get-tuple-element.317, s32[]{:T(128)} %get-tuple-element.316, bf16[6144,256]{1,0:T(8,128)(2,1)} %get-tuple-element.326, s32[6144]{0:T(1024)S(1)} %get-tuple-element.325, s32[1024]{0:T(1024)S(1)} %bitcast.76), kind=kOutput, calls=%fused_computation.13.clone.1 | convolution fusion | flops 3227516928 | bytes 4223488 | tf_op jit(solution)/shard_map/while/body/eval_jaxpr/dot_general | solution.py:20
  159.7 12.8 %while.43 = (s32[]{:T(128)}, f32[3,1024,256]{2,1,0:T(8,128)}, s32[3,1024]{1,0:T(4,128)S(1)}, s32[3072]{0:T(1024)S(1)}, bf16[3072,256]{1,0:T(8,128)(2,1)}, /*index=5*/s32[]{:T(128)}) while((s32[]{:T(128)}, f32[3,1024,256]{2,1,0:T(8,128)}, s32[3,1024]{1,0:T(4,128)S(1)}, s32[3072]{0:T(1024)S(1)}, bf16[3072,256]{1,0:T(8,128)(2,1)}, ...), condition=%wide.region_11.12_spmd, body=%wide.region_10.11_spmd.sunk | while | flops 1613758464 | bytes 2646601 | solution.py:22
  159.8 4.3 %fusion.107 = f32[3,1024,256]{2,1,0:T(8,128)} fusion(f32[3,1024,256]{2,1,0:T(8,128)} %get-tuple-element.353, s32[]{:T(128)} %get-tuple-element.352, bf16[3072,256]{1,0:T(8,128)(2,1)} %get-tuple-element.362, s32[3072]{0:T(1024)S(1)} %get-tuple-element.361, s32[1024]{0:T(1024)S(1)} %bitcast.77), kind=kOutput, calls=%fused_computation.27.clone.1 | convolution fusion | flops 1613758464 | bytes 2638336 | tf_op jit(solution)/shard_map/while/body/eval_jaxpr/dot_general | solution.py:20
  164.0 4.3 %fusion.107 = f32[3,1024,256]{2,1,0:T(8,128)} fusion(f32[3,1024,256]{2,1,0:T(8,128)} %get-tuple-element.353, s32[]{:T(128)} %get-tuple-element.352, bf16[3072,256]{1,0:T(8,128)(2,1)} %get-tuple-element.362, s32[3072]{0:T(1024)S(1)} %get-tuple-element.361, s32[1024]{0:T(1024)S(1)} %bitcast.77), kind=kOutput, calls=%fused_computation.27.clone.1 | convolution fusion | flops 1613758464 | bytes 2638336 | tf_op jit(solution)/shard_map/while/body/eval_jaxpr/dot_general | solution.py:20
  168.3 4.3 %fusion.107 = f32[3,1024,256]{2,1,0:T(8,128)} fusion(f32[3,1024,256]{2,1,0:T(8,128)} %get-tuple-element.353, s32[]{:T(128)} %get-tuple-element.352, bf16[3072,256]{1,0:T(8,128)(2,1)} %get-tuple-element.362, s32[3072]{0:T(1024)S(1)} %get-tuple-element.361, s32[1024]{0:T(1024)S(1)} %bitcast.77), kind=kOutput, calls=%fused_computation.27.clone.1 | convolution fusion | flops 1613758464 | bytes 2638336 | tf_op jit(solution)/shard_map/while/body/eval_jaxpr/dot_general | solution.py:20
  172.6 7.0 %multiply_reduce_fusion.1 = (f32[3,1024]{1,0:T(4,128)S(1)}, f32[3,1024,256]{2,1,0:T(8,128)}) fusion(f32[3,1024,256]{2,1,0:T(8,128)} %bitcast.67, f32[3,1024,256]{2,1,0:T(8,128)} %get-tuple-element.113, f32[7,1024,256]{2,1,0:T(8,128)} %get-tuple-element.111, f32[7,1024,256]{2,1,0:T(8,128)} %get-tuple-element.110), kind=kLoop, calls=%fused_computation.53 | loop fusion | flops 3929088 | bytes 15740928 | tf_op jit(solution)/shard_map/reduce_sum | solution.py:9
  179.6 4.6 %multiply_convert_fusion.1 = bf16[32,96,256]{2,1,0:T(8,128)(2,1)} fusion(f32[32,96,256]{2,1,0:T(8,128)} %bitcast.68, f32[32,96,256]{2,1,0:T(8,128)} %bitcast.69, f32[32,96]{1,0:T(8,128)S(1)} %rsqrt.30), kind=kLoop, calls=%fused_computation.52 | loop fusion | flops 2359296 | bytes 7876608 | tf_op jit(solution)/shard_map/convert_element_type | solution.py:10
  184.2 8.3 %all-to-all-start.2 = ((bf16[32,96,256]{2,1,0:T(8,128)(2,1)}), bf16[32,96,256]{2,1,0:T(8,128)(2,1)}, u32[]{:S(2)}, u32[]{:S(2)}) async-start(bf16[32,96,256]{2,1,0:T(8,128)(2,1)} %multiply_convert_fusion.1), calls=%async_computation.2 | async-start | bytes 3145728 | tf_op jit(solution)/shard_map/all_to_all | solution.py:94
  192.5 11.5 %while.42 = (s32[]{:T(128)}, f32[4,1024,256]{2,1,0:T(8,128)}, s32[4,1024]{1,0:T(4,128)S(1)}, s32[3072]{0:T(1024)S(1)}, bf16[3072,256]{1,0:T(8,128)(2,1)S(1)}, /*index=5*/s32[]{:T(128)}) while((s32[]{:T(128)}, f32[4,1024,256]{2,1,0:T(8,128)}, s32[4,1024]{1,0:T(4,128)S(1)}, s32[3072]{0:T(1024)S(1)}, bf16[3072,256]{1,0:T(8,128)(2,1)S(1)}, ...), condition=%wide.region_8.9_spmd, body=%wide.region_7.8_spmd.sunk | while | flops 1613758464 | bytes 2646601 | solution.py:22
  204.0 5.5 %add_add_fusion = f32[4,1024,256]{2,1,0:T(8,128)S(1)} fusion(f32[4,1024,256]{2,1,0:T(8,128)} %get-tuple-element.112, f32[7,1024,256]{2,1,0:T(8,128)} %get-tuple-element.111, f32[7,1024,256]{2,1,0:T(8,128)} %get-tuple-element.110), kind=kLoop, calls=%fused_computation.47 | loop fusion | flops 2097152 | bytes 16777216 | tf_op jit(solution)/shard_map/add | solution.py:96
  212.0 3.0 %multiply_convert_fusion = bf16[4096,256]{1,0:T(8,128)(2,1)} fusion(f32[4,1024,256]{2,1,0:T(8,128)S(1)} %add_add_fusion, f32[4096]{0:T(1024)S(1)} %add_rsqrt_fusion.1, bf16[16384,256]{1,0:T(8,128)(2,1)} %param.17, s32[]{:T(128)S(6)} %select_n.38), kind=kLoop, calls=%fused_computation.45 | loop fusion | flops 4194304 | bytes 8404996 | tf_op jit(solution)/shard_map/convert_element_type | solution.py:10
  215.2 4.4 %fusion.57 = bf16[1024,256]{0,1:T(8,128)(2,1)S(1)} fusion(bf16[3072,256]{1,0:T(8,128)(2,1)} %bitcast.15, s32[1024]{0:T(1024)S(1)} %get-tuple-element.164, f32[1024,256]{0,1:T(8,128)} %get-tuple-element.167, f32[1024]{0:T(1024)S(1)} %add_rsqrt_fusion.2), kind=kOutput, calls=%fused_computation.59 | convolution fusion | flops 1615069184 | bytes 3153920 | tf_op jit(solution)/shard_map/dot_general | solution.py:99
  (90 shorter events, 52.9 us)
Async XLA Ops:
  0.6 12.7 %copy-start = (bf16[1024,1024]{1,0:T(8,128)(2,1)S(1)}, bf16[1024,1024]{1,0:T(8,128)(2,1)}, u32[]{:S(2)}) copy-start(bf16[1024,1024]{1,0:T(8,128)(2,1)} %param.13) | copy-start | bytes 6291460
  4.8 19.4 %all-to-all-start = ((s32[32,96,1]{1,2,0:T(1,128)}), s32[32,96,1]{1,2,0:T(1,128)S(1)}, u32[]{:S(2)}, u32[]{:S(2)}) async-start(s32[32,96,1]{1,2,0:T(1,128)} %all_to_all.24), calls=%async_computation | async-start | bytes 32768 | tf_op jit(solution)/shard_map/all_to_all | solution.py:58
  24.2 30.1 %all-to-all-start.1 = ((bf16[32,96,256]{2,1,0:T(8,128)(2,1)}), bf16[32,96,256]{2,1,0:T(8,128)(2,1)S(1)}, u32[]{:S(2)}, u32[]{:S(2)}) async-start(bf16[32,96,256]{2,1,0:T(8,128)(2,1)} %bitcast.72), calls=%async_computation.1 | async-start | bytes 3145728 | tf_op jit(solution)/shard_map/all_to_all | solution.py:57
  55.5 41.5 %collective-permute-start.1 = (bf16[3104,256]{1,0:T(8,128)(2,1)}, bf16[3104,256]{1,0:T(8,128)(2,1)}, u32[]{:S(2)}, u32[]{:S(2)}) collective-permute-start(bf16[3104,256]{1,0:T(8,128)(2,1)} %pad_maximum_fusion.1), channel_id=1, source_target_pairs={{0,3},{1,0},{2,1},{3,2},{4,7},{5,4},{6,5},{7,6},{8,11},{9,8},{10,9... | collective-permute-start | bytes 4767752 | tf_op jit(solution)/shard_map/ppermute | solution.py:66
  59.3 37.0 %collective-permute-start = (bf16[3104,256]{1,0:T(8,128)(2,1)}, bf16[3104,256]{1,0:T(8,128)(2,1)}, u32[]{:S(2)}, u32[]{:S(2)}) collective-permute-start(bf16[3104,256]{1,0:T(8,128)(2,1)} %pad_maximum_fusion.1), channel_id=1, source_target_pairs={{0,1},{1,2},{2,3},{3,0},{4,5},{5,6},{6,7},{7,4},{8,9},{9,10},{10,1... | collective-permute-start | bytes 4767752 | tf_op jit(solution)/shard_map/ppermute | solution.py:66
  99.8 56.7 %collective-permute-start.2 = (bf16[1552,256]{1,0:T(8,128)(2,1)}, bf16[1552,256]{1,0:T(8,128)(2,1)}, u32[]{:S(2)}, u32[]{:S(2)}) collective-permute-start(bf16[1552,256]{1,0:T(8,128)(2,1)} %slice.101), channel_id=1, source_target_pairs={{0,3},{1,0},{2,1},{3,2},{4,7},{5,4},{6,5},{7,6},{8,11},{9,8},{10,9... | collective-permute-start | bytes 2383880 | tf_op jit(solution)/shard_map/ppermute | solution.py:66
  101.9 56.6 %collective-permute-start.3 = (bf16[1552,256]{1,0:T(8,128)(2,1)}, bf16[1552,256]{1,0:T(8,128)(2,1)S(1)}, u32[]{:S(2)}, u32[]{:S(2)}) collective-permute-start(bf16[1552,256]{1,0:T(8,128)(2,1)} %slice.105), channel_id=1, source_target_pairs={{0,1},{1,2},{2,3},{3,0},{4,5},{5,6},{6,7},{7,4},{8,9},{9,10},{10,1... | collective-permute-start | bytes 2383880 | tf_op jit(solution)/shard_map/ppermute | solution.py:66
  184.2 8.3 %copy-start.2 = (bf16[3072,256]{1,0:T(8,128)(2,1)S(1)}, bf16[3072,256]{1,0:T(8,128)(2,1)}, u32[]{:S(2)}) copy-start(bf16[3072,256]{1,0:T(8,128)(2,1)} %get-tuple-element.365) | copy-start | bytes 4718596
  184.2 31.0 %all-to-all-start.2 = ((bf16[32,96,256]{2,1,0:T(8,128)(2,1)}), bf16[32,96,256]{2,1,0:T(8,128)(2,1)}, u32[]{:S(2)}, u32[]{:S(2)}) async-start(bf16[32,96,256]{2,1,0:T(8,128)(2,1)} %multiply_convert_fusion.1), calls=%async_computation.2 | async-start | bytes 3145728 | tf_op jit(solution)/shard_map/all_to_all | solution.py:94
  215.2 5.4 %copy-start.1 = (bf16[1024,1024]{1,0:T(8,128)(2,1)S(1)}, bf16[1024,1024]{1,0:T(8,128)(2,1)}, u32[]{:S(2)}) copy-start(bf16[1024,1024]{1,0:T(8,128)(2,1)} %param.13) | copy-start | bytes 6291460

commit v10 on v6

--- a/solution.py
+++ b/solution.py
@@ -10,8 +10,9 @@
     ).astype(jnp.bfloat16)
 
 
-def match_sums(queries, keys, rows, block_rows=1024):
+def match_sums(queries, keys, rows, block_rows=None):
     count = queries.shape[0]
+    block_rows = block_rows or count
     padded = -(-count // block_rows) * block_rows
     blocks = jnp.pad(queries, (0, padded - count), constant_values=-1).reshape(-1, block_rows)
 
@@ -100,16 +101,16 @@
     own_cent = lax.dynamic_slice_in_dim(centroids, first_row, share_rows, 0)
 
     queries = jnp.concatenate([in_ids, share_ids])
-    own_sums = match_sums(queries, in_ids, incoming)
-    sums_a = match_sums(queries, keys_a, near_a)
-    sums_b = match_sums(queries, keys_b, near_b)
+    own_sums = match_sums(queries, in_ids, incoming, queries.shape[0] // 2)
+    sums_a = match_sums(queries, keys_a, near_a, queries.shape[0] // 2)
+    sums_b = match_sums(queries, keys_b, near_b, queries.shape[0] // 2)
     look_sum = (own_sums[:slots] + sums_a[:slots] + sums_b[:slots]
-                + match_sums(in_ids, keys_far, far))
+                + match_sums(in_ids, keys_far, far, 1024))
     picked = normalize(look_cent.astype(jnp.float32) + look_sum)
     returned = lax.all_to_all(picked, "wide", split_axis=0, concat_axis=0, tiled=True)
 
     share_sum = (own_sums[slots:] + sums_a[slots:] + sums_b[slots:]
-                 + match_sums(share_ids, keys_far, far))
+                 + match_sums(share_ids, keys_far, far, 1024))
     own_rows = normalize(own_cent.astype(jnp.float32) + share_sum)
 
     gathered_rows = jnp.dot(place_bf.T, returned, preferred_element_type=jnp.float32)

time: 213 us -> 194 us (0.911)
  matrix products: 100 us -> 86.1 us
  other arithmetic: 41.1 us -> 29.2 us
  local copies, waits for them, and re-layouts: 36.5 us -> 42 us
  waiting for transfers between devices: 0.97 us -> 3.56 us
    dot_general x28 -> x13, matrix products: 84.5 us -> 72.6 us  [one_block(): return jnp.dot(selector, rows, preferred_element_type=jnp.float32)]
    add x1 -> x0, other arithmetic: 6.93 us -> none  [body(): own_sums[slots:] + sums_a[slots:] + sums_b[slots:]]
    dynamic_slice x28 -> x13, local copies, waits for them, and re-layouts: 0.22 us -> 5.46 us  [match_sums(): return lax.map(one_block, blocks).reshape(padded, -1)[:count]]
    convert_element_type x2, other arithmetic: 7.6 us -> 3.3 us  [normalize(): return (updated * lax.rsqrt(jnp.mean(updated * updated, axis=-1, keepdims...]
    convert_element_type x1 -> x0, other arithmetic: 3.29 us -> none  [body(): picked = normalize(look_cent.astype(jnp.float32) + look_sum)]
    all_to_all x1, waiting for transfers between devices: 0.94 us -> 3.54 us  [body(): lax.all_to_all(outgoing, 'wide', split_axis=0, concat_axis=0, tiled=True)]
  transfers between devices with their start and end apart: 9 -> 9, of which waited for: 1 -> 1; matrix products, arithmetic and copies ran while one was open for 65% -> 63% of each run, Pallas kernels for 0% -> 0%
where the time goes in v10:
time: 194 us; the launch traced here: 192 us
  matrix products  86.1 us (44%)
  local copies, waits for them, and re-layouts  42 us (22%)
  starting transfers between devices  30.4 us (16%)
  other arithmetic  29.2 us (15%)
  waiting for transfers between devices  3.56 us (2%)
    dot_general x13, matrix products, one_block(): return jnp.dot(selector, rows, preferred_element_type=jnp.float32)  72.6 us
    gather x1, local copies, waits for them, and re-layouts, body(): look_cent = centroids[in_ids]  16.7 us
    reduce_sum x2, other arithmetic, normalize(): jnp.mean(updated * updated, axis=-1, keepdims=True) + 1e-06  12.4 us
    another operation x3, local copies, waits for them, and re-layouts  10.3 us
    all_to_all x1, starting transfers between devices, body(): lax.all_to_all(out_ids, 'wide', split_axis=0, concat_axis=0, tiled=True)  8.57 us
    ppermute x6, starting transfers between devices, shift(): lax.ppermute(x, 'rep', [(i, (i + step) % replicas) for i in range(replica...  8.2 us
    all_to_all x1, starting transfers between devices, body(): lax.all_to_all(outgoing, 'wide', split_axis=0, concat_axis=0, tiled=True)  7.38 us
    all_to_all x1, starting transfers between devices, body(): lax.all_to_all(picked, 'wide', split_axis=0, concat_axis=0, tiled=True)  6.23 us
  transfers between devices with their start and end apart: 9, of which 1 were waited for; matrix products, arithmetic and copies ran while one was open for 63% of the time, Pallas kernels for 0%

profile of v10, /device:TPU:1, one launch (start us, length us, event | category | flops | bytes accessed | tf_op | source)
XLA Modules:
  0.0 192.3 jit_solution(15615557462808150724)
XLA Ops:
  4.8 8.6 %all-to-all-start = ((s32[32,96,1]{1,2,0:T(1,128)}), s32[32,96,1]{1,2,0:T(1,128)S(1)}, u32[]{:S(2)}, u32[]{:S(2)}) async-start(s32[32,96,1]{1,2,0:T(1,128)} %all_to_all.26), calls=%async_computation | async-start | bytes 32768 | tf_op jit(solution)/shard_map/all_to_all | solution.py:59
  13.4 5.0 %multiply_reduce_fusion.2 = (f32[1024]{0:T(1024)S(1)}, f32[1024,256]{0,1:T(8,128)S(1)}) fusion(bf16[1024,256]{1,0:T(8,128)(2,1)} %param.18, bf16[1024,1024]{1,0:T(8,128)(2,1)S(1)} %copy-done, bf16[1024,1024]{1,0:T(8,128)(2,1)} %param.17), kind=kOutput, calls=%fused_computation.75 | convolution fusion | flops 2694315008 | bytes 5771264 | tf_op jit(solution)/shard_map/dot_general | solution.py:51
  18.4 3.6 %fusion.65 = bf16[3072,256]{1,0:T(8,128)(2,1)} fusion(s32[1024]{0:T(1024)S(1)} %get-tuple-element.212, f32[1024,256]{0,1:T(8,128)S(1)} %get-tuple-element.215, f32[1024]{0:T(1024)S(1)} %add_rsqrt_fusion.2), kind=kOutput, calls=%fused_computation.59 | convolution fusion | flops 1615069184 | bytes 2629632 | tf_op jit(solution)/shard_map/dot_general | solution.py:56
  22.7 7.4 %all-to-all-start.1 = ((bf16[32,96,256]{2,1,0:T(8,128)(2,1)}), bf16[32,96,256]{2,1,0:T(8,128)(2,1)S(1)}, u32[]{:S(2)}, u32[]{:S(2)}) async-start(bf16[32,96,256]{2,1,0:T(8,128)(2,1)} %bitcast.82), calls=%async_computation.1 | async-start | bytes 3145728 | tf_op jit(solution)/shard_map/all_to_all | solution.py:58
  32.5 16.7 %gather_fusion = bf16[3072,256]{1,0:T(8,128)(2,1)} fusion(bf16[16384,256]{1,0:T(8,128)(2,1)} %param.19, s32[3072]{0:T(1024)S(1)} %broadcast_clamp_fusion), kind=kCustom, calls=%fused_computation | custom fusion | bytes 3158016 | tf_op jit(solution)/shard_map/gather | solution.py:100
  49.2 3.5 %all-to-all-done.1 = bf16[32,96,256]{2,1,0:T(8,128)(2,1)S(1)} async-done(((bf16[32,96,256]{2,1,0:T(8,128)(2,1)}), bf16[32,96,256]{2,1,0:T(8,128)(2,1)S(1)}, u32[]{:S(2)}, u32[]{:S(2)}) %all-to-all-start.1) | async-done | bytes 1572896 | tf_op jit(solution)/shard_map/all_to_all | solution.py:58
  57.6 3.4 %broadcast.99.clone.2 = f32[2,3584,256]{2,1,0:T(8,128)} broadcast(f32[]{:T(128)} %constant.120.clone.1), dimensions={} | broadcast | bytes 7340036 | tf_op jit(solution)/shard_map/broadcast.4
  60.9 16.3 %while.50 = (s32[]{:T(128)}, f32[2,3584,256]{2,1,0:T(8,128)}, s32[2,3584]{1,0:T(2,128)S(1)}, s32[3072]{0:T(1024)S(1)}, bf16[3072,256]{1,0:T(8,128)(2,1)S(1)}, /*index=5*/s32[]{:T(128)}) while((s32[]{:T(128)}, f32[2,3584,256]{2,1,0:T(8,128)}, s32[2,3584]{1,0:T(2,128)S(1)}, s32[3072]{0:T(1024)S(1)}, bf16[3072,256]{1,0:T(8,128)(2,1)S(1)}, ...), condition=%wide.region_4.5_spmd, body=%wide.region_3.4_spmd.sunk | while | flops 5648154624 | bytes 5298761 | solution.py:23
  61.0 8.1 %fusion.126 = f32[2,3584,256]{2,1,0:T(8,128)} fusion(f32[2,3584,256]{2,1,0:T(8,128)} %get-tuple-element.432, s32[]{:T(128)} %get-tuple-element.431, bf16[3072,256]{1,0:T(8,128)(2,1)S(1)} %get-tuple-element.441, s32[3072]{0:T(1024)S(1)} %get-tuple-element.440, s32[3584]{0:T(1024)S(1)} %dynamic-slice_reduce_fusion.6), kind=kOutput, calls=%fused_computation.20.clone.1 | convolution fusion | flops 5648154624 | bytes 5270016 | tf_op jit(solution)/shard_map/while/body/eval_jaxpr/dot_general | solution.py:21
  69.1 8.1 %fusion.126 = f32[2,3584,256]{2,1,0:T(8,128)} fusion(f32[2,3584,256]{2,1,0:T(8,128)} %get-tuple-element.432, s32[]{:T(128)} %get-tuple-element.431, bf16[3072,256]{1,0:T(8,128)(2,1)S(1)} %get-tuple-element.441, s32[3072]{0:T(1024)S(1)} %get-tuple-element.440, s32[3584]{0:T(1024)S(1)} %dynamic-slice_reduce_fusion.6), kind=kOutput, calls=%fused_computation.20.clone.1 | convolution fusion | flops 5648154624 | bytes 5270016 | tf_op jit(solution)/shard_map/while/body/eval_jaxpr/dot_general | solution.py:21
  84.7 3.5 %broadcast.99.clone.1 = f32[2,3584,256]{2,1,0:T(8,128)} broadcast(f32[]{:T(128)} %constant.120.clone.1), dimensions={} | broadcast | bytes 7340036 | tf_op jit(solution)/shard_map/broadcast.4
  88.2 16.2 %while.51 = (s32[]{:T(128)}, f32[2,3584,256]{2,1,0:T(8,128)}, s32[2,3584]{1,0:T(2,128)S(1)}, s32[3072]{0:T(1024)S(1)}, bf16[3072,256]{1,0:T(8,128)(2,1)S(1)}, /*index=5*/s32[]{:T(128)}) while((s32[]{:T(128)}, f32[2,3584,256]{2,1,0:T(8,128)}, s32[2,3584]{1,0:T(2,128)S(1)}, s32[3072]{0:T(1024)S(1)}, bf16[3072,256]{1,0:T(8,128)(2,1)S(1)}, ...), condition=%wide.region_6.7_spmd, body=%wide.region_5.6_spmd.sunk | while | flops 5648154624 | bytes 5298761 | solution.py:23
  88.3 8.1 %fusion.129 = f32[2,3584,256]{2,1,0:T(8,128)} fusion(f32[2,3584,256]{2,1,0:T(8,128)} %get-tuple-element.414, s32[]{:T(128)} %get-tuple-element.413, bf16[3072,256]{1,0:T(8,128)(2,1)S(1)} %get-tuple-element.423, s32[3072]{0:T(1024)S(1)} %get-tuple-element.422, s32[3584]{0:T(1024)S(1)} %dynamic-slice_reduce_fusion.7), kind=kOutput, calls=%fused_computation.27.clone.1 | convolution fusion | flops 5648154624 | bytes 5270016 | tf_op jit(solution)/shard_map/while/body/eval_jaxpr/dot_general | solution.py:21
  96.4 8.0 %fusion.129 = f32[2,3584,256]{2,1,0:T(8,128)} fusion(f32[2,3584,256]{2,1,0:T(8,128)} %get-tuple-element.414, s32[]{:T(128)} %get-tuple-element.413, bf16[3072,256]{1,0:T(8,128)(2,1)S(1)} %get-tuple-element.423, s32[3072]{0:T(1024)S(1)} %get-tuple-element.422, s32[3584]{0:T(1024)S(1)} %dynamic-slice_reduce_fusion.7), kind=kOutput, calls=%fused_computation.27.clone.1 | convolution fusion | flops 5648154624 | bytes 5270016 | tf_op jit(solution)/shard_map/while/body/eval_jaxpr/dot_general | solution.py:21
  107.7 3.0 %collective-permute-start.5 = (bf16[1552,256]{1,0:T(8,128)(2,1)S(1)}, bf16[1552,256]{1,0:T(8,128)(2,1)}, u32[]{:S(2)}, u32[]{:S(2)}) collective-permute-start(bf16[1552,256]{1,0:T(8,128)(2,1)S(1)} %collective-permute-done.3), channel_id=1, source_target_pairs={{0,3},{1,0},{2,1},{3,2},{4,7},{5,4},{6,5},{7,6},{8,11},{9,8},{10,9... | collective-permute-start | bytes 2383880 | tf_op jit(solution)/shard_map/ppermute | solution.py:83
  110.7 3.4 %broadcast.99.clone = f32[2,3584,256]{2,1,0:T(8,128)} broadcast(f32[]{:T(128)} %constant.120.clone.1), dimensions={} | broadcast | bytes 7340036 | tf_op jit(solution)/shard_map/broadcast.4
  114.1 16.2 %while.52 = (s32[]{:T(128)}, f32[2,3584,256]{2,1,0:T(8,128)}, s32[2,3584]{1,0:T(2,128)S(1)}, s32[3072]{0:T(1024)S(1)}, bf16[3072,256]{1,0:T(8,128)(2,1)S(1)}, /*index=5*/s32[]{:T(128)}) while((s32[]{:T(128)}, f32[2,3584,256]{2,1,0:T(8,128)}, s32[2,3584]{1,0:T(2,128)S(1)}, s32[3072]{0:T(1024)S(1)}, bf16[3072,256]{1,0:T(8,128)(2,1)S(1)}, ...), condition=%wide.region_8.9_spmd, body=%wide.region_7.8_spmd.sunk | while | flops 5648154624 | bytes 5298761 | solution.py:23
  114.1 8.1 %fusion.132 = f32[2,3584,256]{2,1,0:T(8,128)} fusion(f32[2,3584,256]{2,1,0:T(8,128)} %get-tuple-element.396, s32[]{:T(128)} %get-tuple-element.395, bf16[3072,256]{1,0:T(8,128)(2,1)S(1)} %get-tuple-element.405, s32[3072]{0:T(1024)S(1)} %get-tuple-element.404, s32[3584]{0:T(1024)S(1)} %dynamic-slice_reduce_fusion.8), kind=kOutput, calls=%fused_computation.34.clone.1 | convolution fusion | flops 5648154624 | bytes 5270016 | tf_op jit(solution)/shard_map/while/body/eval_jaxpr/dot_general | solution.py:21
  122.2 8.1 %fusion.132 = f32[2,3584,256]{2,1,0:T(8,128)} fusion(f32[2,3584,256]{2,1,0:T(8,128)} %get-tuple-element.396, s32[]{:T(128)} %get-tuple-element.395, bf16[3072,256]{1,0:T(8,128)(2,1)S(1)} %get-tuple-element.405, s32[3072]{0:T(1024)S(1)} %get-tuple-element.404, s32[3584]{0:T(1024)S(1)} %dynamic-slice_reduce_fusion.8), kind=kOutput, calls=%fused_computation.34.clone.1 | convolution fusion | flops 5648154624 | bytes 5270016 | tf_op jit(solution)/shard_map/while/body/eval_jaxpr/dot_general | solution.py:21
  135.4 15.0 %while.54 = (s32[]{:T(128)}, f32[3,1024,256]{2,1,0:T(8,128)}, s32[3,1024]{1,0:T(4,128)}, s32[3072]{0:T(1024)S(1)}, bf16[3072,256]{1,0:T(8,128)(2,1)}, /*index=5*/s32[]{:T(128)}) while((s32[]{:T(128)}, f32[3,1024,256]{2,1,0:T(8,128)}, s32[3,1024]{1,0:T(4,128)}, s32[3072]{0:T(1024)S(1)}, bf16[3072,256]{1,0:T(8,128)(2,1)}, ...), condition=%wide.region_13.14_spmd, body=%wide.region_12.13_spmd.sunk | while | flops 1613758464 | bytes 2646601 | solution.py:23
  136.3 4.2 %fusion.138 = f32[3,1024,256]{2,1,0:T(8,128)} fusion(f32[3,1024,256]{2,1,0:T(8,128)} %get-tuple-element.450, s32[]{:T(128)} %get-tuple-element.449, bf16[3072,256]{1,0:T(8,128)(2,1)} %get-tuple-element.459, s32[3072]{0:T(1024)S(1)} %get-tuple-element.458, s32[1024]{0:T(1024)S(1)} %bitcast.85), kind=kOutput, calls=%fused_computation.13.clone.1 | convolution fusion | flops 1613758464 | bytes 2638336 | tf_op jit(solution)/shard_map/while/body/eval_jaxpr/dot_general | solution.py:21
  141.2 4.2 %fusion.138 = f32[3,1024,256]{2,1,0:T(8,128)} fusion(f32[3,1024,256]{2,1,0:T(8,128)} %get-tuple-element.450, s32[]{:T(128)} %get-tuple-element.449, bf16[3072,256]{1,0:T(8,128)(2,1)} %get-tuple-element.459, s32[3072]{0:T(1024)S(1)} %get-tuple-element.458, s32[1024]{0:T(1024)S(1)} %bitcast.85), kind=kOutput, calls=%fused_computation.13.clone.1 | convolution fusion | flops 1613758464 | bytes 2638336 | tf_op jit(solution)/shard_map/while/body/eval_jaxpr/dot_general | solution.py:21
  146.2 4.2 %fusion.138 = f32[3,1024,256]{2,1,0:T(8,128)} fusion(f32[3,1024,256]{2,1,0:T(8,128)} %get-tuple-element.450, s32[]{:T(128)} %get-tuple-element.449, bf16[3072,256]{1,0:T(8,128)(2,1)} %get-tuple-element.459, s32[3072]{0:T(1024)S(1)} %get-tuple-element.458, s32[1024]{0:T(1024)S(1)} %bitcast.85), kind=kOutput, calls=%fused_computation.13.clone.1 | convolution fusion | flops 1613758464 | bytes 2638336 | tf_op jit(solution)/shard_map/while/body/eval_jaxpr/dot_general | solution.py:21
  150.4 5.4 %multiply_reduce_fusion.1 = (f32[3072]{0:T(1024)S(1)}, f32[3072,256]{1,0:T(8,128)S(1)}) fusion(f32[3,1024,256]{2,1,0:T(8,128)} %get-tuple-element.143, f32[7168,256]{1,0:T(8,128)} %bitcast.73, f32[7168,256]{1,0:T(8,128)} %bitcast.77, f32[7168,256]{1,0:T(8,128)} %bitcast.75, bf16[3072,256]{1,0:T(8,128)(2,1)S(1)} %copy-done.2), kind=kLoop, calls=%fused_computation.65 | loop fusion | flops 5501952 | bytes 17313792 | tf_op jit(solution)/shard_map/reduce_sum | solution.py:9
  157.5 6.2 %all-to-all-start.2 = ((bf16[32,96,256]{2,1,0:T(8,128)(2,1)}), bf16[32,96,256]{2,1,0:T(8,128)(2,1)}, u32[]{:S(2)}, u32[]{:S(2)}) async-start(bf16[32,96,256]{2,1,0:T(8,128)(2,1)} %bitcast.17), calls=%async_computation.2 | async-start | bytes 3145728 | tf_op jit(solution)/shard_map/all_to_all | solution.py:110
  163.7 14.4 %while.53 = (s32[]{:T(128)}, f32[4,1024,256]{2,1,0:T(8,128)}, s32[4,1024]{1,0:T(4,128)}, s32[3072]{0:T(1024)S(1)}, bf16[3072,256]{1,0:T(8,128)(2,1)S(1)}, /*index=5*/s32[]{:T(128)}) while((s32[]{:T(128)}, f32[4,1024,256]{2,1,0:T(8,128)}, s32[4,1024]{1,0:T(4,128)}, s32[3072]{0:T(1024)S(1)}, bf16[3072,256]{1,0:T(8,128)(2,1)S(1)}, ...), condition=%wide.region_10.11_spmd, body=%wide.region_9.10_spmd.sunk | while | flops 1613758464 | bytes 2646601 | solution.py:23
  164.5 2.9 %fusion.135 = f32[4,1024,256]{2,1,0:T(8,128)} fusion(f32[4,1024,256]{2,1,0:T(8,128)} %get-tuple-element.378, s32[]{:T(128)} %get-tuple-element.377, bf16[3072,256]{1,0:T(8,128)(2,1)S(1)} %get-tuple-element.387, s32[3072]{0:T(1024)S(1)} %get-tuple-element.386, s32[1024]{0:T(1024)S(1)} %bitcast.86), kind=kOutput, calls=%fused_computation.6.clone.1 | convolution fusion | flops 1613758464 | bytes 2638336 | tf_op jit(solution)/shard_map/while/body/eval_jaxpr/dot_general | solution.py:21
  168.1 2.9 %fusion.135 = f32[4,1024,256]{2,1,0:T(8,128)} fusion(f32[4,1024,256]{2,1,0:T(8,128)} %get-tuple-element.378, s32[]{:T(128)} %get-tuple-element.377, bf16[3072,256]{1,0:T(8,128)(2,1)S(1)} %get-tuple-element.387, s32[3072]{0:T(1024)S(1)} %get-tuple-element.386, s32[1024]{0:T(1024)S(1)} %bitcast.86), kind=kOutput, calls=%fused_computation.6.clone.1 | convolution fusion | flops 1613758464 | bytes 2638336 | tf_op jit(solution)/shard_map/while/body/eval_jaxpr/dot_general | solution.py:21
  171.7 2.9 %fusion.135 = f32[4,1024,256]{2,1,0:T(8,128)} fusion(f32[4,1024,256]{2,1,0:T(8,128)} %get-tuple-element.378, s32[]{:T(128)} %get-tuple-element.377, bf16[3072,256]{1,0:T(8,128)(2,1)S(1)} %get-tuple-element.387, s32[3072]{0:T(1024)S(1)} %get-tuple-element.386, s32[1024]{0:T(1024)S(1)} %bitcast.86), kind=kOutput, calls=%fused_computation.6.clone.1 | convolution fusion | flops 1613758464 | bytes 2638336 | tf_op jit(solution)/shard_map/while/body/eval_jaxpr/dot_general | solution.py:21
  175.2 2.9 %fusion.135 = f32[4,1024,256]{2,1,0:T(8,128)} fusion(f32[4,1024,256]{2,1,0:T(8,128)} %get-tuple-element.378, s32[]{:T(128)} %get-tuple-element.377, bf16[3072,256]{1,0:T(8,128)(2,1)S(1)} %get-tuple-element.387, s32[3072]{0:T(1024)S(1)} %get-tuple-element.386, s32[1024]{0:T(1024)S(1)} %bitcast.86), kind=kOutput, calls=%fused_computation.6.clone.1 | convolution fusion | flops 1613758464 | bytes 2638336 | tf_op jit(solution)/shard_map/while/body/eval_jaxpr/dot_general | solution.py:21
  178.1 6.9 %multiply_reduce_fusion = (f32[4096]{0:T(1024)S(1)}, f32[4096,256]{1,0:T(8,128)S(1)}) fusion(f32[4,1024,256]{2,1,0:T(8,128)} %get-tuple-element.142, f32[7168,256]{1,0:T(8,128)} %bitcast.74, f32[7168,256]{1,0:T(8,128)} %bitcast.78, f32[7168,256]{1,0:T(8,128)} %bitcast.76, bf16[16384,256]{1,0:T(8,128)(2,1)} %param.19, s32[]{:T(128)S(6)} %select_n.45), kind=kLoop, calls=%fused_computation.56 | loop fusion | flops 7335936 | bytes 23085060 | tf_op jit(solution)/shard_map/reduce_sum | solution.py:9
  186.8 4.4 %fusion.71 = bf16[1024,256]{0,1:T(8,128)(2,1)S(1)} fusion(bf16[3072,256]{1,0:T(8,128)(2,1)} %bitcast.18, s32[1024]{0:T(1024)S(1)} %copy-done.9, f32[1024,256]{0,1:T(8,128)} %copy-done.11, f32[1024]{0:T(1024)S(1)} %copy-done.7), kind=kOutput, calls=%fused_computation.71 | convolution fusion | flops 1615069184 | bytes 3153920 | tf_op jit(solution)/shard_map/dot_general | solution.py:116
  (118 shorter events, 37.5 us)
Async XLA Ops:
  0.6 12.7 %copy-start = (bf16[1024,1024]{1,0:T(8,128)(2,1)S(1)}, bf16[1024,1024]{1,0:T(8,128)(2,1)}, u32[]{:S(2)}) copy-start(bf16[1024,1024]{1,0:T(8,128)(2,1)} %param.15) | copy-start | bytes 6291460
  2.7 15.7 %copy-start.8 = (s32[1024]{0:T(1024)}, s32[1024]{0:T(1024)S(1)}, u32[]{:S(2)}) copy-start(s32[1024]{0:T(1024)S(1)} %get-tuple-element.212) | copy-start | bytes 12292
  4.8 17.9 %all-to-all-start = ((s32[32,96,1]{1,2,0:T(1,128)}), s32[32,96,1]{1,2,0:T(1,128)S(1)}, u32[]{:S(2)}, u32[]{:S(2)}) async-start(s32[32,96,1]{1,2,0:T(1,128)} %all_to_all.26), calls=%async_computation | async-start | bytes 32768 | tf_op jit(solution)/shard_map/all_to_all | solution.py:59
  18.4 3.7 %copy-start.11 = (f32[1024,256]{0,1:T(8,128)}, f32[1024,256]{0,1:T(8,128)S(1)}, u32[]{:S(2)}) copy-start(f32[1024,256]{0,1:T(8,128)S(1)} %get-tuple-element.215) | copy-start | bytes 3145732
  18.4 3.7 %copy-start.6 = (f32[1024]{0:T(1024)}, f32[1024]{0:T(1024)S(1)}, u32[]{:S(2)}) copy-start(f32[1024]{0:T(1024)S(1)} %add_rsqrt_fusion.2) | copy-start | bytes 12292
  22.7 30.1 %all-to-all-start.1 = ((bf16[32,96,256]{2,1,0:T(8,128)(2,1)}), bf16[32,96,256]{2,1,0:T(8,128)(2,1)S(1)}, u32[]{:S(2)}, u32[]{:S(2)}) async-start(bf16[32,96,256]{2,1,0:T(8,128)(2,1)} %bitcast.82), calls=%async_computation.1 | async-start | bytes 3145728 | tf_op jit(solution)/shard_map/all_to_all | solution.py:58
  53.8 24.4 %collective-permute-start = (bf16[1552,256]{1,0:T(8,128)(2,1)}, bf16[1552,256]{1,0:T(8,128)(2,1)}, u32[]{:S(2)}, u32[]{:S(2)}) collective-permute-start(bf16[1552,256]{1,0:T(8,128)(2,1)} %pad_maximum_fusion.3), channel_id=1, source_target_pairs={{0,1},{1,2},{2,3},{3,0},{4,5},{5,6},{6,7},{7,4},{8,9},{9,10},{10,1... | collective-permute-start | bytes 2383880 | tf_op jit(solution)/shard_map/ppermute | solution.py:83
  55.4 22.7 %collective-permute-start.1 = (bf16[1552,256]{1,0:T(8,128)(2,1)}, bf16[1552,256]{1,0:T(8,128)(2,1)}, u32[]{:S(2)}, u32[]{:S(2)}) collective-permute-start(bf16[1552,256]{1,0:T(8,128)(2,1)} %pad_maximum_fusion.3), channel_id=1, source_target_pairs={{0,3},{1,0},{2,1},{3,2},{4,7},{5,4},{6,5},{7,6},{8,11},{9,8},{10,9... | collective-permute-start | bytes 2383880 | tf_op jit(solution)/shard_map/ppermute | solution.py:83
  78.2 26.3 %collective-permute-start.3 = (bf16[1552,256]{1,0:T(8,128)(2,1)}, bf16[1552,256]{1,0:T(8,128)(2,1)S(1)}, u32[]{:S(2)}, u32[]{:S(2)}) collective-permute-start(bf16[1552,256]{1,0:T(8,128)(2,1)} %pad_maximum_fusion.4), channel_id=1, source_target_pairs={{0,3},{1,0},{2,1},{3,2},{4,7},{5,4},{6,5},{7,6},{8,11},{9,8},{10,9... | collective-permute-start | bytes 2383880 | tf_op jit(solution)/shard_map/ppermute | solution.py:83
  79.6 24.8 %collective-permute-start.2 = (bf16[1552,256]{1,0:T(8,128)(2,1)}, bf16[1552,256]{1,0:T(8,128)(2,1)}, u32[]{:S(2)}, u32[]{:S(2)}) collective-permute-start(bf16[1552,256]{1,0:T(8,128)(2,1)} %pad_maximum_fusion.4), channel_id=1, source_target_pairs={{0,1},{1,2},{2,3},{3,0},{4,5},{5,6},{6,7},{7,4},{8,9},{9,10},{10,1... | collective-permute-start | bytes 2383880 | tf_op jit(solution)/shard_map/ppermute | solution.py:83
  84.7 3.5 %copy-start.5 = (bf16[3072,256]{1,0:T(8,128)(2,1)S(1)}, bf16[3072,256]{1,0:T(8,128)(2,1)}, u32[]{:S(2)}) copy-start(bf16[3072,256]{1,0:T(8,128)(2,1)} %pad_maximum_fusion) | copy-start | bytes 4718596
  104.4 25.9 %collective-permute-start.4 = (bf16[1552,256]{1,0:T(8,128)(2,1)}, bf16[1552,256]{1,0:T(8,128)(2,1)}, u32[]{:S(2)}, u32[]{:S(2)}) collective-permute-start(bf16[1552,256]{1,0:T(8,128)(2,1)} %collective-permute-done), channel_id=1, source_target_pairs={{0,1},{1,2},{2,3},{3,0},{4,5},{5,6},{6,7},{7,4},{8,9},{9,10},{10,1... | collective-permute-start | bytes 2383880 | tf_op jit(solution)/shard_map/ppermute | solution.py:83
  107.7 6.4 %copy-start.4 = (bf16[3072,256]{1,0:T(8,128)(2,1)S(1)}, bf16[3072,256]{1,0:T(8,128)(2,1)}, u32[]{:S(2)}) copy-start(bf16[3072,256]{1,0:T(8,128)(2,1)} %pad_maximum_fusion.1) | copy-start | bytes 4718596
  107.7 24.6 %collective-permute-start.5 = (bf16[1552,256]{1,0:T(8,128)(2,1)S(1)}, bf16[1552,256]{1,0:T(8,128)(2,1)}, u32[]{:S(2)}, u32[]{:S(2)}) collective-permute-start(bf16[1552,256]{1,0:T(8,128)(2,1)S(1)} %collective-permute-done.3), channel_id=1, source_target_pairs={{0,3},{1,0},{2,1},{3,2},{4,7},{5,4},{6,5},{7,6},{8,11},{9,8},{10,9... | collective-permute-start | bytes 2383880 | tf_op jit(solution)/shard_map/ppermute | solution.py:83
  114.1 18.1 %copy-start.10 = (s32[3072]{0:T(1024)S(1)}, s32[3072]{0:T(1024)}, u32[]{:S(2)}) copy-start(s32[3072]{0:T(1024)} %custom-call) | copy-start | bytes 36868
  135.4 15.0 %copy-start.2 = (bf16[3072,256]{1,0:T(8,128)(2,1)S(1)}, bf16[3072,256]{1,0:T(8,128)(2,1)}, u32[]{:S(2)}) copy-start(bf16[3072,256]{1,0:T(8,128)(2,1)} %gather_fusion) | copy-start | bytes 4718596
  155.9 7.9 %copy-start.3 = (bf16[3072,256]{1,0:T(8,128)(2,1)S(1)}, bf16[3072,256]{1,0:T(8,128)(2,1)}, u32[]{:S(2)}) copy-start(bf16[3072,256]{1,0:T(8,128)(2,1)} %get-tuple-element.464) | copy-start | bytes 4718596
  157.5 29.3 %all-to-all-start.2 = ((bf16[32,96,256]{2,1,0:T(8,128)(2,1)}), bf16[32,96,256]{2,1,0:T(8,128)(2,1)}, u32[]{:S(2)}, u32[]{:S(2)}) async-start(bf16[32,96,256]{2,1,0:T(8,128)(2,1)} %bitcast.17), calls=%async_computation.2 | async-start | bytes 3145728 | tf_op jit(solution)/shard_map/all_to_all | solution.py:110
  185.1 1.7 copy-start.7
  185.1 1.7 copy-start.9
  186.8 5.4 %copy-start.1 = (bf16[1024,1024]{1,0:T(8,128)(2,1)S(1)}, bf16[1024,1024]{1,0:T(8,128)(2,1)}, u32[]{:S(2)}) copy-start(bf16[1024,1024]{1,0:T(8,128)(2,1)} %param.15) | copy-start | bytes 6291460

commit v11 on v10

--- a/solution.py
+++ b/solution.py
@@ -110,7 +110,7 @@
     returned = lax.all_to_all(picked, "wide", split_axis=0, concat_axis=0, tiled=True)
 
     share_sum = (own_sums[slots:] + sums_a[slots:] + sums_b[slots:]
-                 + match_sums(share_ids, keys_far, far, 1024))
+                 + match_sums(share_ids, keys_far, far, share_rows // 2))
     own_rows = normalize(own_cent.astype(jnp.float32) + share_sum)
 
     gathered_rows = jnp.dot(place_bf.T, returned, preferred_element_type=jnp.float32)

time: 194 us -> 193 us (level)
  waiting for transfers between devices: 3.56 us -> 7.03 us
  local copies, waits for them, and re-layouts: 42 us -> 39.1 us
    all_to_all x1, waiting for transfers between devices: 0.01 us -> 3.54 us  [body(): lax.all_to_all(picked, 'wide', split_axis=0, concat_axis=0, tiled=True)]
    dynamic_slice x13 -> x11, local copies, waits for them, and re-layouts: 5.46 us -> 2.59 us  [match_sums(): return lax.map(one_block, blocks).reshape(padded, -1)[:count]]
    dot_general x13 -> x11, matrix products: 72.6 us -> 71.6 us  [one_block(): return jnp.dot(selector, rows, preferred_element_type=jnp.float32)]
  transfers between devices with their start and end apart: 9 -> 9, of which waited for: 1 -> 2; matrix products, arithmetic and copies ran while one was open for 63% -> 61% of each run, Pallas kernels for 0% -> 0%
where the time goes in v11:
time: 193 us; the launch traced here: 192 us
  matrix products  85.2 us (44%)
  local copies, waits for them, and re-layouts  39.1 us (20%)
  starting transfers between devices  30.4 us (16%)
  other arithmetic  29.3 us (15%)
  waiting for transfers between devices  7.03 us (4%)
    dot_general x11, matrix products, one_block(): return jnp.dot(selector, rows, preferred_element_type=jnp.float32)  71.6 us
    gather x1, local copies, waits for them, and re-layouts, body(): look_cent = centroids[in_ids]  16.6 us
    reduce_sum x2, other arithmetic, normalize(): jnp.mean(updated * updated, axis=-1, keepdims=True) + 1e-06  12.4 us
    another operation x3, local copies, waits for them, and re-layouts  10.3 us
    all_to_all x1, starting transfers between devices, body(): lax.all_to_all(out_ids, 'wide', split_axis=0, concat_axis=0, tiled=True)  8.57 us
    ppermute x6, starting transfers between devices, shift(): lax.ppermute(x, 'rep', [(i, (i + step) % replicas) for i in range(replica...  8.19 us
    all_to_all x1, starting transfers between devices, body(): lax.all_to_all(outgoing, 'wide', split_axis=0, concat_axis=0, tiled=True)  7.39 us
    all_to_all x1, starting transfers between devices, body(): lax.all_to_all(picked, 'wide', split_axis=0, concat_axis=0, tiled=True)  6.25 us
  transfers between devices with their start and end apart: 9, of which 2 were waited for; matrix products, arithmetic and copies ran while one was open for 61% of the time, Pallas kernels for 0%

profile of v11, /device:TPU:1, one launch (start us, length us, event | category | flops | bytes accessed | tf_op | source)
XLA Modules:
  0.0 192.1 jit_solution(11482895343408975524)
XLA Ops:
  4.8 8.6 %all-to-all-start = ((s32[32,96,1]{1,2,0:T(1,128)}), s32[32,96,1]{1,2,0:T(1,128)S(1)}, u32[]{:S(2)}, u32[]{:S(2)}) async-start(s32[32,96,1]{1,2,0:T(1,128)} %all_to_all.26), calls=%async_computation | async-start | bytes 32768 | tf_op jit(solution)/shard_map/all_to_all | solution.py:59
  13.4 5.0 %multiply_reduce_fusion.2 = (f32[1024]{0:T(1024)S(1)}, f32[1024,256]{0,1:T(8,128)S(1)}) fusion(bf16[1024,256]{1,0:T(8,128)(2,1)} %param.18, bf16[1024,1024]{1,0:T(8,128)(2,1)S(1)} %copy-done, bf16[1024,1024]{1,0:T(8,128)(2,1)} %param.17), kind=kOutput, calls=%fused_computation.75 | convolution fusion | flops 2694315008 | bytes 5771264 | tf_op jit(solution)/shard_map/dot_general | solution.py:51
  19.1 3.6 %fusion.65 = bf16[3072,256]{1,0:T(8,128)(2,1)} fusion(s32[1024]{0:T(1024)S(1)} %get-tuple-element.212, f32[1024,256]{0,1:T(8,128)S(1)} %get-tuple-element.215, f32[1024]{0:T(1024)S(1)} %add_rsqrt_fusion.2), kind=kOutput, calls=%fused_computation.59 | convolution fusion | flops 1615069184 | bytes 2629632 | tf_op jit(solution)/shard_map/dot_general | solution.py:56
  22.8 7.4 %all-to-all-start.1 = ((bf16[32,96,256]{2,1,0:T(8,128)(2,1)}), bf16[32,96,256]{2,1,0:T(8,128)(2,1)S(1)}, u32[]{:S(2)}, u32[]{:S(2)}) async-start(bf16[32,96,256]{2,1,0:T(8,128)(2,1)} %bitcast.82), calls=%async_computation.1 | async-start | bytes 3145728 | tf_op jit(solution)/shard_map/all_to_all | solution.py:58
  32.7 16.6 %gather_fusion = bf16[3072,256]{1,0:T(8,128)(2,1)} fusion(bf16[16384,256]{1,0:T(8,128)(2,1)} %param.19, s32[3072]{0:T(1024)S(1)} %broadcast_clamp_fusion), kind=kCustom, calls=%fused_computation | custom fusion | bytes 3158016 | tf_op jit(solution)/shard_map/gather | solution.py:100
  49.4 3.5 %all-to-all-done.1 = bf16[32,96,256]{2,1,0:T(8,128)(2,1)S(1)} async-done(((bf16[32,96,256]{2,1,0:T(8,128)(2,1)}), bf16[32,96,256]{2,1,0:T(8,128)(2,1)S(1)}, u32[]{:S(2)}, u32[]{:S(2)}) %all-to-all-start.1) | async-done | bytes 1572896 | tf_op jit(solution)/shard_map/all_to_all | solution.py:58
  55.5 2.1 %collective-permute-start.1 = (bf16[1552,256]{1,0:T(8,128)(2,1)}, bf16[1552,256]{1,0:T(8,128)(2,1)}, u32[]{:S(2)}, u32[]{:S(2)}) collective-permute-start(bf16[1552,256]{1,0:T(8,128)(2,1)} %pad_maximum_fusion.3), channel_id=1, source_target_pairs={{0,3},{1,0},{2,1},{3,2},{4,7},{5,4},{6,5},{7,6},{8,11},{9,8},{10,9... | collective-permute-start | bytes 2383880 | tf_op jit(solution)/shard_map/ppermute | solution.py:83
  57.7 3.4 %broadcast.99.clone.2 = f32[2,3584,256]{2,1,0:T(8,128)} broadcast(f32[]{:T(128)} %constant.120.clone.1), dimensions={} | broadcast | bytes 7340036 | tf_op jit(solution)/shard_map/broadcast.4
  61.1 16.3 %while.50 = (s32[]{:T(128)}, f32[2,3584,256]{2,1,0:T(8,128)}, s32[2,3584]{1,0:T(2,128)S(1)}, s32[3072]{0:T(1024)S(1)}, bf16[3072,256]{1,0:T(8,128)(2,1)S(1)}, /*index=5*/s32[]{:T(128)}) while((s32[]{:T(128)}, f32[2,3584,256]{2,1,0:T(8,128)}, s32[2,3584]{1,0:T(2,128)S(1)}, s32[3072]{0:T(1024)S(1)}, bf16[3072,256]{1,0:T(8,128)(2,1)S(1)}, ...), condition=%wide.region_4.5_spmd, body=%wide.region_3.4_spmd.sunk | while | flops 5648154624 | bytes 5298761 | solution.py:23
  61.1 8.1 %fusion.126 = f32[2,3584,256]{2,1,0:T(8,128)} fusion(f32[2,3584,256]{2,1,0:T(8,128)} %get-tuple-element.432, s32[]{:T(128)} %get-tuple-element.431, bf16[3072,256]{1,0:T(8,128)(2,1)S(1)} %get-tuple-element.441, s32[3072]{0:T(1024)S(1)} %get-tuple-element.440, s32[3584]{0:T(1024)S(1)} %dynamic-slice_reduce_fusion.6), kind=kOutput, calls=%fused_computation.20.clone.1 | convolution fusion | flops 5648154624 | bytes 5270016 | tf_op jit(solution)/shard_map/while/body/eval_jaxpr/dot_general | solution.py:21
  69.2 8.1 %fusion.126 = f32[2,3584,256]{2,1,0:T(8,128)} fusion(f32[2,3584,256]{2,1,0:T(8,128)} %get-tuple-element.432, s32[]{:T(128)} %get-tuple-element.431, bf16[3072,256]{1,0:T(8,128)(2,1)S(1)} %get-tuple-element.441, s32[3072]{0:T(1024)S(1)} %get-tuple-element.440, s32[3584]{0:T(1024)S(1)} %dynamic-slice_reduce_fusion.6), kind=kOutput, calls=%fused_computation.20.clone.1 | convolution fusion | flops 5648154624 | bytes 5270016 | tf_op jit(solution)/shard_map/while/body/eval_jaxpr/dot_general | solution.py:21
  84.8 3.5 %broadcast.99.clone.1 = f32[2,3584,256]{2,1,0:T(8,128)} broadcast(f32[]{:T(128)} %constant.120.clone.1), dimensions={} | broadcast | bytes 7340036 | tf_op jit(solution)/shard_map/broadcast.4
  88.3 16.2 %while.51 = (s32[]{:T(128)}, f32[2,3584,256]{2,1,0:T(8,128)}, s32[2,3584]{1,0:T(2,128)S(1)}, s32[3072]{0:T(1024)S(1)}, bf16[3072,256]{1,0:T(8,128)(2,1)S(1)}, /*index=5*/s32[]{:T(128)}) while((s32[]{:T(128)}, f32[2,3584,256]{2,1,0:T(8,128)}, s32[2,3584]{1,0:T(2,128)S(1)}, s32[3072]{0:T(1024)S(1)}, bf16[3072,256]{1,0:T(8,128)(2,1)S(1)}, ...), condition=%wide.region_6.7_spmd, body=%wide.region_5.6_spmd.sunk | while | flops 5648154624 | bytes 5298761 | solution.py:23
  88.3 8.1 %fusion.129 = f32[2,3584,256]{2,1,0:T(8,128)} fusion(f32[2,3584,256]{2,1,0:T(8,128)} %get-tuple-element.414, s32[]{:T(128)} %get-tuple-element.413, bf16[3072,256]{1,0:T(8,128)(2,1)S(1)} %get-tuple-element.423, s32[3072]{0:T(1024)S(1)} %get-tuple-element.422, s32[3584]{0:T(1024)S(1)} %dynamic-slice_reduce_fusion.7), kind=kOutput, calls=%fused_computation.27.clone.1 | convolution fusion | flops 5648154624 | bytes 5270016 | tf_op jit(solution)/shard_map/while/body/eval_jaxpr/dot_general | solution.py:21
  96.5 8.0 %fusion.129 = f32[2,3584,256]{2,1,0:T(8,128)} fusion(f32[2,3584,256]{2,1,0:T(8,128)} %get-tuple-element.414, s32[]{:T(128)} %get-tuple-element.413, bf16[3072,256]{1,0:T(8,128)(2,1)S(1)} %get-tuple-element.423, s32[3072]{0:T(1024)S(1)} %get-tuple-element.422, s32[3584]{0:T(1024)S(1)} %dynamic-slice_reduce_fusion.7), kind=kOutput, calls=%fused_computation.27.clone.1 | convolution fusion | flops 5648154624 | bytes 5270016 | tf_op jit(solution)/shard_map/while/body/eval_jaxpr/dot_general | solution.py:21
  107.8 3.0 %collective-permute-start.5 = (bf16[1552,256]{1,0:T(8,128)(2,1)S(1)}, bf16[1552,256]{1,0:T(8,128)(2,1)}, u32[]{:S(2)}, u32[]{:S(2)}) collective-permute-start(bf16[1552,256]{1,0:T(8,128)(2,1)S(1)} %collective-permute-done.3), channel_id=1, source_target_pairs={{0,3},{1,0},{2,1},{3,2},{4,7},{5,4},{6,5},{7,6},{8,11},{9,8},{10,9... | collective-permute-start | bytes 2383880 | tf_op jit(solution)/shard_map/ppermute | solution.py:83
  110.8 3.4 %broadcast.99.clone = f32[2,3584,256]{2,1,0:T(8,128)} broadcast(f32[]{:T(128)} %constant.120.clone.1), dimensions={} | broadcast | bytes 7340036 | tf_op jit(solution)/shard_map/broadcast.4
  114.2 16.2 %while.52 = (s32[]{:T(128)}, f32[2,3584,256]{2,1,0:T(8,128)}, s32[2,3584]{1,0:T(2,128)S(1)}, s32[3072]{0:T(1024)S(1)}, bf16[3072,256]{1,0:T(8,128)(2,1)S(1)}, /*index=5*/s32[]{:T(128)}) while((s32[]{:T(128)}, f32[2,3584,256]{2,1,0:T(8,128)}, s32[2,3584]{1,0:T(2,128)S(1)}, s32[3072]{0:T(1024)S(1)}, bf16[3072,256]{1,0:T(8,128)(2,1)S(1)}, ...), condition=%wide.region_8.9_spmd, body=%wide.region_7.8_spmd.sunk | while | flops 5648154624 | bytes 5298761 | solution.py:23
  114.2 8.1 %fusion.132 = f32[2,3584,256]{2,1,0:T(8,128)} fusion(f32[2,3584,256]{2,1,0:T(8,128)} %get-tuple-element.396, s32[]{:T(128)} %get-tuple-element.395, bf16[3072,256]{1,0:T(8,128)(2,1)S(1)} %get-tuple-element.405, s32[3072]{0:T(1024)S(1)} %get-tuple-element.404, s32[3584]{0:T(1024)S(1)} %dynamic-slice_reduce_fusion.8), kind=kOutput, calls=%fused_computation.34.clone.1 | convolution fusion | flops 5648154624 | bytes 5270016 | tf_op jit(solution)/shard_map/while/body/eval_jaxpr/dot_general | solution.py:21
  122.3 8.1 %fusion.132 = f32[2,3584,256]{2,1,0:T(8,128)} fusion(f32[2,3584,256]{2,1,0:T(8,128)} %get-tuple-element.396, s32[]{:T(128)} %get-tuple-element.395, bf16[3072,256]{1,0:T(8,128)(2,1)S(1)} %get-tuple-element.405, s32[3072]{0:T(1024)S(1)} %get-tuple-element.404, s32[3584]{0:T(1024)S(1)} %dynamic-slice_reduce_fusion.8), kind=kOutput, calls=%fused_computation.34.clone.1 | convolution fusion | flops 5648154624 | bytes 5270016 | tf_op jit(solution)/shard_map/while/body/eval_jaxpr/dot_general | solution.py:21
  135.5 15.0 %while.54 = (s32[]{:T(128)}, f32[3,1024,256]{2,1,0:T(8,128)}, s32[3,1024]{1,0:T(4,128)}, s32[3072]{0:T(1024)S(1)}, bf16[3072,256]{1,0:T(8,128)(2,1)}, /*index=5*/s32[]{:T(128)}) while((s32[]{:T(128)}, f32[3,1024,256]{2,1,0:T(8,128)}, s32[3,1024]{1,0:T(4,128)}, s32[3072]{0:T(1024)S(1)}, bf16[3072,256]{1,0:T(8,128)(2,1)}, ...), condition=%wide.region_13.14_spmd, body=%wide.region_12.13_spmd.sunk | while | flops 1613758464 | bytes 2646601 | solution.py:23
  136.3 4.2 %fusion.138 = f32[3,1024,256]{2,1,0:T(8,128)} fusion(f32[3,1024,256]{2,1,0:T(8,128)} %get-tuple-element.450, s32[]{:T(128)} %get-tuple-element.449, bf16[3072,256]{1,0:T(8,128)(2,1)} %get-tuple-element.459, s32[3072]{0:T(1024)S(1)} %get-tuple-element.458, s32[1024]{0:T(1024)S(1)} %bitcast.86), kind=kOutput, calls=%fused_computation.13.clone.1 | convolution fusion | flops 1613758464 | bytes 2638336 | tf_op jit(solution)/shard_map/while/body/eval_jaxpr/dot_general | solution.py:21
  141.3 4.2 %fusion.138 = f32[3,1024,256]{2,1,0:T(8,128)} fusion(f32[3,1024,256]{2,1,0:T(8,128)} %get-tuple-element.450, s32[]{:T(128)} %get-tuple-element.449, bf16[3072,256]{1,0:T(8,128)(2,1)} %get-tuple-element.459, s32[3072]{0:T(1024)S(1)} %get-tuple-element.458, s32[1024]{0:T(1024)S(1)} %bitcast.86), kind=kOutput, calls=%fused_computation.13.clone.1 | convolution fusion | flops 1613758464 | bytes 2638336 | tf_op jit(solution)/shard_map/while/body/eval_jaxpr/dot_general | solution.py:21
  146.3 4.3 %fusion.138 = f32[3,1024,256]{2,1,0:T(8,128)} fusion(f32[3,1024,256]{2,1,0:T(8,128)} %get-tuple-element.450, s32[]{:T(128)} %get-tuple-element.449, bf16[3072,256]{1,0:T(8,128)(2,1)} %get-tuple-element.459, s32[3072]{0:T(1024)S(1)} %get-tuple-element.458, s32[1024]{0:T(1024)S(1)} %bitcast.86), kind=kOutput, calls=%fused_computation.13.clone.1 | convolution fusion | flops 1613758464 | bytes 2638336 | tf_op jit(solution)/shard_map/while/body/eval_jaxpr/dot_general | solution.py:21
  150.5 5.4 %multiply_reduce_fusion.1 = (f32[3072]{0:T(1024)S(1)}, f32[3072,256]{1,0:T(8,128)S(1)}) fusion(f32[3,1024,256]{2,1,0:T(8,128)} %get-tuple-element.143, f32[7168,256]{1,0:T(8,128)} %bitcast.73, f32[7168,256]{1,0:T(8,128)} %bitcast.77, f32[7168,256]{1,0:T(8,128)} %bitcast.75, bf16[3072,256]{1,0:T(8,128)(2,1)S(1)} %copy-done.2), kind=kLoop, calls=%fused_computation.65 | loop fusion | flops 5501952 | bytes 17313792 | tf_op jit(solution)/shard_map/reduce_sum | solution.py:9
  157.6 6.2 %all-to-all-start.2 = ((bf16[32,96,256]{2,1,0:T(8,128)(2,1)}), bf16[32,96,256]{2,1,0:T(8,128)(2,1)}, u32[]{:S(2)}, u32[]{:S(2)}) async-start(bf16[32,96,256]{2,1,0:T(8,128)(2,1)} %bitcast.17), calls=%async_computation.2 | async-start | bytes 3145728 | tf_op jit(solution)/shard_map/all_to_all | solution.py:110
  163.9 10.6 %while.53 = (s32[]{:T(128)}, f32[2,2048,256]{2,1,0:T(8,128)}, s32[2,2048]{1,0:T(2,128)S(1)}, s32[3072]{0:T(1024)S(1)}, bf16[3072,256]{1,0:T(8,128)(2,1)S(1)}, /*index=5*/s32[]{:T(128)}) while((s32[]{:T(128)}, f32[2,2048,256]{2,1,0:T(8,128)}, s32[2,2048]{1,0:T(2,128)S(1)}, s32[3072]{0:T(1024)S(1)}, bf16[3072,256]{1,0:T(8,128)(2,1)S(1)}, ...), condition=%wide.region_10.11_spmd, body=%wide.region_9.10_spmd.sunk | while | flops 3227516928 | bytes 3707465 | solution.py:23
  163.9 5.3 %fusion.135 = f32[2,2048,256]{2,1,0:T(8,128)} fusion(f32[2,2048,256]{2,1,0:T(8,128)} %get-tuple-element.378, s32[]{:T(128)} %get-tuple-element.377, bf16[3072,256]{1,0:T(8,128)(2,1)S(1)} %get-tuple-element.387, s32[3072]{0:T(1024)S(1)} %get-tuple-element.386, s32[2048]{0:T(1024)S(1)} %bitcast.85), kind=kOutput, calls=%fused_computation.6.clone.1 | convolution fusion | flops 3227516928 | bytes 3691008 | tf_op jit(solution)/shard_map/while/body/eval_jaxpr/dot_general | solution.py:21
  169.2 5.3 %fusion.135 = f32[2,2048,256]{2,1,0:T(8,128)} fusion(f32[2,2048,256]{2,1,0:T(8,128)} %get-tuple-element.378, s32[]{:T(128)} %get-tuple-element.377, bf16[3072,256]{1,0:T(8,128)(2,1)S(1)} %get-tuple-element.387, s32[3072]{0:T(1024)S(1)} %get-tuple-element.386, s32[2048]{0:T(1024)S(1)} %bitcast.85), kind=kOutput, calls=%fused_computation.6.clone.1 | convolution fusion | flops 3227516928 | bytes 3691008 | tf_op jit(solution)/shard_map/while/body/eval_jaxpr/dot_general | solution.py:21
  174.5 6.9 %multiply_reduce_fusion = (f32[4096]{0:T(1024)S(1)}, f32[4096,256]{1,0:T(8,128)S(1)}) fusion(f32[2,2048,256]{2,1,0:T(8,128)} %get-tuple-element.142, f32[7168,256]{1,0:T(8,128)} %bitcast.74, f32[7168,256]{1,0:T(8,128)} %bitcast.78, f32[7168,256]{1,0:T(8,128)} %bitcast.76, bf16[16384,256]{1,0:T(8,128)(2,1)} %param.19, s32[]{:T(128)S(6)} %select_n.45), kind=kLoop, calls=%fused_computation.56 | loop fusion | flops 7335936 | bytes 23085060 | tf_op jit(solution)/shard_map/reduce_sum | solution.py:9
  183.2 3.5 %all-to-all-done.2 = bf16[32,96,256]{2,1,0:T(8,128)(2,1)} async-done(((bf16[32,96,256]{2,1,0:T(8,128)(2,1)}), bf16[32,96,256]{2,1,0:T(8,128)(2,1)}, u32[]{:S(2)}, u32[]{:S(2)}) %all-to-all-start.2) | async-done | bytes 1572896 | tf_op jit(solution)/shard_map/all_to_all | solution.py:110
  186.7 4.4 %fusion.71 = bf16[1024,256]{0,1:T(8,128)(2,1)S(1)} fusion(bf16[3072,256]{1,0:T(8,128)(2,1)} %bitcast.18, s32[1024]{0:T(1024)S(1)} %copy-done.10, f32[1024,256]{0,1:T(8,128)} %copy-done.12, f32[1024]{0:T(1024)S(1)} %copy-done.8), kind=kOutput, calls=%fused_computation.71 | convolution fusion | flops 1615069184 | bytes 3153920 | tf_op jit(solution)/shard_map/dot_general | solution.py:116
  (116 shorter events, 32.7 us)
Async XLA Ops:
  0.6 12.7 %copy-start = (bf16[1024,1024]{1,0:T(8,128)(2,1)S(1)}, bf16[1024,1024]{1,0:T(8,128)(2,1)}, u32[]{:S(2)}) copy-start(bf16[1024,1024]{1,0:T(8,128)(2,1)} %param.15) | copy-start | bytes 6291460
  2.7 16.4 %copy-start.9 = (s32[1024]{0:T(1024)}, s32[1024]{0:T(1024)S(1)}, u32[]{:S(2)}) copy-start(s32[1024]{0:T(1024)S(1)} %get-tuple-element.212) | copy-start | bytes 12292
  4.8 18.0 %all-to-all-start = ((s32[32,96,1]{1,2,0:T(1,128)}), s32[32,96,1]{1,2,0:T(1,128)S(1)}, u32[]{:S(2)}, u32[]{:S(2)}) async-start(s32[32,96,1]{1,2,0:T(1,128)} %all_to_all.26), calls=%async_computation | async-start | bytes 32768 | tf_op jit(solution)/shard_map/all_to_all | solution.py:59
  18.4 4.4 %copy-start.12 = (f32[1024,256]{0,1:T(8,128)}, f32[1024,256]{0,1:T(8,128)S(1)}, u32[]{:S(2)}) copy-start(f32[1024,256]{0,1:T(8,128)S(1)} %get-tuple-element.215) | copy-start | bytes 3145732
  18.4 4.3 %copy-start.7 = (f32[1024]{0:T(1024)}, f32[1024]{0:T(1024)S(1)}, u32[]{:S(2)}) copy-start(f32[1024]{0:T(1024)S(1)} %add_rsqrt_fusion.2) | copy-start | bytes 12292
  22.8 30.1 %all-to-all-start.1 = ((bf16[32,96,256]{2,1,0:T(8,128)(2,1)}), bf16[32,96,256]{2,1,0:T(8,128)(2,1)S(1)}, u32[]{:S(2)}, u32[]{:S(2)}) async-start(bf16[32,96,256]{2,1,0:T(8,128)(2,1)} %bitcast.82), calls=%async_computation.1 | async-start | bytes 3145728 | tf_op jit(solution)/shard_map/all_to_all | solution.py:58
  53.9 24.4 %collective-permute-start = (bf16[1552,256]{1,0:T(8,128)(2,1)}, bf16[1552,256]{1,0:T(8,128)(2,1)}, u32[]{:S(2)}, u32[]{:S(2)}) collective-permute-start(bf16[1552,256]{1,0:T(8,128)(2,1)} %pad_maximum_fusion.3), channel_id=1, source_target_pairs={{0,1},{1,2},{2,3},{3,0},{4,5},{5,6},{6,7},{7,4},{8,9},{9,10},{10,1... | collective-permute-start | bytes 2383880 | tf_op jit(solution)/shard_map/ppermute | solution.py:83
  55.5 22.7 %collective-permute-start.1 = (bf16[1552,256]{1,0:T(8,128)(2,1)}, bf16[1552,256]{1,0:T(8,128)(2,1)}, u32[]{:S(2)}, u32[]{:S(2)}) collective-permute-start(bf16[1552,256]{1,0:T(8,128)(2,1)} %pad_maximum_fusion.3), channel_id=1, source_target_pairs={{0,3},{1,0},{2,1},{3,2},{4,7},{5,4},{6,5},{7,6},{8,11},{9,8},{10,9... | collective-permute-start | bytes 2383880 | tf_op jit(solution)/shard_map/ppermute | solution.py:83
  78.3 26.3 %collective-permute-start.3 = (bf16[1552,256]{1,0:T(8,128)(2,1)}, bf16[1552,256]{1,0:T(8,128)(2,1)S(1)}, u32[]{:S(2)}, u32[]{:S(2)}) collective-permute-start(bf16[1552,256]{1,0:T(8,128)(2,1)} %pad_maximum_fusion.4), channel_id=1, source_target_pairs={{0,3},{1,0},{2,1},{3,2},{4,7},{5,4},{6,5},{7,6},{8,11},{9,8},{10,9... | collective-permute-start | bytes 2383880 | tf_op jit(solution)/shard_map/ppermute | solution.py:83
  79.7 24.8 %collective-permute-start.2 = (bf16[1552,256]{1,0:T(8,128)(2,1)}, bf16[1552,256]{1,0:T(8,128)(2,1)}, u32[]{:S(2)}, u32[]{:S(2)}) collective-permute-start(bf16[1552,256]{1,0:T(8,128)(2,1)} %pad_maximum_fusion.4), channel_id=1, source_target_pairs={{0,1},{1,2},{2,3},{3,0},{4,5},{5,6},{6,7},{7,4},{8,9},{9,10},{10,1... | collective-permute-start | bytes 2383880 | tf_op jit(solution)/shard_map/ppermute | solution.py:83
  84.8 3.5 %copy-start.5 = (bf16[3072,256]{1,0:T(8,128)(2,1)S(1)}, bf16[3072,256]{1,0:T(8,128)(2,1)}, u32[]{:S(2)}) copy-start(bf16[3072,256]{1,0:T(8,128)(2,1)} %pad_maximum_fusion) | copy-start | bytes 4718596
  104.5 25.9 %collective-permute-start.4 = (bf16[1552,256]{1,0:T(8,128)(2,1)}, bf16[1552,256]{1,0:T(8,128)(2,1)}, u32[]{:S(2)}, u32[]{:S(2)}) collective-permute-start(bf16[1552,256]{1,0:T(8,128)(2,1)} %collective-permute-done), channel_id=1, source_target_pairs={{0,1},{1,2},{2,3},{3,0},{4,5},{5,6},{6,7},{7,4},{8,9},{9,10},{10,1... | collective-permute-start | bytes 2383880 | tf_op jit(solution)/shard_map/ppermute | solution.py:83
  107.8 6.4 %copy-start.4 = (bf16[3072,256]{1,0:T(8,128)(2,1)S(1)}, bf16[3072,256]{1,0:T(8,128)(2,1)}, u32[]{:S(2)}) copy-start(bf16[3072,256]{1,0:T(8,128)(2,1)} %pad_maximum_fusion.1) | copy-start | bytes 4718596
  107.8 24.5 %collective-permute-start.5 = (bf16[1552,256]{1,0:T(8,128)(2,1)S(1)}, bf16[1552,256]{1,0:T(8,128)(2,1)}, u32[]{:S(2)}, u32[]{:S(2)}) collective-permute-start(bf16[1552,256]{1,0:T(8,128)(2,1)S(1)} %collective-permute-done.3), channel_id=1, source_target_pairs={{0,3},{1,0},{2,1},{3,2},{4,7},{5,4},{6,5},{7,6},{8,11},{9,8},{10,9... | collective-permute-start | bytes 2383880 | tf_op jit(solution)/shard_map/ppermute | solution.py:83
  114.2 18.1 %copy-start.11 = (s32[3072]{0:T(1024)S(1)}, s32[3072]{0:T(1024)}, u32[]{:S(2)}) copy-start(s32[3072]{0:T(1024)} %custom-call) | copy-start | bytes 36868
  135.5 15.0 %copy-start.2 = (bf16[3072,256]{1,0:T(8,128)(2,1)S(1)}, bf16[3072,256]{1,0:T(8,128)(2,1)}, u32[]{:S(2)}) copy-start(bf16[3072,256]{1,0:T(8,128)(2,1)} %gather_fusion) | copy-start | bytes 4718596
  156.0 7.9 %copy-start.3 = (bf16[3072,256]{1,0:T(8,128)(2,1)S(1)}, bf16[3072,256]{1,0:T(8,128)(2,1)}, u32[]{:S(2)}) copy-start(bf16[3072,256]{1,0:T(8,128)(2,1)} %get-tuple-element.464) | copy-start | bytes 4718596
  156.0 7.9 %copy-start.6 = (s32[2,2048]{1,0:T(2,128)S(1)}, s32[2,2048]{1,0:T(2,128)}, u32[]{:S(2)}) copy-start(s32[2,2048]{1,0:T(2,128)} %add_add_fusion) | copy-start | bytes 49156
  157.6 29.1 %all-to-all-start.2 = ((bf16[32,96,256]{2,1,0:T(8,128)(2,1)}), bf16[32,96,256]{2,1,0:T(8,128)(2,1)}, u32[]{:S(2)}, u32[]{:S(2)}) async-start(bf16[32,96,256]{2,1,0:T(8,128)(2,1)} %bitcast.17), calls=%async_computation.2 | async-start | bytes 3145728 | tf_op jit(solution)/shard_map/all_to_all | solution.py:110
  181.5 5.2 %copy-start.8 = (f32[1024]{0:T(1024)S(1)}, f32[1024]{0:T(1024)}, u32[]{:S(2)}) copy-start(f32[1024]{0:T(1024)} %copy-done.7) | copy-start | bytes 12292
  181.5 5.2 %copy-start.10 = (s32[1024]{0:T(1024)S(1)}, s32[1024]{0:T(1024)}, u32[]{:S(2)}) copy-start(s32[1024]{0:T(1024)} %copy-done.9) | copy-start | bytes 12292
  186.7 5.4 %copy-start.1 = (bf16[1024,1024]{1,0:T(8,128)(2,1)S(1)}, bf16[1024,1024]{1,0:T(8,128)(2,1)}, u32[]{:S(2)}) copy-start(bf16[1024,1024]{1,0:T(8,128)(2,1)} %param.15) | copy-start | bytes 6291460

commit v12 on v10

--- a/solution.py
+++ b/solution.py
@@ -105,7 +105,7 @@
     sums_a = match_sums(queries, keys_a, near_a, queries.shape[0] // 2)
     sums_b = match_sums(queries, keys_b, near_b, queries.shape[0] // 2)
     look_sum = (own_sums[:slots] + sums_a[:slots] + sums_b[:slots]
-                + match_sums(in_ids, keys_far, far, 1024))
+                + match_sums(in_ids, keys_far, far, slots // 2))
     picked = normalize(look_cent.astype(jnp.float32) + look_sum)
     returned = lax.all_to_all(picked, "wide", split_axis=0, concat_axis=0, tiled=True)
 

time: 194 us -> 190 us (0.979)
  local copies, waits for them, and re-layouts: 42 us -> 39.7 us
    dynamic_slice x13 -> x12, local copies, waits for them, and re-layouts: 5.46 us -> 3.23 us  [match_sums(): return lax.map(one_block, blocks).reshape(padded, -1)[:count]]
    dot_general x13 -> x12, matrix products: 72.6 us -> 70.9 us  [one_block(): return jnp.dot(selector, rows, preferred_element_type=jnp.float32)]
  transfers between devices with their start and end apart: 9 -> 9, of which waited for: 1 -> 1; matrix products, arithmetic and copies ran while one was open for 63% -> 64% of each run, Pallas kernels for 0% -> 0%
where the time goes in v12:
time: 190 us; the launch traced here: 188 us
  matrix products  84.5 us (44%)
  local copies, waits for them, and re-layouts  39.7 us (21%)
  starting transfers between devices  30.4 us (16%)
  other arithmetic  29.2 us (15%)
  waiting for transfers between devices  3.56 us (2%)
    dot_general x12, matrix products, one_block(): return jnp.dot(selector, rows, preferred_element_type=jnp.float32)  70.9 us
    gather x1, local copies, waits for them, and re-layouts, body(): look_cent = centroids[in_ids]  16.7 us
    reduce_sum x2, other arithmetic, normalize(): jnp.mean(updated * updated, axis=-1, keepdims=True) + 1e-06  12.4 us
    another operation x3, local copies, waits for them, and re-layouts  10.3 us
    all_to_all x1, starting transfers between devices, body(): lax.all_to_all(out_ids, 'wide', split_axis=0, concat_axis=0, tiled=True)  8.57 us
    ppermute x6, starting transfers between devices, shift(): lax.ppermute(x, 'rep', [(i, (i + step) % replicas) for i in range(replica...  8.2 us
    all_to_all x1, starting transfers between devices, body(): lax.all_to_all(outgoing, 'wide', split_axis=0, concat_axis=0, tiled=True)  7.38 us
    all_to_all x1, starting transfers between devices, body(): lax.all_to_all(picked, 'wide', split_axis=0, concat_axis=0, tiled=True)  6.24 us
  transfers between devices with their start and end apart: 9, of which 1 were waited for; matrix products, arithmetic and copies ran while one was open for 64% of the time, Pallas kernels for 0%

profile of v12, /device:TPU:1, one launch (start us, length us, event | category | flops | bytes accessed | tf_op | source)
XLA Modules:
  0.0 188.4 jit_solution(13140409591829276331)
XLA Ops:
  4.8 8.6 %all-to-all-start = ((s32[32,96,1]{1,2,0:T(1,128)}), s32[32,96,1]{1,2,0:T(1,128)S(1)}, u32[]{:S(2)}, u32[]{:S(2)}) async-start(s32[32,96,1]{1,2,0:T(1,128)} %all_to_all.26), calls=%async_computation | async-start | bytes 32768 | tf_op jit(solution)/shard_map/all_to_all | solution.py:59
  13.4 5.0 %multiply_reduce_fusion.2 = (f32[1024]{0:T(1024)S(1)}, f32[1024,256]{0,1:T(8,128)S(1)}) fusion(bf16[1024,256]{1,0:T(8,128)(2,1)} %param.18, bf16[1024,1024]{1,0:T(8,128)(2,1)S(1)} %copy-done, bf16[1024,1024]{1,0:T(8,128)(2,1)} %param.17), kind=kOutput, calls=%fused_computation.75 | convolution fusion | flops 2694315008 | bytes 5771264 | tf_op jit(solution)/shard_map/dot_general | solution.py:51
  18.4 3.6 %fusion.65 = bf16[3072,256]{1,0:T(8,128)(2,1)} fusion(s32[1024]{0:T(1024)S(1)} %get-tuple-element.212, f32[1024,256]{0,1:T(8,128)S(1)} %get-tuple-element.215, f32[1024]{0:T(1024)S(1)} %add_rsqrt_fusion.2), kind=kOutput, calls=%fused_computation.59 | convolution fusion | flops 1615069184 | bytes 2629632 | tf_op jit(solution)/shard_map/dot_general | solution.py:56
  22.7 7.4 %all-to-all-start.1 = ((bf16[32,96,256]{2,1,0:T(8,128)(2,1)}), bf16[32,96,256]{2,1,0:T(8,128)(2,1)S(1)}, u32[]{:S(2)}, u32[]{:S(2)}) async-start(bf16[32,96,256]{2,1,0:T(8,128)(2,1)} %bitcast.79), calls=%async_computation.1 | async-start | bytes 3145728 | tf_op jit(solution)/shard_map/all_to_all | solution.py:58
  32.5 16.7 %gather_fusion = bf16[3072,256]{1,0:T(8,128)(2,1)} fusion(bf16[16384,256]{1,0:T(8,128)(2,1)} %param.19, s32[3072]{0:T(1024)S(1)} %broadcast_clamp_fusion), kind=kCustom, calls=%fused_computation | custom fusion | bytes 3158016 | tf_op jit(solution)/shard_map/gather | solution.py:100
  49.2 3.5 %all-to-all-done.1 = bf16[32,96,256]{2,1,0:T(8,128)(2,1)S(1)} async-done(((bf16[32,96,256]{2,1,0:T(8,128)(2,1)}), bf16[32,96,256]{2,1,0:T(8,128)(2,1)S(1)}, u32[]{:S(2)}, u32[]{:S(2)}) %all-to-all-start.1) | async-done | bytes 1572896 | tf_op jit(solution)/shard_map/all_to_all | solution.py:58
  55.4 2.1 %collective-permute-start.1 = (bf16[1552,256]{1,0:T(8,128)(2,1)}, bf16[1552,256]{1,0:T(8,128)(2,1)}, u32[]{:S(2)}, u32[]{:S(2)}) collective-permute-start(bf16[1552,256]{1,0:T(8,128)(2,1)} %pad_maximum_fusion.3), channel_id=1, source_target_pairs={{0,3},{1,0},{2,1},{3,2},{4,7},{5,4},{6,5},{7,6},{8,11},{9,8},{10,9... | collective-permute-start | bytes 2383880 | tf_op jit(solution)/shard_map/ppermute | solution.py:83
  57.6 3.4 %broadcast.99.clone.2 = f32[2,3584,256]{2,1,0:T(8,128)} broadcast(f32[]{:T(128)} %constant.120.clone.1), dimensions={} | broadcast | bytes 7340036 | tf_op jit(solution)/shard_map/broadcast.4
  61.0 16.3 %while.50 = (s32[]{:T(128)}, f32[2,3584,256]{2,1,0:T(8,128)}, s32[2,3584]{1,0:T(2,128)S(1)}, s32[3072]{0:T(1024)S(1)}, bf16[3072,256]{1,0:T(8,128)(2,1)S(1)}, /*index=5*/s32[]{:T(128)}) while((s32[]{:T(128)}, f32[2,3584,256]{2,1,0:T(8,128)}, s32[2,3584]{1,0:T(2,128)S(1)}, s32[3072]{0:T(1024)S(1)}, bf16[3072,256]{1,0:T(8,128)(2,1)S(1)}, ...), condition=%wide.region_4.5_spmd, body=%wide.region_3.4_spmd.sunk | while | flops 5648154624 | bytes 5298761 | solution.py:23
  61.0 8.1 %fusion.126 = f32[2,3584,256]{2,1,0:T(8,128)} fusion(f32[2,3584,256]{2,1,0:T(8,128)} %get-tuple-element.432, s32[]{:T(128)} %get-tuple-element.431, bf16[3072,256]{1,0:T(8,128)(2,1)S(1)} %get-tuple-element.441, s32[3072]{0:T(1024)S(1)} %get-tuple-element.440, s32[3584]{0:T(1024)S(1)} %dynamic-slice_reduce_fusion.8), kind=kOutput, calls=%fused_computation.13.clone.1 | convolution fusion | flops 5648154624 | bytes 5270016 | tf_op jit(solution)/shard_map/while/body/eval_jaxpr/dot_general | solution.py:21
  69.2 8.1 %fusion.126 = f32[2,3584,256]{2,1,0:T(8,128)} fusion(f32[2,3584,256]{2,1,0:T(8,128)} %get-tuple-element.432, s32[]{:T(128)} %get-tuple-element.431, bf16[3072,256]{1,0:T(8,128)(2,1)S(1)} %get-tuple-element.441, s32[3072]{0:T(1024)S(1)} %get-tuple-element.440, s32[3584]{0:T(1024)S(1)} %dynamic-slice_reduce_fusion.8), kind=kOutput, calls=%fused_computation.13.clone.1 | convolution fusion | flops 5648154624 | bytes 5270016 | tf_op jit(solution)/shard_map/while/body/eval_jaxpr/dot_general | solution.py:21
  84.7 3.5 %broadcast.99.clone.1 = f32[2,3584,256]{2,1,0:T(8,128)} broadcast(f32[]{:T(128)} %constant.120.clone.1), dimensions={} | broadcast | bytes 7340036 | tf_op jit(solution)/shard_map/broadcast.4
  88.2 16.2 %while.51 = (s32[]{:T(128)}, f32[2,3584,256]{2,1,0:T(8,128)}, s32[2,3584]{1,0:T(2,128)S(1)}, s32[3072]{0:T(1024)S(1)}, bf16[3072,256]{1,0:T(8,128)(2,1)S(1)}, /*index=5*/s32[]{:T(128)}) while((s32[]{:T(128)}, f32[2,3584,256]{2,1,0:T(8,128)}, s32[2,3584]{1,0:T(2,128)S(1)}, s32[3072]{0:T(1024)S(1)}, bf16[3072,256]{1,0:T(8,128)(2,1)S(1)}, ...), condition=%wide.region_6.7_spmd, body=%wide.region_5.6_spmd.sunk | while | flops 5648154624 | bytes 5298761 | solution.py:23
  88.3 8.1 %fusion.129 = f32[2,3584,256]{2,1,0:T(8,128)} fusion(f32[2,3584,256]{2,1,0:T(8,128)} %get-tuple-element.414, s32[]{:T(128)} %get-tuple-element.413, bf16[3072,256]{1,0:T(8,128)(2,1)S(1)} %get-tuple-element.423, s32[3072]{0:T(1024)S(1)} %get-tuple-element.422, s32[3584]{0:T(1024)S(1)} %dynamic-slice_reduce_fusion.9), kind=kOutput, calls=%fused_computation.20.clone.1 | convolution fusion | flops 5648154624 | bytes 5270016 | tf_op jit(solution)/shard_map/while/body/eval_jaxpr/dot_general | solution.py:21
  96.4 8.0 %fusion.129 = f32[2,3584,256]{2,1,0:T(8,128)} fusion(f32[2,3584,256]{2,1,0:T(8,128)} %get-tuple-element.414, s32[]{:T(128)} %get-tuple-element.413, bf16[3072,256]{1,0:T(8,128)(2,1)S(1)} %get-tuple-element.423, s32[3072]{0:T(1024)S(1)} %get-tuple-element.422, s32[3584]{0:T(1024)S(1)} %dynamic-slice_reduce_fusion.9), kind=kOutput, calls=%fused_computation.20.clone.1 | convolution fusion | flops 5648154624 | bytes 5270016 | tf_op jit(solution)/shard_map/while/body/eval_jaxpr/dot_general | solution.py:21
  107.7 3.0 %collective-permute-start.5 = (bf16[1552,256]{1,0:T(8,128)(2,1)S(1)}, bf16[1552,256]{1,0:T(8,128)(2,1)}, u32[]{:S(2)}, u32[]{:S(2)}) collective-permute-start(bf16[1552,256]{1,0:T(8,128)(2,1)S(1)} %collective-permute-done.3), channel_id=1, source_target_pairs={{0,3},{1,0},{2,1},{3,2},{4,7},{5,4},{6,5},{7,6},{8,11},{9,8},{10,9... | collective-permute-start | bytes 2383880 | tf_op jit(solution)/shard_map/ppermute | solution.py:83
  110.7 3.4 %broadcast.99.clone = f32[2,3584,256]{2,1,0:T(8,128)} broadcast(f32[]{:T(128)} %constant.120.clone.1), dimensions={} | broadcast | bytes 7340036 | tf_op jit(solution)/shard_map/broadcast.4
  114.1 16.2 %while.52 = (s32[]{:T(128)}, f32[2,3584,256]{2,1,0:T(8,128)}, s32[2,3584]{1,0:T(2,128)S(1)}, s32[3072]{0:T(1024)S(1)}, bf16[3072,256]{1,0:T(8,128)(2,1)S(1)}, /*index=5*/s32[]{:T(128)}) while((s32[]{:T(128)}, f32[2,3584,256]{2,1,0:T(8,128)}, s32[2,3584]{1,0:T(2,128)S(1)}, s32[3072]{0:T(1024)S(1)}, bf16[3072,256]{1,0:T(8,128)(2,1)S(1)}, ...), condition=%wide.region_8.9_spmd, body=%wide.region_7.8_spmd.sunk | while | flops 5648154624 | bytes 5298761 | solution.py:23
  114.2 8.1 %fusion.132 = f32[2,3584,256]{2,1,0:T(8,128)} fusion(f32[2,3584,256]{2,1,0:T(8,128)} %get-tuple-element.396, s32[]{:T(128)} %get-tuple-element.395, bf16[3072,256]{1,0:T(8,128)(2,1)S(1)} %get-tuple-element.405, s32[3072]{0:T(1024)S(1)} %get-tuple-element.404, s32[3584]{0:T(1024)S(1)} %dynamic-slice_reduce_fusion.10), kind=kOutput, calls=%fused_computation.27.clone.1 | convolution fusion | flops 5648154624 | bytes 5270016 | tf_op jit(solution)/shard_map/while/body/eval_jaxpr/dot_general | solution.py:21
  122.3 8.1 %fusion.132 = f32[2,3584,256]{2,1,0:T(8,128)} fusion(f32[2,3584,256]{2,1,0:T(8,128)} %get-tuple-element.396, s32[]{:T(128)} %get-tuple-element.395, bf16[3072,256]{1,0:T(8,128)(2,1)S(1)} %get-tuple-element.405, s32[3072]{0:T(1024)S(1)} %get-tuple-element.404, s32[3584]{0:T(1024)S(1)} %dynamic-slice_reduce_fusion.10), kind=kOutput, calls=%fused_computation.27.clone.1 | convolution fusion | flops 5648154624 | bytes 5270016 | tf_op jit(solution)/shard_map/while/body/eval_jaxpr/dot_general | solution.py:21
  135.5 11.1 %while.54 = (s32[]{:T(128)}, f32[2,1536,256]{2,1,0:T(8,128)}, s32[2,1536]{1,0:T(2,128)S(1)}, s32[3072]{0:T(1024)S(1)}, bf16[3072,256]{1,0:T(8,128)(2,1)}, /*index=5*/s32[]{:T(128)}) while((s32[]{:T(128)}, f32[2,1536,256]{2,1,0:T(8,128)}, s32[2,1536]{1,0:T(2,128)S(1)}, s32[3072]{0:T(1024)S(1)}, bf16[3072,256]{1,0:T(8,128)(2,1)}, ...), condition=%wide.region_13.14_spmd, body=%wide.region_12.13_spmd.sunk | while | flops 2420637696 | bytes 3177033 | solution.py:23
  135.5 5.6 %fusion.138 = f32[2,1536,256]{2,1,0:T(8,128)} fusion(f32[2,1536,256]{2,1,0:T(8,128)} %get-tuple-element.450, s32[]{:T(128)} %get-tuple-element.449, bf16[3072,256]{1,0:T(8,128)(2,1)} %get-tuple-element.459, s32[3072]{0:T(1024)S(1)} %get-tuple-element.458, s32[1536]{0:T(1024)S(1)} %dynamic-slice_reduce_fusion.11), kind=kOutput, calls=%fused_computation.34.clone.1 | convolution fusion | flops 2420637696 | bytes 3164672 | tf_op jit(solution)/shard_map/while/body/eval_jaxpr/dot_general | solution.py:21
  141.1 5.4 %fusion.138 = f32[2,1536,256]{2,1,0:T(8,128)} fusion(f32[2,1536,256]{2,1,0:T(8,128)} %get-tuple-element.450, s32[]{:T(128)} %get-tuple-element.449, bf16[3072,256]{1,0:T(8,128)(2,1)} %get-tuple-element.459, s32[3072]{0:T(1024)S(1)} %get-tuple-element.458, s32[1536]{0:T(1024)S(1)} %dynamic-slice_reduce_fusion.11), kind=kOutput, calls=%fused_computation.34.clone.1 | convolution fusion | flops 2420637696 | bytes 3164672 | tf_op jit(solution)/shard_map/while/body/eval_jaxpr/dot_general | solution.py:21
  146.6 5.4 %multiply_reduce_fusion.1 = (f32[3072]{0:T(1024)S(1)}, f32[3072,256]{1,0:T(8,128)S(1)}) fusion(f32[2,1536,256]{2,1,0:T(8,128)} %get-tuple-element.143, f32[7168,256]{1,0:T(8,128)} %bitcast.70, f32[7168,256]{1,0:T(8,128)} %bitcast.74, f32[7168,256]{1,0:T(8,128)} %bitcast.72, bf16[3072,256]{1,0:T(8,128)(2,1)S(1)} %copy-done.2), kind=kLoop, calls=%fused_computation.65 | loop fusion | flops 5501952 | bytes 17313792 | tf_op jit(solution)/shard_map/reduce_sum | solution.py:9
  153.7 6.2 %all-to-all-start.2 = ((bf16[32,96,256]{2,1,0:T(8,128)(2,1)}), bf16[32,96,256]{2,1,0:T(8,128)(2,1)}, u32[]{:S(2)}, u32[]{:S(2)}) async-start(bf16[32,96,256]{2,1,0:T(8,128)(2,1)} %bitcast.16), calls=%async_computation.2 | async-start | bytes 3145728 | tf_op jit(solution)/shard_map/all_to_all | solution.py:110
  159.9 14.4 %while.53 = (s32[]{:T(128)}, f32[4,1024,256]{2,1,0:T(8,128)}, s32[4,1024]{1,0:T(4,128)}, s32[3072]{0:T(1024)S(1)}, bf16[3072,256]{1,0:T(8,128)(2,1)S(1)}, /*index=5*/s32[]{:T(128)}) while((s32[]{:T(128)}, f32[4,1024,256]{2,1,0:T(8,128)}, s32[4,1024]{1,0:T(4,128)}, s32[3072]{0:T(1024)S(1)}, bf16[3072,256]{1,0:T(8,128)(2,1)S(1)}, ...), condition=%wide.region_10.11_spmd, body=%wide.region_9.10_spmd.sunk | while | flops 1613758464 | bytes 2646601 | solution.py:23
  160.7 2.9 %fusion.135 = f32[4,1024,256]{2,1,0:T(8,128)} fusion(f32[4,1024,256]{2,1,0:T(8,128)} %get-tuple-element.378, s32[]{:T(128)} %get-tuple-element.377, bf16[3072,256]{1,0:T(8,128)(2,1)S(1)} %get-tuple-element.387, s32[3072]{0:T(1024)S(1)} %get-tuple-element.386, s32[1024]{0:T(1024)S(1)} %bitcast.82), kind=kOutput, calls=%fused_computation.6.clone.1 | convolution fusion | flops 1613758464 | bytes 2638336 | tf_op jit(solution)/shard_map/while/body/eval_jaxpr/dot_general | solution.py:21
  164.2 2.9 %fusion.135 = f32[4,1024,256]{2,1,0:T(8,128)} fusion(f32[4,1024,256]{2,1,0:T(8,128)} %get-tuple-element.378, s32[]{:T(128)} %get-tuple-element.377, bf16[3072,256]{1,0:T(8,128)(2,1)S(1)} %get-tuple-element.387, s32[3072]{0:T(1024)S(1)} %get-tuple-element.386, s32[1024]{0:T(1024)S(1)} %bitcast.82), kind=kOutput, calls=%fused_computation.6.clone.1 | convolution fusion | flops 1613758464 | bytes 2638336 | tf_op jit(solution)/shard_map/while/body/eval_jaxpr/dot_general | solution.py:21
  167.8 2.8 %fusion.135 = f32[4,1024,256]{2,1,0:T(8,128)} fusion(f32[4,1024,256]{2,1,0:T(8,128)} %get-tuple-element.378, s32[]{:T(128)} %get-tuple-element.377, bf16[3072,256]{1,0:T(8,128)(2,1)S(1)} %get-tuple-element.387, s32[3072]{0:T(1024)S(1)} %get-tuple-element.386, s32[1024]{0:T(1024)S(1)} %bitcast.82), kind=kOutput, calls=%fused_computation.6.clone.1 | convolution fusion | flops 1613758464 | bytes 2638336 | tf_op jit(solution)/shard_map/while/body/eval_jaxpr/dot_general | solution.py:21
  171.4 2.9 %fusion.135 = f32[4,1024,256]{2,1,0:T(8,128)} fusion(f32[4,1024,256]{2,1,0:T(8,128)} %get-tuple-element.378, s32[]{:T(128)} %get-tuple-element.377, bf16[3072,256]{1,0:T(8,128)(2,1)S(1)} %get-tuple-element.387, s32[3072]{0:T(1024)S(1)} %get-tuple-element.386, s32[1024]{0:T(1024)S(1)} %bitcast.82), kind=kOutput, calls=%fused_computation.6.clone.1 | convolution fusion | flops 1613758464 | bytes 2638336 | tf_op jit(solution)/shard_map/while/body/eval_jaxpr/dot_general | solution.py:21
  174.3 6.9 %multiply_reduce_fusion = (f32[4096]{0:T(1024)S(1)}, f32[4096,256]{1,0:T(8,128)S(1)}) fusion(f32[4,1024,256]{2,1,0:T(8,128)} %get-tuple-element.142, f32[7168,256]{1,0:T(8,128)} %bitcast.71, f32[7168,256]{1,0:T(8,128)} %bitcast.75, f32[7168,256]{1,0:T(8,128)} %bitcast.73, bf16[16384,256]{1,0:T(8,128)(2,1)} %param.19, s32[]{:T(128)S(6)} %select_n.45), kind=kLoop, calls=%fused_computation.56 | loop fusion | flops 7335936 | bytes 23085060 | tf_op jit(solution)/shard_map/reduce_sum | solution.py:9
  183.0 4.4 %fusion.71 = bf16[1024,256]{0,1:T(8,128)(2,1)S(1)} fusion(bf16[3072,256]{1,0:T(8,128)(2,1)} %bitcast.17, s32[1024]{0:T(1024)S(1)} %copy-done.10, f32[1024,256]{0,1:T(8,128)} %copy-done.12, f32[1024]{0:T(1024)S(1)} %copy-done.8), kind=kOutput, calls=%fused_computation.71 | convolution fusion | flops 1615069184 | bytes 3153920 | tf_op jit(solution)/shard_map/dot_general | solution.py:116
  (118 shorter events, 33.1 us)
Async XLA Ops:
  0.6 12.7 %copy-start = (bf16[1024,1024]{1,0:T(8,128)(2,1)S(1)}, bf16[1024,1024]{1,0:T(8,128)(2,1)}, u32[]{:S(2)}) copy-start(bf16[1024,1024]{1,0:T(8,128)(2,1)} %param.15) | copy-start | bytes 6291460
  2.7 15.7 %copy-start.9 = (s32[1024]{0:T(1024)}, s32[1024]{0:T(1024)S(1)}, u32[]{:S(2)}) copy-start(s32[1024]{0:T(1024)S(1)} %get-tuple-element.212) | copy-start | bytes 12292
  4.8 17.9 %all-to-all-start = ((s32[32,96,1]{1,2,0:T(1,128)}), s32[32,96,1]{1,2,0:T(1,128)S(1)}, u32[]{:S(2)}, u32[]{:S(2)}) async-start(s32[32,96,1]{1,2,0:T(1,128)} %all_to_all.26), calls=%async_computation | async-start | bytes 32768 | tf_op jit(solution)/shard_map/all_to_all | solution.py:59
  18.4 3.7 %copy-start.12 = (f32[1024,256]{0,1:T(8,128)}, f32[1024,256]{0,1:T(8,128)S(1)}, u32[]{:S(2)}) copy-start(f32[1024,256]{0,1:T(8,128)S(1)} %get-tuple-element.215) | copy-start | bytes 3145732
  18.4 3.7 %copy-start.7 = (f32[1024]{0:T(1024)}, f32[1024]{0:T(1024)S(1)}, u32[]{:S(2)}) copy-start(f32[1024]{0:T(1024)S(1)} %add_rsqrt_fusion.2) | copy-start | bytes 12292
  22.7 30.0 %all-to-all-start.1 = ((bf16[32,96,256]{2,1,0:T(8,128)(2,1)}), bf16[32,96,256]{2,1,0:T(8,128)(2,1)S(1)}, u32[]{:S(2)}, u32[]{:S(2)}) async-start(bf16[32,96,256]{2,1,0:T(8,128)(2,1)} %bitcast.79), calls=%async_computation.1 | async-start | bytes 3145728 | tf_op jit(solution)/shard_map/all_to_all | solution.py:58
  53.8 24.4 %collective-permute-start = (bf16[1552,256]{1,0:T(8,128)(2,1)}, bf16[1552,256]{1,0:T(8,128)(2,1)}, u32[]{:S(2)}, u32[]{:S(2)}) collective-permute-start(bf16[1552,256]{1,0:T(8,128)(2,1)} %pad_maximum_fusion.3), channel_id=1, source_target_pairs={{0,1},{1,2},{2,3},{3,0},{4,5},{5,6},{6,7},{7,4},{8,9},{9,10},{10,1... | collective-permute-start | bytes 2383880 | tf_op jit(solution)/shard_map/ppermute | solution.py:83
  55.4 22.8 %collective-permute-start.1 = (bf16[1552,256]{1,0:T(8,128)(2,1)}, bf16[1552,256]{1,0:T(8,128)(2,1)}, u32[]{:S(2)}, u32[]{:S(2)}) collective-permute-start(bf16[1552,256]{1,0:T(8,128)(2,1)} %pad_maximum_fusion.3), channel_id=1, source_target_pairs={{0,3},{1,0},{2,1},{3,2},{4,7},{5,4},{6,5},{7,6},{8,11},{9,8},{10,9... | collective-permute-start | bytes 2383880 | tf_op jit(solution)/shard_map/ppermute | solution.py:83
  78.2 26.3 %collective-permute-start.3 = (bf16[1552,256]{1,0:T(8,128)(2,1)}, bf16[1552,256]{1,0:T(8,128)(2,1)S(1)}, u32[]{:S(2)}, u32[]{:S(2)}) collective-permute-start(bf16[1552,256]{1,0:T(8,128)(2,1)} %pad_maximum_fusion.4), channel_id=1, source_target_pairs={{0,3},{1,0},{2,1},{3,2},{4,7},{5,4},{6,5},{7,6},{8,11},{9,8},{10,9... | collective-permute-start | bytes 2383880 | tf_op jit(solution)/shard_map/ppermute | solution.py:83
  79.6 24.8 %collective-permute-start.2 = (bf16[1552,256]{1,0:T(8,128)(2,1)}, bf16[1552,256]{1,0:T(8,128)(2,1)}, u32[]{:S(2)}, u32[]{:S(2)}) collective-permute-start(bf16[1552,256]{1,0:T(8,128)(2,1)} %pad_maximum_fusion.4), channel_id=1, source_target_pairs={{0,1},{1,2},{2,3},{3,0},{4,5},{5,6},{6,7},{7,4},{8,9},{9,10},{10,1... | collective-permute-start | bytes 2383880 | tf_op jit(solution)/shard_map/ppermute | solution.py:83
  84.7 3.5 %copy-start.5 = (bf16[3072,256]{1,0:T(8,128)(2,1)S(1)}, bf16[3072,256]{1,0:T(8,128)(2,1)}, u32[]{:S(2)}) copy-start(bf16[3072,256]{1,0:T(8,128)(2,1)} %pad_maximum_fusion) | copy-start | bytes 4718596
  104.4 25.9 %collective-permute-start.4 = (bf16[1552,256]{1,0:T(8,128)(2,1)}, bf16[1552,256]{1,0:T(8,128)(2,1)}, u32[]{:S(2)}, u32[]{:S(2)}) collective-permute-start(bf16[1552,256]{1,0:T(8,128)(2,1)} %collective-permute-done), channel_id=1, source_target_pairs={{0,1},{1,2},{2,3},{3,0},{4,5},{5,6},{6,7},{7,4},{8,9},{9,10},{10,1... | collective-permute-start | bytes 2383880 | tf_op jit(solution)/shard_map/ppermute | solution.py:83
  107.7 6.4 %copy-start.4 = (bf16[3072,256]{1,0:T(8,128)(2,1)S(1)}, bf16[3072,256]{1,0:T(8,128)(2,1)}, u32[]{:S(2)}) copy-start(bf16[3072,256]{1,0:T(8,128)(2,1)} %pad_maximum_fusion.1) | copy-start | bytes 4718596
  107.7 24.6 %collective-permute-start.5 = (bf16[1552,256]{1,0:T(8,128)(2,1)S(1)}, bf16[1552,256]{1,0:T(8,128)(2,1)}, u32[]{:S(2)}, u32[]{:S(2)}) collective-permute-start(bf16[1552,256]{1,0:T(8,128)(2,1)S(1)} %collective-permute-done.3), channel_id=1, source_target_pairs={{0,3},{1,0},{2,1},{3,2},{4,7},{5,4},{6,5},{7,6},{8,11},{9,8},{10,9... | collective-permute-start | bytes 2383880 | tf_op jit(solution)/shard_map/ppermute | solution.py:83
  114.1 18.2 %copy-start.11 = (s32[3072]{0:T(1024)S(1)}, s32[3072]{0:T(1024)}, u32[]{:S(2)}) copy-start(s32[3072]{0:T(1024)} %custom-call) | copy-start | bytes 36868
  131.1 4.4 %copy-start.6 = (s32[2,1536]{1,0:T(2,128)S(1)}, s32[2,1536]{1,0:T(2,128)}, u32[]{:S(2)}) copy-start(s32[2,1536]{1,0:T(2,128)} %reshape.171) | copy-start | bytes 36868
  135.5 11.1 %copy-start.2 = (bf16[3072,256]{1,0:T(8,128)(2,1)S(1)}, bf16[3072,256]{1,0:T(8,128)(2,1)}, u32[]{:S(2)}) copy-start(bf16[3072,256]{1,0:T(8,128)(2,1)} %gather_fusion) | copy-start | bytes 4718596
  152.0 7.9 %copy-start.3 = (bf16[3072,256]{1,0:T(8,128)(2,1)S(1)}, bf16[3072,256]{1,0:T(8,128)(2,1)}, u32[]{:S(2)}) copy-start(bf16[3072,256]{1,0:T(8,128)(2,1)} %get-tuple-element.464) | copy-start | bytes 4718596
  153.7 29.3 %all-to-all-start.2 = ((bf16[32,96,256]{2,1,0:T(8,128)(2,1)}), bf16[32,96,256]{2,1,0:T(8,128)(2,1)}, u32[]{:S(2)}, u32[]{:S(2)}) async-start(bf16[32,96,256]{2,1,0:T(8,128)(2,1)} %bitcast.16), calls=%async_computation.2 | async-start | bytes 3145728 | tf_op jit(solution)/shard_map/all_to_all | solution.py:110
  181.3 1.7 copy-start.8
  181.3 1.7 copy-start.10
  183.0 5.4 %copy-start.1 = (bf16[1024,1024]{1,0:T(8,128)(2,1)S(1)}, bf16[1024,1024]{1,0:T(8,128)(2,1)}, u32[]{:S(2)}) copy-start(bf16[1024,1024]{1,0:T(8,128)(2,1)} %param.15) | copy-start | bytes 6291460

commit v13 on v12

--- a/solution.py
+++ b/solution.py
@@ -105,7 +105,7 @@
     sums_a = match_sums(queries, keys_a, near_a, queries.shape[0] // 2)
     sums_b = match_sums(queries, keys_b, near_b, queries.shape[0] // 2)
     look_sum = (own_sums[:slots] + sums_a[:slots] + sums_b[:slots]
-                + match_sums(in_ids, keys_far, far, slots // 2))
+                + match_sums(in_ids, keys_far, far, slots))
     picked = normalize(look_cent.astype(jnp.float32) + look_sum)
     returned = lax.all_to_all(picked, "wide", split_axis=0, concat_axis=0, tiled=True)
 

time: 190 us -> 183 us (0.963)
  other arithmetic: 29.2 us -> 23.8 us
    reduce_sum x2 -> x1, other arithmetic: 12.4 us -> 7.03 us  [normalize(): jnp.mean(updated * updated, axis=-1, keepdims=True) + 1e-06]
    dot_general x12 -> x11, matrix products: 70.9 us -> 69.8 us  [one_block(): return jnp.dot(selector, rows, preferred_element_type=jnp.float32)]
  transfers between devices with their start and end apart: 9 -> 9, of which waited for: 1 -> 1; matrix products, arithmetic and copies ran while one was open for 64% -> 66% of each run, Pallas kernels for 0% -> 0%
where the time goes in v13:
time: 183 us; the launch traced here: 182 us
  matrix products  83.4 us (46%)
  local copies, waits for them, and re-layouts  38.8 us (21%)
  starting transfers between devices  30.4 us (17%)
  other arithmetic  23.8 us (13%)
  waiting for transfers between devices  4.35 us (2%)
    dot_general x11, matrix products, one_block(): return jnp.dot(selector, rows, preferred_element_type=jnp.float32)  69.8 us
    gather x1, local copies, waits for them, and re-layouts, body(): look_cent = centroids[in_ids]  16.6 us
    another operation x3, local copies, waits for them, and re-layouts  10.2 us
    all_to_all x1, starting transfers between devices, body(): lax.all_to_all(out_ids, 'wide', split_axis=0, concat_axis=0, tiled=True)  8.57 us
    ppermute x6, starting transfers between devices, shift(): lax.ppermute(x, 'rep', [(i, (i + step) % replicas) for i in range(replica...  8.2 us
    all_to_all x1, starting transfers between devices, body(): lax.all_to_all(outgoing, 'wide', split_axis=0, concat_axis=0, tiled=True)  7.38 us
    reduce_sum x1, other arithmetic, normalize(): jnp.mean(updated * updated, axis=-1, keepdims=True) + 1e-06  7.03 us
    all_to_all x1, starting transfers between devices, body(): lax.all_to_all(picked, 'wide', split_axis=0, concat_axis=0, tiled=True)  6.24 us
  transfers between devices with their start and end apart: 9, of which 1 were waited for; matrix products, arithmetic and copies ran while one was open for 66% of the time, Pallas kernels for 0%

profile of v13, /device:TPU:1, one launch (start us, length us, event | category | flops | bytes accessed | tf_op | source)
XLA Modules:
  0.0 181.8 jit_solution(16782344150068267445)
XLA Ops:
  4.8 8.6 %all-to-all-start = ((s32[32,96,1]{1,2,0:T(1,128)}), s32[32,96,1]{1,2,0:T(1,128)S(1)}, u32[]{:S(2)}, u32[]{:S(2)}) async-start(s32[32,96,1]{1,2,0:T(1,128)} %bitcast.5), calls=%async_computation | async-start | bytes 32768 | tf_op jit(solution)/shard_map/all_to_all | solution.py:59
  13.4 5.0 %multiply_reduce_fusion.2 = (f32[1024]{0:T(1024)S(1)}, f32[1024,256]{0,1:T(8,128)S(1)}) fusion(bf16[1024,256]{1,0:T(8,128)(2,1)} %param.16, bf16[1024,1024]{1,0:T(8,128)(2,1)S(1)} %copy-done, bf16[1024,1024]{1,0:T(8,128)(2,1)} %param.15), kind=kOutput, calls=%fused_computation.72 | convolution fusion | flops 2694315008 | bytes 5771264 | tf_op jit(solution)/shard_map/dot_general | solution.py:51
  18.4 3.6 %fusion.65 = bf16[3072,256]{1,0:T(8,128)(2,1)} fusion(s32[1024]{0:T(1024)S(1)} %get-tuple-element.189, f32[1024,256]{0,1:T(8,128)S(1)} %get-tuple-element.192, f32[1024]{0:T(1024)S(1)} %add_rsqrt_fusion.2), kind=kOutput, calls=%fused_computation.58 | convolution fusion | flops 1615069184 | bytes 2629632 | tf_op jit(solution)/shard_map/dot_general | solution.py:56
  22.7 7.4 %all-to-all-start.1 = ((bf16[32,96,256]{2,1,0:T(8,128)(2,1)}), bf16[32,96,256]{2,1,0:T(8,128)(2,1)S(1)}, u32[]{:S(2)}, u32[]{:S(2)}) async-start(bf16[32,96,256]{2,1,0:T(8,128)(2,1)} %bitcast.68), calls=%async_computation.1 | async-start | bytes 3145728 | tf_op jit(solution)/shard_map/all_to_all | solution.py:58
  31.8 16.6 %gather_fusion = bf16[3072,256]{1,0:T(8,128)(2,1)} fusion(bf16[16384,256]{1,0:T(8,128)(2,1)} %param.17, s32[3072]{0:T(1024)S(1)} %broadcast_clamp_fusion), kind=kCustom, calls=%fused_computation | custom fusion | bytes 3158016 | tf_op jit(solution)/shard_map/gather | solution.py:100
  48.4 4.3 %all-to-all-done.1 = bf16[32,96,256]{2,1,0:T(8,128)(2,1)S(1)} async-done(((bf16[32,96,256]{2,1,0:T(8,128)(2,1)}), bf16[32,96,256]{2,1,0:T(8,128)(2,1)S(1)}, u32[]{:S(2)}, u32[]{:S(2)}) %all-to-all-start.1) | async-done | bytes 1572896 | tf_op jit(solution)/shard_map/all_to_all | solution.py:58
  53.8 1.6 collective-permute-start
  55.4 2.1 %collective-permute-start.1 = (bf16[1552,256]{1,0:T(8,128)(2,1)}, bf16[1552,256]{1,0:T(8,128)(2,1)}, u32[]{:S(2)}, u32[]{:S(2)}) collective-permute-start(bf16[1552,256]{1,0:T(8,128)(2,1)} %pad_maximum_fusion.3), channel_id=1, source_target_pairs={{0,3},{1,0},{2,1},{3,2},{4,7},{5,4},{6,5},{7,6},{8,11},{9,8},{10,9... | collective-permute-start | bytes 2383880 | tf_op jit(solution)/shard_map/ppermute | solution.py:83
  57.5 3.4 %broadcast.99.clone.2 = f32[2,3584,256]{2,1,0:T(8,128)} broadcast(f32[]{:T(128)} %constant.119.clone.1), dimensions={} | broadcast | bytes 7340036 | tf_op jit(solution)/shard_map/broadcast.4
  61.0 16.3 %while.44 = (s32[]{:T(128)}, f32[2,3584,256]{2,1,0:T(8,128)}, s32[2,3584]{1,0:T(2,128)S(1)}, s32[3072]{0:T(1024)S(1)}, bf16[3072,256]{1,0:T(8,128)(2,1)S(1)}, /*index=5*/s32[]{:T(128)}) while((s32[]{:T(128)}, f32[2,3584,256]{2,1,0:T(8,128)}, s32[2,3584]{1,0:T(2,128)S(1)}, s32[3072]{0:T(1024)S(1)}, bf16[3072,256]{1,0:T(8,128)(2,1)S(1)}, ...), condition=%wide.region_4.5_spmd, body=%wide.region_3.4_spmd.sunk | while | flops 5648154624 | bytes 5298761 | solution.py:23
  61.0 8.2 %fusion.119 = f32[2,3584,256]{2,1,0:T(8,128)} fusion(f32[2,3584,256]{2,1,0:T(8,128)} %get-tuple-element.380, s32[]{:T(128)} %get-tuple-element.379, bf16[3072,256]{1,0:T(8,128)(2,1)S(1)} %get-tuple-element.389, s32[3072]{0:T(1024)S(1)} %get-tuple-element.388, s32[3584]{0:T(1024)S(1)} %dynamic-slice_reduce_fusion.6), kind=kOutput, calls=%fused_computation.13.clone.1 | convolution fusion | flops 5648154624 | bytes 5270016 | tf_op jit(solution)/shard_map/while/body/eval_jaxpr/dot_general | solution.py:21
  69.2 8.1 %fusion.119 = f32[2,3584,256]{2,1,0:T(8,128)} fusion(f32[2,3584,256]{2,1,0:T(8,128)} %get-tuple-element.380, s32[]{:T(128)} %get-tuple-element.379, bf16[3072,256]{1,0:T(8,128)(2,1)S(1)} %get-tuple-element.389, s32[3072]{0:T(1024)S(1)} %get-tuple-element.388, s32[3584]{0:T(1024)S(1)} %dynamic-slice_reduce_fusion.6), kind=kOutput, calls=%fused_computation.13.clone.1 | convolution fusion | flops 5648154624 | bytes 5270016 | tf_op jit(solution)/shard_map/while/body/eval_jaxpr/dot_general | solution.py:21
  84.8 3.4 %broadcast.99.clone.1 = f32[2,3584,256]{2,1,0:T(8,128)} broadcast(f32[]{:T(128)} %constant.119.clone.1), dimensions={} | broadcast | bytes 7340036 | tf_op jit(solution)/shard_map/broadcast.4
  88.2 16.2 %while.45 = (s32[]{:T(128)}, f32[2,3584,256]{2,1,0:T(8,128)}, s32[2,3584]{1,0:T(2,128)S(1)}, s32[3072]{0:T(1024)S(1)}, bf16[3072,256]{1,0:T(8,128)(2,1)S(1)}, /*index=5*/s32[]{:T(128)}) while((s32[]{:T(128)}, f32[2,3584,256]{2,1,0:T(8,128)}, s32[2,3584]{1,0:T(2,128)S(1)}, s32[3072]{0:T(1024)S(1)}, bf16[3072,256]{1,0:T(8,128)(2,1)S(1)}, ...), condition=%wide.region_6.7_spmd, body=%wide.region_5.6_spmd.sunk | while | flops 5648154624 | bytes 5298761 | solution.py:23
  88.2 8.0 %fusion.122 = f32[2,3584,256]{2,1,0:T(8,128)} fusion(f32[2,3584,256]{2,1,0:T(8,128)} %get-tuple-element.362, s32[]{:T(128)} %get-tuple-element.361, bf16[3072,256]{1,0:T(8,128)(2,1)S(1)} %get-tuple-element.371, s32[3072]{0:T(1024)S(1)} %get-tuple-element.370, s32[3584]{0:T(1024)S(1)} %dynamic-slice_reduce_fusion.7), kind=kOutput, calls=%fused_computation.20.clone.1 | convolution fusion | flops 5648154624 | bytes 5270016 | tf_op jit(solution)/shard_map/while/body/eval_jaxpr/dot_general | solution.py:21
  96.3 8.1 %fusion.122 = f32[2,3584,256]{2,1,0:T(8,128)} fusion(f32[2,3584,256]{2,1,0:T(8,128)} %get-tuple-element.362, s32[]{:T(128)} %get-tuple-element.361, bf16[3072,256]{1,0:T(8,128)(2,1)S(1)} %get-tuple-element.371, s32[3072]{0:T(1024)S(1)} %get-tuple-element.370, s32[3584]{0:T(1024)S(1)} %dynamic-slice_reduce_fusion.7), kind=kOutput, calls=%fused_computation.20.clone.1 | convolution fusion | flops 5648154624 | bytes 5270016 | tf_op jit(solution)/shard_map/while/body/eval_jaxpr/dot_general | solution.py:21
  107.7 3.0 %collective-permute-start.5 = (bf16[1552,256]{1,0:T(8,128)(2,1)S(1)}, bf16[1552,256]{1,0:T(8,128)(2,1)}, u32[]{:S(2)}, u32[]{:S(2)}) collective-permute-start(bf16[1552,256]{1,0:T(8,128)(2,1)S(1)} %collective-permute-done.3), channel_id=1, source_target_pairs={{0,3},{1,0},{2,1},{3,2},{4,7},{5,4},{6,5},{7,6},{8,11},{9,8},{10,9... | collective-permute-start | bytes 2383880 | tf_op jit(solution)/shard_map/ppermute | solution.py:83
  110.6 3.4 %broadcast.99.clone = f32[2,3584,256]{2,1,0:T(8,128)} broadcast(f32[]{:T(128)} %constant.119.clone.1), dimensions={} | broadcast | bytes 7340036 | tf_op jit(solution)/shard_map/broadcast.4
  114.1 16.3 %while.46 = (s32[]{:T(128)}, f32[2,3584,256]{2,1,0:T(8,128)}, s32[2,3584]{1,0:T(2,128)S(1)}, s32[3072]{0:T(1024)S(1)}, bf16[3072,256]{1,0:T(8,128)(2,1)S(1)}, /*index=5*/s32[]{:T(128)}) while((s32[]{:T(128)}, f32[2,3584,256]{2,1,0:T(8,128)}, s32[2,3584]{1,0:T(2,128)S(1)}, s32[3072]{0:T(1024)S(1)}, bf16[3072,256]{1,0:T(8,128)(2,1)S(1)}, ...), condition=%wide.region_8.9_spmd, body=%wide.region_7.8_spmd.sunk | while | flops 5648154624 | bytes 5298761 | solution.py:23
  114.1 8.1 %fusion.125 = f32[2,3584,256]{2,1,0:T(8,128)} fusion(f32[2,3584,256]{2,1,0:T(8,128)} %get-tuple-element.344, s32[]{:T(128)} %get-tuple-element.343, bf16[3072,256]{1,0:T(8,128)(2,1)S(1)} %get-tuple-element.353, s32[3072]{0:T(1024)S(1)} %get-tuple-element.352, s32[3584]{0:T(1024)S(1)} %dynamic-slice_reduce_fusion.8), kind=kOutput, calls=%fused_computation.27.clone.1 | convolution fusion | flops 5648154624 | bytes 5270016 | tf_op jit(solution)/shard_map/while/body/eval_jaxpr/dot_general | solution.py:21
  122.3 8.1 %fusion.125 = f32[2,3584,256]{2,1,0:T(8,128)} fusion(f32[2,3584,256]{2,1,0:T(8,128)} %get-tuple-element.344, s32[]{:T(128)} %get-tuple-element.343, bf16[3072,256]{1,0:T(8,128)(2,1)S(1)} %get-tuple-element.353, s32[3072]{0:T(1024)S(1)} %get-tuple-element.352, s32[3584]{0:T(1024)S(1)} %dynamic-slice_reduce_fusion.8), kind=kOutput, calls=%fused_computation.27.clone.1 | convolution fusion | flops 5648154624 | bytes 5270016 | tf_op jit(solution)/shard_map/while/body/eval_jaxpr/dot_general | solution.py:21
  135.5 9.9 %multiply_reduce_fusion.1 = (f32[3072]{0:T(1024)S(1)}, f32[3072,256]{1,0:T(8,128)S(1)}) fusion(bf16[1536,256]{1,0:T(8,128)(2,1)S(1)} %slice.214, bf16[1536,256]{1,0:T(8,128)(2,1)S(1)} %slice.213, s32[3072]{0:T(1024)S(1)} %constant_dynamic-update-slice_fusion, s32[3072]{0:T(1024)S(1)} %get-tuple-element.399, f32[7168,256]{1,0:T(8,128)} %bitcast.59, ...), kind=kOutput, calls=%fused_computation.62 | convolution fusion | flops 4849923072 | bytes 15765504 | tf_op jit(solution)/shard_map/while/body/eval_jaxpr/dot_general | solution.py:21
  145.4 1.6 multiply_convert_fusion.1
  147.0 6.2 %all-to-all-start.2 = ((bf16[32,96,256]{2,1,0:T(8,128)(2,1)}), bf16[32,96,256]{2,1,0:T(8,128)(2,1)}, u32[]{:S(2)}, u32[]{:S(2)}) async-start(bf16[32,96,256]{2,1,0:T(8,128)(2,1)} %bitcast.15), calls=%async_computation.2 | async-start | bytes 3145728 | tf_op jit(solution)/shard_map/all_to_all | solution.py:110
  153.3 14.3 %while.47 = (s32[]{:T(128)}, f32[4,1024,256]{2,1,0:T(8,128)}, s32[4,1024]{1,0:T(4,128)}, s32[3072]{0:T(1024)S(1)}, bf16[3072,256]{1,0:T(8,128)(2,1)S(1)}, /*index=5*/s32[]{:T(128)}) while((s32[]{:T(128)}, f32[4,1024,256]{2,1,0:T(8,128)}, s32[4,1024]{1,0:T(4,128)}, s32[3072]{0:T(1024)S(1)}, bf16[3072,256]{1,0:T(8,128)(2,1)S(1)}, ...), condition=%wide.region_10.11_spmd, body=%wide.region_9.10_spmd.sunk | while | flops 1613758464 | bytes 2646601 | solution.py:23
  154.0 2.9 %fusion.128 = f32[4,1024,256]{2,1,0:T(8,128)} fusion(f32[4,1024,256]{2,1,0:T(8,128)} %get-tuple-element.326, s32[]{:T(128)} %get-tuple-element.325, bf16[3072,256]{1,0:T(8,128)(2,1)S(1)} %get-tuple-element.335, s32[3072]{0:T(1024)S(1)} %get-tuple-element.334, s32[1024]{0:T(1024)S(1)} %bitcast.70), kind=kOutput, calls=%fused_computation.6.clone.1 | convolution fusion | flops 1613758464 | bytes 2638336 | tf_op jit(solution)/shard_map/while/body/eval_jaxpr/dot_general | solution.py:21
  157.6 2.9 %fusion.128 = f32[4,1024,256]{2,1,0:T(8,128)} fusion(f32[4,1024,256]{2,1,0:T(8,128)} %get-tuple-element.326, s32[]{:T(128)} %get-tuple-element.325, bf16[3072,256]{1,0:T(8,128)(2,1)S(1)} %get-tuple-element.335, s32[3072]{0:T(1024)S(1)} %get-tuple-element.334, s32[1024]{0:T(1024)S(1)} %bitcast.70), kind=kOutput, calls=%fused_computation.6.clone.1 | convolution fusion | flops 1613758464 | bytes 2638336 | tf_op jit(solution)/shard_map/while/body/eval_jaxpr/dot_general | solution.py:21
  161.2 2.8 %fusion.128 = f32[4,1024,256]{2,1,0:T(8,128)} fusion(f32[4,1024,256]{2,1,0:T(8,128)} %get-tuple-element.326, s32[]{:T(128)} %get-tuple-element.325, bf16[3072,256]{1,0:T(8,128)(2,1)S(1)} %get-tuple-element.335, s32[3072]{0:T(1024)S(1)} %get-tuple-element.334, s32[1024]{0:T(1024)S(1)} %bitcast.70), kind=kOutput, calls=%fused_computation.6.clone.1 | convolution fusion | flops 1613758464 | bytes 2638336 | tf_op jit(solution)/shard_map/while/body/eval_jaxpr/dot_general | solution.py:21
  164.8 2.8 %fusion.128 = f32[4,1024,256]{2,1,0:T(8,128)} fusion(f32[4,1024,256]{2,1,0:T(8,128)} %get-tuple-element.326, s32[]{:T(128)} %get-tuple-element.325, bf16[3072,256]{1,0:T(8,128)(2,1)S(1)} %get-tuple-element.335, s32[3072]{0:T(1024)S(1)} %get-tuple-element.334, s32[1024]{0:T(1024)S(1)} %bitcast.70), kind=kOutput, calls=%fused_computation.6.clone.1 | convolution fusion | flops 1613758464 | bytes 2638336 | tf_op jit(solution)/shard_map/while/body/eval_jaxpr/dot_general | solution.py:21
  167.6 7.0 %multiply_reduce_fusion = (f32[4096]{0:T(1024)S(1)}, f32[4096,256]{1,0:T(8,128)S(1)}) fusion(f32[4,1024,256]{2,1,0:T(8,128)} %get-tuple-element.130, f32[7168,256]{1,0:T(8,128)} %bitcast.60, f32[7168,256]{1,0:T(8,128)} %bitcast.64, f32[7168,256]{1,0:T(8,128)} %bitcast.62, bf16[16384,256]{1,0:T(8,128)(2,1)} %param.17, s32[]{:T(128)S(6)} %select_n.45), kind=kLoop, calls=%fused_computation.53 | loop fusion | flops 7335936 | bytes 23085060 | tf_op jit(solution)/shard_map/reduce_sum | solution.py:9
  174.7 1.7 multiply_convert_fusion
  176.4 4.4 %fusion.69 = bf16[1024,256]{0,1:T(8,128)(2,1)S(1)} fusion(bf16[3072,256]{1,0:T(8,128)(2,1)} %bitcast.16, s32[1024]{0:T(1024)S(1)} %copy-done.8, f32[1024,256]{0,1:T(8,128)} %copy-done.10, f32[1024]{0:T(1024)S(1)} %copy-done.6), kind=kOutput, calls=%fused_computation.68 | convolution fusion | flops 1615069184 | bytes 3153920 | tf_op jit(solution)/shard_map/dot_general | solution.py:116
  (107 shorter events, 27.4 us)
Async XLA Ops:
  0.6 12.7 %copy-start = (bf16[1024,1024]{1,0:T(8,128)(2,1)S(1)}, bf16[1024,1024]{1,0:T(8,128)(2,1)}, u32[]{:S(2)}) copy-start(bf16[1024,1024]{1,0:T(8,128)(2,1)} %param.13) | copy-start | bytes 6291460
  2.7 15.7 %copy-start.7 = (s32[1024]{0:T(1024)}, s32[1024]{0:T(1024)S(1)}, u32[]{:S(2)}) copy-start(s32[1024]{0:T(1024)S(1)} %get-tuple-element.189) | copy-start | bytes 12292
  4.8 17.9 %all-to-all-start = ((s32[32,96,1]{1,2,0:T(1,128)}), s32[32,96,1]{1,2,0:T(1,128)S(1)}, u32[]{:S(2)}, u32[]{:S(2)}) async-start(s32[32,96,1]{1,2,0:T(1,128)} %bitcast.5), calls=%async_computation | async-start | bytes 32768 | tf_op jit(solution)/shard_map/all_to_all | solution.py:59
  18.3 3.7 %copy-start.10 = (f32[1024,256]{0,1:T(8,128)}, f32[1024,256]{0,1:T(8,128)S(1)}, u32[]{:S(2)}) copy-start(f32[1024,256]{0,1:T(8,128)S(1)} %get-tuple-element.192) | copy-start | bytes 3145732
  18.4 3.7 %copy-start.5 = (f32[1024]{0:T(1024)}, f32[1024]{0:T(1024)S(1)}, u32[]{:S(2)}) copy-start(f32[1024]{0:T(1024)S(1)} %add_rsqrt_fusion.2) | copy-start | bytes 12292
  22.7 30.1 %all-to-all-start.1 = ((bf16[32,96,256]{2,1,0:T(8,128)(2,1)}), bf16[32,96,256]{2,1,0:T(8,128)(2,1)S(1)}, u32[]{:S(2)}, u32[]{:S(2)}) async-start(bf16[32,96,256]{2,1,0:T(8,128)(2,1)} %bitcast.68), calls=%async_computation.1 | async-start | bytes 3145728 | tf_op jit(solution)/shard_map/all_to_all | solution.py:58
  53.8 24.5 %collective-permute-start = (bf16[1552,256]{1,0:T(8,128)(2,1)}, bf16[1552,256]{1,0:T(8,128)(2,1)}, u32[]{:S(2)}, u32[]{:S(2)}) collective-permute-start(bf16[1552,256]{1,0:T(8,128)(2,1)} %pad_maximum_fusion.3), channel_id=1, source_target_pairs={{0,1},{1,2},{2,3},{3,0},{4,5},{5,6},{6,7},{7,4},{8,9},{9,10},{10,1... | collective-permute-start | bytes 2383880 | tf_op jit(solution)/shard_map/ppermute | solution.py:83
  55.4 22.8 %collective-permute-start.1 = (bf16[1552,256]{1,0:T(8,128)(2,1)}, bf16[1552,256]{1,0:T(8,128)(2,1)}, u32[]{:S(2)}, u32[]{:S(2)}) collective-permute-start(bf16[1552,256]{1,0:T(8,128)(2,1)} %pad_maximum_fusion.3), channel_id=1, source_target_pairs={{0,3},{1,0},{2,1},{3,2},{4,7},{5,4},{6,5},{7,6},{8,11},{9,8},{10,9... | collective-permute-start | bytes 2383880 | tf_op jit(solution)/shard_map/ppermute | solution.py:83
  78.3 26.2 %collective-permute-start.3 = (bf16[1552,256]{1,0:T(8,128)(2,1)}, bf16[1552,256]{1,0:T(8,128)(2,1)S(1)}, u32[]{:S(2)}, u32[]{:S(2)}) collective-permute-start(bf16[1552,256]{1,0:T(8,128)(2,1)} %pad_maximum_fusion.4), channel_id=1, source_target_pairs={{0,3},{1,0},{2,1},{3,2},{4,7},{5,4},{6,5},{7,6},{8,11},{9,8},{10,9... | collective-permute-start | bytes 2383880 | tf_op jit(solution)/shard_map/ppermute | solution.py:83
  79.7 24.7 %collective-permute-start.2 = (bf16[1552,256]{1,0:T(8,128)(2,1)}, bf16[1552,256]{1,0:T(8,128)(2,1)}, u32[]{:S(2)}, u32[]{:S(2)}) collective-permute-start(bf16[1552,256]{1,0:T(8,128)(2,1)} %pad_maximum_fusion.4), channel_id=1, source_target_pairs={{0,1},{1,2},{2,3},{3,0},{4,5},{5,6},{6,7},{7,4},{8,9},{9,10},{10,1... | collective-permute-start | bytes 2383880 | tf_op jit(solution)/shard_map/ppermute | solution.py:83
  84.8 3.4 %copy-start.4 = (bf16[3072,256]{1,0:T(8,128)(2,1)S(1)}, bf16[3072,256]{1,0:T(8,128)(2,1)}, u32[]{:S(2)}) copy-start(bf16[3072,256]{1,0:T(8,128)(2,1)} %pad_maximum_fusion) | copy-start | bytes 4718596
  104.4 26.0 %collective-permute-start.4 = (bf16[1552,256]{1,0:T(8,128)(2,1)}, bf16[1552,256]{1,0:T(8,128)(2,1)}, u32[]{:S(2)}, u32[]{:S(2)}) collective-permute-start(bf16[1552,256]{1,0:T(8,128)(2,1)} %collective-permute-done), channel_id=1, source_target_pairs={{0,1},{1,2},{2,3},{3,0},{4,5},{5,6},{6,7},{7,4},{8,9},{9,10},{10,1... | collective-permute-start | bytes 2383880 | tf_op jit(solution)/shard_map/ppermute | solution.py:83
  107.7 6.4 %copy-start.3 = (bf16[3072,256]{1,0:T(8,128)(2,1)S(1)}, bf16[3072,256]{1,0:T(8,128)(2,1)}, u32[]{:S(2)}) copy-start(bf16[3072,256]{1,0:T(8,128)(2,1)} %pad_maximum_fusion.1) | copy-start | bytes 4718596
  107.7 24.6 %collective-permute-start.5 = (bf16[1552,256]{1,0:T(8,128)(2,1)S(1)}, bf16[1552,256]{1,0:T(8,128)(2,1)}, u32[]{:S(2)}, u32[]{:S(2)}) collective-permute-start(bf16[1552,256]{1,0:T(8,128)(2,1)S(1)} %collective-permute-done.3), channel_id=1, source_target_pairs={{0,3},{1,0},{2,1},{3,2},{4,7},{5,4},{6,5},{7,6},{8,11},{9,8},{10,9... | collective-permute-start | bytes 2383880 | tf_op jit(solution)/shard_map/ppermute | solution.py:83
  114.1 18.2 %copy-start.9 = (s32[3072]{0:T(1024)S(1)}, s32[3072]{0:T(1024)}, u32[]{:S(2)}) copy-start(s32[3072]{0:T(1024)} %custom-call) | copy-start | bytes 36868
  145.4 7.9 %copy-start.2 = (bf16[3072,256]{1,0:T(8,128)(2,1)S(1)}, bf16[3072,256]{1,0:T(8,128)(2,1)}, u32[]{:S(2)}) copy-start(bf16[3072,256]{1,0:T(8,128)(2,1)} %pad_maximum_fusion.2) | copy-start | bytes 4718596
  147.0 29.3 %all-to-all-start.2 = ((bf16[32,96,256]{2,1,0:T(8,128)(2,1)}), bf16[32,96,256]{2,1,0:T(8,128)(2,1)}, u32[]{:S(2)}, u32[]{:S(2)}) async-start(bf16[32,96,256]{2,1,0:T(8,128)(2,1)} %bitcast.15), calls=%async_computation.2 | async-start | bytes 3145728 | tf_op jit(solution)/shard_map/all_to_all | solution.py:110
  174.7 1.7 copy-start.6
  174.7 1.7 copy-start.8
  176.4 5.4 %copy-start.1 = (bf16[1024,1024]{1,0:T(8,128)(2,1)S(1)}, bf16[1024,1024]{1,0:T(8,128)(2,1)}, u32[]{:S(2)}) copy-start(bf16[1024,1024]{1,0:T(8,128)(2,1)} %param.13) | copy-start | bytes 6291460

commit v14 on v13

--- a/solution.py
+++ b/solution.py
@@ -110,7 +110,7 @@
     returned = lax.all_to_all(picked, "wide", split_axis=0, concat_axis=0, tiled=True)
 
     share_sum = (own_sums[slots:] + sums_a[slots:] + sums_b[slots:]
-                 + match_sums(share_ids, keys_far, far, 1024))
+                 + match_sums(share_ids, keys_far, far, share_rows // 2))
     own_rows = normalize(own_cent.astype(jnp.float32) + share_sum)
 
     gathered_rows = jnp.dot(place_bf.T, returned, preferred_element_type=jnp.float32)

time: 183 us -> 183 us (level)
  waiting for transfers between devices: 4.35 us -> 7.92 us
  local copies, waits for them, and re-layouts: 38.8 us -> 35.9 us
    all_to_all x1, waiting for transfers between devices: 0.01 us -> 3.52 us  [body(): lax.all_to_all(picked, 'wide', split_axis=0, concat_axis=0, tiled=True)]
    dynamic_slice x10 -> x8, local copies, waits for them, and re-layouts: 3.18 us -> 0.3 us  [match_sums(): return lax.map(one_block, blocks).reshape(padded, -1)[:count]]
    dot_general x11 -> x9, matrix products: 69.8 us -> 68.9 us  [one_block(): return jnp.dot(selector, rows, preferred_element_type=jnp.float32)]
  transfers between devices with their start and end apart: 9 -> 9, of which waited for: 1 -> 2; matrix products, arithmetic and copies ran while one was open for 66% -> 64% of each run, Pallas kernels for 0% -> 0%
where the time goes in v14:
time: 183 us; the launch traced here: 182 us
  matrix products  82.5 us (45%)
  local copies, waits for them, and re-layouts  35.9 us (20%)
  starting transfers between devices  30.4 us (17%)
  other arithmetic  23.8 us (13%)
  waiting for transfers between devices  7.92 us (4%)
    dot_general x9, matrix products, one_block(): return jnp.dot(selector, rows, preferred_element_type=jnp.float32)  68.9 us
    gather x1, local copies, waits for them, and re-layouts, body(): look_cent = centroids[in_ids]  16.7 us
    another operation x3, local copies, waits for them, and re-layouts  10.2 us
    all_to_all x1, starting transfers between devices, body(): lax.all_to_all(out_ids, 'wide', split_axis=0, concat_axis=0, tiled=True)  8.57 us
    ppermute x6, starting transfers between devices, shift(): lax.ppermute(x, 'rep', [(i, (i + step) % replicas) for i in range(replica...  8.2 us
    all_to_all x1, starting transfers between devices, body(): lax.all_to_all(outgoing, 'wide', split_axis=0, concat_axis=0, tiled=True)  7.4 us
    reduce_sum x1, other arithmetic, normalize(): jnp.mean(updated * updated, axis=-1, keepdims=True) + 1e-06  6.99 us
    all_to_all x1, starting transfers between devices, body(): lax.all_to_all(picked, 'wide', split_axis=0, concat_axis=0, tiled=True)  6.24 us
  transfers between devices with their start and end apart: 9, of which 2 were waited for; matrix products, arithmetic and copies ran while one was open for 64% of the time, Pallas kernels for 0%

profile of v14, /device:TPU:1, one launch (start us, length us, event | category | flops | bytes accessed | tf_op | source)
XLA Modules:
  0.0 181.6 jit_solution(18006801077388109748)
XLA Ops:
  4.8 8.6 %all-to-all-start = ((s32[32,96,1]{1,2,0:T(1,128)}), s32[32,96,1]{1,2,0:T(1,128)S(1)}, u32[]{:S(2)}, u32[]{:S(2)}) async-start(s32[32,96,1]{1,2,0:T(1,128)} %bitcast.5), calls=%async_computation | async-start | bytes 32768 | tf_op jit(solution)/shard_map/all_to_all | solution.py:59
  13.4 5.0 %multiply_reduce_fusion.2 = (f32[1024]{0:T(1024)S(1)}, f32[1024,256]{0,1:T(8,128)S(1)}) fusion(bf16[1024,256]{1,0:T(8,128)(2,1)} %param.16, bf16[1024,1024]{1,0:T(8,128)(2,1)S(1)} %copy-done, bf16[1024,1024]{1,0:T(8,128)(2,1)} %param.15), kind=kOutput, calls=%fused_computation.72 | convolution fusion | flops 2694315008 | bytes 5771264 | tf_op jit(solution)/shard_map/dot_general | solution.py:51
  19.1 3.6 %fusion.65 = bf16[3072,256]{1,0:T(8,128)(2,1)} fusion(s32[1024]{0:T(1024)S(1)} %get-tuple-element.189, f32[1024,256]{0,1:T(8,128)S(1)} %get-tuple-element.192, f32[1024]{0:T(1024)S(1)} %add_rsqrt_fusion.2), kind=kOutput, calls=%fused_computation.58 | convolution fusion | flops 1615069184 | bytes 2629632 | tf_op jit(solution)/shard_map/dot_general | solution.py:56
  22.8 7.4 %all-to-all-start.1 = ((bf16[32,96,256]{2,1,0:T(8,128)(2,1)}), bf16[32,96,256]{2,1,0:T(8,128)(2,1)S(1)}, u32[]{:S(2)}, u32[]{:S(2)}) async-start(bf16[32,96,256]{2,1,0:T(8,128)(2,1)} %bitcast.68), calls=%async_computation.1 | async-start | bytes 3145728 | tf_op jit(solution)/shard_map/all_to_all | solution.py:58
  31.8 16.7 %gather_fusion = bf16[3072,256]{1,0:T(8,128)(2,1)} fusion(bf16[16384,256]{1,0:T(8,128)(2,1)} %param.17, s32[3072]{0:T(1024)S(1)} %broadcast_clamp_fusion), kind=kCustom, calls=%fused_computation | custom fusion | bytes 3158016 | tf_op jit(solution)/shard_map/gather | solution.py:100
  48.4 4.4 %all-to-all-done.1 = bf16[32,96,256]{2,1,0:T(8,128)(2,1)S(1)} async-done(((bf16[32,96,256]{2,1,0:T(8,128)(2,1)}), bf16[32,96,256]{2,1,0:T(8,128)(2,1)S(1)}, u32[]{:S(2)}, u32[]{:S(2)}) %all-to-all-start.1) | async-done | bytes 1572896 | tf_op jit(solution)/shard_map/all_to_all | solution.py:58
  53.9 1.6 collective-permute-start
  55.5 2.1 %collective-permute-start.1 = (bf16[1552,256]{1,0:T(8,128)(2,1)}, bf16[1552,256]{1,0:T(8,128)(2,1)}, u32[]{:S(2)}, u32[]{:S(2)}) collective-permute-start(bf16[1552,256]{1,0:T(8,128)(2,1)} %pad_maximum_fusion.3), channel_id=1, source_target_pairs={{0,3},{1,0},{2,1},{3,2},{4,7},{5,4},{6,5},{7,6},{8,11},{9,8},{10,9... | collective-permute-start | bytes 2383880 | tf_op jit(solution)/shard_map/ppermute | solution.py:83
  57.6 3.4 %broadcast.99.clone.2 = f32[2,3584,256]{2,1,0:T(8,128)} broadcast(f32[]{:T(128)} %constant.119.clone.1), dimensions={} | broadcast | bytes 7340036 | tf_op jit(solution)/shard_map/broadcast.4
  61.1 16.4 %while.44 = (s32[]{:T(128)}, f32[2,3584,256]{2,1,0:T(8,128)}, s32[2,3584]{1,0:T(2,128)S(1)}, s32[3072]{0:T(1024)S(1)}, bf16[3072,256]{1,0:T(8,128)(2,1)S(1)}, /*index=5*/s32[]{:T(128)}) while((s32[]{:T(128)}, f32[2,3584,256]{2,1,0:T(8,128)}, s32[2,3584]{1,0:T(2,128)S(1)}, s32[3072]{0:T(1024)S(1)}, bf16[3072,256]{1,0:T(8,128)(2,1)S(1)}, ...), condition=%wide.region_4.5_spmd, body=%wide.region_3.4_spmd.sunk | while | flops 5648154624 | bytes 5298761 | solution.py:23
  61.1 8.2 %fusion.119 = f32[2,3584,256]{2,1,0:T(8,128)} fusion(f32[2,3584,256]{2,1,0:T(8,128)} %get-tuple-element.380, s32[]{:T(128)} %get-tuple-element.379, bf16[3072,256]{1,0:T(8,128)(2,1)S(1)} %get-tuple-element.389, s32[3072]{0:T(1024)S(1)} %get-tuple-element.388, s32[3584]{0:T(1024)S(1)} %dynamic-slice_reduce_fusion.6), kind=kOutput, calls=%fused_computation.13.clone.1 | convolution fusion | flops 5648154624 | bytes 5270016 | tf_op jit(solution)/shard_map/while/body/eval_jaxpr/dot_general | solution.py:21
  69.3 8.1 %fusion.119 = f32[2,3584,256]{2,1,0:T(8,128)} fusion(f32[2,3584,256]{2,1,0:T(8,128)} %get-tuple-element.380, s32[]{:T(128)} %get-tuple-element.379, bf16[3072,256]{1,0:T(8,128)(2,1)S(1)} %get-tuple-element.389, s32[3072]{0:T(1024)S(1)} %get-tuple-element.388, s32[3584]{0:T(1024)S(1)} %dynamic-slice_reduce_fusion.6), kind=kOutput, calls=%fused_computation.13.clone.1 | convolution fusion | flops 5648154624 | bytes 5270016 | tf_op jit(solution)/shard_map/while/body/eval_jaxpr/dot_general | solution.py:21
  78.4 1.5 collective-permute-start.3
  84.9 3.4 %broadcast.99.clone.1 = f32[2,3584,256]{2,1,0:T(8,128)} broadcast(f32[]{:T(128)} %constant.119.clone.1), dimensions={} | broadcast | bytes 7340036 | tf_op jit(solution)/shard_map/broadcast.4
  88.3 16.2 %while.45 = (s32[]{:T(128)}, f32[2,3584,256]{2,1,0:T(8,128)}, s32[2,3584]{1,0:T(2,128)S(1)}, s32[3072]{0:T(1024)S(1)}, bf16[3072,256]{1,0:T(8,128)(2,1)S(1)}, /*index=5*/s32[]{:T(128)}) while((s32[]{:T(128)}, f32[2,3584,256]{2,1,0:T(8,128)}, s32[2,3584]{1,0:T(2,128)S(1)}, s32[3072]{0:T(1024)S(1)}, bf16[3072,256]{1,0:T(8,128)(2,1)S(1)}, ...), condition=%wide.region_6.7_spmd, body=%wide.region_5.6_spmd.sunk | while | flops 5648154624 | bytes 5298761 | solution.py:23
  88.4 8.1 %fusion.122 = f32[2,3584,256]{2,1,0:T(8,128)} fusion(f32[2,3584,256]{2,1,0:T(8,128)} %get-tuple-element.362, s32[]{:T(128)} %get-tuple-element.361, bf16[3072,256]{1,0:T(8,128)(2,1)S(1)} %get-tuple-element.371, s32[3072]{0:T(1024)S(1)} %get-tuple-element.370, s32[3584]{0:T(1024)S(1)} %dynamic-slice_reduce_fusion.7), kind=kOutput, calls=%fused_computation.20.clone.1 | convolution fusion | flops 5648154624 | bytes 5270016 | tf_op jit(solution)/shard_map/while/body/eval_jaxpr/dot_general | solution.py:21
  96.5 8.1 %fusion.122 = f32[2,3584,256]{2,1,0:T(8,128)} fusion(f32[2,3584,256]{2,1,0:T(8,128)} %get-tuple-element.362, s32[]{:T(128)} %get-tuple-element.361, bf16[3072,256]{1,0:T(8,128)(2,1)S(1)} %get-tuple-element.371, s32[3072]{0:T(1024)S(1)} %get-tuple-element.370, s32[3584]{0:T(1024)S(1)} %dynamic-slice_reduce_fusion.7), kind=kOutput, calls=%fused_computation.20.clone.1 | convolution fusion | flops 5648154624 | bytes 5270016 | tf_op jit(solution)/shard_map/while/body/eval_jaxpr/dot_general | solution.py:21
  107.8 3.0 %collective-permute-start.5 = (bf16[1552,256]{1,0:T(8,128)(2,1)S(1)}, bf16[1552,256]{1,0:T(8,128)(2,1)}, u32[]{:S(2)}, u32[]{:S(2)}) collective-permute-start(bf16[1552,256]{1,0:T(8,128)(2,1)S(1)} %collective-permute-done.3), channel_id=1, source_target_pairs={{0,3},{1,0},{2,1},{3,2},{4,7},{5,4},{6,5},{7,6},{8,11},{9,8},{10,9... | collective-permute-start | bytes 2383880 | tf_op jit(solution)/shard_map/ppermute | solution.py:83
  110.8 3.4 %broadcast.99.clone = f32[2,3584,256]{2,1,0:T(8,128)} broadcast(f32[]{:T(128)} %constant.119.clone.1), dimensions={} | broadcast | bytes 7340036 | tf_op jit(solution)/shard_map/broadcast.4
  114.2 16.3 %while.46 = (s32[]{:T(128)}, f32[2,3584,256]{2,1,0:T(8,128)}, s32[2,3584]{1,0:T(2,128)S(1)}, s32[3072]{0:T(1024)S(1)}, bf16[3072,256]{1,0:T(8,128)(2,1)S(1)}, /*index=5*/s32[]{:T(128)}) while((s32[]{:T(128)}, f32[2,3584,256]{2,1,0:T(8,128)}, s32[2,3584]{1,0:T(2,128)S(1)}, s32[3072]{0:T(1024)S(1)}, bf16[3072,256]{1,0:T(8,128)(2,1)S(1)}, ...), condition=%wide.region_8.9_spmd, body=%wide.region_7.8_spmd.sunk | while | flops 5648154624 | bytes 5298761 | solution.py:23
  114.2 8.1 %fusion.125 = f32[2,3584,256]{2,1,0:T(8,128)} fusion(f32[2,3584,256]{2,1,0:T(8,128)} %get-tuple-element.344, s32[]{:T(128)} %get-tuple-element.343, bf16[3072,256]{1,0:T(8,128)(2,1)S(1)} %get-tuple-element.353, s32[3072]{0:T(1024)S(1)} %get-tuple-element.352, s32[3584]{0:T(1024)S(1)} %dynamic-slice_reduce_fusion.8), kind=kOutput, calls=%fused_computation.27.clone.1 | convolution fusion | flops 5648154624 | bytes 5270016 | tf_op jit(solution)/shard_map/while/body/eval_jaxpr/dot_general | solution.py:21
  122.4 8.1 %fusion.125 = f32[2,3584,256]{2,1,0:T(8,128)} fusion(f32[2,3584,256]{2,1,0:T(8,128)} %get-tuple-element.344, s32[]{:T(128)} %get-tuple-element.343, bf16[3072,256]{1,0:T(8,128)(2,1)S(1)} %get-tuple-element.353, s32[3072]{0:T(1024)S(1)} %get-tuple-element.352, s32[3584]{0:T(1024)S(1)} %dynamic-slice_reduce_fusion.8), kind=kOutput, calls=%fused_computation.27.clone.1 | convolution fusion | flops 5648154624 | bytes 5270016 | tf_op jit(solution)/shard_map/while/body/eval_jaxpr/dot_general | solution.py:21
  135.6 9.9 %multiply_reduce_fusion.1 = (f32[3072]{0:T(1024)S(1)}, f32[3072,256]{1,0:T(8,128)S(1)}) fusion(bf16[1536,256]{1,0:T(8,128)(2,1)S(1)} %slice.214, bf16[1536,256]{1,0:T(8,128)(2,1)S(1)} %slice.213, s32[3072]{0:T(1024)S(1)} %constant_dynamic-update-slice_fusion, s32[3072]{0:T(1024)S(1)} %get-tuple-element.399, f32[7168,256]{1,0:T(8,128)} %bitcast.59, ...), kind=kOutput, calls=%fused_computation.62 | convolution fusion | flops 4849923072 | bytes 15765504 | tf_op jit(solution)/shard_map/while/body/eval_jaxpr/dot_general | solution.py:21
  145.5 1.6 multiply_convert_fusion.1
  147.1 6.2 %all-to-all-start.2 = ((bf16[32,96,256]{2,1,0:T(8,128)(2,1)}), bf16[32,96,256]{2,1,0:T(8,128)(2,1)}, u32[]{:S(2)}, u32[]{:S(2)}) async-start(bf16[32,96,256]{2,1,0:T(8,128)(2,1)} %bitcast.15), calls=%async_computation.2 | async-start | bytes 3145728 | tf_op jit(solution)/shard_map/all_to_all | solution.py:110
  153.4 10.5 %while.47 = (s32[]{:T(128)}, f32[2,2048,256]{2,1,0:T(8,128)}, s32[2,2048]{1,0:T(2,128)S(1)}, s32[3072]{0:T(1024)S(1)}, bf16[3072,256]{1,0:T(8,128)(2,1)S(1)}, /*index=5*/s32[]{:T(128)}) while((s32[]{:T(128)}, f32[2,2048,256]{2,1,0:T(8,128)}, s32[2,2048]{1,0:T(2,128)S(1)}, s32[3072]{0:T(1024)S(1)}, bf16[3072,256]{1,0:T(8,128)(2,1)S(1)}, ...), condition=%wide.region_10.11_spmd, body=%wide.region_9.10_spmd.sunk | while | flops 3227516928 | bytes 3707465 | solution.py:23
  153.4 5.3 %fusion.128 = f32[2,2048,256]{2,1,0:T(8,128)} fusion(f32[2,2048,256]{2,1,0:T(8,128)} %get-tuple-element.326, s32[]{:T(128)} %get-tuple-element.325, bf16[3072,256]{1,0:T(8,128)(2,1)S(1)} %get-tuple-element.335, s32[3072]{0:T(1024)S(1)} %get-tuple-element.334, s32[2048]{0:T(1024)S(1)} %bitcast.70), kind=kOutput, calls=%fused_computation.6.clone.1 | convolution fusion | flops 3227516928 | bytes 3691008 | tf_op jit(solution)/shard_map/while/body/eval_jaxpr/dot_general | solution.py:21
  158.7 5.2 %fusion.128 = f32[2,2048,256]{2,1,0:T(8,128)} fusion(f32[2,2048,256]{2,1,0:T(8,128)} %get-tuple-element.326, s32[]{:T(128)} %get-tuple-element.325, bf16[3072,256]{1,0:T(8,128)(2,1)S(1)} %get-tuple-element.335, s32[3072]{0:T(1024)S(1)} %get-tuple-element.334, s32[2048]{0:T(1024)S(1)} %bitcast.70), kind=kOutput, calls=%fused_computation.6.clone.1 | convolution fusion | flops 3227516928 | bytes 3691008 | tf_op jit(solution)/shard_map/while/body/eval_jaxpr/dot_general | solution.py:21
  164.0 7.0 %multiply_reduce_fusion = (f32[4096]{0:T(1024)S(1)}, f32[4096,256]{1,0:T(8,128)S(1)}) fusion(f32[2,2048,256]{2,1,0:T(8,128)} %get-tuple-element.130, f32[7168,256]{1,0:T(8,128)} %bitcast.60, f32[7168,256]{1,0:T(8,128)} %bitcast.64, f32[7168,256]{1,0:T(8,128)} %bitcast.62, bf16[16384,256]{1,0:T(8,128)(2,1)} %param.17, s32[]{:T(128)S(6)} %select_n.45), kind=kLoop, calls=%fused_computation.53 | loop fusion | flops 7335936 | bytes 23085060 | tf_op jit(solution)/shard_map/reduce_sum | solution.py:9
  171.0 1.7 multiply_convert_fusion
  172.7 3.5 %all-to-all-done.2 = bf16[32,96,256]{2,1,0:T(8,128)(2,1)} async-done(((bf16[32,96,256]{2,1,0:T(8,128)(2,1)}), bf16[32,96,256]{2,1,0:T(8,128)(2,1)}, u32[]{:S(2)}, u32[]{:S(2)}) %all-to-all-start.2) | async-done | bytes 1572896 | tf_op jit(solution)/shard_map/all_to_all | solution.py:110
  176.2 4.4 %fusion.69 = bf16[1024,256]{0,1:T(8,128)(2,1)S(1)} fusion(bf16[3072,256]{1,0:T(8,128)(2,1)} %bitcast.16, s32[1024]{0:T(1024)S(1)} %copy-done.9, f32[1024,256]{0,1:T(8,128)} %copy-done.11, f32[1024]{0:T(1024)S(1)} %copy-done.7), kind=kOutput, calls=%fused_computation.68 | convolution fusion | flops 1615069184 | bytes 3153920 | tf_op jit(solution)/shard_map/dot_general | solution.py:116
  (105 shorter events, 23.1 us)
Async XLA Ops:
  0.6 12.7 %copy-start = (bf16[1024,1024]{1,0:T(8,128)(2,1)S(1)}, bf16[1024,1024]{1,0:T(8,128)(2,1)}, u32[]{:S(2)}) copy-start(bf16[1024,1024]{1,0:T(8,128)(2,1)} %param.13) | copy-start | bytes 6291460
  2.7 16.3 %copy-start.8 = (s32[1024]{0:T(1024)}, s32[1024]{0:T(1024)S(1)}, u32[]{:S(2)}) copy-start(s32[1024]{0:T(1024)S(1)} %get-tuple-element.189) | copy-start | bytes 12292
  4.8 18.0 %all-to-all-start = ((s32[32,96,1]{1,2,0:T(1,128)}), s32[32,96,1]{1,2,0:T(1,128)S(1)}, u32[]{:S(2)}, u32[]{:S(2)}) async-start(s32[32,96,1]{1,2,0:T(1,128)} %bitcast.5), calls=%async_computation | async-start | bytes 32768 | tf_op jit(solution)/shard_map/all_to_all | solution.py:59
  18.3 4.4 %copy-start.11 = (f32[1024,256]{0,1:T(8,128)}, f32[1024,256]{0,1:T(8,128)S(1)}, u32[]{:S(2)}) copy-start(f32[1024,256]{0,1:T(8,128)S(1)} %get-tuple-element.192) | copy-start | bytes 3145732
  18.4 4.4 %copy-start.6 = (f32[1024]{0:T(1024)}, f32[1024]{0:T(1024)S(1)}, u32[]{:S(2)}) copy-start(f32[1024]{0:T(1024)S(1)} %add_rsqrt_fusion.2) | copy-start | bytes 12292
  22.8 30.1 %all-to-all-start.1 = ((bf16[32,96,256]{2,1,0:T(8,128)(2,1)}), bf16[32,96,256]{2,1,0:T(8,128)(2,1)S(1)}, u32[]{:S(2)}, u32[]{:S(2)}) async-start(bf16[32,96,256]{2,1,0:T(8,128)(2,1)} %bitcast.68), calls=%async_computation.1 | async-start | bytes 3145728 | tf_op jit(solution)/shard_map/all_to_all | solution.py:58
  53.9 24.5 %collective-permute-start = (bf16[1552,256]{1,0:T(8,128)(2,1)}, bf16[1552,256]{1,0:T(8,128)(2,1)}, u32[]{:S(2)}, u32[]{:S(2)}) collective-permute-start(bf16[1552,256]{1,0:T(8,128)(2,1)} %pad_maximum_fusion.3), channel_id=1, source_target_pairs={{0,1},{1,2},{2,3},{3,0},{4,5},{5,6},{6,7},{7,4},{8,9},{9,10},{10,1... | collective-permute-start | bytes 2383880 | tf_op jit(solution)/shard_map/ppermute | solution.py:83
  55.5 22.9 %collective-permute-start.1 = (bf16[1552,256]{1,0:T(8,128)(2,1)}, bf16[1552,256]{1,0:T(8,128)(2,1)}, u32[]{:S(2)}, u32[]{:S(2)}) collective-permute-start(bf16[1552,256]{1,0:T(8,128)(2,1)} %pad_maximum_fusion.3), channel_id=1, source_target_pairs={{0,3},{1,0},{2,1},{3,2},{4,7},{5,4},{6,5},{7,6},{8,11},{9,8},{10,9... | collective-permute-start | bytes 2383880 | tf_op jit(solution)/shard_map/ppermute | solution.py:83
  78.4 26.2 %collective-permute-start.3 = (bf16[1552,256]{1,0:T(8,128)(2,1)}, bf16[1552,256]{1,0:T(8,128)(2,1)S(1)}, u32[]{:S(2)}, u32[]{:S(2)}) collective-permute-start(bf16[1552,256]{1,0:T(8,128)(2,1)} %pad_maximum_fusion.4), channel_id=1, source_target_pairs={{0,3},{1,0},{2,1},{3,2},{4,7},{5,4},{6,5},{7,6},{8,11},{9,8},{10,9... | collective-permute-start | bytes 2383880 | tf_op jit(solution)/shard_map/ppermute | solution.py:83
  79.8 24.7 %collective-permute-start.2 = (bf16[1552,256]{1,0:T(8,128)(2,1)}, bf16[1552,256]{1,0:T(8,128)(2,1)}, u32[]{:S(2)}, u32[]{:S(2)}) collective-permute-start(bf16[1552,256]{1,0:T(8,128)(2,1)} %pad_maximum_fusion.4), channel_id=1, source_target_pairs={{0,1},{1,2},{2,3},{3,0},{4,5},{5,6},{6,7},{7,4},{8,9},{9,10},{10,1... | collective-permute-start | bytes 2383880 | tf_op jit(solution)/shard_map/ppermute | solution.py:83
  84.9 3.4 %copy-start.4 = (bf16[3072,256]{1,0:T(8,128)(2,1)S(1)}, bf16[3072,256]{1,0:T(8,128)(2,1)}, u32[]{:S(2)}) copy-start(bf16[3072,256]{1,0:T(8,128)(2,1)} %pad_maximum_fusion) | copy-start | bytes 4718596
  104.5 26.0 %collective-permute-start.4 = (bf16[1552,256]{1,0:T(8,128)(2,1)}, bf16[1552,256]{1,0:T(8,128)(2,1)}, u32[]{:S(2)}, u32[]{:S(2)}) collective-permute-start(bf16[1552,256]{1,0:T(8,128)(2,1)} %collective-permute-done), channel_id=1, source_target_pairs={{0,1},{1,2},{2,3},{3,0},{4,5},{5,6},{6,7},{7,4},{8,9},{9,10},{10,1... | collective-permute-start | bytes 2383880 | tf_op jit(solution)/shard_map/ppermute | solution.py:83
  107.8 6.4 %copy-start.3 = (bf16[3072,256]{1,0:T(8,128)(2,1)S(1)}, bf16[3072,256]{1,0:T(8,128)(2,1)}, u32[]{:S(2)}) copy-start(bf16[3072,256]{1,0:T(8,128)(2,1)} %pad_maximum_fusion.1) | copy-start | bytes 4718596
  107.8 24.6 %collective-permute-start.5 = (bf16[1552,256]{1,0:T(8,128)(2,1)S(1)}, bf16[1552,256]{1,0:T(8,128)(2,1)}, u32[]{:S(2)}, u32[]{:S(2)}) collective-permute-start(bf16[1552,256]{1,0:T(8,128)(2,1)S(1)} %collective-permute-done.3), channel_id=1, source_target_pairs={{0,3},{1,0},{2,1},{3,2},{4,7},{5,4},{6,5},{7,6},{8,11},{9,8},{10,9... | collective-permute-start | bytes 2383880 | tf_op jit(solution)/shard_map/ppermute | solution.py:83
  114.2 18.2 %copy-start.10 = (s32[3072]{0:T(1024)S(1)}, s32[3072]{0:T(1024)}, u32[]{:S(2)}) copy-start(s32[3072]{0:T(1024)} %custom-call) | copy-start | bytes 36868
  145.5 7.9 %copy-start.2 = (bf16[3072,256]{1,0:T(8,128)(2,1)S(1)}, bf16[3072,256]{1,0:T(8,128)(2,1)}, u32[]{:S(2)}) copy-start(bf16[3072,256]{1,0:T(8,128)(2,1)} %pad_maximum_fusion.2) | copy-start | bytes 4718596
  145.5 7.9 %copy-start.5 = (s32[2,2048]{1,0:T(2,128)S(1)}, s32[2,2048]{1,0:T(2,128)}, u32[]{:S(2)}) copy-start(s32[2,2048]{1,0:T(2,128)} %add_add_fusion) | copy-start | bytes 49156
  147.1 29.0 %all-to-all-start.2 = ((bf16[32,96,256]{2,1,0:T(8,128)(2,1)}), bf16[32,96,256]{2,1,0:T(8,128)(2,1)}, u32[]{:S(2)}, u32[]{:S(2)}) async-start(bf16[32,96,256]{2,1,0:T(8,128)(2,1)} %bitcast.15), calls=%async_computation.2 | async-start | bytes 3145728 | tf_op jit(solution)/shard_map/all_to_all | solution.py:110
  171.0 5.2 %copy-start.7 = (f32[1024]{0:T(1024)S(1)}, f32[1024]{0:T(1024)}, u32[]{:S(2)}) copy-start(f32[1024]{0:T(1024)} %copy-done.6) | copy-start | bytes 12292
  171.0 5.2 %copy-start.9 = (s32[1024]{0:T(1024)S(1)}, s32[1024]{0:T(1024)}, u32[]{:S(2)}) copy-start(s32[1024]{0:T(1024)} %copy-done.8) | copy-start | bytes 12292
  176.2 5.4 %copy-start.1 = (bf16[1024,1024]{1,0:T(8,128)(2,1)S(1)}, bf16[1024,1024]{1,0:T(8,128)(2,1)}, u32[]{:S(2)}) copy-start(bf16[1024,1024]{1,0:T(8,128)(2,1)} %param.13) | copy-start | bytes 6291460
